TPU v7x, 128 devices: a whole 4x4x4 slice. The times are simulated.
128 devices in a mesh: seq: 16 (over z, y), tp: 8 (over x, core).
Axes of the slice: x: 4, y: 4, z: 4, core: 2. Of those that a mesh axis runs over, the one named last changes fastest.
Arguments:
- tokens: bfloat16 [8192, 3072], P('seq'), may hold values from -6 to 6
- norm_gain: bfloat16 [3072], replicated, may hold values from 0.099609375 to 1.8984375
- w_qkv: bfloat16 [3072, 3, 3072], P(None, None, 'tp'), may hold values from -0.25 to 0.25
- w_out: bfloat16 [3072, 3072], P('tp'), may hold values from -0.0546875 to 0.0546875
- kv_cache: bfloat16 [2, 16, 3584, 3072], P(None, 'seq', None, 'tp')
- cached_lengths: int32 [16], replicated, may hold values from 128 to 3584, as said below
- requests: int32 [16], replicated, may hold values from 8 to 16
- block_start: int32 [16], replicated, may hold values from 0 to 31
Outputs:
- layer_out: bfloat16 [8192, 3072], P(('seq', 'tp'))
- decode_cache: bfloat16 [2, 16, 16, 1, 128, 6144], P(None, 'seq', None, None, None, 'tp')
Inputs may be any that keep to these rules, and one draw needn't show every extreme that they name: `cached_lengths`: every entry is a multiple of 128, and some group has exactly 3584 cached positions.
All inputs are finite; a program needn't handle non-finite values.
Results may differ from a plain program's by a relative error of at most 0.014.
The roundings to bfloat16 on the way count: a program that leaves them out, or rounds other values in their place, can miss the bound.
Values may be sent and summed in bfloat16 or wider, within the bound.
No kernel may reach another device: no remote copies, remote signals or barrier semaphores. Data moves between devices by JAX's collectives and lax.ppermute only.
A program may use at most 192 MiB of HBM per device.

v0:
```python
import math

import jax
import jax.numpy as jnp
from jax import lax
from jax.sharding import PartitionSpec as P

HD = 96
BLK = 128


def from_partner(value, axis, apart):
    mask = 2**apart
    pairs = [(source, source ^ mask) for source in range(lax.axis_size(axis))]
    return lax.ppermute(value, axis, pairs)


def rope_tables(positions, head_size):
    half_size = head_size // 2
    frequency = jnp.exp(
        jnp.arange(half_size, dtype=jnp.float32) * (-2.0 * math.log(10000.0) / head_size)
    )
    angles = positions.astype(jnp.float32)[:, None] * frequency[None, :]
    return (jnp.cos(angles), jnp.sin(angles))


def rope_pair(vectors, cosine_table, sine_table):
    half_size = vectors.shape[-1] // 2
    first_half = vectors[..., :half_size]
    second_half = vectors[..., half_size:]
    cos_wide = cosine_table[:, None, :]
    sin_wide = sine_table[:, None, :]
    return jnp.concatenate(
        [
            first_half * cos_wide - second_half * sin_wide,
            second_half * cos_wide + first_half * sin_wide,
        ],
        axis=-1,
    )


def visibility(group_len, group_requests, row_index, request, key_pos, tok_count):
    offset_rows = key_pos - group_len
    new_key = (offset_rows >= 0) & (offset_rows < tok_count)
    clipped = jnp.clip(offset_rows, 0, tok_count - 1)
    key_request = clipped * group_requests // tok_count
    return (key_pos[None, :] < group_len) | new_key[None, :] & (
        key_request[None, :] == request[:, None]
    ) & (clipped[None, :] <= row_index[:, None])


def attend(queries, full_cache, group_len, group_requests, request, tok_count, head_count):
    context = full_cache.shape[1]
    features = full_cache.shape[2]
    key_heads = full_cache[0].reshape(context, head_count, HD)
    value_heads = full_cache[1].reshape(context, head_count, HD)
    key_pos = jnp.arange(context, dtype=jnp.int32)
    score_scale = 1.0 / math.sqrt(HD)
    block_rows = min(tok_count, 512)
    row_index = 0 + jnp.arange(block_rows, dtype=jnp.int32)
    scores = (
        jnp.einsum("qhd,khd->hqk", queries, key_heads, preferred_element_type=jnp.float32)
        * score_scale
    )
    visible = visibility(group_len, group_requests, row_index, request, key_pos, tok_count)
    masked = jnp.where(visible[None], scores, -1e30)
    row_peak = jnp.max(masked, axis=-1, keepdims=True)
    weights = jnp.exp(masked - row_peak)
    probabilities = (weights / jnp.sum(weights, axis=-1, keepdims=True)).astype(jnp.bfloat16)
    mixed_rows = jnp.einsum(
        "hqk,khd->qhd", probabilities, value_heads, preferred_element_type=jnp.float32
    ).astype(jnp.bfloat16)
    outputs = mixed_rows.reshape(block_rows, features)
    return outputs


def relay_cache(full_cache, group_start, tp_rank, seq_count):
    context = full_cache.shape[1]
    features = full_cache.shape[2]
    rank_count = 2 * seq_count
    slot_count = context // (BLK * rank_count)
    blocks = full_cache.reshape(2, slot_count, rank_count, BLK, features)
    doubled = jnp.concatenate([blocks, blocks], axis=2)
    rotated = lax.dynamic_slice_in_dim(
        doubled, (rank_count - group_start) % rank_count, rank_count, 2
    )
    block_grid = rotated.reshape(2, slot_count, seq_count, 2, BLK, features).transpose(
        0, 2, 1, 3, 4, 5
    )
    member = tp_rank % 2
    own_part = lax.dynamic_index_in_dim(block_grid, member, 3, keepdims=False)
    other_part = lax.dynamic_index_in_dim(block_grid, 1 - member, 3, keepdims=False)
    partner = from_partner(other_part, "tp", 0)
    lower_half = jnp.where(member == 0, own_part, partner)
    upper_half = jnp.where(member == 0, partner, own_part)
    joined = jnp.concatenate([lower_half, upper_half], axis=-1)
    joined = lax.all_to_all(joined, "seq", split_axis=1, concat_axis=1, tiled=True)
    return joined[:, None]


def local(tokens, norm_gain, w_qkv, w_out, kv_cache, cached_lengths, requests, block_start):
    group_idx = lax.axis_index("seq")
    tp_rank = lax.axis_index("tp")
    tp_count = lax.axis_size("tp")
    seq_count = lax.axis_size("seq")
    tok_count, model_width = tokens.shape
    features = w_qkv.shape[2]
    head_count = features // HD
    cache_len = kv_cache.shape[2]
    group_len = lax.dynamic_index_in_dim(cached_lengths, group_idx, keepdims=False)
    group_requests = lax.dynamic_index_in_dim(requests, group_idx, keepdims=False)
    group_start = lax.dynamic_index_in_dim(block_start, group_idx, keepdims=False)
    inputs = tokens.astype(jnp.float32)
    inverse_rms = lax.rsqrt(jnp.mean(inputs * inputs, axis=-1, keepdims=True) + 1e-05)
    normed = (inputs * inverse_rms * norm_gain.astype(jnp.float32)).astype(jnp.bfloat16)
    projected = jnp.dot(
        normed, w_qkv.reshape(model_width, 3 * features), preferred_element_type=jnp.float32
    )
    projected = projected.reshape(tok_count, 3, head_count, HD)
    row_index = jnp.arange(tok_count, dtype=jnp.int32)
    request = row_index * group_requests // tok_count
    first_row = (request * tok_count + group_requests - 1) // group_requests
    positions = group_len + row_index - first_row
    cosine_table, sine_table = rope_tables(positions, HD)
    queries = rope_pair(projected[:, 0], cosine_table, sine_table).astype(jnp.bfloat16)
    new_keys = (
        rope_pair(projected[:, 1], cosine_table, sine_table)
        .astype(jnp.bfloat16)
        .reshape(tok_count, features)
    )
    new_values = projected[:, 2].astype(jnp.bfloat16).reshape(tok_count, features)
    old_cache = kv_cache[:, 0]
    cache_pos = jnp.arange(cache_len, dtype=jnp.int32)
    kept_cache = jnp.where(
        (cache_pos < group_len)[None, :, None], old_cache, jnp.zeros((), jnp.bfloat16)
    )
    padded = jnp.concatenate(
        [kept_cache, jnp.zeros((2, tok_count, features), jnp.bfloat16)], axis=1
    )
    zero_index = jnp.zeros((), jnp.int32)
    full_cache = lax.dynamic_update_slice(
        padded, jnp.stack([new_keys, new_values]), (zero_index, group_len, zero_index)
    )
    attended = attend(
        queries, full_cache, group_len, group_requests, request, tok_count, head_count
    )
    decode_cache = relay_cache(full_cache, group_start, tp_rank, seq_count)
    rows_dev = tok_count // tp_count
    summed = lax.psum_scatter(
        jnp.dot(attended, w_out, preferred_element_type=jnp.float32).astype(jnp.bfloat16),
        "tp",
        scatter_dimension=0,
        tiled=True,
    ).astype(jnp.float32)
    own_rows = lax.dynamic_slice_in_dim(inputs, tp_rank * rows_dev, rows_dev, 0)
    layer_out = (own_rows + summed).astype(jnp.bfloat16)
    return (layer_out, decode_cache)


def solution(mesh):
    placed = (
        P("seq", None),
        P(),
        P(None, None, "tp"),
        P("tp", None),
        P(None, "seq", None, "tp"),
        P(),
        P(),
        P(),
    )
    return jax.shard_map(
        local,
        mesh=mesh,
        in_specs=placed,
        out_specs=(P(("seq", "tp"), None), P(None, "seq", None, None, None, "tp")),
        check_vma=False,
    )
```

profile of v0, /device:TPU:0, one launch (start us, length us, event | category | flops | bytes accessed | tf_op | source)
XLA Modules:
  0.0 278.6 jit_solution(2900629396211322099)
XLA Ops:
  7.2 0.0 copy-start
  7.2 0.0 reduce-scatter.2.cloned.1.call-start
  7.2 10.4 %copy.25 = bf16[3072,3,384]{0,2,1:T(8,128)(2,1)} copy(bf16[3072,3,384]{2,0,1:T(8,128)(2,1)} %param.10) | data formatting | bytes 14155776 | tf_op args[2]
  17.7 2.6 multiply_reduce_fusion
  20.3 0.0 copy-start.6
  20.3 0.0 copy-start.7
  20.3 0.0 copy-start.8
  20.3 7.2 %fusion.12 = f32[512,3,4,96]{0,3,2,1:T(8,128)S(1)} fusion(bf16[3,4,96,3072]{3,2,1,0:T(8,128)(2,1)} %bitcast.46, f32[3072]{0:T(1024)S(1)} %convert_element_type.58, f32[512]{0:T(512)S(1)} %add_rsqrt_fusion, bf16[512,3072]{1,0:T(8,128)(2,1)} %param.8), kind=kOutput, calls=%fused_computation.22 | convolution fusion | flops 3630170112 | bytes 12597248 | tf_op jit(solution)/shard_map/dot_general | solution.py:116
  27.5 0.1 slice.57
  27.6 1.0 slice_bitcast_fusion
  28.7 0.6 dynamic_slice.24
  29.2 0.6 iota_compare_fusion.2
  30.4 0.6 dynamic_slice.26
  31.7 0.9 copy.27
  32.6 0.7 dynamic_slice.25
  33.9 1.3 add_select_fusion.2
  35.2 0.4 multiply_cosine_fusion
  35.6 2.1 subtract_convert_fusion
  37.8 0.2 copy.26
  38.6 4.3 %bitcast_select_fusion = bf16[2,3584,384]{2,1,0:T(8,128)(2,1)S(1)} fusion(bf16[2,1,3584,384]{3,2,1,0:T(8,128)(2,1)} %param.12, pred[3584]{0:T(1024)(128)(4,1)S(1)} %iota_compare_fusion.2), kind=kLoop, calls=%fused_computation.18 | loop fusion | flops 2752512 | bytes 11013632 | tf_op jit(solution)/shard_map/jit(_where)/select_n | solution.py:134
  42.9 0.0 copy-start.2
  42.9 3.3 %concatenate.17 = bf16[2,4096,384]{2,1,0:T(8,128)(2,1)} pad(bf16[2,3584,384]{2,1,0:T(8,128)(2,1)S(1)} %bitcast_select_fusion, bf16[]{:T(256)} %constant.92.clone.1), padding=0_0x0_512x0_0 | pad | bytes 11796482 | tf_op jit(solution)/shard_map/concatenate | solution.py:137
  46.2 0.1 pad_maximum_fusion.1
  46.9 4.5 %dynamic_update_slice.3 = bf16[2,4096,384]{2,1,0:T(8,128)(2,1)} dynamic-update-slice(bf16[2,4096,384]{2,1,0:T(8,128)(2,1)} %concatenate.17, bf16[2,512,384]{2,1,0:T(8,128)(2,1)S(1)} %pad_maximum_fusion.1, s32[]{:T(128)} %constant.87.clone.1, s32[]{:T(128)S(6)} %select_n.87, s32[]{:T(128)} %constant.87.clone.1) | dynamic-update-slice | bytes 1572868 | tf_op jit(solution)/shard_map/dynamic_update_slice | solution.py:141
  51.4 7.6 %fusion.8 = bf16[2,1,32,128,384]{4,3,2,0,1:T(8,128)(2,1)} fusion(s32[]{:T(128)S(6)} %select_n.93, bf16[2,1,32,128,384]{4,3,2,0,1:T(8,128)(2,1)} %bitcast.41), kind=kLoop, calls=%fused_computation.14 | loop fusion | flops 3145728 | bytes 12582916 | tf_op jit(solution)/shard_map/concatenate | solution.py:83
  59.1 4.2 %dynamic-slice_bitcast_fusion = bf16[2,16,1,128,384]{4,3,1,0,2:T(8,128)(2,1)} fusion(bf16[2,16,1,2,128,384]{5,4,3,1,0,2:T(8,128)(2,1)} %bitcast.42, s32[]{:T(128)S(6)} %select_n.95), kind=kLoop, calls=%fused_computation.25 | loop fusion | bytes 6291460 | tf_op jit(solution)/shard_map/jit(dynamic_index_in_dim)/squeeze | solution.py:92
  63.2 0.0 collective-permute-start
  63.2 0.0 copy-done.1
  63.3 3.3 %fusion.42 = (bf16[1,4096,384]{2,1,0:T(8,128)(2,1)}, bf16[1,4096,384]{2,1,0:T(8,128)(2,1)}) fusion(bf16[2,4096,384]{2,1,0:T(8,128)(2,1)S(1)} %copy-done.1), kind=kLoop, calls=%fused_computation.83 | loop fusion | bytes 12582912 | tf_op jit(solution)/shard_map/slice | solution.py:55
  66.6 1.3 add_select_fusion
  67.8 0.6 iota_compare_fusion.1
  68.4 4.7 %copy.29 = bf16[1,4096,384]{1,2,0:T(8,128)(2,1)} copy(bf16[1,4096,384]{2,1,0:T(8,128)(2,1)} %get-tuple-element.8) | data formatting | bytes 6291456 | tf_op jit(solution)/shard_map/slice | solution.py:55
  73.1 15.0 %fusion.18 = f32[4,512,4096]{2,1,0:T(8,128)} fusion(bf16[4096,4,96]{0,2,1:T(8,128)(2,1)} %bitcast.44, bf16[512,4,48]{0,2,1:T(8,128)(2,1)S(1)} %copy-done.4, bf16[512,4,48]{0,2,1:T(8,128)(2,1)S(1)} %copy-done.3), kind=kOutput, calls=%fused_computation.41 | convolution fusion | flops 1611399168 | bytes 37093376 | tf_op jit(solution)/shard_map/qhd,khd->hqk/dot_general | solution.py:62
  88.2 3.9 %fusion.7 = pred[512,4096]{1,0:T(8,128)(4,1)} fusion(s32[4096]{0:T(1024)S(1)} %get-tuple-element.23, s32[4096]{0:T(1024)S(1)} %get-tuple-element.22, s32[512]{0:T(512)S(1)} %get-tuple-element.20, pred[4096]{0:T(1024)(128)(4,1)S(1)} %get-tuple-element.25, pred[4096]{0:T(1024)(128)(4,1)S(1)} %get-tuple-element.24), kind=kLoop, calls=%fused_computation.13 | loop fusion | flops 10485760 | bytes 2140160 | tf_op jit(solution)/shard_map/or | solution.py:47
  92.1 4.6 %copy.28 = bf16[1,4096,384]{1,2,0:T(8,128)(2,1)} copy(bf16[1,4096,384]{2,1,0:T(8,128)(2,1)} %get-tuple-element.9) | data formatting | bytes 6291456 | tf_op jit(solution)/shard_map/slice | solution.py:56
  96.7 15.2 %fusion.43 = f32[4,512]{1,0:T(4,128)S(1)} fusion(pred[512,4096]{1,0:T(8,128)(4,1)} %fusion.7, bf16[4096,4,96]{0,2,1:T(8,128)(2,1)} %bitcast.45, bf16[512,4,48]{0,2,1:T(8,128)(2,1)S(1)} %copy-done.4, bf16[512,4,48]{0,2,1:T(8,128)(2,1)S(1)} %copy-done.3), kind=kOutput, calls=%fused_computation.84 | convolution fusion | flops 1644957696 | bytes 5644288 | tf_op jit(solution)/shard_map/sub | solution.py:68
  111.9 35.3 %fusion.17 = bf16[4,96,512]{2,1,0:T(8,128)(2,1)S(1)} fusion(bf16[4096,4,96]{0,2,1:T(8,128)(2,1)} %bitcast.47, f32[4,512]{1,0:T(4,128)S(1)} %fusion.43, f32[4,512,4096]{2,1,0:T(8,128)} %fusion.18, pred[512,4096]{1,0:T(8,128)(4,1)} %fusion.7), kind=kOutput, calls=%fused_computation.29 | convolution fusion | flops 1669535744 | bytes 39198720 | tf_op jit(solution)/shard_map/hqk,khd->qhd/dot_general | solution.py:70
  147.2 3.5 %convolution_convert_fusion = bf16[512,3072]{1,0:T(8,128)(2,1)} fusion(bf16[512,384]{0,1:T(8,128)(2,1)S(1)} %bitcast.50, bf16[384,3072]{1,0:T(8,128)(2,1)S(1)} %copy-done), kind=kOutput, calls=%fused_computation.19 | convolution fusion | flops 1209532416 | bytes 5898240 | tf_op jit(solution)/shard_map/dot_general | solution.py:150
  150.7 0.0 reduce-scatter.2.cloned.1.call-update
  150.8 5.1 %bitcast_select_fusion.2 = (bf16[2,16,1,128,384]{4,3,1,0,2:T(8,128)(2,1)S(1)}, bf16[2,16,1,128,384]{4,3,1,0,2:T(8,128)(2,1)}) fusion(bf16[2,16,1,128,384]{4,3,1,0,2:T(8,128)(2,1)} %collective-permute-done, pred[]{:T(512)S(6)} %eq.27, bf16[2,16,1,2,128,384]{5,4,3,1,0,2:T(8,128)(2,1)} %bitcast.43, s32[]{:T(128)S(6)} %select_n.94), kind=kLoop, calls=%fused_computation.24 | loop fusion | flops 3145728 | bytes 12582917 | tf_op jit(solution)/shard_map/jit(_where)/select_n | solution.py:94
  155.9 2.7 pad_maximum_fusion
  158.6 3.3 %copy.30 = bf16[2,16,1,128,768]{4,3,0,2,1:T(8,128)(2,1)} copy(bf16[2,16,1,128,768]{4,3,1,0,2:T(8,128)(2,1)S(1)} %pad_maximum_fusion) | data formatting | bytes 12582912 | tf_op jit(solution)/shard_map/concatenate | solution.py:96
  161.9 8.2 %all-to-all-start = ((bf16[2,16,1,128,768]{4,3,0,2,1:T(8,128)(2,1)}), bf16[2,16,1,128,768]{4,3,0,2,1:T(8,128)(2,1)}, u32[]{:S(2)}, u32[]{:S(2)}) async-start(bf16[2,16,1,128,768]{4,3,0,2,1:T(8,128)(2,1)} %copy.30), calls=%async_computation.1 | async-start | bytes 12582912 | tf_op jit(solution)/shard_map/all_to_all | solution.py:97
  170.1 5.4 %convert_element_type.57 = f32[512,3072]{1,0:T(8,128)} convert(bf16[512,3072]{1,0:T(8,128)(2,1)} %param.8) | non-fusion elementwise | flops 1572864 | bytes 9437184 | tf_op jit(solution)/shard_map/convert_element_type | solution.py:113
  175.5 14.5 %reduce-scatter.2.cloned.1.call-done = bf16[64,3072]{1,0:T(8,128)(2,1)} async-done(((bf16[512,3072]{1,0:T(8,128)(2,1)}), bf16[64,3072]{1,0:T(8,128)(2,1)}) %reduce-scatter.2.cloned.1.call-update) | async-done | bytes 393232 | tf_op jit(solution)/shard_map/reduce_scatter | solution.py:149
  190.0 2.1 add_convert_fusion
  192.1 73.5 %all-to-all-done = bf16[2,16,1,128,768]{4,3,0,2,1:T(8,128)(2,1)} async-done(((bf16[2,16,1,128,768]{4,3,0,2,1:T(8,128)(2,1)}), bf16[2,16,1,128,768]{4,3,0,2,1:T(8,128)(2,1)}, u32[]{:S(2)}, u32[]{:S(2)}) %all-to-all-start) | async-done | bytes 6291488 | tf_op jit(solution)/shard_map/all_to_all | solution.py:97
  265.6 6.1 %copy.31 = bf16[2,1,16,1,128,768]{5,4,3,2,1,0:T(8,128)(2,1)} copy(bf16[2,1,16,1,128,768]{5,4,0,2,3,1:T(8,128)(2,1)} %bitcast.21) | data formatting | bytes 12582912
  (17 shorter events, 0.1 us)
Async XLA Ops:
  7.2 140.1 %copy-start = (bf16[384,3072]{1,0:T(8,128)(2,1)S(1)}, bf16[384,3072]{1,0:T(8,128)(2,1)}, u32[]{:S(2)}) copy-start(bf16[384,3072]{1,0:T(8,128)(2,1)} %param.11) | copy-start | bytes 7077892
  7.2 182.8 %reduce-scatter.2.cloned.1.call-start = ((), (), s32[]{:S(2)}) async-start(), calls=%async_computation.2 | async-start | bytes 3538944 | tf_op jit(solution)/shard_map/reduce_scatter | solution.py:149
  7.2 10.5 %copy-start.5 = (bf16[3072]{0:T(1024)(128)(2,1)S(1)}, bf16[3072]{0:T(1024)(128)(2,1)}, u32[]{:S(2)}) copy-start(bf16[3072]{0:T(1024)(128)(2,1)} %param.9) | copy-start | bytes 18436
  20.3 8.4 %copy-start.6 = (s32[16]{0:T(128)S(1)}, s32[16]{0:T(128)}, u32[]{:S(2)}) copy-start(s32[16]{0:T(128)} %param.13) | copy-start | bytes 196
  20.3 10.1 %copy-start.7 = (s32[16]{0:T(128)S(1)}, s32[16]{0:T(128)}, u32[]{:S(2)}) copy-start(s32[16]{0:T(128)} %param.15) | copy-start | bytes 196
  20.3 12.3 %copy-start.8 = (s32[16]{0:T(128)S(1)}, s32[16]{0:T(128)}, u32[]{:S(2)}) copy-start(s32[16]{0:T(128)} %param.14) | copy-start | bytes 196
  42.9 3.3 %copy-start.2 = (bf16[1,512,384]{2,1,0:T(8,128)(2,1)S(1)}, bf16[1,512,384]{2,1,0:T(8,128)(2,1)}, u32[]{:S(2)}) copy-start(bf16[1,512,384]{2,1,0:T(8,128)(2,1)} %copy.27) | copy-start | bytes 1179652
  59.1 4.2 %copy-start.1 = (bf16[2,4096,384]{2,1,0:T(8,128)(2,1)S(1)}, bf16[2,4096,384]{2,1,0:T(8,128)(2,1)}, u32[]{:S(2)}) copy-start(bf16[2,4096,384]{2,1,0:T(8,128)(2,1)} %dynamic_update_slice.3) | copy-start | bytes 18874372
  63.2 87.5 %collective-permute-start = (bf16[2,16,1,128,384]{4,3,1,0,2:T(8,128)(2,1)}, bf16[2,16,1,128,384]{4,3,1,0,2:T(8,128)(2,1)}, u32[]{:S(2)}, u32[]{:S(2)}) collective-permute-start(bf16[2,16,1,128,384]{4,3,1,0,2:T(8,128)(2,1)} %dynamic-slice_bitcast_fusion), channel_id=1, source_target_pairs={{0,1},{1,0},{2,3},{3,2},{4,5},{5,4},{6,7},{7,6},{8,9},{9,8},{10,11... | collective-permute-start | bytes 9437192 | tf_op jit(solution)/shard_map/ppermute | solution.py:15
  66.6 6.6 %copy-start.3 = (bf16[512,4,48]{0,2,1:T(8,128)(2,1)S(1)}, bf16[512,4,48]{0,2,1:T(8,128)(2,1)}, u32[]{:S(2)}) copy-start(bf16[512,4,48]{0,2,1:T(8,128)(2,1)} %get-tuple-element.12) | copy-start | bytes 589828
  66.6 6.6 %copy-start.4 = (bf16[512,4,48]{0,2,1:T(8,128)(2,1)S(1)}, bf16[512,4,48]{0,2,1:T(8,128)(2,1)}, u32[]{:S(2)}) copy-start(bf16[512,4,48]{0,2,1:T(8,128)(2,1)} %get-tuple-element.13) | copy-start | bytes 589828
  161.9 103.8 %all-to-all-start = ((bf16[2,16,1,128,768]{4,3,0,2,1:T(8,128)(2,1)}), bf16[2,16,1,128,768]{4,3,0,2,1:T(8,128)(2,1)}, u32[]{:S(2)}, u32[]{:S(2)}) async-start(bf16[2,16,1,128,768]{4,3,0,2,1:T(8,128)(2,1)} %copy.30), calls=%async_computation.1 | async-start | bytes 12582912 | tf_op jit(solution)/shard_map/all_to_all | solution.py:97
Sparse Core Ops, SparseCore 0:
  150.9 39.1 reduce-scatter.1
where the time goes:
time: 280 us; the launch traced here: 279 us
  waiting for transfers between devices  88 us (31%)
  matrix products  76.2 us (27%)
  local copies, waits for them, and re-layouts  48.6 us (17%)
  other arithmetic  40.2 us (14%)
  between operations  17.3 us (6%)
  starting transfers between devices  8.25 us (3%)
    all_to_all x1, waiting for transfers between devices, relay_cache(): lax.all_to_all(joined, 'seq', split_axis=1, concat_axis=1, tiled=True)  73.5 us
    dot_general x1, matrix products, attend(): jnp.einsum('hqk,khd->qhd', probabilities, value_heads, preferred_element_...  35.3 us
    unnamed x20, local copies, waits for them, and re-layouts  16.7 us
    sub x1, matrix products, attend(): weights = jnp.exp(masked - row_peak)  15.2 us
    dot_general x1, matrix products, attend(): jnp.einsum('qhd,khd->hqk', queries, key_heads, preferred_element_type=jnp...  15 us
    reduce_scatter x1, waiting for transfers between devices, local(): lax.psum_scatter(jnp.dot(attended, w_out, preferred_element_type=jnp.floa...  14.5 us
    all_to_all x1, starting transfers between devices, relay_cache(): lax.all_to_all(joined, 'seq', split_axis=1, concat_axis=1, tiled=True)  8.21 us
    slice x2, local copies, waits for them, and re-layouts, attend(): key_heads = full_cache[0].reshape(context, head_count, HD)  8.01 us
  transfers between devices with their start and end apart: 3, of which 2 were waited for; matrix products, arithmetic and copies ran while one was open for 38% of the time, Pallas kernels for 0%

commit v1 on v0

v1 whole, which is shorter than its diff:
```python
import math

import jax
import jax.numpy as jnp
from jax import lax
from jax.experimental import pallas as pl
from jax.experimental.pallas import tpu as pltpu
from jax.sharding import Mesh
from jax.sharding import PartitionSpec as P

HD = 96
BLK = 128
ROWS = 128


def rope_tables(positions, head_size):
    half_size = head_size // 2
    frequency = jnp.exp(
        jnp.arange(half_size, dtype=jnp.float32) * (-2.0 * math.log(10000.0) / head_size)
    )
    angles = positions.astype(jnp.float32)[:, None] * frequency[None, :]
    return (jnp.cos(angles), jnp.sin(angles))


def rope_pair(vectors, cosine_table, sine_table):
    half_size = vectors.shape[-1] // 2
    first_half = vectors[..., :half_size]
    second_half = vectors[..., half_size:]
    cos_wide = cosine_table[:, None, :]
    sin_wide = sine_table[:, None, :]
    return jnp.concatenate(
        [
            first_half * cos_wide - second_half * sin_wide,
            second_half * cos_wide + first_half * sin_wide,
        ],
        axis=-1,
    )


def request_of(index, group_requests, tok_count):
    scaled = index * group_requests
    if tok_count & (tok_count - 1) == 0:
        return lax.shift_right_logical(scaled, tok_count.bit_length() - 1)
    return scaled // tok_count


def attention_kernel(meta_ref, q_ref, kc_ref, vc_ref, kn_ref, vn_ref, o_ref):
    group_len = meta_ref[0]
    group_requests = meta_ref[1]
    rows = q_ref.shape[1]
    tok_count = kn_ref.shape[1]
    score_scale = 1.0 / math.sqrt(HD)
    dims = (((1,), (1,)), ((), ()))
    q = q_ref[0]
    s_old = lax.dot_general(q, kc_ref[0], dims, preferred_element_type=jnp.float32) * score_scale
    s_new = lax.dot_general(q, kn_ref[0], dims, preferred_element_type=jnp.float32) * score_scale
    col = lax.broadcasted_iota(jnp.int32, s_old.shape, 1)
    s_old = jnp.where(col < group_len, s_old, -1e30)
    row = pl.program_id(1) * rows + lax.broadcasted_iota(jnp.int32, s_new.shape, 0)
    key = lax.broadcasted_iota(jnp.int32, s_new.shape, 1)
    same = request_of(row, group_requests, tok_count) == request_of(key, group_requests, tok_count)
    s_new = jnp.where(same & (key <= row), s_new, -1e30)
    peak = jnp.maximum(
        jnp.max(s_old, axis=1, keepdims=True), jnp.max(s_new, axis=1, keepdims=True)
    )
    e_old = jnp.exp(s_old - peak)
    e_new = jnp.exp(s_new - peak)
    total = jnp.sum(e_old, axis=1, keepdims=True) + jnp.sum(e_new, axis=1, keepdims=True)
    p_old = (e_old / total).astype(jnp.bfloat16)
    p_new = (e_new / total).astype(jnp.bfloat16)
    out = jnp.dot(p_old, vc_ref[0], preferred_element_type=jnp.float32) + jnp.dot(
        p_new, vn_ref[0], preferred_element_type=jnp.float32
    )
    o_ref[0] = out.astype(jnp.bfloat16)


def attend(meta, queries, cache_k, cache_v, new_k, new_v):
    heads, tok_count, _ = queries.shape
    cache_len = cache_k.shape[1]
    q_spec = pl.BlockSpec((1, ROWS, HD), lambda h, r, m: (h, r, 0))
    c_spec = pl.BlockSpec((1, cache_len, HD), lambda h, r, m: (h, 0, 0))
    n_spec = pl.BlockSpec((1, tok_count, HD), lambda h, r, m: (h, 0, 0))
    return pl.pallas_call(
        attention_kernel,
        out_shape=jax.ShapeDtypeStruct(queries.shape, jnp.bfloat16),
        grid_spec=pltpu.PrefetchScalarGridSpec(
            num_scalar_prefetch=1,
            grid=(heads, tok_count // ROWS),
            in_specs=[q_spec, c_spec, c_spec, n_spec, n_spec],
            out_specs=q_spec,
        ),
    )(meta, queries, cache_k, cache_v, new_k, new_v)


def relay_kernel(meta_ref, cache_hbm, new_hbm, out_hbm, zero_buf, sems):
    len_blocks = meta_ref[0]
    group_start = meta_ref[1]
    rank_count = out_hbm.shape[0]
    new_blocks = new_hbm.shape[1] // BLK
    zero_buf[...] = jnp.zeros(zero_buf.shape, zero_buf.dtype)
    for rank in range(rank_count):
        block = (rank - group_start + rank_count) % rank_count
        target = out_hbm.at[rank]

        @pl.when(block < len_blocks)
        def _():
            start = pl.multiple_of(block * BLK, BLK)
            pltpu.make_async_copy(
                cache_hbm.at[:, pl.ds(start, BLK)], target, sems.at[rank]
            ).start()

        fresh = (block >= len_blocks) & (block < len_blocks + new_blocks)

        @pl.when(fresh)
        def _():
            start = pl.multiple_of((block - len_blocks) * BLK, BLK)
            pltpu.make_async_copy(
                new_hbm.at[:, pl.ds(start, BLK)], target, sems.at[rank]
            ).start()

        @pl.when(block >= len_blocks + new_blocks)
        def _():
            pltpu.make_async_copy(zero_buf, target, sems.at[rank]).start()

    for rank in range(rank_count):
        pltpu.make_async_copy(zero_buf, out_hbm.at[rank], sems.at[rank]).wait()


def relay(meta, cache, new_kv, rank_count):
    _, _, features = cache.shape
    return pl.pallas_call(
        relay_kernel,
        out_shape=jax.ShapeDtypeStruct((rank_count, 2, BLK, features), jnp.bfloat16),
        grid_spec=pltpu.PrefetchScalarGridSpec(
            num_scalar_prefetch=1,
            grid=(),
            in_specs=[pl.BlockSpec(memory_space=pl.ANY), pl.BlockSpec(memory_space=pl.ANY)],
            out_specs=pl.BlockSpec(memory_space=pl.ANY),
            scratch_shapes=[
                pltpu.VMEM((2, BLK, features), jnp.bfloat16),
                pltpu.SemaphoreType.DMA((rank_count,)),
            ],
        ),
    )(meta, cache, new_kv)


def head_major(values, head_count):
    rows = values.shape[0]
    return values.reshape(rows, head_count, HD).transpose(1, 0, 2)


def local(tokens, norm_gain, w_qkv, w_out, kv_cache, cached_lengths, requests, block_start):
    group_idx = lax.axis_index("seq")
    tp_rank = lax.axis_index(("x", "core"))
    tp_count = lax.axis_size(("x", "core"))
    seq_count = lax.axis_size("seq")
    tok_count, model_width = tokens.shape
    features = w_qkv.shape[2]
    head_count = features // HD
    cache_len = kv_cache.shape[2]
    group_len = lax.dynamic_index_in_dim(cached_lengths, group_idx, keepdims=False)
    group_requests = lax.dynamic_index_in_dim(requests, group_idx, keepdims=False)
    group_start = lax.dynamic_index_in_dim(block_start, group_idx, keepdims=False)
    inputs = tokens.astype(jnp.float32)
    inverse_rms = lax.rsqrt(jnp.mean(inputs * inputs, axis=-1, keepdims=True) + 1e-05)
    normed = (inputs * inverse_rms * norm_gain.astype(jnp.float32)).astype(jnp.bfloat16)

    def project(part):
        return jnp.dot(normed, w_qkv[:, part, :], preferred_element_type=jnp.float32)

    row_index = jnp.arange(tok_count, dtype=jnp.int32)
    request = row_index * group_requests // tok_count
    first_row = (request * tok_count + group_requests - 1) // group_requests
    positions = group_len + row_index - first_row
    cosine_table, sine_table = rope_tables(positions, HD)

    def rotate(projected):
        heads = projected.reshape(tok_count, head_count, HD)
        return rope_pair(heads, cosine_table, sine_table).astype(jnp.bfloat16)

    new_keys = rotate(project(1)).reshape(tok_count, features)
    new_values = project(2).astype(jnp.bfloat16)
    cache = kv_cache[:, 0]
    relay_meta = jnp.stack([group_len // BLK, group_start]).astype(jnp.int32)
    rank_count = 2 * seq_count
    send = relay(relay_meta, cache, jnp.stack([new_keys, new_values]), rank_count)
    received = lax.all_to_all(send, ("seq", "core"), 0, 0, tiled=True)
    received = received.reshape(seq_count, 2, 2, BLK, features).transpose(2, 0, 3, 1, 4)
    decode_cache = received.reshape(2, 1, seq_count, 1, BLK, 2 * features)

    queries = rotate(project(0)).transpose(1, 0, 2)
    attn_meta = jnp.stack([group_len, group_requests]).astype(jnp.int32)
    cache_heads = kv_cache.reshape(2, cache_len, head_count, HD).transpose(0, 2, 1, 3)
    attended = attend(
        attn_meta,
        queries,
        cache_heads[0],
        cache_heads[1],
        head_major(new_keys, head_count),
        head_major(new_values, head_count),
    )
    attended = attended.transpose(1, 0, 2).reshape(tok_count, features)
    rows_dev = tok_count // tp_count
    partial = jnp.dot(attended, w_out, preferred_element_type=jnp.float32).astype(jnp.bfloat16)
    summed = lax.dynamic_slice_in_dim(partial, tp_rank * rows_dev, rows_dev, 0).astype(jnp.float32)
    for shift in range(1, tp_count):
        target = (tp_rank + shift) % tp_count
        chunk = lax.dynamic_slice_in_dim(partial, target * rows_dev, rows_dev, 0)
        pairs = [(source, (source + shift) % tp_count) for source in range(tp_count)]
        summed = summed + lax.ppermute(chunk, ("x", "core"), pairs).astype(jnp.float32)
    own_rows = lax.dynamic_slice_in_dim(inputs, tp_rank * rows_dev, rows_dev, 0)
    layer_out = (own_rows + summed).astype(jnp.bfloat16)
    return (layer_out, decode_cache)


def solution(mesh):
    seq_count, tp_count = mesh.devices.shape
    split = Mesh(mesh.devices.reshape(seq_count, tp_count // 2, 2), ("seq", "x", "core"))
    tp = ("x", "core")
    placed = (
        P("seq", None),
        P(),
        P(None, None, tp),
        P(tp, None),
        P(None, "seq", None, tp),
        P(),
        P(),
        P(),
    )
    return jax.shard_map(
        local,
        mesh=split,
        in_specs=placed,
        out_specs=(P(("seq",) + tp, None), P(None, "seq", None, None, None, tp)),
        check_vma=False,
    )
```

time: 280 us -> 381 us (1.36)
  Pallas kernels: 0 us -> 176 us
  waiting for transfers between devices: 88 us -> 14.8 us
  matrix products: 76.2 us -> 14.6 us
  starting transfers between devices: 8.25 us -> 62.7 us
  local copies, waits for them, and re-layouts: 48.6 us -> 79 us
  other arithmetic: 40.2 us -> 25.1 us
  between operations: 17.3 us -> 4.02 us
    pallas_call x0 -> x2, Pallas kernels: none -> 176 us  [the longest x1 151 us: relay(): pl.pallas_call(relay_kernel, out_shape=jax.ShapeDtypeStruct((rank_count,...]
    all_to_all x1, waiting for transfers between devices: 73.5 us -> 0.01 us  [local(): received = lax.all_to_all(send, ('seq', 'core'), 0, 0, tiled=True)]
    dot_general x3, matrix products: 57.5 us -> 12.8 us  [project(): jnp.dot(normed, w_qkv[:, part, :], preferred_element_type=jnp.float32)]
    all_to_all x1, starting transfers between devices: 8.21 us -> 45.7 us  [local(): received = lax.all_to_all(send, ('seq', 'core'), 0, 0, tiled=True)]
    reshape x0 -> x3, local copies, waits for them, and re-layouts: none -> 26.1 us  [the longest x1 14.6 us: local(): decode_cache = received.reshape(2, 1, seq_count, 1, BLK, 2 * features)]
    ppermute x1 -> x7, starting transfers between devices: 0.01 us -> 17 us  [local(): lax.ppermute(chunk, ('x', 'core'), pairs).astype(jnp.float32)]
    sub x1 -> x0, matrix products: 15.2 us -> none  [attend(): weights = jnp.exp(masked - row_peak)]
    ppermute x1 -> x7, waiting for transfers between devices: 0.01 us -> 14.8 us  [local(): lax.ppermute(chunk, ('x', 'core'), pairs).astype(jnp.float32)]
  transfers between devices with their start and end apart: 3 -> 8, of which waited for: 2 -> 5; matrix products, arithmetic and copies ran while one was open for 38% -> 14% of each run, Pallas kernels for 0% -> 7%
where the time goes in v1:
time: 381 us; the launch traced here: 376 us
  Pallas kernels  176 us (46%)
  local copies, waits for them, and re-layouts  79 us (21%)
  starting transfers between devices  62.7 us (16%)
  other arithmetic  25.1 us (7%)
  waiting for transfers between devices  14.8 us (4%)
  matrix products  14.6 us (4%)
  between operations  4.02 us (1%)
    pallas_call x1, Pallas kernels, relay(): pl.pallas_call(relay_kernel, out_shape=jax.ShapeDtypeStruct((rank_count,...  151 us
    all_to_all x1, starting transfers between devices, local(): received = lax.all_to_all(send, ('seq', 'core'), 0, 0, tiled=True)  45.7 us
    pallas_call x1, Pallas kernels, attend(): pl.pallas_call(attention_kernel, out_shape=jax.ShapeDtypeStruct(queries.s...  25.3 us
    ppermute x7, starting transfers between devices, local(): lax.ppermute(chunk, ('x', 'core'), pairs).astype(jnp.float32)  17 us
    ppermute x7, waiting for transfers between devices, local(): lax.ppermute(chunk, ('x', 'core'), pairs).astype(jnp.float32)  14.8 us
    reshape x1, local copies, waits for them, and re-layouts, local(): decode_cache = received.reshape(2, 1, seq_count, 1, BLK, 2 * features)  14.6 us
    dot_general x3, local copies, waits for them, and re-layouts, project(): jnp.dot(normed, w_qkv[:, part, :], preferred_element_type=jnp.float32)  13.6 us
    transpose x1, local copies, waits for them, and re-layouts, local(): received.reshape(seq_count, 2, 2, BLK, features).transpose(2, 0, 3, 1, 4)  12.8 us
  transfers between devices with their start and end apart: 8, of which 5 were waited for; matrix products, arithmetic and copies ran while one was open for 14% of the time, Pallas kernels for 7%

profile of v1, /device:TPU:0, one launch (start us, length us, event | category | flops | bytes accessed | tf_op | source)
XLA Modules:
  0.0 376.5 jit_solution(8600464960449270376)
XLA Ops:
  0.7 1.4 dynamic_slice.38
  4.0 1.3 dynamic_slice.39
  5.9 1.4 fusion.16
  8.0 2.6 multiply_reduce_fusion
  10.6 5.1 %slice_bitcast_fusion.2 = (bf16[384,3072]{0,1:T(8,128)(2,1)}, bf16[384,3072]{0,1:T(8,128)(2,1)}) fusion(bf16[3072,3,384]{2,0,1:T(8,128)(2,1)} %param.10), kind=kLoop, calls=%fused_computation.12 | loop fusion | bytes 9437184 | tf_op jit(solution)/shard_map/dot_general | solution.py:169
  15.7 4.3 %copy.25 = bf16[384,3072]{1,0:T(8,128)(2,1)} copy(bf16[384,3072]{0,1:T(8,128)(2,1)} %get-tuple-element.4) | data formatting | bytes 4718592 | tf_op jit(solution)/shard_map/dot_general | solution.py:169
  19.9 5.3 %fusion.7 = bf16[512,384]{1,0:T(8,128)(2,1)} fusion(bf16[3072,3,384]{2,0,1:T(8,128)(2,1)} %param.10, f32[3072]{0:T(1024)S(1)} %convert_element_type.64, f32[512]{0:T(512)S(1)} %add_rsqrt_fusion, bf16[512,3072]{1,0:T(8,128)(2,1)} %param.8), kind=kOutput, calls=%fused_computation.14 | convolution fusion | flops 1214447616 | bytes 5912576 | tf_op jit(solution)/shard_map/dot_general | solution.py:169
  25.3 2.8 fusion
  29.4 1.0 multiply_cosine_fusion
  31.1 2.0 multiply_subtract_fusion
  33.1 1.1 maximum_convert_fusion
  34.2 2.0 copy.32
  36.2 1.9 copy.33
  38.1 1.2 pad_add_fusion.1.meta_ref
  39.3 2.1 pad_maximum_fusion.new_hbm
  41.4 151.0 %shard_map.96 = bf16[32,2,128,384]{3,2,1,0:T(8,128)(2,1)} custom-call(s32[2]{0:T(128)} %pad_add_fusion.1.meta_ref, bf16[2,3584,384]{2,1,0:T(8,128)(2,1)} %bitcast.50, bf16[2,512,384]{2,1,0:T(8,128)(2,1)} %pad_maximum_fusion.new_hbm), custom_call_target="tpu_custom_call" | custom-call | tf_op jit(solution)/shard_map/pallas_call | solution.py:131
  192.3 45.7 %all-to-all-start = ((bf16[32,2,128,384]{3,2,1,0:T(8,128)(2,1)}), bf16[32,2,128,384]{3,2,1,0:T(8,128)(2,1)}, u32[]{:S(2)}, u32[]{:S(2)}) async-start(bf16[32,2,128,384]{3,2,1,0:T(8,128)(2,1)} %shard_map.96), calls=%async_computation | async-start | bytes 12582912 | tf_op jit(solution)/shard_map/all_to_all | solution.py:187
  238.0 1.9 copy.29
  240.0 8.3 %copy.23 = bf16[2,1,3584,384]{2,3,0,1:T(8,128)(2,1)} copy(bf16[2,1,3584,384]{3,2,1,0:T(8,128)(2,1)} %param.12) | data formatting | bytes 11010048 | tf_op args[4]
  248.2 4.3 %copy.20 = bf16[384,3072]{1,0:T(8,128)(2,1)} copy(bf16[384,3072]{0,1:T(8,128)(2,1)} %get-tuple-element.5) | data formatting | bytes 4718592 | tf_op jit(solution)/shard_map/dot_general | solution.py:169
  252.5 2.0 copy.30
  254.5 9.5 %copy.24 = bf16[2,3584,4,96]{3,1,2,0:T(8,128)(2,1)} copy(bf16[2,3584,4,96]{1,3,2,0:T(8,128)(2,1)} %bitcast.51) | data formatting | bytes 11010048 | tf_op jit(solution)/shard_map/reshape | solution.py:193
  264.1 1.8 pad_add_fusion.meta_ref
  265.9 1.1 fusion.23.kn_ref
  267.0 4.6 %fusion.2 = f32[512,4,96]{2,0,1:T(8,128)S(1)} fusion(bf16[4,96,3072]{2,1,0:T(8,128)(2,1)} %bitcast.52, f32[3072]{0:T(1024)S(1)} %convert_element_type.64, f32[512]{0:T(512)S(1)} %add_rsqrt_fusion, bf16[512,3072]{1,0:T(8,128)(2,1)} %param.8), kind=kOutput, calls=%fused_computation.7 | convolution fusion | flops 1214251008 | bytes 6305792 | tf_op jit(solution)/shard_map/dot_general | solution.py:169
  272.1 1.1 maximum_bitcast_fusion.q_ref
  273.2 3.5 slice_bitcast_fusion
  276.7 25.3 %shard_map.95 = bf16[4,512,96]{2,1,0:T(8,128)(2,1)} custom-call(s32[2]{0:T(128)} %pad_add_fusion.meta_ref, bf16[4,512,96]{2,1,0:T(8,128)(2,1)} %maximum_bitcast_fusion.q_ref, bf16[4,3584,96]{2,1,0:T(8,128)(2,1)} %get-tuple-element.3.kc_ref, bf16[4,3584,96]{2,1,0:T(8,128)(2,1)} %get-tuple-element.2.vc_ref, bf16[4,512,96]{2,1,0:T(8,128)(2,1)} %fusion.23.kn_ref, ...), custom_call_target="tpu_custom_call" | custom-call | tf_op jit(solution)/shard_map/pallas_call | solution.py:83
  302.1 1.2 copy.31
  303.4 1.8 convolution_convert_fusion
  305.2 1.6 copy-done.2
  306.8 1.1 constant_dynamic-slice_fusion.6
  308.0 1.5 collective-permute-start.1
  309.5 2.1 collective-permute-start.2
  311.5 2.0 collective-permute-start.3
  313.5 1.6 collective-permute-start.4
  315.1 4.8 %collective-permute-done = bf16[64,3072]{1,0:T(8,128)(2,1)S(1)} collective-permute-done((bf16[64,3072]{1,0:T(8,128)(2,1)S(1)}, bf16[64,3072]{1,0:T(8,128)(2,1)S(1)}, u32[]{:S(2)}, u32[]{:S(2)}) %collective-permute-start) | collective-permute-done | bytes 393248 | tf_op jit(solution)/shard_map/ppermute | solution.py:210
  319.9 1.5 collective-permute-start.5
  321.5 0.8 copy-done.8
  322.3 8.2 %collective-permute-start.6 = (bf16[64,3072]{1,0:T(8,128)(2,1)S(1)}, bf16[64,3072]{1,0:T(8,128)(2,1)}, u32[]{:S(2)}, u32[]{:S(2)}) collective-permute-start(bf16[64,3072]{1,0:T(8,128)(2,1)S(1)} %get-tuple-element.7), channel_id=1, source_target_pairs={{0,7},{1,0},{2,1},{3,2},{4,3},{5,4},{6,5},{7,6},{8,15},{9,8},{10,9... | collective-permute-start | bytes 1179656 | tf_op jit(solution)/shard_map/ppermute | solution.py:210
  330.5 5.4 %convert_element_type.63 = f32[512,3072]{1,0:T(8,128)} convert(bf16[512,3072]{1,0:T(8,128)(2,1)} %param.8) | non-fusion elementwise | flops 1572864 | bytes 9437184 | tf_op jit(solution)/shard_map/convert_element_type | solution.py:164
  335.9 2.0 collective-permute-done.2
  337.9 1.2 collective-permute-done.3
  339.1 4.6 %collective-permute-done.4 = bf16[64,3072]{1,0:T(8,128)(2,1)} collective-permute-done((bf16[64,3072]{1,0:T(8,128)(2,1)}, bf16[64,3072]{1,0:T(8,128)(2,1)}, u32[]{:S(2)}, u32[]{:S(2)}) %collective-permute-start.4) | collective-permute-done | bytes 393248 | tf_op jit(solution)/shard_map/ppermute | solution.py:210
  343.7 2.2 collective-permute-done.6
  345.9 3.2 add_convert_fusion.1
  349.1 12.8 %copy.34 = bf16[2,16,128,2,384]{4,3,2,1,0:T(2,128)(2,1)} copy(bf16[2,16,128,2,384]{4,2,0,3,1:T(8,128)(2,1)} %bitcast.25) | data formatting | bytes 12582912 | tf_op jit(solution)/shard_map/transpose | solution.py:188
  361.9 14.6 %reshape.133 = bf16[2,1,16,1,128,768]{5,4,3,2,1,0:T(8,128)(2,1)} reshape(bf16[2,16,128,2,384]{4,3,2,1,0:T(2,128)(2,1)} %copy.34) | data formatting | bytes 12582912 | tf_op jit(solution)/shard_map/reshape | solution.py:189
  (32 shorter events, 2.6 us)
Async XLA Ops:
  0.6 302.7 %copy-start = (bf16[384,3072]{1,0:T(8,128)(2,1)S(1)}, bf16[384,3072]{1,0:T(8,128)(2,1)}, u32[]{:S(2)}) copy-start(bf16[384,3072]{1,0:T(8,128)(2,1)} %param.11) | copy-start | bytes 7077892
  19.9 5.3 %copy-start.1 = (bf16[512,3072]{1,0:T(8,128)(2,1)S(1)}, bf16[512,3072]{1,0:T(8,128)(2,1)}, u32[]{:S(2)}) copy-start(bf16[512,3072]{1,0:T(8,128)(2,1)} %param.8) | copy-start | bytes 9437188
  19.9 5.3 %copy-start.7 = (bf16[384,3072]{1,0:T(8,128)(2,1)S(1)}, bf16[384,3072]{1,0:T(8,128)(2,1)}, u32[]{:S(2)}) copy-start(bf16[384,3072]{1,0:T(8,128)(2,1)} %copy.25) | copy-start | bytes 7077892
  25.3 3.5 copy-start.9
  30.4 0.7 copy-start.3
  30.4 2.7 copy-start.5
  192.3 156.8 %all-to-all-start = ((bf16[32,2,128,384]{3,2,1,0:T(8,128)(2,1)}), bf16[32,2,128,384]{3,2,1,0:T(8,128)(2,1)}, u32[]{:S(2)}, u32[]{:S(2)}) async-start(bf16[32,2,128,384]{3,2,1,0:T(8,128)(2,1)} %shard_map.96), calls=%async_computation | async-start | bytes 12582912 | tf_op jit(solution)/shard_map/all_to_all | solution.py:187
  267.0 6.2 %slice-start = ((s8[7340032]{0:T(1024)(128)(4,1)}), s8[4194304]{0:T(1024)(128)(4,1)S(1)}, s32[]{:S(2)}) async-start(s8[7340032]{0:T(1024)(128)(4,1)} %bitcast.47), calls=%async_computation.1 | async-start | bytes 8388608
  267.0 4.6 %copy-start.4 = (f32[512,48]{1,0:T(8,128)S(1)}, f32[512,48]{1,0:T(8,128)}, u32[]{:S(2)}) copy-start(f32[512,48]{1,0:T(8,128)} %copy-done.3) | copy-start | bytes 294916
  267.0 4.6 %copy-start.6 = (f32[512,48]{1,0:T(8,128)S(1)}, f32[512,48]{1,0:T(8,128)}, u32[]{:S(2)}) copy-start(f32[512,48]{1,0:T(8,128)} %copy-done.5) | copy-start | bytes 294916
  267.0 6.2 %slice-start.1 = ((s8[7340032]{0:T(1024)(128)(4,1)}), s8[3145728]{0:T(1024)(128)(4,1)S(1)}, s32[]{:S(2)}) async-start(s8[7340032]{0:T(1024)(128)(4,1)} %bitcast.47), calls=%async_computation.2 | async-start | bytes 6291456
  305.2 1.6 copy-start.2
  307.9 12.0 %collective-permute-start = (bf16[64,3072]{1,0:T(8,128)(2,1)S(1)}, bf16[64,3072]{1,0:T(8,128)(2,1)S(1)}, u32[]{:S(2)}, u32[]{:S(2)}) collective-permute-start(bf16[64,3072]{1,0:T(8,128)(2,1)S(1)} %get-tuple-element.6), channel_id=1, source_target_pairs={{0,1},{1,2},{2,3},{3,4},{4,5},{5,6},{6,7},{7,0},{8,9},{9,10},{10,1... | collective-permute-start | bytes 1179656 | tf_op jit(solution)/shard_map/ppermute | solution.py:210
  308.0 13.5 %collective-permute-start.1 = (bf16[64,3072]{1,0:T(8,128)(2,1)S(1)}, bf16[64,3072]{1,0:T(8,128)(2,1)S(1)}, u32[]{:S(2)}, u32[]{:S(2)}) collective-permute-start(bf16[64,3072]{1,0:T(8,128)(2,1)S(1)} %get-tuple-element.12), channel_id=1, source_target_pairs={{0,2},{1,3},{2,4},{3,5},{4,6},{5,7},{6,0},{7,1},{8,10},{9,11},{10,... | collective-permute-start | bytes 1179656 | tf_op jit(solution)/shard_map/ppermute | solution.py:210
  309.5 28.4 %collective-permute-start.2 = (bf16[64,3072]{1,0:T(8,128)(2,1)}, bf16[64,3072]{1,0:T(8,128)(2,1)}, u32[]{:S(2)}, u32[]{:S(2)}) collective-permute-start(bf16[64,3072]{1,0:T(8,128)(2,1)} %get-tuple-element.11), channel_id=1, source_target_pairs={{0,3},{1,4},{2,5},{3,6},{4,7},{5,0},{6,1},{7,2},{8,11},{9,12},{10,... | collective-permute-start | bytes 1179656 | tf_op jit(solution)/shard_map/ppermute | solution.py:210
  311.5 27.6 %collective-permute-start.3 = (bf16[64,3072]{1,0:T(8,128)(2,1)}, bf16[64,3072]{1,0:T(8,128)(2,1)}, u32[]{:S(2)}, u32[]{:S(2)}) collective-permute-start(bf16[64,3072]{1,0:T(8,128)(2,1)} %get-tuple-element.10), channel_id=1, source_target_pairs={{0,4},{1,5},{2,6},{3,7},{4,0},{5,1},{6,2},{7,3},{8,12},{9,13},{10,... | collective-permute-start | bytes 1179656 | tf_op jit(solution)/shard_map/ppermute | solution.py:210
  313.5 30.2 %collective-permute-start.4 = (bf16[64,3072]{1,0:T(8,128)(2,1)}, bf16[64,3072]{1,0:T(8,128)(2,1)}, u32[]{:S(2)}, u32[]{:S(2)}) collective-permute-start(bf16[64,3072]{1,0:T(8,128)(2,1)} %get-tuple-element.9), channel_id=1, source_target_pairs={{0,5},{1,6},{2,7},{3,0},{4,1},{5,2},{6,3},{7,4},{8,13},{9,14},{10,... | collective-permute-start | bytes 1179656 | tf_op jit(solution)/shard_map/ppermute | solution.py:210
  319.9 23.8 %collective-permute-start.5 = (bf16[64,3072]{1,0:T(8,128)(2,1)S(1)}, bf16[64,3072]{1,0:T(8,128)(2,1)}, u32[]{:S(2)}, u32[]{:S(2)}) collective-permute-start(bf16[64,3072]{1,0:T(8,128)(2,1)S(1)} %get-tuple-element.8), channel_id=1, source_target_pairs={{0,6},{1,7},{2,0},{3,1},{4,2},{5,3},{6,4},{7,5},{8,14},{9,15},{10,... | collective-permute-start | bytes 1179656 | tf_op jit(solution)/shard_map/ppermute | solution.py:210
  321.5 0.8 copy-start.8
  322.3 23.6 %collective-permute-start.6 = (bf16[64,3072]{1,0:T(8,128)(2,1)S(1)}, bf16[64,3072]{1,0:T(8,128)(2,1)}, u32[]{:S(2)}, u32[]{:S(2)}) collective-permute-start(bf16[64,3072]{1,0:T(8,128)(2,1)S(1)} %get-tuple-element.7), channel_id=1, source_target_pairs={{0,7},{1,0},{2,1},{3,2},{4,3},{5,4},{6,5},{7,6},{8,15},{9,8},{10,9... | collective-permute-start | bytes 1179656 | tf_op jit(solution)/shard_map/ppermute | solution.py:210

commit v2 on v1

v2 whole, which is shorter than its diff:
```python
import math

import jax
import jax.numpy as jnp
from jax import lax
from jax.experimental import pallas as pl
from jax.experimental.pallas import tpu as pltpu
from jax.sharding import Mesh
from jax.sharding import PartitionSpec as P

HD = 96
BLK = 128
ROWS = 128


def rope_tables(positions, head_size):
    half_size = head_size // 2
    frequency = jnp.exp(
        jnp.arange(half_size, dtype=jnp.float32) * (-2.0 * math.log(10000.0) / head_size)
    )
    angles = positions.astype(jnp.float32)[:, None] * frequency[None, :]
    return (jnp.cos(angles), jnp.sin(angles))


def rope_pair(vectors, cosine_table, sine_table):
    half_size = vectors.shape[-1] // 2
    first_half = vectors[..., :half_size]
    second_half = vectors[..., half_size:]
    cos_wide = cosine_table[:, None, :]
    sin_wide = sine_table[:, None, :]
    return jnp.concatenate(
        [
            first_half * cos_wide - second_half * sin_wide,
            second_half * cos_wide + first_half * sin_wide,
        ],
        axis=-1,
    )


def request_of(index, group_requests, tok_count):
    scaled = index * group_requests
    if tok_count & (tok_count - 1) == 0:
        return lax.shift_right_logical(scaled, tok_count.bit_length() - 1)
    return scaled // tok_count


def head_picker(features, head):
    rows = lax.broadcasted_iota(jnp.int32, (features, HD), 0)
    cols = lax.broadcasted_iota(jnp.int32, (features, HD), 1)
    return (rows == cols + head * HD).astype(jnp.bfloat16)


def attention_kernel(
    meta_ref, q_ref, kc_ref, vc_ref, kn_ref, vn_ref, o_ref, kh_buf, vh_buf, qh_buf, acc_ref
):
    group_len = meta_ref[0]
    group_requests = meta_ref[1]
    head = pl.program_id(0)
    tok_count, features = q_ref.shape
    score_scale = 1.0 / math.sqrt(HD)
    picker = head_picker(features, head)

    def pick(values):
        return jnp.dot(values, picker, preferred_element_type=jnp.float32).astype(jnp.bfloat16)

    kh_buf[...] = pick(kc_ref[0, 0])
    vh_buf[...] = pick(vc_ref[0, 0])
    qh_buf[...] = pick(q_ref[...])
    kn = pick(kn_ref[0])
    vn = pick(vn_ref[0])
    dims = (((1,), (1,)), ((), ()))
    for chunk in range(tok_count // ROWS):
        rows = pl.ds(chunk * ROWS, ROWS)
        q = qh_buf[rows, :]
        s_old = lax.dot_general(q, kh_buf[...], dims, preferred_element_type=jnp.float32)
        s_new = lax.dot_general(q, kn, dims, preferred_element_type=jnp.float32)
        s_old = s_old * score_scale
        s_new = s_new * score_scale
        col = lax.broadcasted_iota(jnp.int32, s_old.shape, 1)
        s_old = jnp.where(col < group_len, s_old, -1e30)
        row = chunk * ROWS + lax.broadcasted_iota(jnp.int32, s_new.shape, 0)
        key = lax.broadcasted_iota(jnp.int32, s_new.shape, 1)
        same = request_of(row, group_requests, tok_count) == request_of(
            key, group_requests, tok_count
        )
        s_new = jnp.where(same & (key <= row), s_new, -1e30)
        peak = jnp.maximum(
            jnp.max(s_old, axis=1, keepdims=True), jnp.max(s_new, axis=1, keepdims=True)
        )
        e_old = jnp.exp(s_old - peak)
        e_new = jnp.exp(s_new - peak)
        total = jnp.sum(e_old, axis=1, keepdims=True) + jnp.sum(e_new, axis=1, keepdims=True)
        p_old = (e_old / total).astype(jnp.bfloat16)
        p_new = (e_new / total).astype(jnp.bfloat16)
        out = jnp.dot(p_old, vh_buf[...], preferred_element_type=jnp.float32) + jnp.dot(
            p_new, vn, preferred_element_type=jnp.float32
        )
        placed = lax.dot_general(
            out.astype(jnp.bfloat16), picker, dims, preferred_element_type=jnp.float32
        )

        @pl.when(head == 0)
        def _():
            acc_ref[rows, :] = placed

        @pl.when(head > 0)
        def _():
            acc_ref[rows, :] = acc_ref[rows, :] + placed

    @pl.when(head == pl.num_programs(0) - 1)
    def _():
        o_ref[...] = acc_ref[...].astype(jnp.bfloat16)


def attend(meta, queries, kv_cache, new_kv):
    tok_count, features = queries.shape
    cache_len = kv_cache.shape[2]
    full_q = pl.BlockSpec((tok_count, features), lambda h, m: (0, 0))
    cache_k = pl.BlockSpec((1, 1, cache_len, features), lambda h, m: (0, 0, 0, 0))
    cache_v = pl.BlockSpec((1, 1, cache_len, features), lambda h, m: (1, 0, 0, 0))
    new_k = pl.BlockSpec((1, tok_count, features), lambda h, m: (0, 0, 0))
    new_v = pl.BlockSpec((1, tok_count, features), lambda h, m: (1, 0, 0))
    return pl.pallas_call(
        attention_kernel,
        out_shape=jax.ShapeDtypeStruct(queries.shape, jnp.bfloat16),
        grid_spec=pltpu.PrefetchScalarGridSpec(
            num_scalar_prefetch=1,
            grid=(features // HD,),
            in_specs=[full_q, cache_k, cache_v, new_k, new_v],
            out_specs=full_q,
            scratch_shapes=[
                pltpu.VMEM((cache_len, HD), jnp.bfloat16),
                pltpu.VMEM((cache_len, HD), jnp.bfloat16),
                pltpu.VMEM((tok_count, HD), jnp.bfloat16),
                pltpu.VMEM((tok_count, features), jnp.float32),
            ],
        ),
    )(meta, queries, kv_cache, kv_cache, new_kv, new_kv)


def relay_kernel(meta_ref, cache_ref, new_ref, out_ref):
    len_blocks = meta_ref[0]
    group_start = meta_ref[1]
    core = meta_ref[2]
    part = pl.program_id(0)
    dest = pl.program_id(1)
    rank_count = 2 * pl.num_programs(1)
    new_blocks = meta_ref[3]
    block = (2 * dest + (core + part) % 2 - group_start + rank_count) % rank_count
    old = block < len_blocks
    fresh = (block >= len_blocks) & (block < len_blocks + new_blocks)
    zero = jnp.zeros(new_ref.shape[1:], new_ref.dtype)
    for kv in range(2):
        out_ref[0, kv, 0] = jnp.where(
            old, cache_ref[kv, 0], jnp.where(fresh, new_ref[kv], zero)
        )


def relay(meta, kv_cache, new_kv, seq_count):
    features = kv_cache.shape[3]
    new_blocks = new_kv.shape[1] // BLK

    def block_of(p, d, m):
        rank_count = 2 * seq_count
        return (2 * d + (m[2] + p) % 2 - m[1] + rank_count) % rank_count

    def cache_map(p, d, m):
        return (0, 0, jnp.clip(block_of(p, d, m), 0, m[0] - 1), 0)

    def new_map(p, d, m):
        return (0, jnp.clip(block_of(p, d, m) - m[0], 0, new_blocks - 1), 0)

    return pl.pallas_call(
        relay_kernel,
        out_shape=jax.ShapeDtypeStruct((2, 2, seq_count, BLK, features), jnp.bfloat16),
        grid_spec=pltpu.PrefetchScalarGridSpec(
            num_scalar_prefetch=1,
            grid=(2, seq_count),
            in_specs=[
                pl.BlockSpec((2, 1, BLK, features), cache_map),
                pl.BlockSpec((2, BLK, features), new_map),
            ],
            out_specs=pl.BlockSpec((1, 2, 1, BLK, features), lambda p, d, m: (p, 0, d, 0, 0)),
        ),
    )(meta, kv_cache, new_kv)


def local(tokens, norm_gain, w_qkv, w_out, kv_cache, cached_lengths, requests, block_start):
    group_idx = lax.axis_index("seq")
    tp_rank = lax.axis_index(("x", "core"))
    tp_count = lax.axis_size(("x", "core"))
    seq_count = lax.axis_size("seq")
    tok_count, model_width = tokens.shape
    features = w_qkv.shape[2]
    head_count = features // HD
    cache_len = kv_cache.shape[2]
    group_len = lax.dynamic_index_in_dim(cached_lengths, group_idx, keepdims=False)
    group_requests = lax.dynamic_index_in_dim(requests, group_idx, keepdims=False)
    group_start = lax.dynamic_index_in_dim(block_start, group_idx, keepdims=False)
    inputs = tokens.astype(jnp.float32)
    inverse_rms = lax.rsqrt(jnp.mean(inputs * inputs, axis=-1, keepdims=True) + 1e-05)
    normed = (inputs * inverse_rms * norm_gain.astype(jnp.float32)).astype(jnp.bfloat16)

    def project(part):
        return jnp.dot(normed, w_qkv[:, part, :], preferred_element_type=jnp.float32)

    row_index = jnp.arange(tok_count, dtype=jnp.int32)
    request = row_index * group_requests // tok_count
    first_row = (request * tok_count + group_requests - 1) // group_requests
    positions = group_len + row_index - first_row
    cosine_table, sine_table = rope_tables(positions, HD)

    def rotate(projected):
        heads = projected.reshape(tok_count, head_count, HD)
        return rope_pair(heads, cosine_table, sine_table).astype(jnp.bfloat16)

    new_keys = rotate(project(1)).reshape(tok_count, features)
    new_values = project(2).astype(jnp.bfloat16)
    new_kv = jnp.stack([new_keys, new_values])
    core = lax.axis_index("core")
    relay_meta = jnp.stack(
        [group_len // BLK, group_start, core, jnp.int32(tok_count // BLK)]
    ).astype(jnp.int32)
    parts = relay(relay_meta, kv_cache, new_kv, seq_count)
    partner = lax.ppermute(parts[1], "core", [(0, 1), (1, 0)])
    lower = jnp.where(core == 0, parts[0], partner)
    upper = jnp.where(core == 0, partner, parts[0])
    joined = jnp.concatenate([lower, upper], axis=-1)
    queries = rotate(project(0)).reshape(tok_count, features)
    joined, queries = lax.optimization_barrier((joined, queries))
    received = lax.all_to_all(joined, "seq", 1, 1, tiled=True)
    decode_cache = received.reshape(2, 1, seq_count, 1, BLK, 2 * features)

    attn_meta = jnp.stack([group_len, group_requests]).astype(jnp.int32)
    attended = attend(attn_meta, queries, kv_cache, new_kv)
    received, attended = lax.optimization_barrier((received, attended))
    rows_dev = tok_count // tp_count
    partial = jnp.dot(attended, w_out, preferred_element_type=jnp.float32).astype(jnp.bfloat16)
    partial = partial.reshape(tp_count, rows_dev, model_width)
    gathered = lax.all_to_all(partial, ("x", "core"), 0, 0, tiled=True)
    summed = jnp.sum(gathered.astype(jnp.float32), axis=0)
    own_rows = lax.dynamic_slice_in_dim(inputs, tp_rank * rows_dev, rows_dev, 0)
    layer_out = (own_rows + summed).astype(jnp.bfloat16)
    return (layer_out, decode_cache)


def solution(mesh):
    seq_count, tp_count = mesh.devices.shape
    split = Mesh(mesh.devices.reshape(seq_count, tp_count // 2, 2), ("seq", "x", "core"))
    tp = ("x", "core")
    placed = (
        P("seq", None),
        P(),
        P(None, None, tp),
        P(tp, None),
        P(None, "seq", None, tp),
        P(),
        P(),
        P(),
    )
    return jax.shard_map(
        local,
        mesh=split,
        in_specs=placed,
        out_specs=(P(("seq",) + tp, None), P(None, "seq", None, None, None, tp)),
        check_vma=False,
    )
```

time: 381 us -> 239 us (0.63)
  Pallas kernels: 176 us -> 53.6 us
  waiting for transfers between devices: 14.8 us -> 89.3 us
  starting transfers between devices: 62.7 us -> 13.8 us
  local copies, waits for them, and re-layouts: 79 us -> 32.4 us
    pallas_call x1, Pallas kernels: 151 us -> 18.7 us  [relay(): pl.pallas_call(relay_kernel, out_shape=jax.ShapeDtypeStruct((2, 2, seq_co...]
    all_to_all x1 -> x2, waiting for transfers between devices: 0.01 us -> 83.3 us  [the longest x1 56.4 us: local(): received = lax.all_to_all(joined, 'seq', 1, 1, tiled=True)]
    all_to_all x1 -> x2, starting transfers between devices: 45.7 us -> 13.8 us  [the longest x1 9.33 us: local(): received = lax.all_to_all(joined, 'seq', 1, 1, tiled=True)]
    reshape x3 -> x0, local copies, waits for them, and re-layouts: 26.1 us -> none  [the longest x1 14.6 us: local(): decode_cache = received.reshape(2, 1, seq_count, 1, BLK, 2 * features)]
    ppermute x7 -> x1, starting transfers between devices: 17 us -> 0.01 us  [local(): partner = lax.ppermute(parts[1], 'core', [(0, 1), (1, 0)])]
    transpose x2 -> x0, local copies, waits for them, and re-layouts: 14 us -> none  [the longest x1 12.8 us: local(): received.reshape(seq_count, 2, 2, BLK, features).transpose(2, 0, 3, 1, 4)]
    pallas_call x1, Pallas kernels: 25.3 us -> 34.9 us  [attend(): pl.pallas_call(attention_kernel, out_shape=jax.ShapeDtypeStruct(queries.s...]
    ppermute x7 -> x1, waiting for transfers between devices: 14.8 us -> 5.97 us  [local(): partner = lax.ppermute(parts[1], 'core', [(0, 1), (1, 0)])]
  transfers between devices with their start and end apart: 8 -> 3, of which waited for: 5 -> 3; matrix products, arithmetic and copies ran while one was open for 14% -> 6% of each run, Pallas kernels for 7% -> 15%
where the time goes in v2:
time: 239 us; the launch traced here: 237 us
  waiting for transfers between devices  89.3 us (37%)
  Pallas kernels  53.6 us (22%)
  local copies, waits for them, and re-layouts  32.4 us (14%)
  other arithmetic  27.6 us (12%)
  matrix products  16.4 us (7%)
  starting transfers between devices  13.8 us (6%)
  between operations  4.11 us (2%)
    all_to_all x1, waiting for transfers between devices, local(): received = lax.all_to_all(joined, 'seq', 1, 1, tiled=True)  56.4 us
    pallas_call x1, Pallas kernels, attend(): pl.pallas_call(attention_kernel, out_shape=jax.ShapeDtypeStruct(queries.s...  34.9 us
    all_to_all x1, waiting for transfers between devices, local(): gathered = lax.all_to_all(partial, ('x', 'core'), 0, 0, tiled=True)  26.9 us
    pallas_call x1, Pallas kernels, relay(): pl.pallas_call(relay_kernel, out_shape=jax.ShapeDtypeStruct((2, 2, seq_co...  18.7 us
    dot_general x3, local copies, waits for them, and re-layouts, project(): jnp.dot(normed, w_qkv[:, part, :], preferred_element_type=jnp.float32)  13.6 us
    dot_general x3, matrix products, project(): jnp.dot(normed, w_qkv[:, part, :], preferred_element_type=jnp.float32)  11.9 us
    all_to_all x1, starting transfers between devices, local(): received = lax.all_to_all(joined, 'seq', 1, 1, tiled=True)  9.33 us
    unnamed x11, local copies, waits for them, and re-layouts  6.17 us
  transfers between devices with their start and end apart: 3, of which 3 were waited for; matrix products, arithmetic and copies ran while one was open for 6% of the time, Pallas kernels for 15%

profile of v2, /device:TPU:0, one launch (start us, length us, event | category | flops | bytes accessed | tf_op | source)
XLA Modules:
  0.0 237.2 jit_solution(5910173319575625691)
XLA Ops:
  0.6 0.0 copy-start
  0.6 0.0 copy-start.4
  0.7 1.5 dynamic_slice.14
  4.2 1.3 dynamic_slice.15
  5.5 1.3 dynamic_slice.16
  8.1 1.4 fusion.19
  9.5 2.6 %multiply_reduce_fusion = f32[512]{0:T(512)S(1)} fusion(bf16[512,3072]{1,0:T(8,128)(2,1)} %param.8), kind=kLoop, calls=%fused_computation.3 | loop fusion | flops 4718080 | bytes 3147776 | tf_op jit(solution)/shard_map/reduce_sum | solution.py:201
  12.1 0.0 copy-done.4
  12.1 5.0 %slice_bitcast_fusion.2 = (bf16[384,3072]{0,1:T(8,128)(2,1)}, bf16[384,3072]{0,1:T(8,128)(2,1)}) fusion(bf16[3072,3,384]{2,0,1:T(8,128)(2,1)} %param.10), kind=kLoop, calls=%fused_computation.15 | loop fusion | bytes 9437184 | tf_op jit(solution)/shard_map/dot_general | solution.py:205
  17.1 4.3 %copy.22 = bf16[384,3072]{1,0:T(8,128)(2,1)} copy(bf16[384,3072]{0,1:T(8,128)(2,1)} %get-tuple-element.16) | data formatting | bytes 4718592 | tf_op jit(solution)/shard_map/dot_general | solution.py:205
  21.4 0.0 copy-start.1
  21.4 0.0 copy-start.2
  21.4 5.3 %fusion.10 = bf16[1,512,384]{2,1,0:T(8,128)(2,1)} fusion(bf16[3072,3,384]{2,0,1:T(8,128)(2,1)} %param.10, f32[3072]{0:T(1024)S(1)} %convert_element_type.45, f32[512]{0:T(512)S(1)} %add_rsqrt_fusion, bf16[512,3072]{1,0:T(8,128)(2,1)} %param.8), kind=kOutput, calls=%fused_computation.19 | convolution fusion | flops 1214447616 | bytes 5912576 | tf_op jit(solution)/shard_map/dot_general | solution.py:205
  26.8 0.0 copy-done.1
  26.8 0.0 copy-done.2
  26.8 2.4 %fusion = f32[512,4,96]{0,2,1:T(8,128)} fusion(bf16[4,96,3072]{2,1,0:T(8,128)(2,1)S(1)} %bitcast.46, f32[3072]{0:T(1024)S(1)} %convert_element_type.45, f32[512]{0:T(512)S(1)} %add_rsqrt_fusion, bf16[512,3072]{1,0:T(8,128)(2,1)S(1)} %copy-done.1), kind=kOutput, calls=%fused_computation.7 | convolution fusion | flops 1214251008 | bytes 6305792 | tf_op jit(solution)/shard_map/dot_general | solution.py:205
  29.2 4.3 %copy.20 = bf16[384,3072]{1,0:T(8,128)(2,1)} copy(bf16[384,3072]{0,1:T(8,128)(2,1)} %get-tuple-element.17) | data formatting | bytes 4718592 | tf_op jit(solution)/shard_map/dot_general | solution.py:205
  33.5 0.0 copy-start.3
  33.5 4.2 %fusion.2 = f32[512,4,96]{0,2,1:T(8,128)S(1)} fusion(bf16[4,96,3072]{2,1,0:T(8,128)(2,1)} %bitcast.45, f32[3072]{0:T(1024)S(1)} %convert_element_type.45, f32[512]{0:T(512)S(1)} %add_rsqrt_fusion, bf16[512,3072]{1,0:T(8,128)(2,1)} %param.8), kind=kOutput, calls=%fused_computation.9 | convolution fusion | flops 1214251008 | bytes 6305792 | tf_op jit(solution)/shard_map/dot_general | solution.py:205
  37.6 0.4 multiply_cosine_fusion
  38.1 0.0 copy-done.3
  38.1 0.3 subtract_convert_fusion
  38.4 0.2 copy.21
  38.6 2.0 pad_maximum_fusion.1.new_ref.kn_ref.vn_ref
  40.6 1.3 pad_add_fusion.meta_ref
  41.9 18.7 %shard_map.95 = bf16[2,2,16,128,384]{4,3,2,1,0:T(8,128)(2,1)} custom-call(s32[4]{0:T(128)} %pad_add_fusion.meta_ref, bf16[2,1,3584,384]{3,2,1,0:T(8,128)(2,1)} %vc_ref.1, bf16[2,512,384]{2,1,0:T(8,128)(2,1)} %pad_maximum_fusion.1.new_ref.kn_ref.vn_ref), custom_call_target="tpu_custom_call" | custom-call | tf_op jit(solution)/shard_map/pallas_call | solution.py:173
  60.5 4.1 %slice_bitcast_fusion = bf16[2,16,128,384]{3,2,1,0:T(8,128)(2,1)} fusion(bf16[2,2,16,128,384]{4,3,2,1,0:T(8,128)(2,1)} %shard_map.95), kind=kLoop, calls=%fused_computation.5 | loop fusion | bytes 6291456 | tf_op jit(solution)/shard_map/squeeze | solution.py:225
  64.6 0.0 collective-permute-start
  64.7 6.0 %collective-permute-done = bf16[2,16,128,384]{3,2,1,0:T(8,128)(2,1)} collective-permute-done((bf16[2,16,128,384]{3,2,1,0:T(8,128)(2,1)}, bf16[2,16,128,384]{3,2,1,0:T(8,128)(2,1)}, u32[]{:S(2)}, u32[]{:S(2)}) %collective-permute-start) | collective-permute-done | bytes 3145760 | tf_op jit(solution)/shard_map/ppermute | solution.py:225
  70.6 5.1 %broadcast_select_fusion.1 = (bf16[2,16,128,384]{3,2,1,0:T(8,128)(2,1)S(1)}, bf16[2,16,128,384]{3,2,1,0:T(8,128)(2,1)}) fusion(bf16[2,16,128,384]{3,2,1,0:T(8,128)(2,1)} %collective-permute-done, pred[]{:T(512)S(6)} %eq.4, bf16[2,2,16,128,384]{4,3,2,1,0:T(8,128)(2,1)} %shard_map.95), kind=kLoop, calls=%fused_computation.12 | loop fusion | flops 3145728 | bytes 12582913 | tf_op jit(solution)/shard_map/jit(_where)/select_n | solution.py:226
  75.8 2.7 %pad_maximum_fusion = bf16[2,16,128,768]{3,2,1,0:T(8,128)(2,1)S(1)} fusion(bf16[2,16,128,384]{3,2,1,0:T(8,128)(2,1)} %get-tuple-element.15, bf16[2,16,128,384]{3,2,1,0:T(8,128)(2,1)S(1)} %get-tuple-element.14), kind=kLoop, calls=%fused_computation | loop fusion | flops 12582912 | bytes 12582912 | tf_op jit(solution)/shard_map/concatenate | solution.py:228
  78.5 3.4 %copy.23 = bf16[2,16,128,768]{3,2,0,1:T(8,128)(2,1)} copy(bf16[2,16,128,768]{3,2,1,0:T(8,128)(2,1)S(1)} %pad_maximum_fusion) | data formatting | bytes 12582912 | tf_op jit(solution)/shard_map/optimization_barrier | solution.py:230
  81.8 9.3 %all-to-all-start = ((bf16[2,16,128,768]{3,2,0,1:T(8,128)(2,1)}), bf16[2,16,128,768]{3,2,0,1:T(8,128)(2,1)}, u32[]{:S(2)}, u32[]{:S(2)}) async-start(bf16[2,16,128,768]{3,2,0,1:T(8,128)(2,1)} %copy.23), calls=%async_computation | async-start | bytes 12582912 | tf_op jit(solution)/shard_map/all_to_all | solution.py:231
  91.2 1.9 pad_add_fusion.1.meta_ref
  93.1 0.9 copy.24.q_ref
  94.0 34.9 %shard_map.96 = bf16[512,384]{1,0:T(8,128)(2,1)} custom-call(s32[2]{0:T(128)} %pad_add_fusion.1.meta_ref, bf16[512,384]{1,0:T(8,128)(2,1)} %copy.24.q_ref, bf16[2,1,3584,384]{3,2,1,0:T(8,128)(2,1)} %vc_ref.1, bf16[2,1,3584,384]{3,2,1,0:T(8,128)(2,1)} %vc_ref.1, bf16[2,512,384]{2,1,0:T(8,128)(2,1)} %pad_maximum_fusion.1.new_ref.kn_ref.vn_ref, ...), custom_call_target="tpu_custom_call" | custom-call | tf_op jit(solution)/shard_map/pallas_call | solution.py:123
  128.9 56.4 %all-to-all-done = bf16[2,16,128,768]{3,2,0,1:T(8,128)(2,1)} async-done(((bf16[2,16,128,768]{3,2,0,1:T(8,128)(2,1)}), bf16[2,16,128,768]{3,2,0,1:T(8,128)(2,1)}, u32[]{:S(2)}, u32[]{:S(2)}) %all-to-all-start) | async-done | bytes 6291488 | tf_op jit(solution)/shard_map/all_to_all | solution.py:231
  185.3 0.0 copy-done
  185.3 4.4 %convolution_convert_fusion = bf16[512,3072]{1,0:T(8,128)(2,1)} fusion(bf16[512,384]{1,0:T(8,128)(2,1)} %shard_map.96, bf16[384,3072]{1,0:T(8,128)(2,1)S(1)} %copy-done), kind=kOutput, calls=%fused_computation.4 | convolution fusion | flops 1209532416 | bytes 5898240 | tf_op jit(solution)/shard_map/dot_general | solution.py:238
  189.8 4.4 %all-to-all-start.1 = ((bf16[8,64,3072]{2,1,0:T(8,128)(2,1)}), bf16[8,64,3072]{2,1,0:T(8,128)(2,1)}, u32[]{:S(2)}, u32[]{:S(2)}) async-start(bf16[8,64,3072]{2,1,0:T(8,128)(2,1)} %bitcast.44), calls=%async_computation.1 | async-start | bytes 6291456 | tf_op jit(solution)/shard_map/all_to_all | solution.py:240
  194.2 5.3 %convert_element_type.44 = f32[512,3072]{1,0:T(8,128)} convert(bf16[512,3072]{1,0:T(8,128)(2,1)} %param.8) | non-fusion elementwise | flops 1572864 | bytes 9437184 | tf_op jit(solution)/shard_map/convert_element_type | solution.py:200
  199.6 6.1 %copy.25 = bf16[2,1,16,1,128,768]{5,4,3,2,1,0:T(8,128)(2,1)} copy(bf16[2,1,16,1,128,768]{5,4,0,2,3,1:T(8,128)(2,1)} %bitcast.18) | data formatting | bytes 12582912
  205.7 26.9 %all-to-all-done.1 = bf16[8,64,3072]{2,1,0:T(8,128)(2,1)} async-done(((bf16[8,64,3072]{2,1,0:T(8,128)(2,1)}), bf16[8,64,3072]{2,1,0:T(8,128)(2,1)}, u32[]{:S(2)}, u32[]{:S(2)}) %all-to-all-start.1) | async-done | bytes 3145760 | tf_op jit(solution)/shard_map/all_to_all | solution.py:240
  232.6 2.5 %convert_reduce_fusion = f32[64,3072]{1,0:T(8,128)S(1)} fusion(bf16[8,64,3072]{2,1,0:T(8,128)(2,1)} %all-to-all-done.1), kind=kLoop, calls=%fused_computation.1 | loop fusion | flops 2949120 | bytes 3932160 | tf_op jit(solution)/shard_map/reduce_sum | solution.py:241
  235.2 2.0 add_convert_fusion
  (5 shorter events, 0.1 us)
Async XLA Ops:
  0.6 184.7 %copy-start = (bf16[384,3072]{1,0:T(8,128)(2,1)S(1)}, bf16[384,3072]{1,0:T(8,128)(2,1)}, u32[]{:S(2)}) copy-start(bf16[384,3072]{1,0:T(8,128)(2,1)} %param.11) | copy-start | bytes 7077892
  0.6 11.4 %copy-start.4 = (bf16[3072]{0:T(1024)(128)(2,1)S(1)}, bf16[3072]{0:T(1024)(128)(2,1)}, u32[]{:S(2)}) copy-start(bf16[3072]{0:T(1024)(128)(2,1)} %param.9) | copy-start | bytes 18436
  21.4 5.3 %copy-start.1 = (bf16[512,3072]{1,0:T(8,128)(2,1)S(1)}, bf16[512,3072]{1,0:T(8,128)(2,1)}, u32[]{:S(2)}) copy-start(bf16[512,3072]{1,0:T(8,128)(2,1)} %param.8) | copy-start | bytes 9437188
  21.4 5.3 %copy-start.2 = (bf16[384,3072]{1,0:T(8,128)(2,1)S(1)}, bf16[384,3072]{1,0:T(8,128)(2,1)}, u32[]{:S(2)}) copy-start(bf16[384,3072]{1,0:T(8,128)(2,1)} %copy.22) | copy-start | bytes 7077892
  33.5 4.6 %copy-start.3 = (f32[512,4,96]{0,2,1:T(8,128)S(1)}, f32[512,4,96]{0,2,1:T(8,128)}, u32[]{:S(2)}) copy-start(f32[512,4,96]{0,2,1:T(8,128)} %fusion) | copy-start | bytes 2359300
  64.6 6.0 %collective-permute-start = (bf16[2,16,128,384]{3,2,1,0:T(8,128)(2,1)}, bf16[2,16,128,384]{3,2,1,0:T(8,128)(2,1)}, u32[]{:S(2)}, u32[]{:S(2)}) collective-permute-start(bf16[2,16,128,384]{3,2,1,0:T(8,128)(2,1)} %slice_bitcast_fusion), channel_id=1, source_target_pairs={{0,1},{1,0},{2,3},{3,2},{4,5},{5,4},{6,7},{7,6},{8,9},{9,8},{10,11... | collective-permute-start | bytes 9437192 | tf_op jit(solution)/shard_map/ppermute | solution.py:225
  81.8 103.5 %all-to-all-start = ((bf16[2,16,128,768]{3,2,0,1:T(8,128)(2,1)}), bf16[2,16,128,768]{3,2,0,1:T(8,128)(2,1)}, u32[]{:S(2)}, u32[]{:S(2)}) async-start(bf16[2,16,128,768]{3,2,0,1:T(8,128)(2,1)} %copy.23), calls=%async_computation | async-start | bytes 12582912 | tf_op jit(solution)/shard_map/all_to_all | solution.py:231
  189.8 42.9 %all-to-all-start.1 = ((bf16[8,64,3072]{2,1,0:T(8,128)(2,1)}), bf16[8,64,3072]{2,1,0:T(8,128)(2,1)}, u32[]{:S(2)}, u32[]{:S(2)}) async-start(bf16[8,64,3072]{2,1,0:T(8,128)(2,1)} %bitcast.44), calls=%async_computation.1 | async-start | bytes 6291456 | tf_op jit(solution)/shard_map/all_to_all | solution.py:240

commit v3 on v2

--- a/solution.py
+++ b/solution.py
@@ -138,51 +138,79 @@
     )(meta, queries, kv_cache, kv_cache, new_kv, new_kv)
 
 
-def relay_kernel(meta_ref, cache_ref, new_ref, out_ref):
+def relay_kernel(meta_ref, own_c, own_n, other_c, other_n, own_ref, other_ref):
     len_blocks = meta_ref[0]
     group_start = meta_ref[1]
     core = meta_ref[2]
-    part = pl.program_id(0)
-    dest = pl.program_id(1)
-    rank_count = 2 * pl.num_programs(1)
     new_blocks = meta_ref[3]
-    block = (2 * dest + (core + part) % 2 - group_start + rank_count) % rank_count
-    old = block < len_blocks
-    fresh = (block >= len_blocks) & (block < len_blocks + new_blocks)
-    zero = jnp.zeros(new_ref.shape[1:], new_ref.dtype)
-    for kv in range(2):
-        out_ref[0, kv, 0] = jnp.where(
-            old, cache_ref[kv, 0], jnp.where(fresh, new_ref[kv], zero)
-        )
+    dest = pl.program_id(0)
+    rank_count = 2 * pl.num_programs(0)
+    zero = jnp.zeros(own_n.shape[1:], own_n.dtype)
+    for part, cache_ref, new_ref, out_ref in ((0, own_c, own_n, own_ref), (1, other_c, other_n, other_ref)):
+        block = (2 * dest + (core + part) % 2 - group_start + rank_count) % rank_count
+        old = block < len_blocks
+        fresh = (block >= len_blocks) & (block < len_blocks + new_blocks)
+        for kv in range(2):
+            out_ref[0, kv] = jnp.where(
+                old, cache_ref[kv, 0], jnp.where(fresh, new_ref[kv], zero)
+            )
 
 
 def relay(meta, kv_cache, new_kv, seq_count):
     features = kv_cache.shape[3]
     new_blocks = new_kv.shape[1] // BLK
-
-    def block_of(p, d, m):
-        rank_count = 2 * seq_count
-        return (2 * d + (m[2] + p) % 2 - m[1] + rank_count) % rank_count
-
-    def cache_map(p, d, m):
-        return (0, 0, jnp.clip(block_of(p, d, m), 0, m[0] - 1), 0)
-
-    def new_map(p, d, m):
-        return (0, jnp.clip(block_of(p, d, m) - m[0], 0, new_blocks - 1), 0)
+    rank_count = 2 * seq_count
+
+    def block_of(part, d, m):
+        return (2 * d + (m[2] + part) % 2 - m[1] + rank_count) % rank_count
+
+    def cache_spec(part):
+        return pl.BlockSpec(
+            (2, 1, BLK, features),
+            lambda d, m: (0, 0, jnp.clip(block_of(part, d, m), 0, m[0] - 1), 0),
+        )
+
+    def new_spec(part):
+        return pl.BlockSpec(
+            (2, BLK, features),
+            lambda d, m: (0, jnp.clip(block_of(part, d, m) - m[0], 0, new_blocks - 1), 0),
+        )
 
     return pl.pallas_call(
         relay_kernel,
-        out_shape=jax.ShapeDtypeStruct((2, 2, seq_count, BLK, features), jnp.bfloat16),
+        out_shape=(
+            jax.ShapeDtypeStruct((seq_count, 2, BLK, 2 * features), jnp.bfloat16),
+            jax.ShapeDtypeStruct((seq_count, 2, BLK, features), jnp.bfloat16),
+        ),
         grid_spec=pltpu.PrefetchScalarGridSpec(
             num_scalar_prefetch=1,
-            grid=(2, seq_count),
-            in_specs=[
-                pl.BlockSpec((2, 1, BLK, features), cache_map),
-                pl.BlockSpec((2, BLK, features), new_map),
-            ],
-            out_specs=pl.BlockSpec((1, 2, 1, BLK, features), lambda p, d, m: (p, 0, d, 0, 0)),
+            grid=(seq_count,),
+            in_specs=[cache_spec(0), new_spec(0), cache_spec(1), new_spec(1)],
+            out_specs=(
+                pl.BlockSpec((1, 2, BLK, features), lambda d, m: (d, 0, 0, m[2])),
+                pl.BlockSpec((1, 2, BLK, features), lambda d, m: (d, 0, 0, 0)),
+            ),
         ),
-    )(meta, kv_cache, new_kv)
+    )(meta, kv_cache, new_kv, kv_cache, new_kv)
+
+
+def projection_kernel(x_ref, w_ref, o_ref):
+    o_ref[0] = jnp.dot(x_ref[...], w_ref[0], preferred_element_type=jnp.float32)
+
+
+def project_all(normed, weights):
+    parts, width, features = weights.shape
+    rows = normed.shape[0]
+    return pl.pallas_call(
+        projection_kernel,
+        out_shape=jax.ShapeDtypeStruct((parts, rows, features), jnp.float32),
+        grid=(parts,),
+        in_specs=[
+            pl.BlockSpec((rows, width), lambda k: (0, 0)),
+            pl.BlockSpec((1, width, features), lambda k: (k, 0, 0)),
+        ],
+        out_specs=pl.BlockSpec((1, rows, features), lambda k: (k, 0, 0)),
+    )(normed, weights)
 
 
 def local(tokens, norm_gain, w_qkv, w_out, kv_cache, cached_lengths, requests, block_start):
@@ -201,8 +229,10 @@
     inverse_rms = lax.rsqrt(jnp.mean(inputs * inputs, axis=-1, keepdims=True) + 1e-05)
     normed = (inputs * inverse_rms * norm_gain.astype(jnp.float32)).astype(jnp.bfloat16)
 
+    projected = project_all(normed, jnp.transpose(w_qkv, (1, 0, 2)))
+
     def project(part):
-        return jnp.dot(normed, w_qkv[:, part, :], preferred_element_type=jnp.float32)
+        return projected[part]
 
     row_index = jnp.arange(tok_count, dtype=jnp.int32)
     request = row_index * group_requests // tok_count
@@ -221,24 +251,27 @@
     relay_meta = jnp.stack(
         [group_len // BLK, group_start, core, jnp.int32(tok_count // BLK)]
     ).astype(jnp.int32)
-    parts = relay(relay_meta, kv_cache, new_kv, seq_count)
-    partner = lax.ppermute(parts[1], "core", [(0, 1), (1, 0)])
-    lower = jnp.where(core == 0, parts[0], partner)
-    upper = jnp.where(core == 0, partner, parts[0])
-    joined = jnp.concatenate([lower, upper], axis=-1)
+    own, other = relay(relay_meta, kv_cache, new_kv, seq_count)
+    partner = lax.ppermute(other, "core", [(0, 1), (1, 0)])
+    zero_index = jnp.zeros((), jnp.int32)
+    joined = lax.dynamic_update_slice(
+        own, partner, (zero_index, zero_index, zero_index, (1 - core) * features)
+    )
     queries = rotate(project(0)).reshape(tok_count, features)
     joined, queries = lax.optimization_barrier((joined, queries))
-    received = lax.all_to_all(joined, "seq", 1, 1, tiled=True)
-    decode_cache = received.reshape(2, 1, seq_count, 1, BLK, 2 * features)
+    received = lax.all_to_all(joined, "seq", 0, 0, tiled=True)
+    decode_cache = received.transpose(1, 0, 2, 3).reshape(2, 1, seq_count, 1, BLK, 2 * features)
 
     attn_meta = jnp.stack([group_len, group_requests]).astype(jnp.int32)
     attended = attend(attn_meta, queries, kv_cache, new_kv)
-    received, attended = lax.optimization_barrier((received, attended))
     rows_dev = tok_count // tp_count
     partial = jnp.dot(attended, w_out, preferred_element_type=jnp.float32).astype(jnp.bfloat16)
-    partial = partial.reshape(tp_count, rows_dev, model_width)
-    gathered = lax.all_to_all(partial, ("x", "core"), 0, 0, tiled=True)
-    summed = jnp.sum(gathered.astype(jnp.float32), axis=0)
+    summed = lax.dynamic_slice_in_dim(partial, tp_rank * rows_dev, rows_dev, 0).astype(jnp.float32)
+    for shift in range(1, tp_count):
+        target = (tp_rank + shift) % tp_count
+        chunk = lax.dynamic_slice_in_dim(partial, target * rows_dev, rows_dev, 0)
+        pairs = [(source, (source + shift) % tp_count) for source in range(tp_count)]
+        summed = summed + lax.ppermute(chunk, ("x", "core"), pairs).astype(jnp.float32)
     own_rows = lax.dynamic_slice_in_dim(inputs, tp_rank * rows_dev, rows_dev, 0)
     layer_out = (own_rows + summed).astype(jnp.bfloat16)
     return (layer_out, decode_cache)

time: 239 us -> 169 us (0.71)
  waiting for transfers between devices: 89.3 us -> 30.7 us
  matrix products: 16.4 us -> 2.8 us
  starting transfers between devices: 13.8 us -> 25.3 us
  local copies, waits for them, and re-layouts: 32.4 us -> 24.5 us
  other arithmetic: 27.6 us -> 24.9 us
  Pallas kernels: 53.6 us -> 56.2 us
    all_to_all x2 -> x1, waiting for transfers between devices: 83.3 us -> 9.95 us  [local(): received = lax.all_to_all(joined, 'seq', 0, 0, tiled=True)]
    ppermute x1 -> x8, starting transfers between devices: 0.01 us -> 17 us  [the longest x7 17 us: local(): lax.ppermute(chunk, ('x', 'core'), pairs).astype(jnp.float32)]
    ppermute x1 -> x8, waiting for transfers between devices: 5.97 us -> 20.7 us  [the longest x7 14.8 us: local(): lax.ppermute(chunk, ('x', 'core'), pairs).astype(jnp.float32)]
    dot_general x3 -> x0, local copies, waits for them, and re-layouts: 13.6 us -> none  [project(): jnp.dot(normed, w_qkv[:, part, :], preferred_element_type=jnp.float32)]
    dot_general x3 -> x0, matrix products: 11.9 us -> none  [project(): jnp.dot(normed, w_qkv[:, part, :], preferred_element_type=jnp.float32)]
    slice x0 -> x4, local copies, waits for them, and re-layouts: none -> 6.97 us  [project(): return projected[part]]
    all_to_all x2 -> x1, starting transfers between devices: 13.8 us -> 8.35 us  [local(): received = lax.all_to_all(joined, 'seq', 0, 0, tiled=True)]
    select_n x1 -> x0, other arithmetic: 5.11 us -> none  [local(): lower = jnp.where(core == 0, parts[0], partner)]
  transfers between devices with their start and end apart: 3 -> 9, of which waited for: 3 -> 7; matrix products, arithmetic and copies ran while one was open for 6% -> 9% of each run, Pallas kernels for 15% -> 21%
where the time goes in v3:
time: 169 us; the launch traced here: 168 us
  Pallas kernels  56.2 us (33%)
  waiting for transfers between devices  30.7 us (18%)
  starting transfers between devices  25.3 us (15%)
  other arithmetic  24.9 us (15%)
  local copies, waits for them, and re-layouts  24.5 us (14%)
  between operations  3.76 us (2%)
  matrix products  2.8 us (2%)
    pallas_call x1, Pallas kernels, attend(): pl.pallas_call(attention_kernel, out_shape=jax.ShapeDtypeStruct(queries.s...  34.9 us
    ppermute x7, starting transfers between devices, local(): lax.ppermute(chunk, ('x', 'core'), pairs).astype(jnp.float32)  17 us
    ppermute x7, waiting for transfers between devices, local(): lax.ppermute(chunk, ('x', 'core'), pairs).astype(jnp.float32)  14.8 us
    pallas_call x1, Pallas kernels, relay(): pl.pallas_call(relay_kernel, out_shape=(jax.ShapeDtypeStruct((seq_count,...  12.2 us
    all_to_all x1, waiting for transfers between devices, local(): received = lax.all_to_all(joined, 'seq', 0, 0, tiled=True)  9.95 us
    pallas_call x1, Pallas kernels, project_all(): pl.pallas_call(projection_kernel, out_shape=jax.ShapeDtypeStruct((parts,...  9.03 us
    unnamed x15, local copies, waits for them, and re-layouts  8.58 us
    all_to_all x1, starting transfers between devices, local(): received = lax.all_to_all(joined, 'seq', 0, 0, tiled=True)  8.35 us
  transfers between devices with their start and end apart: 9, of which 7 were waited for; matrix products, arithmetic and copies ran while one was open for 9% of the time, Pallas kernels for 21%

profile of v3, /device:TPU:0, one launch (start us, length us, event | category | flops | bytes accessed | tf_op | source)
XLA Modules:
  0.0 168.2 jit_solution(4445674744177749133)
XLA Ops:
  0.6 0.0 copy-start
  0.7 1.4 dynamic_slice.38
  3.7 0.7 convert_element_type.65
  4.4 2.6 %multiply_reduce_fusion = f32[512]{0:T(512)S(1)} fusion(bf16[512,3072]{1,0:T(8,128)(2,1)} %param.8), kind=kLoop, calls=%fused_computation.1 | loop fusion | flops 4718080 | bytes 3147776 | tf_op jit(solution)/shard_map/reduce_sum | solution.py:229
  7.0 4.7 %multiply_convert_fusion.x_ref = bf16[512,3072]{1,0:T(8,128)(2,1)} fusion(f32[3072]{0:T(1024)S(1)} %convert_element_type.65, f32[512]{0:T(512)S(1)} %add_rsqrt_fusion, bf16[512,3072]{1,0:T(8,128)(2,1)} %param.8), kind=kLoop, calls=%fused_computation | loop fusion | flops 6291456 | bytes 6305792 | tf_op jit(solution)/shard_map/convert_element_type | solution.py:230
  11.7 9.0 %shard_map.95 = f32[3,512,384]{2,1,0:T(8,128)} custom-call(bf16[512,3072]{1,0:T(8,128)(2,1)} %multiply_convert_fusion.x_ref, bf16[3,3072,384]{2,1,0:T(8,128)(2,1)} %bitcast.14), custom_call_target="tpu_custom_call" | custom-call | tf_op jit(solution)/shard_map/pallas_call | solution.py:204
  20.7 2.4 %fusion.9 = (f32[1,512,384]{2,1,0:T(8,128)S(1)}, f32[1,512,384]{2,1,0:T(8,128)}) fusion(f32[3,512,384]{2,1,0:T(8,128)} %shard_map.95), kind=kLoop, calls=%fused_computation.44 | loop fusion | bytes 3145728 | tf_op jit(solution)/shard_map/slice | solution.py:235
  23.1 1.2 slice.45
  24.8 0.6 dynamic_slice.40
  25.4 0.6 dynamic_slice.39
  26.7 1.4 fusion.6
  28.1 2.3 %copy.11 = f32[1,512,384]{1,2,0:T(8,128)} copy(f32[1,512,384]{2,1,0:T(8,128)} %get-tuple-element.22) | data formatting | bytes 1572864 | tf_op jit(solution)/shard_map/slice | solution.py:235
  30.4 1.1 copy.13
  31.5 0.4 multiply_cosine_fusion
  31.9 2.3 %subtract_convert_fusion = (bf16[512,4,48]{0,2,1:T(8,128)(2,1)}, bf16[512,4,48]{0,2,1:T(8,128)(2,1)}, bf16[512,4,48]{0,2,1:T(8,128)(2,1)S(1)}, bf16[512,4,48]{0,2,1:T(8,128)(2,1)S(1)}) fusion(f32[512,4,96]{0,2,1:T(8,128)} %bitcast.16, f32[512,48]{0,1:T(8,128)S(1)} %get-tuple-element.30, f32[512,48]{0,1:T(8,128)S(1)} %get-tuple-element.29, ...), kind=kLoop, calls=%fused_computation.9 | loop fusion | flops 1572864 | bytes 2555904 | tf_op jit(solution)/shard_map/convert
  34.3 0.2 copy.12
  34.6 1.0 pad_maximum_fusion.own_n.other_n.kn_ref.vn_ref
  35.6 1.2 pad_add_fusion.1.meta_ref
  36.8 12.2 %shard_map.96 = (bf16[16,2,128,768]{3,2,1,0:T(8,128)(2,1)}, bf16[16,2,128,384]{3,2,1,0:T(8,128)(2,1)}) custom-call(s32[4]{0:T(128)} %pad_add_fusion.1.meta_ref, bf16[2,1,3584,384]{3,2,1,0:T(8,128)(2,1)} %vc_ref.1, bf16[2,512,384]{2,1,0:T(8,128)(2,1)} %pad_maximum_fusion.own_n.other_n.kn_ref.vn_ref, bf16[2,1,3584,384]{3,2,1,0:T(8,128)(2,1)} %vc_ref.1, ...), custom_call_target="tpu_custom_call" | custom-call | tf_op jit(solution)/shard_map/pallas_call | solution.py:179
  49.1 0.0 collective-permute-start
  49.1 5.9 %collective-permute-done = bf16[16,2,128,384]{3,2,1,0:T(8,128)(2,1)} collective-permute-done((bf16[16,2,128,384]{3,2,1,0:T(8,128)(2,1)}, bf16[16,2,128,384]{3,2,1,0:T(8,128)(2,1)}, u32[]{:S(2)}, u32[]{:S(2)}) %collective-permute-start) | collective-permute-done | bytes 3145760 | tf_op jit(solution)/shard_map/ppermute | solution.py:255
  55.1 4.2 %constant_dynamic-update-slice_fusion = bf16[16,2,128,768]{3,2,1,0:T(8,128)(2,1)} fusion(bf16[16,2,128,768]{3,2,1,0:T(8,128)(2,1)} %get-tuple-element.6, bf16[16,2,128,384]{3,2,1,0:T(8,128)(2,1)} %collective-permute-done, s32[]{:T(128)S(6)} %select_n.91), kind=kLoop, calls=%fused_computation.26 | loop fusion | bytes 6291460 | tf_op jit(solution)/shard_map/dynamic_update_slice | solution.py:257
  59.2 8.3 %all-to-all-start = ((bf16[16,2,128,768]{3,2,1,0:T(8,128)(2,1)}), bf16[16,2,128,768]{3,2,1,0:T(8,128)(2,1)}, u32[]{:S(2)}, u32[]{:S(2)}) async-start(bf16[16,2,128,768]{3,2,1,0:T(8,128)(2,1)} %constant_dynamic-update-slice_fusion), calls=%async_computation | async-start | bytes 12582912 | tf_op jit(solution)/shard_map/all_to_all | solution.py:262
  67.7 1.9 %pad_add_fusion.meta_ref = s32[2]{0:T(128)} fusion(s32[1]{0:T(128)} %dynamic_slice.39, s32[1]{0:T(128)} %dynamic_slice.38), kind=kLoop, calls=%fused_computation.41 | loop fusion | flops 2 | bytes 16 | tf_op jit(solution)/shard_map/stack | solution.py:265
  69.5 0.9 copy.14.q_ref
  70.5 34.9 %shard_map.97 = bf16[512,384]{1,0:T(8,128)(2,1)} custom-call(s32[2]{0:T(128)} %pad_add_fusion.meta_ref, bf16[512,384]{1,0:T(8,128)(2,1)} %copy.14.q_ref, bf16[2,1,3584,384]{3,2,1,0:T(8,128)(2,1)} %vc_ref.1, bf16[2,1,3584,384]{3,2,1,0:T(8,128)(2,1)} %vc_ref.1, bf16[2,512,384]{2,1,0:T(8,128)(2,1)} %pad_maximum_fusion.own_n.other_n.kn_ref.vn_ref, ...), custom_call_target="tpu_custom_call" | custom-call | tf_op jit(solution)/shard_map/pallas_call | solution.py:123
  105.4 2.8 %convolution_convert_fusion = bf16[512,3072]{1,0:T(8,128)(2,1)S(1)} fusion(bf16[512,384]{1,0:T(8,128)(2,1)} %shard_map.97, bf16[384,3072]{1,0:T(8,128)(2,1)S(1)} %copy-done), kind=kOutput, calls=%fused_computation.2 | convolution fusion | flops 1209532416 | bytes 5898240 | tf_op jit(solution)/shard_map/dot_general | solution.py:268
  108.2 1.6 copy-done.1
  109.8 1.1 constant_dynamic-slice_fusion.6
  110.9 0.0 collective-permute-start.1
  111.0 1.5 collective-permute-start.2
  112.4 2.1 %collective-permute-start.3 = (bf16[64,3072]{1,0:T(8,128)(2,1)}, bf16[64,3072]{1,0:T(8,128)(2,1)}, u32[]{:S(2)}, u32[]{:S(2)}) collective-permute-start(bf16[64,3072]{1,0:T(8,128)(2,1)} %get-tuple-element.19), channel_id=1, source_target_pairs={{0,3},{1,4},{2,5},{3,6},{4,7},{5,0},{6,1},{7,2},{8,11},{9,12},{10,... | collective-permute-start | bytes 1179656 | tf_op jit(solution)/shard_map/ppermute | solution.py:274
  114.6 2.0 %collective-permute-start.4 = (bf16[64,3072]{1,0:T(8,128)(2,1)}, bf16[64,3072]{1,0:T(8,128)(2,1)}, u32[]{:S(2)}, u32[]{:S(2)}) collective-permute-start(bf16[64,3072]{1,0:T(8,128)(2,1)} %get-tuple-element.18), channel_id=1, source_target_pairs={{0,4},{1,5},{2,6},{3,7},{4,0},{5,1},{6,2},{7,3},{8,12},{9,13},{10,... | collective-permute-start | bytes 1179656 | tf_op jit(solution)/shard_map/ppermute | solution.py:274
  116.6 1.6 collective-permute-start.5
  118.1 4.8 %collective-permute-done.1 = bf16[64,3072]{1,0:T(8,128)(2,1)S(1)} collective-permute-done((bf16[64,3072]{1,0:T(8,128)(2,1)S(1)}, bf16[64,3072]{1,0:T(8,128)(2,1)S(1)}, u32[]{:S(2)}, u32[]{:S(2)}) %collective-permute-start.1) | collective-permute-done | bytes 393248 | tf_op jit(solution)/shard_map/ppermute | solution.py:274
  123.0 1.5 collective-permute-start.6
  124.5 0.0 collective-permute-done.2
  124.5 0.8 copy-done.4
  125.3 8.2 %collective-permute-start.7 = (bf16[64,3072]{1,0:T(8,128)(2,1)S(1)}, bf16[64,3072]{1,0:T(8,128)(2,1)}, u32[]{:S(2)}, u32[]{:S(2)}) collective-permute-start(bf16[64,3072]{1,0:T(8,128)(2,1)S(1)} %get-tuple-element.15), channel_id=1, source_target_pairs={{0,7},{1,0},{2,1},{3,2},{4,3},{5,4},{6,5},{7,6},{8,15},{9,8},{10,9... | collective-permute-start | bytes 1179656 | tf_op jit(solution)/shard_map/ppermute | solution.py:274
  133.6 5.4 %convert_element_type.64 = f32[512,3072]{1,0:T(8,128)} convert(bf16[512,3072]{1,0:T(8,128)(2,1)} %param.8) | non-fusion elementwise | flops 1572864 | bytes 9437184 | tf_op jit(solution)/shard_map/convert_element_type | solution.py:228
  139.0 2.0 %collective-permute-done.3 = bf16[64,3072]{1,0:T(8,128)(2,1)} collective-permute-done((bf16[64,3072]{1,0:T(8,128)(2,1)}, bf16[64,3072]{1,0:T(8,128)(2,1)}, u32[]{:S(2)}, u32[]{:S(2)}) %collective-permute-start.3) | collective-permute-done | bytes 393248 | tf_op jit(solution)/shard_map/ppermute | solution.py:274
  140.9 1.2 collective-permute-done.4
  142.1 4.7 %collective-permute-done.5 = bf16[64,3072]{1,0:T(8,128)(2,1)} collective-permute-done((bf16[64,3072]{1,0:T(8,128)(2,1)}, bf16[64,3072]{1,0:T(8,128)(2,1)}, u32[]{:S(2)}, u32[]{:S(2)}) %collective-permute-start.5) | collective-permute-done | bytes 393248 | tf_op jit(solution)/shard_map/ppermute | solution.py:274
  146.8 0.0 collective-permute-done.6
  146.8 2.1 %collective-permute-done.7 = bf16[64,3072]{1,0:T(8,128)(2,1)} collective-permute-done((bf16[64,3072]{1,0:T(8,128)(2,1)S(1)}, bf16[64,3072]{1,0:T(8,128)(2,1)}, u32[]{:S(2)}, u32[]{:S(2)}) %collective-permute-start.7) | collective-permute-done | bytes 393248 | tf_op jit(solution)/shard_map/ppermute | solution.py:274
  148.9 3.2 %add_convert_fusion = bf16[64,3072]{1,0:T(8,128)(2,1)} fusion(bf16[64,3072]{1,0:T(8,128)(2,1)} %collective-permute-done.7, bf16[64,3072]{1,0:T(8,128)(2,1)} %collective-permute-done.6, bf16[64,3072]{1,0:T(8,128)(2,1)} %collective-permute-done.5, bf16[64,3072]{1,0:T(8,128)(2,1)} %collective-permute-done.4, bf16[64,3072]{1,0:T(8,128)(2,1)} %collective-permute-done.3, ...), kind=kLoop, calls=%fused_computation.5 | loop fusion | flops 3342336 | bytes 4325380 | tf_op jit(solution)/shard_map/convert_element_type | solution.py:276
  152.1 9.9 %all-to-all-done = bf16[16,2,128,768]{3,2,1,0:T(8,128)(2,1)} async-done(((bf16[16,2,128,768]{3,2,1,0:T(8,128)(2,1)}), bf16[16,2,128,768]{3,2,1,0:T(8,128)(2,1)}, u32[]{:S(2)}, u32[]{:S(2)}) %all-to-all-start) | async-done | bytes 6291488 | tf_op jit(solution)/shard_map/all_to_all | solution.py:262
  162.1 6.1 %copy.15 = bf16[2,1,16,1,128,768]{5,4,3,2,1,0:T(8,128)(2,1)} copy(bf16[2,1,16,1,128,768]{5,4,0,2,3,1:T(8,128)(2,1)} %bitcast.10) | data formatting | bytes 12582912
  (15 shorter events, 0.1 us)
Async XLA Ops:
  0.6 104.7 %copy-start = (bf16[384,3072]{1,0:T(8,128)(2,1)S(1)}, bf16[384,3072]{1,0:T(8,128)(2,1)}, u32[]{:S(2)}) copy-start(bf16[384,3072]{1,0:T(8,128)(2,1)} %param.11) | copy-start | bytes 7077892
  11.7 13.1 %copy-start.5 = (s32[16]{0:T(128)S(1)}, s32[16]{0:T(128)}, u32[]{:S(2)}) copy-start(s32[16]{0:T(128)} %param.15) | copy-start | bytes 196
  11.7 13.7 %copy-start.6 = (s32[16]{0:T(128)S(1)}, s32[16]{0:T(128)}, u32[]{:S(2)}) copy-start(s32[16]{0:T(128)} %param.14) | copy-start | bytes 196
  36.8 12.2 %copy-start.2 = (bf16[512,4,48]{0,2,1:T(8,128)(2,1)S(1)}, bf16[512,4,48]{0,2,1:T(8,128)(2,1)}, u32[]{:S(2)}) copy-start(bf16[512,4,48]{0,2,1:T(8,128)(2,1)} %get-tuple-element.23) | copy-start | bytes 589828
  36.8 12.2 %copy-start.3 = (bf16[512,4,48]{0,2,1:T(8,128)(2,1)S(1)}, bf16[512,4,48]{0,2,1:T(8,128)(2,1)}, u32[]{:S(2)}) copy-start(bf16[512,4,48]{0,2,1:T(8,128)(2,1)} %get-tuple-element.24) | copy-start | bytes 589828
  49.1 6.0 %collective-permute-start = (bf16[16,2,128,384]{3,2,1,0:T(8,128)(2,1)}, bf16[16,2,128,384]{3,2,1,0:T(8,128)(2,1)}, u32[]{:S(2)}, u32[]{:S(2)}) collective-permute-start(bf16[16,2,128,384]{3,2,1,0:T(8,128)(2,1)} %get-tuple-element.7), channel_id=1, source_target_pairs={{0,1},{1,0},{2,3},{3,2},{4,5},{5,4},{6,7},{7,6},{8,9},{9,8},{10,11... | collective-permute-start | bytes 9437192 | tf_op jit(solution)/shard_map/ppermute | solution.py:255
  59.2 102.8 %all-to-all-start = ((bf16[16,2,128,768]{3,2,1,0:T(8,128)(2,1)}), bf16[16,2,128,768]{3,2,1,0:T(8,128)(2,1)}, u32[]{:S(2)}, u32[]{:S(2)}) async-start(bf16[16,2,128,768]{3,2,1,0:T(8,128)(2,1)} %constant_dynamic-update-slice_fusion), calls=%async_computation | async-start | bytes 12582912 | tf_op jit(solution)/shard_map/all_to_all | solution.py:262
  108.2 1.6 copy-start.1
  110.9 12.0 %collective-permute-start.1 = (bf16[64,3072]{1,0:T(8,128)(2,1)S(1)}, bf16[64,3072]{1,0:T(8,128)(2,1)S(1)}, u32[]{:S(2)}, u32[]{:S(2)}) collective-permute-start(bf16[64,3072]{1,0:T(8,128)(2,1)S(1)} %get-tuple-element.14), channel_id=1, source_target_pairs={{0,1},{1,2},{2,3},{3,4},{4,5},{5,6},{6,7},{7,0},{8,9},{9,10},{10,1... | collective-permute-start | bytes 1179656 | tf_op jit(solution)/shard_map/ppermute | solution.py:274
  111.0 13.6 %collective-permute-start.2 = (bf16[64,3072]{1,0:T(8,128)(2,1)S(1)}, bf16[64,3072]{1,0:T(8,128)(2,1)S(1)}, u32[]{:S(2)}, u32[]{:S(2)}) collective-permute-start(bf16[64,3072]{1,0:T(8,128)(2,1)S(1)} %get-tuple-element.20), channel_id=1, source_target_pairs={{0,2},{1,3},{2,4},{3,5},{4,6},{5,7},{6,0},{7,1},{8,10},{9,11},{10,... | collective-permute-start | bytes 1179656 | tf_op jit(solution)/shard_map/ppermute | solution.py:274
  112.4 28.5 %collective-permute-start.3 = (bf16[64,3072]{1,0:T(8,128)(2,1)}, bf16[64,3072]{1,0:T(8,128)(2,1)}, u32[]{:S(2)}, u32[]{:S(2)}) collective-permute-start(bf16[64,3072]{1,0:T(8,128)(2,1)} %get-tuple-element.19), channel_id=1, source_target_pairs={{0,3},{1,4},{2,5},{3,6},{4,7},{5,0},{6,1},{7,2},{8,11},{9,12},{10,... | collective-permute-start | bytes 1179656 | tf_op jit(solution)/shard_map/ppermute | solution.py:274
  114.6 27.5 %collective-permute-start.4 = (bf16[64,3072]{1,0:T(8,128)(2,1)}, bf16[64,3072]{1,0:T(8,128)(2,1)}, u32[]{:S(2)}, u32[]{:S(2)}) collective-permute-start(bf16[64,3072]{1,0:T(8,128)(2,1)} %get-tuple-element.18), channel_id=1, source_target_pairs={{0,4},{1,5},{2,6},{3,7},{4,0},{5,1},{6,2},{7,3},{8,12},{9,13},{10,... | collective-permute-start | bytes 1179656 | tf_op jit(solution)/shard_map/ppermute | solution.py:274
  116.6 30.2 %collective-permute-start.5 = (bf16[64,3072]{1,0:T(8,128)(2,1)}, bf16[64,3072]{1,0:T(8,128)(2,1)}, u32[]{:S(2)}, u32[]{:S(2)}) collective-permute-start(bf16[64,3072]{1,0:T(8,128)(2,1)} %get-tuple-element.17), channel_id=1, source_target_pairs={{0,5},{1,6},{2,7},{3,0},{4,1},{5,2},{6,3},{7,4},{8,13},{9,14},{10,... | collective-permute-start | bytes 1179656 | tf_op jit(solution)/shard_map/ppermute | solution.py:274
  123.0 23.8 %collective-permute-start.6 = (bf16[64,3072]{1,0:T(8,128)(2,1)S(1)}, bf16[64,3072]{1,0:T(8,128)(2,1)}, u32[]{:S(2)}, u32[]{:S(2)}) collective-permute-start(bf16[64,3072]{1,0:T(8,128)(2,1)S(1)} %get-tuple-element.16), channel_id=1, source_target_pairs={{0,6},{1,7},{2,0},{3,1},{4,2},{5,3},{6,4},{7,5},{8,14},{9,15},{10,... | collective-permute-start | bytes 1179656 | tf_op jit(solution)/shard_map/ppermute | solution.py:274
  124.5 0.8 copy-start.4
  125.3 23.6 %collective-permute-start.7 = (bf16[64,3072]{1,0:T(8,128)(2,1)S(1)}, bf16[64,3072]{1,0:T(8,128)(2,1)}, u32[]{:S(2)}, u32[]{:S(2)}) collective-permute-start(bf16[64,3072]{1,0:T(8,128)(2,1)S(1)} %get-tuple-element.15), channel_id=1, source_target_pairs={{0,7},{1,0},{2,1},{3,2},{4,3},{5,4},{6,5},{7,6},{8,15},{9,8},{10,9... | collective-permute-start | bytes 1179656 | tf_op jit(solution)/shard_map/ppermute | solution.py:274

commit v4 on v3

--- a/solution.py
+++ b/solution.py
@@ -195,22 +195,51 @@
 
 
 def projection_kernel(x_ref, w_ref, o_ref):
-    o_ref[0] = jnp.dot(x_ref[...], w_ref[0], preferred_element_type=jnp.float32)
-
-
-def project_all(normed, weights):
-    parts, width, features = weights.shape
+    o_ref[...] = jnp.dot(x_ref[...], w_ref[0], preferred_element_type=jnp.float32).astype(
+        o_ref.dtype
+    )
+
+
+def rope_projection_kernel(x_ref, w_ref, cos_ref, sin_ref, o_ref):
+    weights = w_ref[0]
+    features = weights.shape[1]
+    half = HD // 2
+    rows = lax.broadcasted_iota(jnp.int32, (features, features), 0)
+    cols = lax.broadcasted_iota(jnp.int32, (features, features), 1)
+    first = cols % HD < half
+    swap = jnp.where(
+        first & (rows == cols + half),
+        -1.0,
+        jnp.where(jnp.logical_not(first) & (rows == cols - half), 1.0, 0.0),
+    ).astype(jnp.bfloat16)
+    swapped = jnp.dot(weights, swap, preferred_element_type=jnp.float32).astype(jnp.bfloat16)
+    plain = jnp.dot(x_ref[...], weights, preferred_element_type=jnp.float32)
+    paired = jnp.dot(x_ref[...], swapped, preferred_element_type=jnp.float32)
+    o_ref[...] = (plain * cos_ref[...] + paired * sin_ref[...]).astype(o_ref.dtype)
+
+
+def project(normed, weights, part, tables=None):
+    _, width, features = weights.shape
     rows = normed.shape[0]
+    x_spec = pl.BlockSpec((rows, width), lambda i: (0, 0))
+    w_spec = pl.BlockSpec((1, width, features), lambda i: (part, 0, 0))
+    o_spec = pl.BlockSpec((rows, features), lambda i: (0, 0))
+    out_shape = jax.ShapeDtypeStruct((rows, features), jnp.bfloat16)
+    if tables is None:
+        return pl.pallas_call(
+            projection_kernel,
+            out_shape=out_shape,
+            grid=(1,),
+            in_specs=[x_spec, w_spec],
+            out_specs=o_spec,
+        )(normed, weights)
     return pl.pallas_call(
-        projection_kernel,
-        out_shape=jax.ShapeDtypeStruct((parts, rows, features), jnp.float32),
-        grid=(parts,),
-        in_specs=[
-            pl.BlockSpec((rows, width), lambda k: (0, 0)),
-            pl.BlockSpec((1, width, features), lambda k: (k, 0, 0)),
-        ],
-        out_specs=pl.BlockSpec((1, rows, features), lambda k: (k, 0, 0)),
-    )(normed, weights)
+        rope_projection_kernel,
+        out_shape=out_shape,
+        grid=(1,),
+        in_specs=[x_spec, w_spec, o_spec, o_spec],
+        out_specs=o_spec,
+    )(normed, weights, *tables)
 
 
 def local(tokens, norm_gain, w_qkv, w_out, kv_cache, cached_lengths, requests, block_start):
@@ -229,23 +258,16 @@
     inverse_rms = lax.rsqrt(jnp.mean(inputs * inputs, axis=-1, keepdims=True) + 1e-05)
     normed = (inputs * inverse_rms * norm_gain.astype(jnp.float32)).astype(jnp.bfloat16)
 
-    projected = project_all(normed, jnp.transpose(w_qkv, (1, 0, 2)))
-
-    def project(part):
-        return projected[part]
-
+    weights = jnp.transpose(w_qkv, (1, 0, 2))
     row_index = jnp.arange(tok_count, dtype=jnp.int32)
     request = row_index * group_requests // tok_count
     first_row = (request * tok_count + group_requests - 1) // group_requests
     positions = group_len + row_index - first_row
     cosine_table, sine_table = rope_tables(positions, HD)
-
-    def rotate(projected):
-        heads = projected.reshape(tok_count, head_count, HD)
-        return rope_pair(heads, cosine_table, sine_table).astype(jnp.bfloat16)
-
-    new_keys = rotate(project(1)).reshape(tok_count, features)
-    new_values = project(2).astype(jnp.bfloat16)
+    repeat = (1, features // (HD // 2))
+    tables = (jnp.tile(cosine_table, repeat), jnp.tile(sine_table, repeat))
+    new_keys = project(normed, weights, 1, tables)
+    new_values = project(normed, weights, 2)
     new_kv = jnp.stack([new_keys, new_values])
     core = lax.axis_index("core")
     relay_meta = jnp.stack(
@@ -257,7 +279,7 @@
     joined = lax.dynamic_update_slice(
         own, partner, (zero_index, zero_index, zero_index, (1 - core) * features)
     )
-    queries = rotate(project(0)).reshape(tok_count, features)
+    queries = project(normed, weights, 0, tables)
     joined, queries = lax.optimization_barrier((joined, queries))
     received = lax.all_to_all(joined, "seq", 0, 0, tiled=True)
     decode_cache = received.transpose(1, 0, 2, 3).reshape(2, 1, seq_count, 1, BLK, 2 * features)

time: 169 us -> 174 us (1.030)
  Pallas kernels: 56.2 us -> 66.9 us
  waiting for transfers between devices: 30.7 us -> 39.5 us
  starting transfers between devices: 25.3 us -> 17.2 us
  local copies, waits for them, and re-layouts: 24.5 us -> 20.4 us
  other arithmetic: 24.9 us -> 21.7 us
    ppermute x7, waiting for transfers between devices: 14.8 us -> 36 us  [local(): lax.ppermute(chunk, ('x', 'core'), pairs).astype(jnp.float32)]
    pallas_call x1 -> x3, Pallas kernels: 9.03 us -> 22.3 us  [the longest x2 17.2 us: project(): pl.pallas_call(rope_projection_kernel, out_shape=out_shape, grid=(1,), in...]
    ppermute x7, starting transfers between devices: 17 us -> 6.12 us  [local(): lax.ppermute(chunk, ('x', 'core'), pairs).astype(jnp.float32)]
    slice x4 -> x0, local copies, waits for them, and re-layouts: 6.97 us -> none  [project(): return projected[part]]
    all_to_all x1, waiting for transfers between devices: 9.95 us -> 3.51 us  [local(): received = lax.all_to_all(joined, 'seq', 0, 0, tiled=True)]
    ppermute x1, waiting for transfers between devices: 5.94 us -> 0.01 us  [local(): partner = lax.ppermute(other, 'core', [(0, 1), (1, 0)])]
    all_to_all x1, starting transfers between devices: 8.35 us -> 11.1 us  [local(): received = lax.all_to_all(joined, 'seq', 0, 0, tiled=True)]
    pallas_call x1, Pallas kernels: 12.2 us -> 9.67 us  [relay(): pl.pallas_call(relay_kernel, out_shape=(jax.ShapeDtypeStruct((seq_count,...]
  transfers between devices with their start and end apart: 9 -> 9, of which waited for: 7 -> 4; matrix products, arithmetic and copies ran while one was open for 9% -> 7% of each run, Pallas kernels for 21% -> 25%
where the time goes in v4:
time: 174 us; the launch traced here: 173 us
  Pallas kernels  66.9 us (38%)
  waiting for transfers between devices  39.5 us (23%)
  other arithmetic  21.7 us (12%)
  local copies, waits for them, and re-layouts  20.4 us (12%)
  starting transfers between devices  17.2 us (10%)
  between operations  4.21 us (2%)
  matrix products  2.94 us (2%)
    ppermute x7, waiting for transfers between devices, local(): lax.ppermute(chunk, ('x', 'core'), pairs).astype(jnp.float32)  36 us
    pallas_call x1, Pallas kernels, attend(): pl.pallas_call(attention_kernel, out_shape=jax.ShapeDtypeStruct(queries.s...  34.9 us
    pallas_call x2, Pallas kernels, project(): pl.pallas_call(rope_projection_kernel, out_shape=out_shape, grid=(1,), in...  17.2 us
    all_to_all x1, starting transfers between devices, local(): received = lax.all_to_all(joined, 'seq', 0, 0, tiled=True)  11.1 us
    pallas_call x1, Pallas kernels, relay(): pl.pallas_call(relay_kernel, out_shape=(jax.ShapeDtypeStruct((seq_count,...  9.67 us
    unnamed x11, local copies, waits for them, and re-layouts  8.55 us
    ppermute x7, starting transfers between devices, local(): lax.ppermute(chunk, ('x', 'core'), pairs).astype(jnp.float32)  6.12 us
    pallas_call x1, Pallas kernels, project(): pl.pallas_call(projection_kernel, out_shape=out_shape, grid=(1,), in_spec...  5.15 us
  transfers between devices with their start and end apart: 9, of which 4 were waited for; matrix products, arithmetic and copies ran while one was open for 7% of the time, Pallas kernels for 25%

profile of v4, /device:TPU:0, one launch (start us, length us, event | category | flops | bytes accessed | tf_op | source)
XLA Modules:
  0.0 172.9 jit_solution(8777198451203998552)
XLA Ops:
  0.6 0.0 copy-start
  0.7 1.5 dynamic_slice.38
  4.2 1.3 dynamic_slice.39
  5.5 1.2 dynamic_slice.40
  7.4 0.7 convert_element_type.47
  8.1 2.6 %multiply_reduce_fusion = f32[512]{0:T(512)S(1)} fusion(bf16[512,3072]{1,0:T(8,128)(2,1)} %param.8), kind=kLoop, calls=%fused_computation.1 | loop fusion | flops 4718080 | bytes 3147776 | tf_op jit(solution)/shard_map/reduce_sum | solution.py:258
  11.3 1.4 fusion.6
  12.8 0.4 multiply_sine_fusion
  13.2 0.1 tile.8
  13.3 1.2 copy.11.cos_ref
  14.5 0.1 tile.20
  14.6 1.2 copy.12.sin_ref
  15.7 4.7 %multiply_convert_fusion.x_ref = bf16[512,3072]{1,0:T(8,128)(2,1)} fusion(f32[3072]{0:T(1024)S(1)} %convert_element_type.47, f32[512]{0:T(512)S(1)} %add_rsqrt_fusion, bf16[512,3072]{1,0:T(8,128)(2,1)} %param.8), kind=kLoop, calls=%fused_computation | loop fusion | flops 6291456 | bytes 6305792 | tf_op jit(solution)/shard_map/convert_element_type | solution.py:259
  20.5 5.1 %shard_map.96 = bf16[512,384]{1,0:T(8,128)(2,1)} custom-call(bf16[512,3072]{1,0:T(8,128)(2,1)} %multiply_convert_fusion.x_ref, bf16[3,3072,384]{2,1,0:T(8,128)(2,1)} %bitcast.14), custom_call_target="tpu_custom_call" | custom-call | tf_op jit(solution)/shard_map/pallas_call | solution.py:229
  25.6 8.6 %shard_map.95 = bf16[512,384]{1,0:T(8,128)(2,1)} custom-call(bf16[512,3072]{1,0:T(8,128)(2,1)} %multiply_convert_fusion.x_ref, bf16[3,3072,384]{2,1,0:T(8,128)(2,1)} %bitcast.15, f32[512,384]{1,0:T(8,128)} %copy.11.cos_ref, f32[512,384]{1,0:T(8,128)} %copy.12.sin_ref), custom_call_target="tpu_custom_call" | custom-call | tf_op jit(solution)/shard_map/pallas_call | solution.py:236
  34.2 2.0 %pad_maximum_fusion.own_n.other_n.kn_ref.vn_ref = bf16[2,512,384]{2,1,0:T(8,128)(2,1)} fusion(bf16[1,512,384]{2,1,0:T(8,128)(2,1)S(1)} %bitcast.20, bf16[1,512,384]{2,1,0:T(8,128)(2,1)} %bitcast.19), kind=kLoop, calls=%fused_computation.3 | loop fusion | flops 393216 | bytes 1572864 | tf_op jit(solution)/shard_map/stack | solution.py:271
  36.3 1.2 pad_add_fusion.1.meta_ref
  37.5 9.7 %shard_map.97 = (bf16[16,2,128,768]{3,2,1,0:T(8,128)(2,1)}, bf16[16,2,128,384]{3,2,1,0:T(8,128)(2,1)}) custom-call(s32[4]{0:T(128)} %pad_add_fusion.1.meta_ref, bf16[2,1,3584,384]{3,2,1,0:T(8,128)(2,1)} %vc_ref.1, bf16[2,512,384]{2,1,0:T(8,128)(2,1)} %pad_maximum_fusion.own_n.other_n.kn_ref.vn_ref, bf16[2,1,3584,384]{3,2,1,0:T(8,128)(2,1)} %vc_ref.1, ...), custom_call_target="tpu_custom_call" | custom-call | tf_op jit(solution)/shard_map/pallas_call | solution.py:179
  47.2 0.0 collective-permute-start
  47.2 8.6 %shard_map.98.q_ref = bf16[512,384]{1,0:T(8,128)(2,1)} custom-call(bf16[512,3072]{1,0:T(8,128)(2,1)} %multiply_convert_fusion.x_ref, bf16[3,3072,384]{2,1,0:T(8,128)(2,1)} %bitcast.16, f32[512,384]{1,0:T(8,128)} %copy.11.cos_ref, f32[512,384]{1,0:T(8,128)} %copy.12.sin_ref), custom_call_target="tpu_custom_call" | custom-call | tf_op jit(solution)/shard_map/pallas_call | solution.py:236
  55.7 0.0 collective-permute-done
  55.7 4.2 %constant_dynamic-update-slice_fusion = bf16[16,2,128,768]{3,2,1,0:T(8,128)(2,1)} fusion(bf16[16,2,128,768]{3,2,1,0:T(8,128)(2,1)} %get-tuple-element.6, bf16[16,2,128,384]{3,2,1,0:T(8,128)(2,1)} %collective-permute-done, s32[]{:T(128)S(6)} %select_n.91), kind=kLoop, calls=%fused_computation.19 | loop fusion | bytes 6291460 | tf_op jit(solution)/shard_map/dynamic_update_slice | solution.py:279
  59.9 11.1 %all-to-all-start = ((bf16[16,2,128,768]{3,2,1,0:T(8,128)(2,1)}), bf16[16,2,128,768]{3,2,1,0:T(8,128)(2,1)}, u32[]{:S(2)}, u32[]{:S(2)}) async-start(bf16[16,2,128,768]{3,2,1,0:T(8,128)(2,1)} %constant_dynamic-update-slice_fusion), calls=%async_computation | async-start | bytes 12582912 | tf_op jit(solution)/shard_map/all_to_all | solution.py:284
  71.1 1.9 %pad_add_fusion.meta_ref = s32[2]{0:T(128)} fusion(s32[1]{0:T(128)} %dynamic_slice.39, s32[1]{0:T(128)} %dynamic_slice.38), kind=kLoop, calls=%fused_computation.34 | loop fusion | flops 2 | bytes 16 | tf_op jit(solution)/shard_map/stack | solution.py:287
  73.0 34.9 %shard_map.99 = bf16[512,384]{1,0:T(8,128)(2,1)} custom-call(s32[2]{0:T(128)} %pad_add_fusion.meta_ref, bf16[512,384]{1,0:T(8,128)(2,1)} %shard_map.98.q_ref, bf16[2,1,3584,384]{3,2,1,0:T(8,128)(2,1)} %vc_ref.1, bf16[2,1,3584,384]{3,2,1,0:T(8,128)(2,1)} %vc_ref.1, bf16[2,512,384]{2,1,0:T(8,128)(2,1)} %pad_maximum_fusion.own_n.other_n.kn_ref.vn_ref, ...), custom_call_target="tpu_custom_call" | custom-call | tf_op jit(solution)/shard_map/pallas_call | solution.py:123
  107.9 2.9 %convolution_convert_fusion = bf16[512,3072]{1,0:T(8,128)(2,1)S(1)} fusion(bf16[512,384]{1,0:T(8,128)(2,1)} %shard_map.99, bf16[384,3072]{1,0:T(8,128)(2,1)S(1)} %copy-done), kind=kOutput, calls=%fused_computation.2 | convolution fusion | flops 1209532416 | bytes 5898240 | tf_op jit(solution)/shard_map/dot_general | solution.py:290
  110.9 1.6 copy-done.2
  112.5 1.1 constant_dynamic-slice_fusion.6
  113.6 2.6 %collective-permute-start.7 = (bf16[64,3072]{1,0:T(8,128)(2,1)S(1)}, bf16[64,3072]{1,0:T(8,128)(2,1)S(1)}, u32[]{:S(2)}, u32[]{:S(2)}) collective-permute-start(bf16[64,3072]{1,0:T(8,128)(2,1)S(1)} %get-tuple-element.15), channel_id=1, source_target_pairs={{0,7},{1,0},{2,1},{3,2},{4,3},{5,4},{6,5},{7,6},{8,15},{9,8},{10,9... | collective-permute-start | bytes 1179656 | tf_op jit(solution)/shard_map/ppermute | solution.py:296
  116.2 0.8 collective-permute-start.6
  117.1 0.0 collective-permute-start.5
  117.1 2.7 %collective-permute-start.4 = (bf16[64,3072]{1,0:T(8,128)(2,1)}, bf16[64,3072]{1,0:T(8,128)(2,1)}, u32[]{:S(2)}, u32[]{:S(2)}) collective-permute-start(bf16[64,3072]{1,0:T(8,128)(2,1)} %get-tuple-element.18), channel_id=1, source_target_pairs={{0,4},{1,5},{2,6},{3,7},{4,0},{5,1},{6,2},{7,3},{8,12},{9,13},{10,... | collective-permute-start | bytes 1179656 | tf_op jit(solution)/shard_map/ppermute | solution.py:296
  119.8 0.0 collective-permute-start.3
  119.8 6.0 %collective-permute-done.7 = bf16[64,3072]{1,0:T(8,128)(2,1)S(1)} collective-permute-done((bf16[64,3072]{1,0:T(8,128)(2,1)S(1)}, bf16[64,3072]{1,0:T(8,128)(2,1)S(1)}, u32[]{:S(2)}, u32[]{:S(2)}) %collective-permute-start.7) | collective-permute-done | bytes 393248 | tf_op jit(solution)/shard_map/ppermute | solution.py:296
  125.7 0.0 collective-permute-start.2
  125.7 25.0 %collective-permute-done.6 = bf16[64,3072]{1,0:T(8,128)(2,1)S(1)} collective-permute-done((bf16[64,3072]{1,0:T(8,128)(2,1)S(1)}, bf16[64,3072]{1,0:T(8,128)(2,1)S(1)}, u32[]{:S(2)}, u32[]{:S(2)}) %collective-permute-start.6) | collective-permute-done | bytes 393248 | tf_op jit(solution)/shard_map/ppermute | solution.py:296
  150.7 0.7 copy-done.4
  151.5 0.0 collective-permute-start.1
  151.5 0.0 copy-done.1
  151.5 3.5 %convert_element_type.46 = f32[512,3072]{1,0:T(8,128)} convert(bf16[512,3072]{1,0:T(8,128)(2,1)S(1)} %copy-done.1) | non-fusion elementwise | flops 1572864 | bytes 9437184 | tf_op jit(solution)/shard_map/convert_element_type | solution.py:257
  155.0 0.0 collective-permute-done.5
  155.0 0.0 collective-permute-done.4
  155.0 0.0 collective-permute-done.3
  155.0 0.0 collective-permute-done.2
  155.0 5.0 %collective-permute-done.1 = bf16[64,3072]{1,0:T(8,128)(2,1)} collective-permute-done((bf16[64,3072]{1,0:T(8,128)(2,1)S(1)}, bf16[64,3072]{1,0:T(8,128)(2,1)}, u32[]{:S(2)}, u32[]{:S(2)}) %collective-permute-start.1) | collective-permute-done | bytes 393248 | tf_op jit(solution)/shard_map/ppermute | solution.py:296
  160.0 3.2 %add_convert_fusion = bf16[64,3072]{1,0:T(8,128)(2,1)} fusion(bf16[64,3072]{1,0:T(8,128)(2,1)S(1)} %collective-permute-done.7, bf16[64,3072]{1,0:T(8,128)(2,1)} %copy-done.4, bf16[64,3072]{1,0:T(8,128)(2,1)} %collective-permute-done.5, bf16[64,3072]{1,0:T(8,128)(2,1)} %collective-permute-done.4, bf16[64,3072]{1,0:T(8,128)(2,1)} %collective-permute-done.3, ...), kind=kLoop, calls=%fused_computation.4 | loop fusion | flops 3342336 | bytes 4325380 | tf_op jit(solution)/shard_map/convert_element_type | solution.py:298
  163.2 3.5 %all-to-all-done = bf16[16,2,128,768]{3,2,1,0:T(8,128)(2,1)} async-done(((bf16[16,2,128,768]{3,2,1,0:T(8,128)(2,1)}), bf16[16,2,128,768]{3,2,1,0:T(8,128)(2,1)}, u32[]{:S(2)}, u32[]{:S(2)}) %all-to-all-start) | async-done | bytes 6291488 | tf_op jit(solution)/shard_map/all_to_all | solution.py:284
  166.7 6.1 %copy.15 = bf16[2,1,16,1,128,768]{5,4,3,2,1,0:T(8,128)(2,1)} copy(bf16[2,1,16,1,128,768]{5,4,0,2,3,1:T(8,128)(2,1)} %bitcast.10) | data formatting | bytes 12582912
  (8 shorter events, 0.0 us)
Async XLA Ops:
  0.6 107.3 %copy-start = (bf16[384,3072]{1,0:T(8,128)(2,1)S(1)}, bf16[384,3072]{1,0:T(8,128)(2,1)}, u32[]{:S(2)}) copy-start(bf16[384,3072]{1,0:T(8,128)(2,1)} %param.11) | copy-start | bytes 7077892
  25.6 8.6 %copy-start.3 = (bf16[512,384]{1,0:T(8,128)(2,1)S(1)}, bf16[512,384]{1,0:T(8,128)(2,1)}, u32[]{:S(2)}) copy-start(bf16[512,384]{1,0:T(8,128)(2,1)} %shard_map.96) | copy-start | bytes 1179652
  47.2 8.6 %collective-permute-start = (bf16[16,2,128,384]{3,2,1,0:T(8,128)(2,1)}, bf16[16,2,128,384]{3,2,1,0:T(8,128)(2,1)}, u32[]{:S(2)}, u32[]{:S(2)}) collective-permute-start(bf16[16,2,128,384]{3,2,1,0:T(8,128)(2,1)} %get-tuple-element.7), channel_id=1, source_target_pairs={{0,1},{1,0},{2,3},{3,2},{4,5},{5,4},{6,7},{7,6},{8,9},{9,8},{10,11... | collective-permute-start | bytes 9437192 | tf_op jit(solution)/shard_map/ppermute | solution.py:277
  59.9 106.8 %all-to-all-start = ((bf16[16,2,128,768]{3,2,1,0:T(8,128)(2,1)}), bf16[16,2,128,768]{3,2,1,0:T(8,128)(2,1)}, u32[]{:S(2)}, u32[]{:S(2)}) async-start(bf16[16,2,128,768]{3,2,1,0:T(8,128)(2,1)} %constant_dynamic-update-slice_fusion), calls=%async_computation | async-start | bytes 12582912 | tf_op jit(solution)/shard_map/all_to_all | solution.py:284
  107.9 43.6 %copy-start.1 = (bf16[512,3072]{1,0:T(8,128)(2,1)S(1)}, bf16[512,3072]{1,0:T(8,128)(2,1)}, u32[]{:S(2)}) copy-start(bf16[512,3072]{1,0:T(8,128)(2,1)} %param.8) | copy-start | bytes 9437188
  110.9 1.6 copy-start.2
  113.6 12.1 %collective-permute-start.7 = (bf16[64,3072]{1,0:T(8,128)(2,1)S(1)}, bf16[64,3072]{1,0:T(8,128)(2,1)S(1)}, u32[]{:S(2)}, u32[]{:S(2)}) collective-permute-start(bf16[64,3072]{1,0:T(8,128)(2,1)S(1)} %get-tuple-element.15), channel_id=1, source_target_pairs={{0,7},{1,0},{2,1},{3,2},{4,3},{5,4},{6,5},{7,6},{8,15},{9,8},{10,9... | collective-permute-start | bytes 1179656 | tf_op jit(solution)/shard_map/ppermute | solution.py:296
  116.2 34.5 %collective-permute-start.6 = (bf16[64,3072]{1,0:T(8,128)(2,1)S(1)}, bf16[64,3072]{1,0:T(8,128)(2,1)S(1)}, u32[]{:S(2)}, u32[]{:S(2)}) collective-permute-start(bf16[64,3072]{1,0:T(8,128)(2,1)S(1)} %get-tuple-element.16), channel_id=1, source_target_pairs={{0,6},{1,7},{2,0},{3,1},{4,2},{5,3},{6,4},{7,5},{8,14},{9,15},{10,... | collective-permute-start | bytes 1179656 | tf_op jit(solution)/shard_map/ppermute | solution.py:296
  117.1 38.0 %collective-permute-start.5 = (bf16[64,3072]{1,0:T(8,128)(2,1)}, bf16[64,3072]{1,0:T(8,128)(2,1)}, u32[]{:S(2)}, u32[]{:S(2)}) collective-permute-start(bf16[64,3072]{1,0:T(8,128)(2,1)} %get-tuple-element.17), channel_id=1, source_target_pairs={{0,5},{1,6},{2,7},{3,0},{4,1},{5,2},{6,3},{7,4},{8,13},{9,14},{10,... | collective-permute-start | bytes 1179656 | tf_op jit(solution)/shard_map/ppermute | solution.py:296
  117.1 38.0 %collective-permute-start.4 = (bf16[64,3072]{1,0:T(8,128)(2,1)}, bf16[64,3072]{1,0:T(8,128)(2,1)}, u32[]{:S(2)}, u32[]{:S(2)}) collective-permute-start(bf16[64,3072]{1,0:T(8,128)(2,1)} %get-tuple-element.18), channel_id=1, source_target_pairs={{0,4},{1,5},{2,6},{3,7},{4,0},{5,1},{6,2},{7,3},{8,12},{9,13},{10,... | collective-permute-start | bytes 1179656 | tf_op jit(solution)/shard_map/ppermute | solution.py:296
  119.8 35.3 %collective-permute-start.3 = (bf16[64,3072]{1,0:T(8,128)(2,1)}, bf16[64,3072]{1,0:T(8,128)(2,1)}, u32[]{:S(2)}, u32[]{:S(2)}) collective-permute-start(bf16[64,3072]{1,0:T(8,128)(2,1)} %get-tuple-element.19), channel_id=1, source_target_pairs={{0,3},{1,4},{2,5},{3,6},{4,7},{5,0},{6,1},{7,2},{8,11},{9,12},{10,... | collective-permute-start | bytes 1179656 | tf_op jit(solution)/shard_map/ppermute | solution.py:296
  125.7 29.3 %collective-permute-start.2 = (bf16[64,3072]{1,0:T(8,128)(2,1)S(1)}, bf16[64,3072]{1,0:T(8,128)(2,1)}, u32[]{:S(2)}, u32[]{:S(2)}) collective-permute-start(bf16[64,3072]{1,0:T(8,128)(2,1)S(1)} %get-tuple-element.20), channel_id=1, source_target_pairs={{0,2},{1,3},{2,4},{3,5},{4,6},{5,7},{6,0},{7,1},{8,10},{9,11},{10,... | collective-permute-start | bytes 1179656 | tf_op jit(solution)/shard_map/ppermute | solution.py:296
  150.7 0.8 copy-start.4
  151.5 8.5 %collective-permute-start.1 = (bf16[64,3072]{1,0:T(8,128)(2,1)S(1)}, bf16[64,3072]{1,0:T(8,128)(2,1)}, u32[]{:S(2)}, u32[]{:S(2)}) collective-permute-start(bf16[64,3072]{1,0:T(8,128)(2,1)S(1)} %get-tuple-element.14), channel_id=1, source_target_pairs={{0,1},{1,2},{2,3},{3,4},{4,5},{5,6},{6,7},{7,0},{8,9},{9,10},{10,1... | collective-permute-start | bytes 1179656 | tf_op jit(solution)/shard_map/ppermute | solution.py:296

commit v5 on v3

--- a/solution.py
+++ b/solution.py
@@ -194,23 +194,66 @@
     )(meta, kv_cache, new_kv, kv_cache, new_kv)
 
 
-def projection_kernel(x_ref, w_ref, o_ref):
-    o_ref[0] = jnp.dot(x_ref[...], w_ref[0], preferred_element_type=jnp.float32)
-
-
-def project_all(normed, weights):
+def half_swap(features):
+    half = HD // 2
+    rows = lax.broadcasted_iota(jnp.int32, (features, features), 0)
+    cols = lax.broadcasted_iota(jnp.int32, (features, features), 1)
+    first = cols % HD < half
+    return jnp.where(
+        first & (rows == cols + half),
+        -1.0,
+        jnp.where(jnp.logical_not(first) & (rows == cols - half), 1.0, 0.0),
+    ).astype(jnp.bfloat16)
+
+
+def projection_kernel(x_ref, scale_ref, gain_ref, w_ref, cos_ref, sin_ref, q_ref, k_ref, v_ref, acc_ref):
+    step = pl.program_id(0)
+    features = w_ref.shape[2]
+    swap = half_swap(features)
+    normed = (x_ref[...].astype(jnp.float32) * scale_ref[...] * gain_ref[...]).astype(
+        jnp.bfloat16
+    )
+
+    @pl.when(step == 0)
+    def _():
+        acc_ref[...] = jnp.zeros(acc_ref.shape, acc_ref.dtype)
+
+    for part in range(2):
+        weights = w_ref[part]
+        swapped = jnp.dot(weights, swap, preferred_element_type=jnp.float32).astype(jnp.bfloat16)
+        acc_ref[2 * part] += jnp.dot(normed, weights, preferred_element_type=jnp.float32)
+        acc_ref[2 * part + 1] += jnp.dot(normed, swapped, preferred_element_type=jnp.float32)
+    acc_ref[4] += jnp.dot(normed, w_ref[2], preferred_element_type=jnp.float32)
+
+    @pl.when(step == pl.num_programs(0) - 1)
+    def _():
+        for part, out_ref in ((0, q_ref), (1, k_ref)):
+            rotated = acc_ref[2 * part] * cos_ref[...] + acc_ref[2 * part + 1] * sin_ref[...]
+            out_ref[...] = rotated.astype(out_ref.dtype)
+        v_ref[...] = acc_ref[4].astype(v_ref.dtype)
+
+
+def project(tokens, scale, gain, weights, tables):
     parts, width, features = weights.shape
-    rows = normed.shape[0]
+    rows = tokens.shape[0]
+    chunk = 512 if width % 512 == 0 else width
+    full = pl.BlockSpec((rows, features), lambda k: (0, 0))
+    out = jax.ShapeDtypeStruct((rows, features), jnp.bfloat16)
     return pl.pallas_call(
         projection_kernel,
-        out_shape=jax.ShapeDtypeStruct((parts, rows, features), jnp.float32),
-        grid=(parts,),
+        out_shape=(out, out, out),
+        grid=(width // chunk,),
         in_specs=[
-            pl.BlockSpec((rows, width), lambda k: (0, 0)),
-            pl.BlockSpec((1, width, features), lambda k: (k, 0, 0)),
+            pl.BlockSpec((rows, chunk), lambda k: (0, k)),
+            pl.BlockSpec((rows, 1), lambda k: (0, 0)),
+            pl.BlockSpec((1, chunk), lambda k: (0, k)),
+            pl.BlockSpec((parts, chunk, features), lambda k: (0, k, 0)),
+            full,
+            full,
         ],
-        out_specs=pl.BlockSpec((1, rows, features), lambda k: (k, 0, 0)),
-    )(normed, weights)
+        out_specs=(full, full, full),
+        scratch_shapes=[pltpu.VMEM((5, rows, features), jnp.float32)],
+    )(tokens, scale, gain, weights, *tables)
 
 
 def local(tokens, norm_gain, w_qkv, w_out, kv_cache, cached_lengths, requests, block_start):
@@ -227,25 +270,18 @@
     group_start = lax.dynamic_index_in_dim(block_start, group_idx, keepdims=False)
     inputs = tokens.astype(jnp.float32)
     inverse_rms = lax.rsqrt(jnp.mean(inputs * inputs, axis=-1, keepdims=True) + 1e-05)
-    normed = (inputs * inverse_rms * norm_gain.astype(jnp.float32)).astype(jnp.bfloat16)
-
-    projected = project_all(normed, jnp.transpose(w_qkv, (1, 0, 2)))
-
-    def project(part):
-        return projected[part]
-
+
+    weights = jnp.transpose(w_qkv, (1, 0, 2))
     row_index = jnp.arange(tok_count, dtype=jnp.int32)
     request = row_index * group_requests // tok_count
     first_row = (request * tok_count + group_requests - 1) // group_requests
     positions = group_len + row_index - first_row
     cosine_table, sine_table = rope_tables(positions, HD)
-
-    def rotate(projected):
-        heads = projected.reshape(tok_count, head_count, HD)
-        return rope_pair(heads, cosine_table, sine_table).astype(jnp.bfloat16)
-
-    new_keys = rotate(project(1)).reshape(tok_count, features)
-    new_values = project(2).astype(jnp.bfloat16)
+    repeat = (1, features // (HD // 2))
+    tables = (jnp.tile(cosine_table, repeat), jnp.tile(sine_table, repeat))
+    queries, new_keys, new_values = project(
+        tokens, inverse_rms, norm_gain.astype(jnp.float32).reshape(1, model_width), weights, tables
+    )
     new_kv = jnp.stack([new_keys, new_values])
     core = lax.axis_index("core")
     relay_meta = jnp.stack(
@@ -257,7 +293,6 @@
     joined = lax.dynamic_update_slice(
         own, partner, (zero_index, zero_index, zero_index, (1 - core) * features)
     )
-    queries = rotate(project(0)).reshape(tok_count, features)
     joined, queries = lax.optimization_barrier((joined, queries))
     received = lax.all_to_all(joined, "seq", 0, 0, tiled=True)
     decode_cache = received.transpose(1, 0, 2, 3).reshape(2, 1, seq_count, 1, BLK, 2 * features)

time: 169 us -> 168 us (level)
  Pallas kernels: 56.2 us -> 64.6 us
  other arithmetic: 24.9 us -> 18.6 us
  local copies, waits for them, and re-layouts: 24.5 us -> 21.1 us
    pallas_call x1, Pallas kernels: 9.03 us -> 17.4 us  [project(): pl.pallas_call(projection_kernel, out_shape=(out, out, out), grid=(width...]
    slice x4 -> x0, local copies, waits for them, and re-layouts: 6.97 us -> none  [project(): return projected[part]]
    convert_element_type x2 -> x0, other arithmetic: 5.44 us -> none  [the longest x1 4.74 us: local(): (inputs * inverse_rms * norm_gain.astype(jnp.float32)).astype(jnp.bfloat16)]
    another operation x0 -> x4, local copies, waits for them, and re-layouts: none -> 2.5 us  [local(): tables = (jnp.tile(cosine_table, repeat), jnp.tile(sine_table, repeat))]
    another operation x1 -> x0, other arithmetic: 2.35 us -> none
    unnamed x15 -> x9, local copies, waits for them, and re-layouts: 8.58 us -> 8.57 us
  transfers between devices with their start and end apart: 9 -> 9, of which waited for: 7 -> 7; matrix products, arithmetic and copies ran while one was open for 9% -> 8% of each run, Pallas kernels for 21% -> 21%
where the time goes in v5:
time: 168 us; the launch traced here: 167 us
  Pallas kernels  64.6 us (38%)
  waiting for transfers between devices  31.5 us (19%)
  starting transfers between devices  25.1 us (15%)
  local copies, waits for them, and re-layouts  21.1 us (13%)
  other arithmetic  18.6 us (11%)
  between operations  3.72 us (2%)
  matrix products  2.8 us (2%)
    pallas_call x1, Pallas kernels, attend(): pl.pallas_call(attention_kernel, out_shape=jax.ShapeDtypeStruct(queries.s...  34.9 us
    pallas_call x1, Pallas kernels, project(): pl.pallas_call(projection_kernel, out_shape=(out, out, out), grid=(width...  17.4 us
    ppermute x7, starting transfers between devices, local(): lax.ppermute(chunk, ('x', 'core'), pairs).astype(jnp.float32)  17 us
    ppermute x7, waiting for transfers between devices, local(): lax.ppermute(chunk, ('x', 'core'), pairs).astype(jnp.float32)  14.8 us
    pallas_call x1, Pallas kernels, relay(): pl.pallas_call(relay_kernel, out_shape=(jax.ShapeDtypeStruct((seq_count,...  12.3 us
    all_to_all x1, waiting for transfers between devices, local(): received = lax.all_to_all(joined, 'seq', 0, 0, tiled=True)  10.7 us
    unnamed x9, local copies, waits for them, and re-layouts  8.57 us
    all_to_all x1, starting transfers between devices, local(): received = lax.all_to_all(joined, 'seq', 0, 0, tiled=True)  8.1 us
  transfers between devices with their start and end apart: 9, of which 7 were waited for; matrix products, arithmetic and copies ran while one was open for 8% of the time, Pallas kernels for 21%

profile of v5, /device:TPU:0, one launch (start us, length us, event | category | flops | bytes accessed | tf_op | source)
XLA Modules:
  0.0 167.4 jit_solution(8782323020980134476)
XLA Ops:
  0.6 0.0 copy-start
  0.6 0.0 copy-start.3
  0.7 1.4 dynamic_slice.38
  4.4 1.3 dynamic_slice.40
  5.6 1.2 dynamic_slice.39
  7.4 1.3 fusion.6
  8.7 0.4 multiply_sine_fusion
  9.1 0.1 tile.8
  9.2 1.2 copy.12.cos_ref
  10.4 0.1 tile.20
  10.5 1.2 copy.13.sin_ref
  11.7 2.6 %multiply_reduce_fusion = f32[512]{0:T(512)S(1)} fusion(bf16[512,3072]{1,0:T(8,128)(2,1)} %x_ref.1), kind=kLoop, calls=%fused_computation | loop fusion | flops 4718080 | bytes 3147776 | tf_op jit(solution)/shard_map/reduce_sum | solution.py:272
  14.2 0.9 copy.11.scale_ref
  15.1 0.0 copy-done.3
  15.1 0.6 reshape.134
  15.7 17.4 %shard_map.95 = (bf16[512,384]{1,0:T(8,128)(2,1)}, bf16[512,384]{1,0:T(8,128)(2,1)}, bf16[512,384]{1,0:T(8,128)(2,1)}) custom-call(bf16[512,3072]{1,0:T(8,128)(2,1)} %x_ref.1, f32[512,1]{1,0:T(8,128)} %copy.11.scale_ref, f32[1,3072]{1,0:T(1,128)} %bitcast.21, bf16[3,3072,384]{2,1,0:T(8,128)(2,1)} %bitcast.16, f32[512,384]{1,0:T(8,128)} %copy.12.cos_ref, ...), custom_call_target="tpu_custom_call" | custom-call | tf_op jit(solution)/shard_map/pallas_call | solution.py:242
  33.1 2.2 %pad_maximum_fusion.own_n.other_n.kn_ref.vn_ref = bf16[2,512,384]{2,1,0:T(8,128)(2,1)} fusion(bf16[1,512,384]{2,1,0:T(8,128)(2,1)} %bitcast.20, bf16[1,512,384]{2,1,0:T(8,128)(2,1)} %bitcast.19), kind=kLoop, calls=%fused_computation.2 | loop fusion | flops 393216 | bytes 1572864 | tf_op jit(solution)/shard_map/stack | solution.py:285
  35.2 1.3 pad_add_fusion.1.meta_ref
  36.5 12.3 %shard_map.96 = (bf16[16,2,128,768]{3,2,1,0:T(8,128)(2,1)}, bf16[16,2,128,384]{3,2,1,0:T(8,128)(2,1)}) custom-call(s32[4]{0:T(128)} %pad_add_fusion.1.meta_ref, bf16[2,1,3584,384]{3,2,1,0:T(8,128)(2,1)} %vc_ref.1, bf16[2,512,384]{2,1,0:T(8,128)(2,1)} %pad_maximum_fusion.own_n.other_n.kn_ref.vn_ref, bf16[2,1,3584,384]{3,2,1,0:T(8,128)(2,1)} %vc_ref.1, ...), custom_call_target="tpu_custom_call" | custom-call | tf_op jit(solution)/shard_map/pallas_call | solution.py:179
  48.8 0.0 collective-permute-start
  48.8 6.0 %collective-permute-done = bf16[16,2,128,384]{3,2,1,0:T(8,128)(2,1)} collective-permute-done((bf16[16,2,128,384]{3,2,1,0:T(8,128)(2,1)}, bf16[16,2,128,384]{3,2,1,0:T(8,128)(2,1)}, u32[]{:S(2)}, u32[]{:S(2)}) %collective-permute-start) | collective-permute-done | bytes 3145760 | tf_op jit(solution)/shard_map/ppermute | solution.py:291
  54.8 4.2 %constant_dynamic-update-slice_fusion = bf16[16,2,128,768]{3,2,1,0:T(8,128)(2,1)} fusion(bf16[16,2,128,768]{3,2,1,0:T(8,128)(2,1)} %get-tuple-element.11, bf16[16,2,128,384]{3,2,1,0:T(8,128)(2,1)} %collective-permute-done, s32[]{:T(128)S(6)} %select_n.91), kind=kLoop, calls=%fused_computation.18 | loop fusion | bytes 6291460 | tf_op jit(solution)/shard_map/dynamic_update_slice | solution.py:293
  59.0 8.1 %all-to-all-start = ((bf16[16,2,128,768]{3,2,1,0:T(8,128)(2,1)}), bf16[16,2,128,768]{3,2,1,0:T(8,128)(2,1)}, u32[]{:S(2)}, u32[]{:S(2)}) async-start(bf16[16,2,128,768]{3,2,1,0:T(8,128)(2,1)} %constant_dynamic-update-slice_fusion), calls=%async_computation | async-start | bytes 12582912 | tf_op jit(solution)/shard_map/all_to_all | solution.py:297
  67.2 1.7 %pad_add_fusion.meta_ref = s32[2]{0:T(128)} fusion(s32[1]{0:T(128)} %dynamic_slice.39, s32[1]{0:T(128)} %dynamic_slice.38), kind=kLoop, calls=%fused_computation.33 | loop fusion | flops 2 | bytes 16 | tf_op jit(solution)/shard_map/stack | solution.py:300
  68.9 34.9 %shard_map.97 = bf16[512,384]{1,0:T(8,128)(2,1)} custom-call(s32[2]{0:T(128)} %pad_add_fusion.meta_ref, bf16[512,384]{1,0:T(8,128)(2,1)} %get-tuple-element.14.q_ref, bf16[2,1,3584,384]{3,2,1,0:T(8,128)(2,1)} %vc_ref.1, bf16[2,1,3584,384]{3,2,1,0:T(8,128)(2,1)} %vc_ref.1, bf16[2,512,384]{2,1,0:T(8,128)(2,1)} %pad_maximum_fusion.own_n.other_n.kn_ref.vn_ref, ...), custom_call_target="tpu_custom_call" | custom-call | tf_op jit(solution)/shard_map/pallas_call | solution.py:123
  103.8 0.0 copy-done
  103.8 2.8 %convolution_convert_fusion = bf16[512,3072]{1,0:T(8,128)(2,1)S(1)} fusion(bf16[512,384]{1,0:T(8,128)(2,1)} %shard_map.97, bf16[384,3072]{1,0:T(8,128)(2,1)S(1)} %copy-done), kind=kOutput, calls=%fused_computation.1 | convolution fusion | flops 1209532416 | bytes 5898240 | tf_op jit(solution)/shard_map/dot_general | solution.py:303
  106.7 1.6 copy-done.1
  108.3 1.1 constant_dynamic-slice_fusion.6
  109.4 0.0 collective-permute-start.1
  109.4 1.5 collective-permute-start.2
  110.9 2.1 %collective-permute-start.3 = (bf16[64,3072]{1,0:T(8,128)(2,1)}, bf16[64,3072]{1,0:T(8,128)(2,1)}, u32[]{:S(2)}, u32[]{:S(2)}) collective-permute-start(bf16[64,3072]{1,0:T(8,128)(2,1)} %get-tuple-element.25), channel_id=1, source_target_pairs={{0,3},{1,4},{2,5},{3,6},{4,7},{5,0},{6,1},{7,2},{8,11},{9,12},{10,... | collective-permute-start | bytes 1179656 | tf_op jit(solution)/shard_map/ppermute | solution.py:309
  113.0 2.0 %collective-permute-start.4 = (bf16[64,3072]{1,0:T(8,128)(2,1)}, bf16[64,3072]{1,0:T(8,128)(2,1)}, u32[]{:S(2)}, u32[]{:S(2)}) collective-permute-start(bf16[64,3072]{1,0:T(8,128)(2,1)} %get-tuple-element.24), channel_id=1, source_target_pairs={{0,4},{1,5},{2,6},{3,7},{4,0},{5,1},{6,2},{7,3},{8,12},{9,13},{10,... | collective-permute-start | bytes 1179656 | tf_op jit(solution)/shard_map/ppermute | solution.py:309
  115.0 1.6 collective-permute-start.5
  116.6 4.8 %collective-permute-done.1 = bf16[64,3072]{1,0:T(8,128)(2,1)S(1)} collective-permute-done((bf16[64,3072]{1,0:T(8,128)(2,1)S(1)}, bf16[64,3072]{1,0:T(8,128)(2,1)S(1)}, u32[]{:S(2)}, u32[]{:S(2)}) %collective-permute-start.1) | collective-permute-done | bytes 393248 | tf_op jit(solution)/shard_map/ppermute | solution.py:309
  121.5 1.5 collective-permute-start.6
  123.0 0.0 collective-permute-done.2
  123.0 0.8 copy-done.2
  123.8 8.2 %collective-permute-start.7 = (bf16[64,3072]{1,0:T(8,128)(2,1)S(1)}, bf16[64,3072]{1,0:T(8,128)(2,1)}, u32[]{:S(2)}, u32[]{:S(2)}) collective-permute-start(bf16[64,3072]{1,0:T(8,128)(2,1)S(1)} %get-tuple-element.21), channel_id=1, source_target_pairs={{0,7},{1,0},{2,1},{3,2},{4,3},{5,4},{6,5},{7,6},{8,15},{9,8},{10,9... | collective-permute-start | bytes 1179656 | tf_op jit(solution)/shard_map/ppermute | solution.py:309
  132.0 5.4 %convert_element_type.41 = f32[512,3072]{1,0:T(8,128)} convert(bf16[512,3072]{1,0:T(8,128)(2,1)} %x_ref.1) | non-fusion elementwise | flops 1572864 | bytes 9437184 | tf_op jit(solution)/shard_map/convert_element_type | solution.py:271
  137.4 2.0 %collective-permute-done.3 = bf16[64,3072]{1,0:T(8,128)(2,1)} collective-permute-done((bf16[64,3072]{1,0:T(8,128)(2,1)}, bf16[64,3072]{1,0:T(8,128)(2,1)}, u32[]{:S(2)}, u32[]{:S(2)}) %collective-permute-start.3) | collective-permute-done | bytes 393248 | tf_op jit(solution)/shard_map/ppermute | solution.py:309
  139.4 1.2 collective-permute-done.4
  140.6 4.7 %collective-permute-done.5 = bf16[64,3072]{1,0:T(8,128)(2,1)} collective-permute-done((bf16[64,3072]{1,0:T(8,128)(2,1)}, bf16[64,3072]{1,0:T(8,128)(2,1)}, u32[]{:S(2)}, u32[]{:S(2)}) %collective-permute-start.5) | collective-permute-done | bytes 393248 | tf_op jit(solution)/shard_map/ppermute | solution.py:309
  145.2 0.0 collective-permute-done.6
  145.2 2.1 %collective-permute-done.7 = bf16[64,3072]{1,0:T(8,128)(2,1)} collective-permute-done((bf16[64,3072]{1,0:T(8,128)(2,1)S(1)}, bf16[64,3072]{1,0:T(8,128)(2,1)}, u32[]{:S(2)}, u32[]{:S(2)}) %collective-permute-start.7) | collective-permute-done | bytes 393248 | tf_op jit(solution)/shard_map/ppermute | solution.py:309
  147.4 3.2 %add_convert_fusion = bf16[64,3072]{1,0:T(8,128)(2,1)} fusion(bf16[64,3072]{1,0:T(8,128)(2,1)} %collective-permute-done.7, bf16[64,3072]{1,0:T(8,128)(2,1)} %collective-permute-done.6, bf16[64,3072]{1,0:T(8,128)(2,1)} %collective-permute-done.5, bf16[64,3072]{1,0:T(8,128)(2,1)} %collective-permute-done.4, bf16[64,3072]{1,0:T(8,128)(2,1)} %collective-permute-done.3, ...), kind=kLoop, calls=%fused_computation.3 | loop fusion | flops 3342336 | bytes 4325380 | tf_op jit(solution)/shard_map/convert_element_type | solution.py:311
  150.6 10.7 %all-to-all-done = bf16[16,2,128,768]{3,2,1,0:T(8,128)(2,1)} async-done(((bf16[16,2,128,768]{3,2,1,0:T(8,128)(2,1)}), bf16[16,2,128,768]{3,2,1,0:T(8,128)(2,1)}, u32[]{:S(2)}, u32[]{:S(2)}) %all-to-all-start) | async-done | bytes 6291488 | tf_op jit(solution)/shard_map/all_to_all | solution.py:297
  161.3 6.1 %copy.14 = bf16[2,1,16,1,128,768]{5,4,3,2,1,0:T(8,128)(2,1)} copy(bf16[2,1,16,1,128,768]{5,4,0,2,3,1:T(8,128)(2,1)} %bitcast.12) | data formatting | bytes 12582912
  (4 shorter events, 0.0 us)
Async XLA Ops:
  0.6 103.2 %copy-start = (bf16[384,3072]{1,0:T(8,128)(2,1)S(1)}, bf16[384,3072]{1,0:T(8,128)(2,1)}, u32[]{:S(2)}) copy-start(bf16[384,3072]{1,0:T(8,128)(2,1)} %param.11) | copy-start | bytes 7077892
  0.6 14.5 %copy-start.3 = (bf16[3072]{0:T(1024)(128)(2,1)S(1)}, bf16[3072]{0:T(1024)(128)(2,1)}, u32[]{:S(2)}) copy-start(bf16[3072]{0:T(1024)(128)(2,1)} %param.9) | copy-start | bytes 18436
  48.8 6.0 %collective-permute-start = (bf16[16,2,128,384]{3,2,1,0:T(8,128)(2,1)}, bf16[16,2,128,384]{3,2,1,0:T(8,128)(2,1)}, u32[]{:S(2)}, u32[]{:S(2)}) collective-permute-start(bf16[16,2,128,384]{3,2,1,0:T(8,128)(2,1)} %get-tuple-element.12), channel_id=1, source_target_pairs={{0,1},{1,0},{2,3},{3,2},{4,5},{5,4},{6,7},{7,6},{8,9},{9,8},{10,11... | collective-permute-start | bytes 9437192 | tf_op jit(solution)/shard_map/ppermute | solution.py:291
  59.0 102.3 %all-to-all-start = ((bf16[16,2,128,768]{3,2,1,0:T(8,128)(2,1)}), bf16[16,2,128,768]{3,2,1,0:T(8,128)(2,1)}, u32[]{:S(2)}, u32[]{:S(2)}) async-start(bf16[16,2,128,768]{3,2,1,0:T(8,128)(2,1)} %constant_dynamic-update-slice_fusion), calls=%async_computation | async-start | bytes 12582912 | tf_op jit(solution)/shard_map/all_to_all | solution.py:297
  106.6 1.6 copy-start.1
  109.4 12.0 %collective-permute-start.1 = (bf16[64,3072]{1,0:T(8,128)(2,1)S(1)}, bf16[64,3072]{1,0:T(8,128)(2,1)S(1)}, u32[]{:S(2)}, u32[]{:S(2)}) collective-permute-start(bf16[64,3072]{1,0:T(8,128)(2,1)S(1)} %get-tuple-element.20), channel_id=1, source_target_pairs={{0,1},{1,2},{2,3},{3,4},{4,5},{5,6},{6,7},{7,0},{8,9},{9,10},{10,1... | collective-permute-start | bytes 1179656 | tf_op jit(solution)/shard_map/ppermute | solution.py:309
  109.4 13.6 %collective-permute-start.2 = (bf16[64,3072]{1,0:T(8,128)(2,1)S(1)}, bf16[64,3072]{1,0:T(8,128)(2,1)S(1)}, u32[]{:S(2)}, u32[]{:S(2)}) collective-permute-start(bf16[64,3072]{1,0:T(8,128)(2,1)S(1)} %get-tuple-element.26), channel_id=1, source_target_pairs={{0,2},{1,3},{2,4},{3,5},{4,6},{5,7},{6,0},{7,1},{8,10},{9,11},{10,... | collective-permute-start | bytes 1179656 | tf_op jit(solution)/shard_map/ppermute | solution.py:309
  110.9 28.5 %collective-permute-start.3 = (bf16[64,3072]{1,0:T(8,128)(2,1)}, bf16[64,3072]{1,0:T(8,128)(2,1)}, u32[]{:S(2)}, u32[]{:S(2)}) collective-permute-start(bf16[64,3072]{1,0:T(8,128)(2,1)} %get-tuple-element.25), channel_id=1, source_target_pairs={{0,3},{1,4},{2,5},{3,6},{4,7},{5,0},{6,1},{7,2},{8,11},{9,12},{10,... | collective-permute-start | bytes 1179656 | tf_op jit(solution)/shard_map/ppermute | solution.py:309
  113.0 27.5 %collective-permute-start.4 = (bf16[64,3072]{1,0:T(8,128)(2,1)}, bf16[64,3072]{1,0:T(8,128)(2,1)}, u32[]{:S(2)}, u32[]{:S(2)}) collective-permute-start(bf16[64,3072]{1,0:T(8,128)(2,1)} %get-tuple-element.24), channel_id=1, source_target_pairs={{0,4},{1,5},{2,6},{3,7},{4,0},{5,1},{6,2},{7,3},{8,12},{9,13},{10,... | collective-permute-start | bytes 1179656 | tf_op jit(solution)/shard_map/ppermute | solution.py:309
  115.0 30.2 %collective-permute-start.5 = (bf16[64,3072]{1,0:T(8,128)(2,1)}, bf16[64,3072]{1,0:T(8,128)(2,1)}, u32[]{:S(2)}, u32[]{:S(2)}) collective-permute-start(bf16[64,3072]{1,0:T(8,128)(2,1)} %get-tuple-element.23), channel_id=1, source_target_pairs={{0,5},{1,6},{2,7},{3,0},{4,1},{5,2},{6,3},{7,4},{8,13},{9,14},{10,... | collective-permute-start | bytes 1179656 | tf_op jit(solution)/shard_map/ppermute | solution.py:309
  121.5 23.8 %collective-permute-start.6 = (bf16[64,3072]{1,0:T(8,128)(2,1)S(1)}, bf16[64,3072]{1,0:T(8,128)(2,1)}, u32[]{:S(2)}, u32[]{:S(2)}) collective-permute-start(bf16[64,3072]{1,0:T(8,128)(2,1)S(1)} %get-tuple-element.22), channel_id=1, source_target_pairs={{0,6},{1,7},{2,0},{3,1},{4,2},{5,3},{6,4},{7,5},{8,14},{9,15},{10,... | collective-permute-start | bytes 1179656 | tf_op jit(solution)/shard_map/ppermute | solution.py:309
  123.0 0.8 copy-start.2
  123.8 23.6 %collective-permute-start.7 = (bf16[64,3072]{1,0:T(8,128)(2,1)S(1)}, bf16[64,3072]{1,0:T(8,128)(2,1)}, u32[]{:S(2)}, u32[]{:S(2)}) collective-permute-start(bf16[64,3072]{1,0:T(8,128)(2,1)S(1)} %get-tuple-element.21), channel_id=1, source_target_pairs={{0,7},{1,0},{2,1},{3,2},{4,3},{5,4},{6,5},{7,6},{8,15},{9,8},{10,9... | collective-permute-start | bytes 1179656 | tf_op jit(solution)/shard_map/ppermute | solution.py:309

commit v6 on v5

--- a/solution.py
+++ b/solution.py
@@ -206,54 +206,58 @@
     ).astype(jnp.bfloat16)
 
 
-def projection_kernel(x_ref, scale_ref, gain_ref, w_ref, cos_ref, sin_ref, q_ref, k_ref, v_ref, acc_ref):
+def projection_kernel(x_ref, gain_ref, w_ref, cos_ref, sin_ref, kv_ref, q_ref, normed_ref):
     step = pl.program_id(0)
-    features = w_ref.shape[2]
-    swap = half_swap(features)
-    normed = (x_ref[...].astype(jnp.float32) * scale_ref[...] * gain_ref[...]).astype(
-        jnp.bfloat16
-    )
 
     @pl.when(step == 0)
     def _():
-        acc_ref[...] = jnp.zeros(acc_ref.shape, acc_ref.dtype)
-
-    for part in range(2):
-        weights = w_ref[part]
+        inputs = x_ref[...].astype(jnp.float32)
+        inverse_rms = lax.rsqrt(jnp.mean(inputs * inputs, axis=-1, keepdims=True) + 1e-05)
+        normed_ref[...] = (inputs * inverse_rms * gain_ref[...]).astype(jnp.bfloat16)
+
+    weights = w_ref[0]
+    plain = jnp.dot(normed_ref[...], weights, preferred_element_type=jnp.float32)
+
+    def rotated():
+        swap = half_swap(weights.shape[1])
         swapped = jnp.dot(weights, swap, preferred_element_type=jnp.float32).astype(jnp.bfloat16)
-        acc_ref[2 * part] += jnp.dot(normed, weights, preferred_element_type=jnp.float32)
-        acc_ref[2 * part + 1] += jnp.dot(normed, swapped, preferred_element_type=jnp.float32)
-    acc_ref[4] += jnp.dot(normed, w_ref[2], preferred_element_type=jnp.float32)
-
-    @pl.when(step == pl.num_programs(0) - 1)
-    def _():
-        for part, out_ref in ((0, q_ref), (1, k_ref)):
-            rotated = acc_ref[2 * part] * cos_ref[...] + acc_ref[2 * part + 1] * sin_ref[...]
-            out_ref[...] = rotated.astype(out_ref.dtype)
-        v_ref[...] = acc_ref[4].astype(v_ref.dtype)
-
-
-def project(tokens, scale, gain, weights, tables):
+        paired = jnp.dot(normed_ref[...], swapped, preferred_element_type=jnp.float32)
+        return (plain * cos_ref[...] + paired * sin_ref[...]).astype(jnp.bfloat16)
+
+    @pl.when(step == 0)
+    def _():
+        kv_ref[0] = rotated()
+
+    @pl.when(step == 1)
+    def _():
+        kv_ref[1] = plain.astype(jnp.bfloat16)
+
+    @pl.when(step == 2)
+    def _():
+        q_ref[...] = rotated()
+
+
+def project(tokens, gain, weights, tables):
     parts, width, features = weights.shape
     rows = tokens.shape[0]
-    chunk = 512 if width % 512 == 0 else width
-    full = pl.BlockSpec((rows, features), lambda k: (0, 0))
-    out = jax.ShapeDtypeStruct((rows, features), jnp.bfloat16)
+    full = pl.BlockSpec((rows, features), lambda s: (0, 0))
     return pl.pallas_call(
         projection_kernel,
-        out_shape=(out, out, out),
-        grid=(width // chunk,),
+        out_shape=(
+            jax.ShapeDtypeStruct((2, rows, features), jnp.bfloat16),
+            jax.ShapeDtypeStruct((rows, features), jnp.bfloat16),
+        ),
+        grid=(parts,),
         in_specs=[
-            pl.BlockSpec((rows, chunk), lambda k: (0, k)),
-            pl.BlockSpec((rows, 1), lambda k: (0, 0)),
-            pl.BlockSpec((1, chunk), lambda k: (0, k)),
-            pl.BlockSpec((parts, chunk, features), lambda k: (0, k, 0)),
+            pl.BlockSpec((rows, width), lambda s: (0, 0)),
+            pl.BlockSpec((1, width), lambda s: (0, 0)),
+            pl.BlockSpec((1, width, features), lambda s: ((s + 1) % parts, 0, 0)),
             full,
             full,
         ],
-        out_specs=(full, full, full),
-        scratch_shapes=[pltpu.VMEM((5, rows, features), jnp.float32)],
-    )(tokens, scale, gain, weights, *tables)
+        out_specs=(pl.BlockSpec((2, rows, features), lambda s: (0, 0, 0)), full),
+        scratch_shapes=[pltpu.VMEM((rows, width), jnp.bfloat16)],
+    )(tokens, gain, weights, *tables)
 
 
 def local(tokens, norm_gain, w_qkv, w_out, kv_cache, cached_lengths, requests, block_start):
@@ -265,11 +269,13 @@
     features = w_qkv.shape[2]
     head_count = features // HD
     cache_len = kv_cache.shape[2]
-    group_len = lax.dynamic_index_in_dim(cached_lengths, group_idx, keepdims=False)
-    group_requests = lax.dynamic_index_in_dim(requests, group_idx, keepdims=False)
-    group_start = lax.dynamic_index_in_dim(block_start, group_idx, keepdims=False)
+    group_params = lax.dynamic_index_in_dim(
+        jnp.stack([cached_lengths, requests, block_start], axis=1), group_idx, keepdims=False
+    )
+    group_len = group_params[0]
+    group_requests = group_params[1]
+    group_start = group_params[2]
     inputs = tokens.astype(jnp.float32)
-    inverse_rms = lax.rsqrt(jnp.mean(inputs * inputs, axis=-1, keepdims=True) + 1e-05)
 
     weights = jnp.transpose(w_qkv, (1, 0, 2))
     row_index = jnp.arange(tok_count, dtype=jnp.int32)
@@ -279,10 +285,9 @@
     cosine_table, sine_table = rope_tables(positions, HD)
     repeat = (1, features // (HD // 2))
     tables = (jnp.tile(cosine_table, repeat), jnp.tile(sine_table, repeat))
-    queries, new_keys, new_values = project(
-        tokens, inverse_rms, norm_gain.astype(jnp.float32).reshape(1, model_width), weights, tables
-    )
-    new_kv = jnp.stack([new_keys, new_values])
+    new_kv, queries = project(
+        tokens, norm_gain.astype(jnp.float32).reshape(1, model_width), weights, tables
+    )
     core = lax.axis_index("core")
     relay_meta = jnp.stack(
         [group_len // BLK, group_start, core, jnp.int32(tok_count // BLK)]

time: 168 us -> 161 us (0.958)
  waiting for transfers between devices: 31.5 us -> 47.6 us
  starting transfers between devices: 25.1 us -> 15.4 us
  other arithmetic: 18.6 us -> 10.3 us
  local copies, waits for them, and re-layouts: 21.1 us -> 16.9 us
    ppermute x7, waiting for transfers between devices: 14.8 us -> 39.1 us  [local(): lax.ppermute(chunk, ('x', 'core'), pairs).astype(jnp.float32)]
    ppermute x7, starting transfers between devices: 17 us -> 6.13 us  [local(): lax.ppermute(chunk, ('x', 'core'), pairs).astype(jnp.float32)]
    all_to_all x1, waiting for transfers between devices: 10.7 us -> 2.48 us  [local(): received = lax.all_to_all(joined, 'seq', 0, 0, tiled=True)]
    convert_element_type x1 -> x0, other arithmetic: 5.39 us -> none  [local(): inputs = tokens.astype(jnp.float32)]
    dynamic_slice x3 -> x1, local copies, waits for them, and re-layouts: 3.88 us -> 0.07 us  [local(): lax.dynamic_index_in_dim(jnp.stack([cached_lengths, requests, block_start...]
    reduce_sum x1 -> x0, other arithmetic: 2.58 us -> none  [local(): jnp.mean(inputs * inputs, axis=-1, keepdims=True) + 1e-05]
    pallas_call x1, Pallas kernels: 12.3 us -> 10.4 us  [relay(): pl.pallas_call(relay_kernel, out_shape=(jax.ShapeDtypeStruct((seq_count,...]
    unnamed x9 -> x7, local copies, waits for them, and re-layouts: 8.57 us -> 8.61 us
  transfers between devices with their start and end apart: 9 -> 9, of which waited for: 7 -> 5; matrix products, arithmetic and copies ran while one was open for 8% -> 6% of each run, Pallas kernels for 21% -> 22%
where the time goes in v6:
time: 161 us; the launch traced here: 160 us
  Pallas kernels  63 us (39%)
  waiting for transfers between devices  47.6 us (30%)
  local copies, waits for them, and re-layouts  16.9 us (10%)
  starting transfers between devices  15.4 us (10%)
  other arithmetic  10.3 us (6%)
  between operations  4.17 us (3%)
  matrix products  2.79 us (2%)
    ppermute x7, waiting for transfers between devices, local(): lax.ppermute(chunk, ('x', 'core'), pairs).astype(jnp.float32)  39.1 us
    pallas_call x1, Pallas kernels, attend(): pl.pallas_call(attention_kernel, out_shape=jax.ShapeDtypeStruct(queries.s...  34.9 us
    pallas_call x1, Pallas kernels, project(): pl.pallas_call(projection_kernel, out_shape=(jax.ShapeDtypeStruct((2, row...  17.7 us
    pallas_call x1, Pallas kernels, relay(): pl.pallas_call(relay_kernel, out_shape=(jax.ShapeDtypeStruct((seq_count,...  10.4 us
    all_to_all x1, starting transfers between devices, local(): received = lax.all_to_all(joined, 'seq', 0, 0, tiled=True)  9.24 us
    unnamed x7, local copies, waits for them, and re-layouts  8.61 us
    ppermute x7, starting transfers between devices, local(): lax.ppermute(chunk, ('x', 'core'), pairs).astype(jnp.float32)  6.13 us
    ppermute x1, waiting for transfers between devices, local(): partner = lax.ppermute(other, 'core', [(0, 1), (1, 0)])  6 us
  transfers between devices with their start and end apart: 9, of which 5 were waited for; matrix products, arithmetic and copies ran while one was open for 6% of the time, Pallas kernels for 22%

profile of v6, /device:TPU:0, one launch (start us, length us, event | category | flops | bytes accessed | tf_op | source)
XLA Modules:
  0.0 160.2 jit_solution(17253969867965877065)
XLA Ops:
  0.6 0.0 copy-start
  0.7 0.8 pad_add_fusion
  1.5 0.1 constant_dynamic-slice_fusion.7
  1.6 0.6 fusion.9
  4.9 1.3 reshape.118
  6.8 1.4 fusion.6
  8.2 0.4 multiply_sine_fusion
  8.6 0.1 tile.8
  8.7 1.2 copy.11.cos_ref
  9.9 0.1 tile.20
  10.0 1.2 copy.12.sin_ref
  11.2 1.3 pad_add_fusion.2.meta_ref
  12.5 17.7 %shard_map.95 = (bf16[2,512,384]{2,1,0:T(8,128)(2,1)}, bf16[512,384]{1,0:T(8,128)(2,1)}) custom-call(bf16[512,3072]{1,0:T(8,128)(2,1)} %x_ref.1, f32[1,3072]{1,0:T(1,128)} %bitcast.22, bf16[3,3072,384]{2,1,0:T(8,128)(2,1)} %bitcast.19, f32[512,384]{1,0:T(8,128)} %copy.11.cos_ref, f32[512,384]{1,0:T(8,128)} %copy.12.sin_ref), custom_call_target="tpu_custom_call" | custom-call | tf_op jit(solution)/shard_map/pallas_call | solution.py:244
  30.2 10.4 %shard_map.96 = (bf16[16,2,128,768]{3,2,1,0:T(8,128)(2,1)}, bf16[16,2,128,384]{3,2,1,0:T(8,128)(2,1)}) custom-call(s32[4]{0:T(128)} %pad_add_fusion.2.meta_ref, bf16[2,1,3584,384]{3,2,1,0:T(8,128)(2,1)} %vc_ref.1, bf16[2,512,384]{2,1,0:T(8,128)(2,1)} %get-tuple-element.8.own_n.other_n.kn_ref.vn_ref, bf16[2,1,3584,384]{3,2,1,0:T(8,128)(2,1)} %vc_ref.1, ...), custom_call_target="tpu_custom_call" | custom-call | tf_op jit(solution)/shard_map/pallas_call | solution.py:179
  40.6 0.0 collective-permute-start
  40.6 6.0 %collective-permute-done = bf16[16,2,128,384]{3,2,1,0:T(8,128)(2,1)} collective-permute-done((bf16[16,2,128,384]{3,2,1,0:T(8,128)(2,1)}, bf16[16,2,128,384]{3,2,1,0:T(8,128)(2,1)}, u32[]{:S(2)}, u32[]{:S(2)}) %collective-permute-start) | collective-permute-done | bytes 3145760 | tf_op jit(solution)/shard_map/ppermute | solution.py:296
  46.6 4.1 %constant_dynamic-update-slice_fusion = bf16[16,2,128,768]{3,2,1,0:T(8,128)(2,1)} fusion(bf16[16,2,128,768]{3,2,1,0:T(8,128)(2,1)} %get-tuple-element.9, bf16[16,2,128,384]{3,2,1,0:T(8,128)(2,1)} %collective-permute-done, s32[]{:T(128)S(6)} %select_n.89), kind=kLoop, calls=%fused_computation.16 | loop fusion | bytes 6291460 | tf_op jit(solution)/shard_map/dynamic_update_slice | solution.py:298
  50.7 9.2 %all-to-all-start = ((bf16[16,2,128,768]{3,2,1,0:T(8,128)(2,1)}), bf16[16,2,128,768]{3,2,1,0:T(8,128)(2,1)}, u32[]{:S(2)}, u32[]{:S(2)}) async-start(bf16[16,2,128,768]{3,2,1,0:T(8,128)(2,1)} %constant_dynamic-update-slice_fusion), calls=%async_computation | async-start | bytes 12582912 | tf_op jit(solution)/shard_map/all_to_all | solution.py:302
  60.0 1.9 %pad_add_fusion.1.meta_ref = s32[2]{0:T(128)} fusion(s32[1]{0:T(128)} %bitcast.4, s32[1]{0:T(128)} %bitcast.3), kind=kLoop, calls=%fused_computation.32 | loop fusion | flops 2 | bytes 16 | tf_op jit(solution)/shard_map/stack | solution.py:305
  61.9 34.9 %shard_map.97 = bf16[512,384]{1,0:T(8,128)(2,1)} custom-call(s32[2]{0:T(128)} %pad_add_fusion.1.meta_ref, bf16[512,384]{1,0:T(8,128)(2,1)} %get-tuple-element.12.q_ref, bf16[2,1,3584,384]{3,2,1,0:T(8,128)(2,1)} %vc_ref.1, bf16[2,1,3584,384]{3,2,1,0:T(8,128)(2,1)} %vc_ref.1, bf16[2,512,384]{2,1,0:T(8,128)(2,1)} %get-tuple-element.8.own_n.other_n.kn_ref.vn_ref, ...), custom_call_target="tpu_custom_call" | custom-call | tf_op jit(solution)/shard_map/pallas_call | solution.py:123
  96.8 0.0 copy-done
  96.8 2.8 %convolution_convert_fusion = bf16[512,3072]{1,0:T(8,128)(2,1)S(1)} fusion(bf16[512,384]{1,0:T(8,128)(2,1)} %shard_map.97, bf16[384,3072]{1,0:T(8,128)(2,1)S(1)} %copy-done), kind=kOutput, calls=%fused_computation | convolution fusion | flops 1209532416 | bytes 5898240 | tf_op jit(solution)/shard_map/dot_general | solution.py:308
  99.6 0.0 copy-start.1
  99.6 1.7 %copy-done.1 = bf16[512,3072]{1,0:T(8,128)(2,1)} copy-done((bf16[512,3072]{1,0:T(8,128)(2,1)}, bf16[512,3072]{1,0:T(8,128)(2,1)S(1)}, u32[]{:S(2)}) %copy-start.1) | copy-done | bytes 3145752
  101.3 1.1 constant_dynamic-slice_fusion.6
  102.4 2.2 %collective-permute-start.7 = (bf16[64,3072]{1,0:T(8,128)(2,1)S(1)}, bf16[64,3072]{1,0:T(8,128)(2,1)S(1)}, u32[]{:S(2)}, u32[]{:S(2)}) collective-permute-start(bf16[64,3072]{1,0:T(8,128)(2,1)S(1)} %get-tuple-element.19), channel_id=1, source_target_pairs={{0,7},{1,0},{2,1},{3,2},{4,3},{5,4},{6,5},{7,6},{8,15},{9,8},{10,9... | collective-permute-start | bytes 1179656 | tf_op jit(solution)/shard_map/ppermute | solution.py:314
  104.6 0.8 collective-permute-start.6
  105.5 0.4 collective-permute-start.5
  105.8 2.7 %collective-permute-start.4 = (bf16[64,3072]{1,0:T(8,128)(2,1)}, bf16[64,3072]{1,0:T(8,128)(2,1)}, u32[]{:S(2)}, u32[]{:S(2)}) collective-permute-start(bf16[64,3072]{1,0:T(8,128)(2,1)} %get-tuple-element.22), channel_id=1, source_target_pairs={{0,4},{1,5},{2,6},{3,7},{4,0},{5,1},{6,2},{7,3},{8,12},{9,13},{10,... | collective-permute-start | bytes 1179656 | tf_op jit(solution)/shard_map/ppermute | solution.py:314
  108.5 0.0 collective-permute-start.3
  108.5 5.5 %collective-permute-done.7 = bf16[64,3072]{1,0:T(8,128)(2,1)S(1)} collective-permute-done((bf16[64,3072]{1,0:T(8,128)(2,1)S(1)}, bf16[64,3072]{1,0:T(8,128)(2,1)S(1)}, u32[]{:S(2)}, u32[]{:S(2)}) %collective-permute-start.7) | collective-permute-done | bytes 393248 | tf_op jit(solution)/shard_map/ppermute | solution.py:314
  114.0 0.0 collective-permute-start.2
  114.1 25.1 %collective-permute-done.6 = bf16[64,3072]{1,0:T(8,128)(2,1)S(1)} collective-permute-done((bf16[64,3072]{1,0:T(8,128)(2,1)S(1)}, bf16[64,3072]{1,0:T(8,128)(2,1)S(1)}, u32[]{:S(2)}, u32[]{:S(2)}) %collective-permute-start.6) | collective-permute-done | bytes 393248 | tf_op jit(solution)/shard_map/ppermute | solution.py:314
  139.2 0.0 copy-start.2
  139.2 0.8 copy-done.2
  139.9 0.0 collective-permute-start.1
  139.9 0.0 collective-permute-done.5
  140.0 0.0 collective-permute-done.4
  140.0 0.0 collective-permute-done.3
  140.0 0.0 collective-permute-done.2
  140.0 8.5 %collective-permute-done.1 = bf16[64,3072]{1,0:T(8,128)(2,1)} collective-permute-done((bf16[64,3072]{1,0:T(8,128)(2,1)S(1)}, bf16[64,3072]{1,0:T(8,128)(2,1)}, u32[]{:S(2)}, u32[]{:S(2)}) %collective-permute-start.1) | collective-permute-done | bytes 393248 | tf_op jit(solution)/shard_map/ppermute | solution.py:314
  148.5 3.1 %add_convert_fusion = bf16[64,3072]{1,0:T(8,128)(2,1)} fusion(bf16[64,3072]{1,0:T(8,128)(2,1)S(1)} %collective-permute-done.7, bf16[64,3072]{1,0:T(8,128)(2,1)} %copy-done.2, bf16[64,3072]{1,0:T(8,128)(2,1)} %collective-permute-done.5, bf16[64,3072]{1,0:T(8,128)(2,1)} %collective-permute-done.4, bf16[64,3072]{1,0:T(8,128)(2,1)} %collective-permute-done.3, ...), kind=kLoop, calls=%fused_computation.1 | loop fusion | flops 3538944 | bytes 3932164 | tf_op jit(solution)/shard_map/convert_element_type | solution.py:316
  151.6 2.5 %all-to-all-done = bf16[16,2,128,768]{3,2,1,0:T(8,128)(2,1)} async-done(((bf16[16,2,128,768]{3,2,1,0:T(8,128)(2,1)}), bf16[16,2,128,768]{3,2,1,0:T(8,128)(2,1)}, u32[]{:S(2)}, u32[]{:S(2)}) %all-to-all-start) | async-done | bytes 6291488 | tf_op jit(solution)/shard_map/all_to_all | solution.py:302
  154.1 6.1 %copy.13 = bf16[2,1,16,1,128,768]{5,4,3,2,1,0:T(8,128)(2,1)} copy(bf16[2,1,16,1,128,768]{5,4,0,2,3,1:T(8,128)(2,1)} %bitcast.15) | data formatting | bytes 12582912
  (1 shorter events, 0.0 us)
Async XLA Ops:
  0.6 96.2 %copy-start = (bf16[384,3072]{1,0:T(8,128)(2,1)S(1)}, bf16[384,3072]{1,0:T(8,128)(2,1)}, u32[]{:S(2)}) copy-start(bf16[384,3072]{1,0:T(8,128)(2,1)} %param.11) | copy-start | bytes 7077892
  40.6 6.0 %collective-permute-start = (bf16[16,2,128,384]{3,2,1,0:T(8,128)(2,1)}, bf16[16,2,128,384]{3,2,1,0:T(8,128)(2,1)}, u32[]{:S(2)}, u32[]{:S(2)}) collective-permute-start(bf16[16,2,128,384]{3,2,1,0:T(8,128)(2,1)} %get-tuple-element.10), channel_id=1, source_target_pairs={{0,1},{1,0},{2,3},{3,2},{4,5},{5,4},{6,7},{7,6},{8,9},{9,8},{10,11... | collective-permute-start | bytes 9437192 | tf_op jit(solution)/shard_map/ppermute | solution.py:296
  50.7 103.4 %all-to-all-start = ((bf16[16,2,128,768]{3,2,1,0:T(8,128)(2,1)}), bf16[16,2,128,768]{3,2,1,0:T(8,128)(2,1)}, u32[]{:S(2)}, u32[]{:S(2)}) async-start(bf16[16,2,128,768]{3,2,1,0:T(8,128)(2,1)} %constant_dynamic-update-slice_fusion), calls=%async_computation | async-start | bytes 12582912 | tf_op jit(solution)/shard_map/all_to_all | solution.py:302
  99.6 1.7 %copy-start.1 = (bf16[512,3072]{1,0:T(8,128)(2,1)}, bf16[512,3072]{1,0:T(8,128)(2,1)S(1)}, u32[]{:S(2)}) copy-start(bf16[512,3072]{1,0:T(8,128)(2,1)S(1)} %convolution_convert_fusion) | copy-start | bytes 9437188
  102.4 11.6 %collective-permute-start.7 = (bf16[64,3072]{1,0:T(8,128)(2,1)S(1)}, bf16[64,3072]{1,0:T(8,128)(2,1)S(1)}, u32[]{:S(2)}, u32[]{:S(2)}) collective-permute-start(bf16[64,3072]{1,0:T(8,128)(2,1)S(1)} %get-tuple-element.19), channel_id=1, source_target_pairs={{0,7},{1,0},{2,1},{3,2},{4,3},{5,4},{6,5},{7,6},{8,15},{9,8},{10,9... | collective-permute-start | bytes 1179656 | tf_op jit(solution)/shard_map/ppermute | solution.py:314
  104.6 34.6 %collective-permute-start.6 = (bf16[64,3072]{1,0:T(8,128)(2,1)S(1)}, bf16[64,3072]{1,0:T(8,128)(2,1)S(1)}, u32[]{:S(2)}, u32[]{:S(2)}) collective-permute-start(bf16[64,3072]{1,0:T(8,128)(2,1)S(1)} %get-tuple-element.20), channel_id=1, source_target_pairs={{0,6},{1,7},{2,0},{3,1},{4,2},{5,3},{6,4},{7,5},{8,14},{9,15},{10,... | collective-permute-start | bytes 1179656 | tf_op jit(solution)/shard_map/ppermute | solution.py:314
  105.5 34.5 %collective-permute-start.5 = (bf16[64,3072]{1,0:T(8,128)(2,1)}, bf16[64,3072]{1,0:T(8,128)(2,1)}, u32[]{:S(2)}, u32[]{:S(2)}) collective-permute-start(bf16[64,3072]{1,0:T(8,128)(2,1)} %get-tuple-element.21), channel_id=1, source_target_pairs={{0,5},{1,6},{2,7},{3,0},{4,1},{5,2},{6,3},{7,4},{8,13},{9,14},{10,... | collective-permute-start | bytes 1179656 | tf_op jit(solution)/shard_map/ppermute | solution.py:314
  105.8 34.2 %collective-permute-start.4 = (bf16[64,3072]{1,0:T(8,128)(2,1)}, bf16[64,3072]{1,0:T(8,128)(2,1)}, u32[]{:S(2)}, u32[]{:S(2)}) collective-permute-start(bf16[64,3072]{1,0:T(8,128)(2,1)} %get-tuple-element.22), channel_id=1, source_target_pairs={{0,4},{1,5},{2,6},{3,7},{4,0},{5,1},{6,2},{7,3},{8,12},{9,13},{10,... | collective-permute-start | bytes 1179656 | tf_op jit(solution)/shard_map/ppermute | solution.py:314
  108.5 31.4 %collective-permute-start.3 = (bf16[64,3072]{1,0:T(8,128)(2,1)}, bf16[64,3072]{1,0:T(8,128)(2,1)}, u32[]{:S(2)}, u32[]{:S(2)}) collective-permute-start(bf16[64,3072]{1,0:T(8,128)(2,1)} %get-tuple-element.23), channel_id=1, source_target_pairs={{0,3},{1,4},{2,5},{3,6},{4,7},{5,0},{6,1},{7,2},{8,11},{9,12},{10,... | collective-permute-start | bytes 1179656 | tf_op jit(solution)/shard_map/ppermute | solution.py:314
  114.0 25.9 %collective-permute-start.2 = (bf16[64,3072]{1,0:T(8,128)(2,1)S(1)}, bf16[64,3072]{1,0:T(8,128)(2,1)}, u32[]{:S(2)}, u32[]{:S(2)}) collective-permute-start(bf16[64,3072]{1,0:T(8,128)(2,1)S(1)} %get-tuple-element.24), channel_id=1, source_target_pairs={{0,2},{1,3},{2,4},{3,5},{4,6},{5,7},{6,0},{7,1},{8,10},{9,11},{10,... | collective-permute-start | bytes 1179656 | tf_op jit(solution)/shard_map/ppermute | solution.py:314
  139.2 0.8 copy-start.2
  139.9 8.5 %collective-permute-start.1 = (bf16[64,3072]{1,0:T(8,128)(2,1)S(1)}, bf16[64,3072]{1,0:T(8,128)(2,1)}, u32[]{:S(2)}, u32[]{:S(2)}) collective-permute-start(bf16[64,3072]{1,0:T(8,128)(2,1)S(1)} %get-tuple-element.18), channel_id=1, source_target_pairs={{0,1},{1,2},{2,3},{3,4},{4,5},{5,6},{6,7},{7,0},{8,9},{9,10},{10,1... | collective-permute-start | bytes 1179656 | tf_op jit(solution)/shard_map/ppermute | solution.py:314

commit v7 on v6

--- a/solution.py
+++ b/solution.py
@@ -1,3 +1,4 @@
+import functools
 import math
 
 import jax
@@ -138,60 +139,52 @@
     )(meta, queries, kv_cache, kv_cache, new_kv, new_kv)
 
 
-def relay_kernel(meta_ref, own_c, own_n, other_c, other_n, own_ref, other_ref):
+def relay_kernel(meta_ref, own_c, own_n, mate_c, mate_n, out_ref):
     len_blocks = meta_ref[0]
     group_start = meta_ref[1]
     core = meta_ref[2]
     new_blocks = meta_ref[3]
     dest = pl.program_id(0)
     rank_count = 2 * pl.num_programs(0)
+    features = own_n.shape[2]
+    block = (2 * dest + core - group_start + rank_count) % rank_count
+    old = block < len_blocks
+    fresh = (block >= len_blocks) & (block < len_blocks + new_blocks)
     zero = jnp.zeros(own_n.shape[1:], own_n.dtype)
-    for part, cache_ref, new_ref, out_ref in ((0, own_c, own_n, own_ref), (1, other_c, other_n, other_ref)):
-        block = (2 * dest + (core + part) % 2 - group_start + rank_count) % rank_count
-        old = block < len_blocks
-        fresh = (block >= len_blocks) & (block < len_blocks + new_blocks)
-        for kv in range(2):
-            out_ref[0, kv] = jnp.where(
-                old, cache_ref[kv, 0], jnp.where(fresh, new_ref[kv], zero)
-            )
-
-
-def relay(meta, kv_cache, new_kv, seq_count):
+    first = core == 0
+    for kv in range(2):
+        mine = jnp.where(old, own_c[kv, 0], jnp.where(fresh, own_n[kv], zero))
+        mate = jnp.where(old, mate_c[kv, 0], jnp.where(fresh, mate_n[kv], zero))
+        out_ref[0, kv, :, :features] = jnp.where(first, mine, mate)
+        out_ref[0, kv, :, features:] = jnp.where(first, mate, mine)
+
+
+def relay(meta, kv_cache, new_kv, mate_cache, mate_new, seq_count):
     features = kv_cache.shape[3]
     new_blocks = new_kv.shape[1] // BLK
     rank_count = 2 * seq_count
 
-    def block_of(part, d, m):
-        return (2 * d + (m[2] + part) % 2 - m[1] + rank_count) % rank_count
-
-    def cache_spec(part):
-        return pl.BlockSpec(
-            (2, 1, BLK, features),
-            lambda d, m: (0, 0, jnp.clip(block_of(part, d, m), 0, m[0] - 1), 0),
-        )
-
-    def new_spec(part):
-        return pl.BlockSpec(
-            (2, BLK, features),
-            lambda d, m: (0, jnp.clip(block_of(part, d, m) - m[0], 0, new_blocks - 1), 0),
-        )
-
+    def block_of(d, m):
+        return (2 * d + m[2] - m[1] + rank_count) % rank_count
+
+    cache_spec = pl.BlockSpec(
+        (2, 1, BLK, features),
+        lambda d, m: (0, 0, jnp.clip(block_of(d, m), 0, m[0] - 1), 0),
+    )
+    new_spec = pl.BlockSpec(
+        (2, BLK, features),
+        lambda d, m: (0, jnp.clip(block_of(d, m) - m[0], 0, new_blocks - 1), 0),
+    )
     return pl.pallas_call(
         relay_kernel,
-        out_shape=(
-            jax.ShapeDtypeStruct((seq_count, 2, BLK, 2 * features), jnp.bfloat16),
-            jax.ShapeDtypeStruct((seq_count, 2, BLK, features), jnp.bfloat16),
-        ),
+        out_shape=jax.ShapeDtypeStruct((seq_count, 2, BLK, 2 * features), jnp.bfloat16),
         grid_spec=pltpu.PrefetchScalarGridSpec(
             num_scalar_prefetch=1,
             grid=(seq_count,),
-            in_specs=[cache_spec(0), new_spec(0), cache_spec(1), new_spec(1)],
-            out_specs=(
-                pl.BlockSpec((1, 2, BLK, features), lambda d, m: (d, 0, 0, m[2])),
-                pl.BlockSpec((1, 2, BLK, features), lambda d, m: (d, 0, 0, 0)),
-            ),
+            in_specs=[cache_spec, new_spec, cache_spec, new_spec],
+            out_specs=pl.BlockSpec((1, 2, BLK, 2 * features), lambda d, m: (d, 0, 0, 0)),
         ),
-    )(meta, kv_cache, new_kv, kv_cache, new_kv)
+    )(meta, kv_cache, new_kv, mate_cache, mate_new)
 
 
 def half_swap(features):
@@ -206,7 +199,9 @@
     ).astype(jnp.bfloat16)
 
 
-def projection_kernel(x_ref, gain_ref, w_ref, cos_ref, sin_ref, kv_ref, q_ref, normed_ref):
+def projection_kernel(part_ref, x_ref, gain_ref, w_ref, cos_ref, sin_ref, *refs, parts):
+    out_refs = refs[:-1]
+    normed_ref = refs[-1]
     step = pl.program_id(0)
 
     @pl.when(step == 0)
@@ -224,40 +219,37 @@
         paired = jnp.dot(normed_ref[...], swapped, preferred_element_type=jnp.float32)
         return (plain * cos_ref[...] + paired * sin_ref[...]).astype(jnp.bfloat16)
 
-    @pl.when(step == 0)
-    def _():
-        kv_ref[0] = rotated()
-
-    @pl.when(step == 1)
-    def _():
-        kv_ref[1] = plain.astype(jnp.bfloat16)
-
-    @pl.when(step == 2)
-    def _():
-        q_ref[...] = rotated()
-
-
-def project(tokens, gain, weights, tables):
-    parts, width, features = weights.shape
+    for index, part in enumerate(parts):
+
+        @pl.when(step == index)
+        def _():
+            value = rotated() if part < 2 else plain.astype(jnp.bfloat16)
+            out_refs[index][...] = value
+
+
+def project(tokens, gain, weights, tables, parts):
+    _, width, features = weights.shape
     rows = tokens.shape[0]
     full = pl.BlockSpec((rows, features), lambda s: (0, 0))
+    table = jnp.asarray(parts, jnp.int32)
+    out = jax.ShapeDtypeStruct((rows, features), jnp.bfloat16)
     return pl.pallas_call(
-        projection_kernel,
-        out_shape=(
-            jax.ShapeDtypeStruct((2, rows, features), jnp.bfloat16),
-            jax.ShapeDtypeStruct((rows, features), jnp.bfloat16),
+        functools.partial(projection_kernel, parts=parts),
+        out_shape=tuple(out for _ in parts),
+        grid_spec=pltpu.PrefetchScalarGridSpec(
+            num_scalar_prefetch=1,
+            grid=(len(parts),),
+            in_specs=[
+                pl.BlockSpec((rows, width), lambda s, t: (0, 0)),
+                pl.BlockSpec((1, width), lambda s, t: (0, 0)),
+                pl.BlockSpec((1, width, features), lambda s, t: (t[s], 0, 0)),
+                pl.BlockSpec((rows, features), lambda s, t: (0, 0)),
+                pl.BlockSpec((rows, features), lambda s, t: (0, 0)),
+            ],
+            out_specs=tuple(pl.BlockSpec((rows, features), lambda s, t: (0, 0)) for _ in parts),
+            scratch_shapes=[pltpu.VMEM((rows, width), jnp.bfloat16)],
         ),
-        grid=(parts,),
-        in_specs=[
-            pl.BlockSpec((rows, width), lambda s: (0, 0)),
-            pl.BlockSpec((1, width), lambda s: (0, 0)),
-            pl.BlockSpec((1, width, features), lambda s: ((s + 1) % parts, 0, 0)),
-            full,
-            full,
-        ],
-        out_specs=(pl.BlockSpec((2, rows, features), lambda s: (0, 0, 0)), full),
-        scratch_shapes=[pltpu.VMEM((rows, width), jnp.bfloat16)],
-    )(tokens, gain, weights, *tables)
+    )(table, tokens, gain, weights, *tables)
 
 
 def local(tokens, norm_gain, w_qkv, w_out, kv_cache, cached_lengths, requests, block_start):
@@ -282,28 +274,30 @@
     request = row_index * group_requests // tok_count
     first_row = (request * tok_count + group_requests - 1) // group_requests
     positions = group_len + row_index - first_row
-    cosine_table, sine_table = rope_tables(positions, HD)
-    repeat = (1, features // (HD // 2))
-    tables = (jnp.tile(cosine_table, repeat), jnp.tile(sine_table, repeat))
-    new_kv, queries = project(
-        tokens, norm_gain.astype(jnp.float32).reshape(1, model_width), weights, tables
-    )
+    half_size = HD // 2
+    frequency = jnp.exp(
+        jnp.arange(half_size, dtype=jnp.float32) * (-2.0 * math.log(10000.0) / HD)
+    )
+    angles = positions.astype(jnp.float32)[:, None] * jnp.tile(frequency, features // half_size)
+    tables = (jnp.cos(angles), jnp.sin(angles))
+    gain = norm_gain.astype(jnp.float32).reshape(1, model_width)
     core = lax.axis_index("core")
+    swap_cores = [(0, 1), (1, 0)]
+    mate_cache = lax.ppermute(kv_cache, "core", swap_cores)
+    new_keys, new_values = project(tokens, gain, weights, tables, (1, 2))
+    new_kv = jnp.stack([new_keys, new_values])
+    mate_new = lax.ppermute(new_kv, "core", swap_cores)
     relay_meta = jnp.stack(
         [group_len // BLK, group_start, core, jnp.int32(tok_count // BLK)]
     ).astype(jnp.int32)
-    own, other = relay(relay_meta, kv_cache, new_kv, seq_count)
-    partner = lax.ppermute(other, "core", [(0, 1), (1, 0)])
-    zero_index = jnp.zeros((), jnp.int32)
-    joined = lax.dynamic_update_slice(
-        own, partner, (zero_index, zero_index, zero_index, (1 - core) * features)
-    )
-    joined, queries = lax.optimization_barrier((joined, queries))
+    joined = relay(relay_meta, kv_cache, new_kv, mate_cache, mate_new, seq_count)
+    (queries,) = project(tokens, gain, weights, tables, (0,))
+    joined, attn_kv = lax.optimization_barrier((joined, new_kv))
     received = lax.all_to_all(joined, "seq", 0, 0, tiled=True)
     decode_cache = received.transpose(1, 0, 2, 3).reshape(2, 1, seq_count, 1, BLK, 2 * features)
 
     attn_meta = jnp.stack([group_len, group_requests]).astype(jnp.int32)
-    attended = attend(attn_meta, queries, kv_cache, new_kv)
+    attended = attend(attn_meta, queries, kv_cache, attn_kv)
     rows_dev = tok_count // tp_count
     partial = jnp.dot(attended, w_out, preferred_element_type=jnp.float32).astype(jnp.bfloat16)
     summed = lax.dynamic_slice_in_dim(partial, tp_rank * rows_dev, rows_dev, 0).astype(jnp.float32)

time: 161 us -> 156 us (0.969)
  waiting for transfers between devices: 47.6 us -> 39.2 us
  local copies, waits for them, and re-layouts: 16.9 us -> 10.4 us
  Pallas kernels: 63 us -> 68.5 us
  other arithmetic: 10.3 us -> 14.7 us
    ppermute x1 -> x2, waiting for transfers between devices: 6 us -> 0.01 us  [the longest x1 0.01 us: local(): mate_new = lax.ppermute(new_kv, 'core', swap_cores)]
    pallas_call x2 -> x3, Pallas kernels: 28.1 us -> 33.6 us  [the longest x2 22.5 us: project(): pl.pallas_call(functools.partial(projection_kernel, parts=parts), out_sha...]
    dynamic_update_slice x1 -> x0, local copies, waits for them, and re-layouts: 4.07 us -> none  [local(): lax.dynamic_update_slice(own, partner, (zero_index, zero_index, zero_inde...]
    sin x1, other arithmetic: 0.42 us -> 3.88 us  [local(): tables = (jnp.cos(angles), jnp.sin(angles))]
    another operation x4 -> x1, local copies, waits for them, and re-layouts: 2.49 us -> 0.01 us  [local(): jnp.tile(frequency, features // half_size)]
    all_to_all x1, waiting for transfers between devices: 2.48 us -> 0.01 us  [local(): received = lax.all_to_all(joined, 'seq', 0, 0, tiled=True)]
    unnamed x7 -> x9, local copies, waits for them, and re-layouts: 8.61 us -> 8.61 us
  transfers between devices with their start and end apart: 9 -> 10, of which waited for: 5 -> 3; matrix products, arithmetic and copies ran while one was open for 6% -> 12% of each run, Pallas kernels for 22% -> 37%
where the time goes in v7:
time: 156 us
  Pallas kernels  68.5 us (44%)
  waiting for transfers between devices  39.2 us (25%)
  starting transfers between devices  16.3 us (10%)
  other arithmetic  14.7 us (9%)
  local copies, waits for them, and re-layouts  10.4 us (7%)
  between operations  3.67 us (2%)
  matrix products  2.79 us (2%)
    ppermute x7, waiting for transfers between devices, local(): lax.ppermute(chunk, ('x', 'core'), pairs).astype(jnp.float32)  39.2 us
    pallas_call x1, Pallas kernels, attend(): pl.pallas_call(attention_kernel, out_shape=jax.ShapeDtypeStruct(queries.s...  34.9 us
    pallas_call x2, Pallas kernels, project(): pl.pallas_call(functools.partial(projection_kernel, parts=parts), out_sha...  22.5 us
    pallas_call x1, Pallas kernels, relay(): pl.pallas_call(relay_kernel, out_shape=jax.ShapeDtypeStruct((seq_count, 2...  11.1 us
    all_to_all x1, starting transfers between devices, local(): received = lax.all_to_all(joined, 'seq', 0, 0, tiled=True)  9.68 us
    unnamed x9, local copies, waits for them, and re-layouts  8.61 us
    ppermute x7, starting transfers between devices, local(): lax.ppermute(chunk, ('x', 'core'), pairs).astype(jnp.float32)  6.13 us
    sin x1, other arithmetic, local(): tables = (jnp.cos(angles), jnp.sin(angles))  3.88 us
  transfers between devices with their start and end apart: 10, of which 3 were waited for; matrix products, arithmetic and copies ran while one was open for 12% of the time, Pallas kernels for 37%

profile of v7, /device:TPU:0, one launch (start us, length us, event | category | flops | bytes accessed | tf_op | source)
XLA Modules:
  0.0 155.6 jit_solution(1707173947948320798)
XLA Ops:
  0.6 0.0 copy-start
  0.6 0.1 collective-permute-start
  0.7 1.4 reshape.60
  2.2 0.1 mul.79
  2.3 0.7 pad_add_fusion
  3.0 0.1 constant_dynamic-slice_fusion.7
  3.1 0.5 fusion.9
  4.2 1.3 fusion.6
  5.6 3.9 %multiply_sine_fusion = (f32[512,384]{1,0:T(8,128)}, f32[512,384]{1,0:T(8,128)}) fusion(f32[384]{0:T(512)S(1)} %mul.79, f32[512]{0:T(512)S(1)} %fusion.6), kind=kLoop, calls=%fused_computation.1 | loop fusion | flops 196608 | bytes 1576448 | tf_op jit(solution)/shard_map/sin | solution.py:282
  9.4 13.2 %shard_map.114 = (bf16[512,384]{1,0:T(8,128)(2,1)}, bf16[512,384]{1,0:T(8,128)(2,1)}) custom-call(s32[2]{0:T(128)} %constant.114.clone.part_ref, bf16[512,3072]{1,0:T(8,128)(2,1)} %x_ref.3, f32[1,3072]{1,0:T(1,128)} %bitcast.23, bf16[3,3072,384]{2,1,0:T(8,128)(2,1)} %bitcast.19, f32[512,384]{1,0:T(8,128)} %get-tuple-element.20.cos_ref, ...), custom_call_target="tpu_custom_call" | custom-call | tf_op jit(solution)/shard_map/pallas_call | solution.py:236
  22.6 1.2 pad_maximum_fusion.own_n.kn_ref.vn_ref
  23.8 0.0 copy-start.1
  23.9 0.4 collective-permute-start.1
  26.5 1.2 pad_add_fusion.2.meta_ref
  27.7 0.0 collective-permute-done.1.mate_n
  27.7 0.0 collective-permute-done.mate_c
  27.7 0.0 copy-done.1
  27.7 11.1 %shard_map.115 = bf16[16,2,128,768]{3,2,1,0:T(8,128)(2,1)} custom-call(s32[4]{0:T(128)} %pad_add_fusion.2.meta_ref, bf16[2,1,3584,384]{3,2,1,0:T(8,128)(2,1)} %vc_ref.1, bf16[2,512,384]{2,1,0:T(8,128)(2,1)} %copy-done.1, bf16[2,1,3584,384]{3,2,1,0:T(8,128)(2,1)} %collective-permute-done.mate_c, bf16[2,512,384]{2,1,0:T(8,128)(2,1)} %collective-permute-done.1.mate_n), custom_call_target="tpu_custom_call" | custom-call | tf_op jit(solution)/shard_map/pallas_call | solution.py:178
  38.8 9.7 %all-to-all-start = ((bf16[16,2,128,768]{3,2,1,0:T(8,128)(2,1)}), bf16[16,2,128,768]{3,2,1,0:T(8,128)(2,1)}, u32[]{:S(2)}, u32[]{:S(2)}) async-start(bf16[16,2,128,768]{3,2,1,0:T(8,128)(2,1)} %shard_map.115), calls=%async_computation | async-start | bytes 12582912 | tf_op jit(solution)/shard_map/all_to_all | solution.py:296
  48.6 9.2 %shard_map.113.q_ref = bf16[512,384]{1,0:T(8,128)(2,1)} custom-call(s32[1]{0:T(128)} %constant.115.clone.part_ref, bf16[512,3072]{1,0:T(8,128)(2,1)} %x_ref.3, f32[1,3072]{1,0:T(1,128)} %bitcast.24, bf16[3,3072,384]{2,1,0:T(8,128)(2,1)} %bitcast.20, f32[512,384]{1,0:T(8,128)} %get-tuple-element.20.cos_ref, f32[512,384]{1,0:T(8,128)} %get-tuple-element.19.sin_ref), custom_call_target="tpu_custom_call" | custom-call | tf_op jit(solution)/shard_map/pallas_call | solution.py:236
  57.8 1.8 %pad_add_fusion.1.meta_ref = s32[2]{0:T(128)} fusion(s32[1]{0:T(128)} %bitcast.4, s32[1]{0:T(128)} %bitcast.3), kind=kLoop, calls=%fused_computation.32 | loop fusion | flops 2 | bytes 16 | tf_op jit(solution)/shard_map/stack | solution.py:299
  59.7 34.9 %shard_map.116 = bf16[512,384]{1,0:T(8,128)(2,1)} custom-call(s32[2]{0:T(128)} %pad_add_fusion.1.meta_ref, bf16[512,384]{1,0:T(8,128)(2,1)} %shard_map.113.q_ref, bf16[2,1,3584,384]{3,2,1,0:T(8,128)(2,1)} %vc_ref.1, bf16[2,1,3584,384]{3,2,1,0:T(8,128)(2,1)} %vc_ref.1, bf16[2,512,384]{2,1,0:T(8,128)(2,1)} %copy-done.1, bf16[2,512,384]{2,1,0:T(8,128)(2,1)} %copy-done.1), custom_call_target="tpu_custom_call" | custom-call | tf_op jit(solution)/shard_map/pallas_call | solution.py:124
  94.6 0.0 copy-done
  94.6 2.8 %convolution_convert_fusion = bf16[512,3072]{1,0:T(8,128)(2,1)S(1)} fusion(bf16[512,384]{1,0:T(8,128)(2,1)} %shard_map.116, bf16[384,3072]{1,0:T(8,128)(2,1)S(1)} %copy-done), kind=kOutput, calls=%fused_computation | convolution fusion | flops 1209532416 | bytes 5898240 | tf_op jit(solution)/shard_map/dot_general | solution.py:302
  97.4 0.0 copy-start.2
  97.4 1.7 %copy-done.2 = bf16[512,3072]{1,0:T(8,128)(2,1)} copy-done((bf16[512,3072]{1,0:T(8,128)(2,1)}, bf16[512,3072]{1,0:T(8,128)(2,1)S(1)}, u32[]{:S(2)}) %copy-start.2) | copy-done | bytes 3145752
  99.1 1.1 constant_dynamic-slice_fusion.6
  100.2 2.3 %collective-permute-start.8 = (bf16[64,3072]{1,0:T(8,128)(2,1)S(1)}, bf16[64,3072]{1,0:T(8,128)(2,1)S(1)}, u32[]{:S(2)}, u32[]{:S(2)}) collective-permute-start(bf16[64,3072]{1,0:T(8,128)(2,1)S(1)} %get-tuple-element.13), channel_id=1, source_target_pairs={{0,7},{1,0},{2,1},{3,2},{4,3},{5,4},{6,5},{7,6},{8,15},{9,8},{10,9... | collective-permute-start | bytes 1179656 | tf_op jit(solution)/shard_map/ppermute | solution.py:308
  102.4 0.8 collective-permute-start.7
  103.2 0.3 collective-permute-start.6
  103.6 2.7 %collective-permute-start.5 = (bf16[64,3072]{1,0:T(8,128)(2,1)}, bf16[64,3072]{1,0:T(8,128)(2,1)}, u32[]{:S(2)}, u32[]{:S(2)}) collective-permute-start(bf16[64,3072]{1,0:T(8,128)(2,1)} %get-tuple-element.16), channel_id=1, source_target_pairs={{0,4},{1,5},{2,6},{3,7},{4,0},{5,1},{6,2},{7,3},{8,12},{9,13},{10,... | collective-permute-start | bytes 1179656 | tf_op jit(solution)/shard_map/ppermute | solution.py:308
  106.3 0.0 collective-permute-start.4
  106.3 5.6 %collective-permute-done.8 = bf16[64,3072]{1,0:T(8,128)(2,1)S(1)} collective-permute-done((bf16[64,3072]{1,0:T(8,128)(2,1)S(1)}, bf16[64,3072]{1,0:T(8,128)(2,1)S(1)}, u32[]{:S(2)}, u32[]{:S(2)}) %collective-permute-start.8) | collective-permute-done | bytes 393248 | tf_op jit(solution)/shard_map/ppermute | solution.py:308
  111.9 0.0 collective-permute-start.3
  111.9 25.1 %collective-permute-done.7 = bf16[64,3072]{1,0:T(8,128)(2,1)S(1)} collective-permute-done((bf16[64,3072]{1,0:T(8,128)(2,1)S(1)}, bf16[64,3072]{1,0:T(8,128)(2,1)S(1)}, u32[]{:S(2)}, u32[]{:S(2)}) %collective-permute-start.7) | collective-permute-done | bytes 393248 | tf_op jit(solution)/shard_map/ppermute | solution.py:308
  137.0 0.0 copy-start.3
  137.0 0.8 copy-done.3
  137.8 0.0 collective-permute-start.2
  137.8 0.0 collective-permute-done.6
  137.8 0.0 collective-permute-done.5
  137.8 0.0 collective-permute-done.4
  137.8 0.0 collective-permute-done.3
  137.8 8.5 %collective-permute-done.2 = bf16[64,3072]{1,0:T(8,128)(2,1)} collective-permute-done((bf16[64,3072]{1,0:T(8,128)(2,1)S(1)}, bf16[64,3072]{1,0:T(8,128)(2,1)}, u32[]{:S(2)}, u32[]{:S(2)}) %collective-permute-start.2) | collective-permute-done | bytes 393248 | tf_op jit(solution)/shard_map/ppermute | solution.py:308
  146.3 3.1 %add_convert_fusion = bf16[64,3072]{1,0:T(8,128)(2,1)} fusion(bf16[64,3072]{1,0:T(8,128)(2,1)S(1)} %collective-permute-done.8, bf16[64,3072]{1,0:T(8,128)(2,1)} %copy-done.3, bf16[64,3072]{1,0:T(8,128)(2,1)} %collective-permute-done.6, bf16[64,3072]{1,0:T(8,128)(2,1)} %collective-permute-done.5, bf16[64,3072]{1,0:T(8,128)(2,1)} %collective-permute-done.4, ...), kind=kLoop, calls=%fused_computation.4 | loop fusion | flops 3538944 | bytes 3932164 | tf_op jit(solution)/shard_map/convert_element_type | solution.py:310
  149.4 0.0 all-to-all-done
  149.4 6.1 %copy.12 = bf16[2,1,16,1,128,768]{5,4,3,2,1,0:T(8,128)(2,1)} copy(bf16[2,1,16,1,128,768]{5,4,0,2,3,1:T(8,128)(2,1)} %bitcast.15) | data formatting | bytes 12582912
  (2 shorter events, 0.0 us)
Async XLA Ops:
  0.6 93.9 %copy-start = (bf16[384,3072]{1,0:T(8,128)(2,1)S(1)}, bf16[384,3072]{1,0:T(8,128)(2,1)}, u32[]{:S(2)}) copy-start(bf16[384,3072]{1,0:T(8,128)(2,1)} %param.13) | copy-start | bytes 7077892
  0.6 27.0 %collective-permute-start = (bf16[2,1,3584,384]{3,2,1,0:T(8,128)(2,1)}, bf16[2,1,3584,384]{3,2,1,0:T(8,128)(2,1)}, u32[]{:S(2)}, u32[]{:S(2)}) collective-permute-start(bf16[2,1,3584,384]{3,2,1,0:T(8,128)(2,1)} %vc_ref.1), channel_id=1, source_target_pairs={{0,1},{1,0},{2,3},{3,2},{4,5},{5,4},{6,7},{7,6},{8,9},{9,8},{10,11... | collective-permute-start | bytes 16515080 | tf_op jit(solution)/shard_map/ppermute | solution.py:286
  23.8 3.8 %copy-start.1 = (bf16[2,512,384]{2,1,0:T(8,128)(2,1)}, bf16[2,512,384]{2,1,0:T(8,128)(2,1)S(1)}, u32[]{:S(2)}) copy-start(bf16[2,512,384]{2,1,0:T(8,128)(2,1)S(1)} %pad_maximum_fusion.own_n.kn_ref.vn_ref) | copy-start | bytes 2359300
  23.9 3.8 %collective-permute-start.1 = (bf16[2,512,384]{2,1,0:T(8,128)(2,1)S(1)}, bf16[2,512,384]{2,1,0:T(8,128)(2,1)}, u32[]{:S(2)}, u32[]{:S(2)}) collective-permute-start(bf16[2,512,384]{2,1,0:T(8,128)(2,1)S(1)} %pad_maximum_fusion.own_n.kn_ref.vn_ref), channel_id=1, source_target_pairs={{0,1},{1,0},{2,3},{3,2},{4,5},{5,4},{6,7},{7,6},{8,9},{9,8},{10,11... | collective-permute-start | bytes 2359304 | tf_op jit(solution)/shard_map/ppermute | solution.py:289
  38.8 110.6 %all-to-all-start = ((bf16[16,2,128,768]{3,2,1,0:T(8,128)(2,1)}), bf16[16,2,128,768]{3,2,1,0:T(8,128)(2,1)}, u32[]{:S(2)}, u32[]{:S(2)}) async-start(bf16[16,2,128,768]{3,2,1,0:T(8,128)(2,1)} %shard_map.115), calls=%async_computation | async-start | bytes 12582912 | tf_op jit(solution)/shard_map/all_to_all | solution.py:296
  97.4 1.7 %copy-start.2 = (bf16[512,3072]{1,0:T(8,128)(2,1)}, bf16[512,3072]{1,0:T(8,128)(2,1)S(1)}, u32[]{:S(2)}) copy-start(bf16[512,3072]{1,0:T(8,128)(2,1)S(1)} %convolution_convert_fusion) | copy-start | bytes 9437188
  100.2 11.7 %collective-permute-start.8 = (bf16[64,3072]{1,0:T(8,128)(2,1)S(1)}, bf16[64,3072]{1,0:T(8,128)(2,1)S(1)}, u32[]{:S(2)}, u32[]{:S(2)}) collective-permute-start(bf16[64,3072]{1,0:T(8,128)(2,1)S(1)} %get-tuple-element.13), channel_id=1, source_target_pairs={{0,7},{1,0},{2,1},{3,2},{4,3},{5,4},{6,5},{7,6},{8,15},{9,8},{10,9... | collective-permute-start | bytes 1179656 | tf_op jit(solution)/shard_map/ppermute | solution.py:308
  102.4 34.6 %collective-permute-start.7 = (bf16[64,3072]{1,0:T(8,128)(2,1)S(1)}, bf16[64,3072]{1,0:T(8,128)(2,1)S(1)}, u32[]{:S(2)}, u32[]{:S(2)}) collective-permute-start(bf16[64,3072]{1,0:T(8,128)(2,1)S(1)} %get-tuple-element.14), channel_id=1, source_target_pairs={{0,6},{1,7},{2,0},{3,1},{4,2},{5,3},{6,4},{7,5},{8,14},{9,15},{10,... | collective-permute-start | bytes 1179656 | tf_op jit(solution)/shard_map/ppermute | solution.py:308
  103.2 34.5 %collective-permute-start.6 = (bf16[64,3072]{1,0:T(8,128)(2,1)}, bf16[64,3072]{1,0:T(8,128)(2,1)}, u32[]{:S(2)}, u32[]{:S(2)}) collective-permute-start(bf16[64,3072]{1,0:T(8,128)(2,1)} %get-tuple-element.15), channel_id=1, source_target_pairs={{0,5},{1,6},{2,7},{3,0},{4,1},{5,2},{6,3},{7,4},{8,13},{9,14},{10,... | collective-permute-start | bytes 1179656 | tf_op jit(solution)/shard_map/ppermute | solution.py:308
  103.6 34.2 %collective-permute-start.5 = (bf16[64,3072]{1,0:T(8,128)(2,1)}, bf16[64,3072]{1,0:T(8,128)(2,1)}, u32[]{:S(2)}, u32[]{:S(2)}) collective-permute-start(bf16[64,3072]{1,0:T(8,128)(2,1)} %get-tuple-element.16), channel_id=1, source_target_pairs={{0,4},{1,5},{2,6},{3,7},{4,0},{5,1},{6,2},{7,3},{8,12},{9,13},{10,... | collective-permute-start | bytes 1179656 | tf_op jit(solution)/shard_map/ppermute | solution.py:308
  106.3 31.5 %collective-permute-start.4 = (bf16[64,3072]{1,0:T(8,128)(2,1)}, bf16[64,3072]{1,0:T(8,128)(2,1)}, u32[]{:S(2)}, u32[]{:S(2)}) collective-permute-start(bf16[64,3072]{1,0:T(8,128)(2,1)} %get-tuple-element.17), channel_id=1, source_target_pairs={{0,3},{1,4},{2,5},{3,6},{4,7},{5,0},{6,1},{7,2},{8,11},{9,12},{10,... | collective-permute-start | bytes 1179656 | tf_op jit(solution)/shard_map/ppermute | solution.py:308
  111.9 25.9 %collective-permute-start.3 = (bf16[64,3072]{1,0:T(8,128)(2,1)S(1)}, bf16[64,3072]{1,0:T(8,128)(2,1)}, u32[]{:S(2)}, u32[]{:S(2)}) collective-permute-start(bf16[64,3072]{1,0:T(8,128)(2,1)S(1)} %get-tuple-element.18), channel_id=1, source_target_pairs={{0,2},{1,3},{2,4},{3,5},{4,6},{5,7},{6,0},{7,1},{8,10},{9,11},{10,... | collective-permute-start | bytes 1179656 | tf_op jit(solution)/shard_map/ppermute | solution.py:308
  137.0 0.8 copy-start.3
  137.8 8.5 %collective-permute-start.2 = (bf16[64,3072]{1,0:T(8,128)(2,1)S(1)}, bf16[64,3072]{1,0:T(8,128)(2,1)}, u32[]{:S(2)}, u32[]{:S(2)}) collective-permute-start(bf16[64,3072]{1,0:T(8,128)(2,1)S(1)} %get-tuple-element.12), channel_id=1, source_target_pairs={{0,1},{1,2},{2,3},{3,4},{4,5},{5,6},{6,7},{7,0},{8,9},{9,10},{10,1... | collective-permute-start | bytes 1179656 | tf_op jit(solution)/shard_map/ppermute | solution.py:308

commit v8 on v7

--- a/solution.py
+++ b/solution.py
@@ -214,9 +214,12 @@
     plain = jnp.dot(normed_ref[...], weights, preferred_element_type=jnp.float32)
 
     def rotated():
-        swap = half_swap(weights.shape[1])
-        swapped = jnp.dot(weights, swap, preferred_element_type=jnp.float32).astype(jnp.bfloat16)
-        paired = jnp.dot(normed_ref[...], swapped, preferred_element_type=jnp.float32)
+        features = plain.shape[1]
+        half = HD // 2
+        lane = lax.broadcasted_iota(jnp.int32, plain.shape, 1)
+        ahead = pltpu.roll(plain, features - half, 1)
+        behind = pltpu.roll(plain, half, 1)
+        paired = jnp.where(lane % HD < half, -ahead, behind)
         return (plain * cos_ref[...] + paired * sin_ref[...]).astype(jnp.bfloat16)
 
     for index, part in enumerate(parts):
@@ -300,12 +303,21 @@
     attended = attend(attn_meta, queries, kv_cache, attn_kv)
     rows_dev = tok_count // tp_count
     partial = jnp.dot(attended, w_out, preferred_element_type=jnp.float32).astype(jnp.bfloat16)
-    summed = lax.dynamic_slice_in_dim(partial, tp_rank * rows_dev, rows_dev, 0).astype(jnp.float32)
-    for shift in range(1, tp_count):
-        target = (tp_rank + shift) % tp_count
-        chunk = lax.dynamic_slice_in_dim(partial, target * rows_dev, rows_dev, 0)
-        pairs = [(source, (source + shift) % tp_count) for source in range(tp_count)]
-        summed = summed + lax.ppermute(chunk, ("x", "core"), pairs).astype(jnp.float32)
+    x_count = tp_count // 2
+    x_rank = lax.axis_index("x")
+    by_owner = partial.reshape(x_count, 2, rows_dev, model_width)
+    mine = lax.dynamic_index_in_dim(by_owner, core, 1, keepdims=False)
+    theirs = lax.dynamic_index_in_dim(by_owner, 1 - core, 1, keepdims=False)
+    pair_sum = mine.astype(jnp.float32) + lax.ppermute(theirs, "core", swap_cores).astype(
+        jnp.float32
+    )
+    pair_sent = pair_sum.astype(jnp.bfloat16)
+    summed = lax.dynamic_index_in_dim(pair_sum, x_rank, 0, keepdims=False)
+    for shift in range(1, x_count):
+        target = (x_rank + shift) % x_count
+        chunk = lax.dynamic_index_in_dim(pair_sent, target, 0, keepdims=False)
+        pairs = [(source, (source + shift) % x_count) for source in range(x_count)]
+        summed = summed + lax.ppermute(chunk, "x", pairs).astype(jnp.float32)
     own_rows = lax.dynamic_slice_in_dim(inputs, tp_rank * rows_dev, rows_dev, 0)
     layer_out = (own_rows + summed).astype(jnp.bfloat16)
     return (layer_out, decode_cache)

time: 156 us -> 147 us (0.942)
  waiting for transfers between devices: 39.2 us -> 32.3 us
  Pallas kernels: 68.5 us -> 63.9 us
  other arithmetic: 14.7 us -> 18.4 us
    ppermute x7 -> x4, waiting for transfers between devices: 39.2 us -> 20.2 us  [the longest x3 16.4 us: local(): summed = summed + lax.ppermute(chunk, 'x', pairs).astype(jnp.float32)]
    all_to_all x1, waiting for transfers between devices: 0.01 us -> 12.2 us  [local(): received = lax.all_to_all(joined, 'seq', 0, 0, tiled=True)]
    pallas_call x2, Pallas kernels: 22.5 us -> 17.1 us  [project(): pl.pallas_call(functools.partial(projection_kernel, parts=parts), out_sha...]
    convert_element_type x0 -> x1, other arithmetic: none -> 4.28 us  [local(): pair_sent = pair_sum.astype(jnp.bfloat16)]
    squeeze x0 -> x2, local copies, waits for them, and re-layouts: none -> 2.07 us  [the longest x1 1.25 us: local(): theirs = lax.dynamic_index_in_dim(by_owner, 1 - core, 1, keepdims=False)]
    unnamed x9 -> x7, local copies, waits for them, and re-layouts: 8.61 us -> 7.8 us
    ppermute x7 -> x4, starting transfers between devices: 6.13 us -> 5.68 us  [the longest x3 5.66 us: local(): summed = summed + lax.ppermute(chunk, 'x', pairs).astype(jnp.float32)]
  transfers between devices with their start and end apart: 10 -> 7, of which waited for: 3 -> 4; matrix products, arithmetic and copies ran while one was open for 12% -> 16% of each run, Pallas kernels for 37% -> 36%
where the time goes in v8:
time: 147 us; the launch traced here: 146 us
  Pallas kernels  63.9 us (43%)
  waiting for transfers between devices  32.3 us (22%)
  other arithmetic  18.4 us (13%)
  starting transfers between devices  14.8 us (10%)
  local copies, waits for them, and re-layouts  10.6 us (7%)
  between operations  3.66 us (2%)
  matrix products  2.79 us (2%)
    pallas_call x1, Pallas kernels, attend(): pl.pallas_call(attention_kernel, out_shape=jax.ShapeDtypeStruct(queries.s...  34.9 us
    pallas_call x2, Pallas kernels, project(): pl.pallas_call(functools.partial(projection_kernel, parts=parts), out_sha...  17.1 us
    ppermute x3, waiting for transfers between devices, local(): summed = summed + lax.ppermute(chunk, 'x', pairs).astype(jnp.float32)  16.4 us
    all_to_all x1, waiting for transfers between devices, local(): received = lax.all_to_all(joined, 'seq', 0, 0, tiled=True)  12.2 us
    pallas_call x1, Pallas kernels, relay(): pl.pallas_call(relay_kernel, out_shape=jax.ShapeDtypeStruct((seq_count, 2...  11.9 us
    all_to_all x1, starting transfers between devices, local(): received = lax.all_to_all(joined, 'seq', 0, 0, tiled=True)  8.58 us
    unnamed x7, local copies, waits for them, and re-layouts  7.8 us
    ppermute x3, starting transfers between devices, local(): summed = summed + lax.ppermute(chunk, 'x', pairs).astype(jnp.float32)  5.66 us
  transfers between devices with their start and end apart: 7, of which 4 were waited for; matrix products, arithmetic and copies ran while one was open for 16% of the time, Pallas kernels for 36%

profile of v8, /device:TPU:0, one launch (start us, length us, event | category | flops | bytes accessed | tf_op | source)
XLA Modules:
  0.0 146.5 jit_solution(17165771625488696283)
XLA Ops:
  0.6 0.0 copy-start
  0.6 0.1 collective-permute-start
  0.7 0.8 pad_add_fusion
  1.6 0.1 constant_dynamic-slice_fusion
  1.7 0.6 fusion.14
  2.9 0.1 mul.57
  3.0 1.3 reshape.66
  4.3 1.3 fusion.10
  5.6 3.9 %multiply_sine_fusion = (f32[512,384]{1,0:T(8,128)}, f32[512,384]{1,0:T(8,128)}) fusion(f32[384]{0:T(512)S(1)} %mul.57, f32[512]{0:T(512)S(1)} %fusion.10), kind=kLoop, calls=%fused_computation.3 | loop fusion | flops 196608 | bytes 1576448 | tf_op jit(solution)/shard_map/sin | solution.py:285
  9.5 10.6 %shard_map.114 = (bf16[512,384]{1,0:T(8,128)(2,1)}, bf16[512,384]{1,0:T(8,128)(2,1)}) custom-call(s32[2]{0:T(128)} %constant.110.clone.part_ref, bf16[512,3072]{1,0:T(8,128)(2,1)} %x_ref.3, f32[1,3072]{1,0:T(1,128)} %bitcast.48, bf16[3,3072,384]{2,1,0:T(8,128)(2,1)} %bitcast.42, f32[512,384]{1,0:T(8,128)} %get-tuple-element.18.cos_ref, ...), custom_call_target="tpu_custom_call" | custom-call | tf_op jit(solution)/shard_map/pallas_call | solution.py:239
  20.1 1.2 pad_maximum_fusion.own_n.kn_ref.vn_ref
  21.3 0.0 copy-start.1
  21.3 0.4 collective-permute-start.1
  24.0 1.2 pad_add_fusion.2.meta_ref
  25.3 0.0 collective-permute-done.1.mate_n
  25.3 0.0 collective-permute-done.mate_c
  25.3 0.0 copy-done.1
  25.3 11.9 %shard_map.115 = bf16[16,2,128,768]{3,2,1,0:T(8,128)(2,1)} custom-call(s32[4]{0:T(128)} %pad_add_fusion.2.meta_ref, bf16[2,1,3584,384]{3,2,1,0:T(8,128)(2,1)} %vc_ref.1, bf16[2,512,384]{2,1,0:T(8,128)(2,1)} %copy-done.1, bf16[2,1,3584,384]{3,2,1,0:T(8,128)(2,1)} %collective-permute-done.mate_c, bf16[2,512,384]{2,1,0:T(8,128)(2,1)} %collective-permute-done.1.mate_n), custom_call_target="tpu_custom_call" | custom-call | tf_op jit(solution)/shard_map/pallas_call | solution.py:178
  37.2 8.6 %all-to-all-start = ((bf16[16,2,128,768]{3,2,1,0:T(8,128)(2,1)}), bf16[16,2,128,768]{3,2,1,0:T(8,128)(2,1)}, u32[]{:S(2)}, u32[]{:S(2)}) async-start(bf16[16,2,128,768]{3,2,1,0:T(8,128)(2,1)} %shard_map.115), calls=%async_computation | async-start | bytes 12582912 | tf_op jit(solution)/shard_map/all_to_all | solution.py:299
  45.8 6.5 %shard_map.113.q_ref = bf16[512,384]{1,0:T(8,128)(2,1)} custom-call(s32[1]{0:T(128)} %constant.111.clone.part_ref, bf16[512,3072]{1,0:T(8,128)(2,1)} %x_ref.3, f32[1,3072]{1,0:T(1,128)} %bitcast.49, bf16[3,3072,384]{2,1,0:T(8,128)(2,1)} %bitcast.43, f32[512,384]{1,0:T(8,128)} %get-tuple-element.18.cos_ref, f32[512,384]{1,0:T(8,128)} %get-tuple-element.17.sin_ref), custom_call_target="tpu_custom_call" | custom-call | tf_op jit(solution)/shard_map/pallas_call | solution.py:239
  52.3 1.9 %pad_add_fusion.1.meta_ref = s32[2]{0:T(128)} fusion(s32[1]{0:T(128)} %bitcast.4, s32[1]{0:T(128)} %bitcast.3), kind=kLoop, calls=%fused_computation.34 | loop fusion | flops 2 | bytes 16 | tf_op jit(solution)/shard_map/stack | solution.py:302
  54.2 34.9 %shard_map.116 = bf16[512,384]{1,0:T(8,128)(2,1)} custom-call(s32[2]{0:T(128)} %pad_add_fusion.1.meta_ref, bf16[512,384]{1,0:T(8,128)(2,1)} %shard_map.113.q_ref, bf16[2,1,3584,384]{3,2,1,0:T(8,128)(2,1)} %vc_ref.1, bf16[2,1,3584,384]{3,2,1,0:T(8,128)(2,1)} %vc_ref.1, bf16[2,512,384]{2,1,0:T(8,128)(2,1)} %copy-done.1, bf16[2,512,384]{2,1,0:T(8,128)(2,1)} %copy-done.1), custom_call_target="tpu_custom_call" | custom-call | tf_op jit(solution)/shard_map/pallas_call | solution.py:124
  89.1 0.0 copy-done
  89.1 2.8 %convolution_convert_fusion = bf16[512,3072]{1,0:T(8,128)(2,1)S(1)} fusion(bf16[512,384]{1,0:T(8,128)(2,1)} %shard_map.116, bf16[384,3072]{1,0:T(8,128)(2,1)S(1)} %copy-done), kind=kOutput, calls=%fused_computation | convolution fusion | flops 1209532416 | bytes 5898240 | tf_op jit(solution)/shard_map/dot_general | solution.py:305
  91.9 0.0 copy-start.2
  91.9 1.6 %copy-done.2 = bf16[512,3072]{1,0:T(8,128)(2,1)} copy-done((bf16[512,3072]{1,0:T(8,128)(2,1)}, bf16[512,3072]{1,0:T(8,128)(2,1)S(1)}, u32[]{:S(2)}) %copy-start.2) | copy-done | bytes 3145752
  93.5 1.3 dynamic-slice_bitcast_fusion
  94.8 0.0 collective-permute-start.2
  94.8 3.7 %collective-permute-done.2 = bf16[4,64,3072]{2,1,0:T(8,128)(2,1)} collective-permute-done((bf16[4,64,3072]{2,1,0:T(8,128)(2,1)}, bf16[4,64,3072]{2,1,0:T(8,128)(2,1)}, u32[]{:S(2)}, u32[]{:S(2)}) %collective-permute-start.2) | collective-permute-done | bytes 1572896 | tf_op jit(solution)/shard_map/ppermute | solution.py:311
  98.5 4.3 %fusion.13 = (bf16[4,64,3072]{2,1,0:T(8,128)(2,1)S(1)}, f32[4,64,3072]{2,1,0:T(8,128)}) fusion(bf16[4,64,3072]{2,1,0:T(8,128)(2,1)} %collective-permute-done.2, bf16[4,2,64,3072]{3,2,1,0:T(8,128)(2,1)} %bitcast.45, s32[]{:T(128)S(6)} %select_n.69), kind=kLoop, calls=%fused_computation.37 | loop fusion | flops 3145728 | bytes 7864324 | tf_op jit(solution)/shard_map/convert_element_type | solution.py:314
  102.8 0.8 dynamic-slice_bitcast_fusion.3
  103.6 1.5 %collective-permute-start.3 = (bf16[64,3072]{1,0:T(8,128)(2,1)}, bf16[64,3072]{1,0:T(8,128)(2,1)S(1)}, u32[]{:S(2)}, u32[]{:S(2)}) collective-permute-start(bf16[64,3072]{1,0:T(8,128)(2,1)} %get-tuple-element.14), channel_id=1, source_target_pairs={{0,2},{2,4},{4,6},{6,0},{1,3},{3,5},{5,7},{7,1},{8,10},{10,12},{12... | collective-permute-start | bytes 1179656 | tf_op jit(solution)/shard_map/ppermute | solution.py:320
  105.1 2.7 %collective-permute-start.4 = (bf16[64,3072]{1,0:T(8,128)(2,1)S(1)}, bf16[64,3072]{1,0:T(8,128)(2,1)}, u32[]{:S(2)}, u32[]{:S(2)}) collective-permute-start(bf16[64,3072]{1,0:T(8,128)(2,1)S(1)} %get-tuple-element.16), channel_id=1, source_target_pairs={{0,4},{2,6},{4,0},{6,2},{1,5},{3,7},{5,1},{7,3},{8,12},{10,14},{12... | collective-permute-start | bytes 1179656 | tf_op jit(solution)/shard_map/ppermute | solution.py:320
  107.8 1.4 collective-permute-start.5
  109.3 6.9 %collective-permute-done.3 = bf16[64,3072]{1,0:T(8,128)(2,1)S(1)} collective-permute-done((bf16[64,3072]{1,0:T(8,128)(2,1)}, bf16[64,3072]{1,0:T(8,128)(2,1)S(1)}, u32[]{:S(2)}, u32[]{:S(2)}) %collective-permute-start.3) | collective-permute-done | bytes 393248 | tf_op jit(solution)/shard_map/ppermute | solution.py:320
  116.2 9.5 %collective-permute-done.4 = bf16[64,3072]{1,0:T(8,128)(2,1)} collective-permute-done((bf16[64,3072]{1,0:T(8,128)(2,1)S(1)}, bf16[64,3072]{1,0:T(8,128)(2,1)}, u32[]{:S(2)}, u32[]{:S(2)}) %collective-permute-start.4) | collective-permute-done | bytes 393248 | tf_op jit(solution)/shard_map/ppermute | solution.py:320
  125.7 0.0 collective-permute-done.5
  125.7 2.4 %fusion.3 = bf16[64,3072]{1,0:T(8,128)(2,1)} fusion(bf16[64,3072]{1,0:T(8,128)(2,1)} %collective-permute-done.5, bf16[64,3072]{1,0:T(8,128)(2,1)} %collective-permute-done.4, bf16[64,3072]{1,0:T(8,128)(2,1)S(1)} %collective-permute-done.3, f32[4,64,3072]{2,1,0:T(8,128)} %get-tuple-element.13, s32[]{:T(128)S(6)} %select_n.71, bf16[512,3072]{1,0:T(8,128)(2,1)} %x_ref.3, ...), kind=kLoop, calls=%fused_computation.10 | loop fusion | flops 1769472 | bytes 2752520 | tf_op jit(solution)/shard_map/convert_element_type | solution.py:322
  128.2 12.2 %all-to-all-done = bf16[16,2,128,768]{3,2,1,0:T(8,128)(2,1)} async-done(((bf16[16,2,128,768]{3,2,1,0:T(8,128)(2,1)}), bf16[16,2,128,768]{3,2,1,0:T(8,128)(2,1)}, u32[]{:S(2)}, u32[]{:S(2)}) %all-to-all-start) | async-done | bytes 6291488 | tf_op jit(solution)/shard_map/all_to_all | solution.py:299
  140.3 6.1 %copy.12 = bf16[2,1,16,1,128,768]{5,4,3,2,1,0:T(8,128)(2,1)} copy(bf16[2,1,16,1,128,768]{5,4,0,2,3,1:T(8,128)(2,1)} %bitcast.22) | data formatting | bytes 12582912
  (2 shorter events, 0.0 us)
Async XLA Ops:
  0.6 88.4 %copy-start = (bf16[384,3072]{1,0:T(8,128)(2,1)S(1)}, bf16[384,3072]{1,0:T(8,128)(2,1)}, u32[]{:S(2)}) copy-start(bf16[384,3072]{1,0:T(8,128)(2,1)} %param.13) | copy-start | bytes 7077892
  0.6 24.6 %collective-permute-start = (bf16[2,1,3584,384]{3,2,1,0:T(8,128)(2,1)}, bf16[2,1,3584,384]{3,2,1,0:T(8,128)(2,1)}, u32[]{:S(2)}, u32[]{:S(2)}) collective-permute-start(bf16[2,1,3584,384]{3,2,1,0:T(8,128)(2,1)} %vc_ref.1), channel_id=1, source_target_pairs={{0,1},{1,0},{2,3},{3,2},{4,5},{5,4},{6,7},{7,6},{8,9},{9,8},{10,11... | collective-permute-start | bytes 16515080 | tf_op jit(solution)/shard_map/ppermute | solution.py:289
  21.3 4.0 %copy-start.1 = (bf16[2,512,384]{2,1,0:T(8,128)(2,1)}, bf16[2,512,384]{2,1,0:T(8,128)(2,1)S(1)}, u32[]{:S(2)}) copy-start(bf16[2,512,384]{2,1,0:T(8,128)(2,1)S(1)} %pad_maximum_fusion.own_n.kn_ref.vn_ref) | copy-start | bytes 2359300
  21.3 4.0 %collective-permute-start.1 = (bf16[2,512,384]{2,1,0:T(8,128)(2,1)S(1)}, bf16[2,512,384]{2,1,0:T(8,128)(2,1)}, u32[]{:S(2)}, u32[]{:S(2)}) collective-permute-start(bf16[2,512,384]{2,1,0:T(8,128)(2,1)S(1)} %pad_maximum_fusion.own_n.kn_ref.vn_ref), channel_id=1, source_target_pairs={{0,1},{1,0},{2,3},{3,2},{4,5},{5,4},{6,7},{7,6},{8,9},{9,8},{10,11... | collective-permute-start | bytes 2359304 | tf_op jit(solution)/shard_map/ppermute | solution.py:292
  37.2 103.1 %all-to-all-start = ((bf16[16,2,128,768]{3,2,1,0:T(8,128)(2,1)}), bf16[16,2,128,768]{3,2,1,0:T(8,128)(2,1)}, u32[]{:S(2)}, u32[]{:S(2)}) async-start(bf16[16,2,128,768]{3,2,1,0:T(8,128)(2,1)} %shard_map.115), calls=%async_computation | async-start | bytes 12582912 | tf_op jit(solution)/shard_map/all_to_all | solution.py:299
  91.9 1.6 %copy-start.2 = (bf16[512,3072]{1,0:T(8,128)(2,1)}, bf16[512,3072]{1,0:T(8,128)(2,1)S(1)}, u32[]{:S(2)}) copy-start(bf16[512,3072]{1,0:T(8,128)(2,1)S(1)} %convolution_convert_fusion) | copy-start | bytes 9437188
  94.8 3.8 %collective-permute-start.2 = (bf16[4,64,3072]{2,1,0:T(8,128)(2,1)}, bf16[4,64,3072]{2,1,0:T(8,128)(2,1)}, u32[]{:S(2)}, u32[]{:S(2)}) collective-permute-start(bf16[4,64,3072]{2,1,0:T(8,128)(2,1)} %dynamic-slice_bitcast_fusion), channel_id=1, source_target_pairs={{0,1},{1,0},{2,3},{3,2},{4,5},{5,4},{6,7},{7,6},{8,9},{9,8},{10,11... | collective-permute-start | bytes 4718600 | tf_op jit(solution)/shard_map/ppermute | solution.py:311
  103.6 12.6 %collective-permute-start.3 = (bf16[64,3072]{1,0:T(8,128)(2,1)}, bf16[64,3072]{1,0:T(8,128)(2,1)S(1)}, u32[]{:S(2)}, u32[]{:S(2)}) collective-permute-start(bf16[64,3072]{1,0:T(8,128)(2,1)} %get-tuple-element.14), channel_id=1, source_target_pairs={{0,2},{2,4},{4,6},{6,0},{1,3},{3,5},{5,7},{7,1},{8,10},{10,12},{12... | collective-permute-start | bytes 1179656 | tf_op jit(solution)/shard_map/ppermute | solution.py:320
  105.1 20.6 %collective-permute-start.4 = (bf16[64,3072]{1,0:T(8,128)(2,1)S(1)}, bf16[64,3072]{1,0:T(8,128)(2,1)}, u32[]{:S(2)}, u32[]{:S(2)}) collective-permute-start(bf16[64,3072]{1,0:T(8,128)(2,1)S(1)} %get-tuple-element.16), channel_id=1, source_target_pairs={{0,4},{2,6},{4,0},{6,2},{1,5},{3,7},{5,1},{7,3},{8,12},{10,14},{12... | collective-permute-start | bytes 1179656 | tf_op jit(solution)/shard_map/ppermute | solution.py:320
  107.8 17.9 %collective-permute-start.5 = (bf16[64,3072]{1,0:T(8,128)(2,1)S(1)}, bf16[64,3072]{1,0:T(8,128)(2,1)}, u32[]{:S(2)}, u32[]{:S(2)}) collective-permute-start(bf16[64,3072]{1,0:T(8,128)(2,1)S(1)} %get-tuple-element.15), channel_id=1, source_target_pairs={{0,6},{2,0},{4,2},{6,4},{1,7},{3,1},{5,3},{7,5},{8,14},{10,8},{12,... | collective-permute-start | bytes 1179656 | tf_op jit(solution)/shard_map/ppermute | solution.py:320

commit v9 on v8

--- a/solution.py
+++ b/solution.py
@@ -139,52 +139,69 @@
     )(meta, queries, kv_cache, kv_cache, new_kv, new_kv)
 
 
-def relay_kernel(meta_ref, own_c, own_n, mate_c, mate_n, out_ref):
+def relay_kernel(meta_ref, *refs):
+    out_ref = refs[-1]
+    sources = refs[:-1]
     len_blocks = meta_ref[0]
     group_start = meta_ref[1]
     core = meta_ref[2]
     new_blocks = meta_ref[3]
-    dest = pl.program_id(0)
-    rank_count = 2 * pl.num_programs(0)
-    features = own_n.shape[2]
-    block = (2 * dest + core - group_start + rank_count) % rank_count
-    old = block < len_blocks
-    fresh = (block >= len_blocks) & (block < len_blocks + new_blocks)
-    zero = jnp.zeros(own_n.shape[1:], own_n.dtype)
+    per_step = out_ref.shape[0]
+    rank_count = 2 * pl.num_programs(0) * per_step
+    features = sources[1].shape[2]
+    zero = jnp.zeros(sources[1].shape[1:], sources[1].dtype)
     first = core == 0
-    for kv in range(2):
-        mine = jnp.where(old, own_c[kv, 0], jnp.where(fresh, own_n[kv], zero))
-        mate = jnp.where(old, mate_c[kv, 0], jnp.where(fresh, mate_n[kv], zero))
-        out_ref[0, kv, :, :features] = jnp.where(first, mine, mate)
-        out_ref[0, kv, :, features:] = jnp.where(first, mate, mine)
+    for slot in range(per_step):
+        own_c, own_n, mate_c, mate_n = sources[4 * slot : 4 * slot + 4]
+        dest = pl.program_id(0) * per_step + slot
+        block = (2 * dest + core - group_start + rank_count) % rank_count
+        old = block < len_blocks
+        fresh = (block >= len_blocks) & (block < len_blocks + new_blocks)
+        for kv in range(2):
+            mine = jnp.where(old, own_c[kv, 0], jnp.where(fresh, own_n[kv], zero))
+            mate = jnp.where(old, mate_c[kv, 0], jnp.where(fresh, mate_n[kv], zero))
+            out_ref[slot, kv, :, :features] = jnp.where(first, mine, mate)
+            out_ref[slot, kv, :, features:] = jnp.where(first, mate, mine)
 
 
 def relay(meta, kv_cache, new_kv, mate_cache, mate_new, seq_count):
     features = kv_cache.shape[3]
     new_blocks = new_kv.shape[1] // BLK
     rank_count = 2 * seq_count
-
-    def block_of(d, m):
-        return (2 * d + m[2] - m[1] + rank_count) % rank_count
-
-    cache_spec = pl.BlockSpec(
-        (2, 1, BLK, features),
-        lambda d, m: (0, 0, jnp.clip(block_of(d, m), 0, m[0] - 1), 0),
-    )
-    new_spec = pl.BlockSpec(
-        (2, BLK, features),
-        lambda d, m: (0, jnp.clip(block_of(d, m) - m[0], 0, new_blocks - 1), 0),
-    )
+    per_step = 2 if seq_count % 2 == 0 else 1
+
+    def block_of(d, slot, m):
+        return (2 * (d * per_step + slot) + m[2] - m[1] + rank_count) % rank_count
+
+    def cache_spec(slot):
+        return pl.BlockSpec(
+            (2, 1, BLK, features),
+            lambda d, m: (0, 0, jnp.clip(block_of(d, slot, m), 0, m[0] - 1), 0),
+        )
+
+    def new_spec(slot):
+        return pl.BlockSpec(
+            (2, BLK, features),
+            lambda d, m: (0, jnp.clip(block_of(d, slot, m) - m[0], 0, new_blocks - 1), 0),
+        )
+
+    in_specs = []
+    operands = []
+    for slot in range(per_step):
+        in_specs += [cache_spec(slot), new_spec(slot), cache_spec(slot), new_spec(slot)]
+        operands += [kv_cache, new_kv, mate_cache, mate_new]
     return pl.pallas_call(
         relay_kernel,
         out_shape=jax.ShapeDtypeStruct((seq_count, 2, BLK, 2 * features), jnp.bfloat16),
         grid_spec=pltpu.PrefetchScalarGridSpec(
             num_scalar_prefetch=1,
-            grid=(seq_count,),
-            in_specs=[cache_spec, new_spec, cache_spec, new_spec],
-            out_specs=pl.BlockSpec((1, 2, BLK, 2 * features), lambda d, m: (d, 0, 0, 0)),
+            grid=(seq_count // per_step,),
+            in_specs=in_specs,
+            out_specs=pl.BlockSpec(
+                (per_step, 2, BLK, 2 * features), lambda d, m: (d, 0, 0, 0)
+            ),
         ),
-    )(meta, kv_cache, new_kv, mate_cache, mate_new)
+    )(meta, *operands)
 
 
 def half_swap(features):
@@ -227,7 +244,7 @@
         @pl.when(step == index)
         def _():
             value = rotated() if part < 2 else plain.astype(jnp.bfloat16)
-            out_refs[index][...] = value
+            out_refs[0][index] = value
 
 
 def project(tokens, gain, weights, tables, parts):
@@ -235,10 +252,10 @@
     rows = tokens.shape[0]
     full = pl.BlockSpec((rows, features), lambda s: (0, 0))
     table = jnp.asarray(parts, jnp.int32)
-    out = jax.ShapeDtypeStruct((rows, features), jnp.bfloat16)
+    out = jax.ShapeDtypeStruct((len(parts), rows, features), jnp.bfloat16)
     return pl.pallas_call(
         functools.partial(projection_kernel, parts=parts),
-        out_shape=tuple(out for _ in parts),
+        out_shape=out,
         grid_spec=pltpu.PrefetchScalarGridSpec(
             num_scalar_prefetch=1,
             grid=(len(parts),),
@@ -249,7 +266,7 @@
                 pl.BlockSpec((rows, features), lambda s, t: (0, 0)),
                 pl.BlockSpec((rows, features), lambda s, t: (0, 0)),
             ],
-            out_specs=tuple(pl.BlockSpec((rows, features), lambda s, t: (0, 0)) for _ in parts),
+            out_specs=pl.BlockSpec((len(parts), rows, features), lambda s, t: (0, 0, 0)),
             scratch_shapes=[pltpu.VMEM((rows, width), jnp.bfloat16)],
         ),
     )(table, tokens, gain, weights, *tables)
@@ -281,20 +298,20 @@
     frequency = jnp.exp(
         jnp.arange(half_size, dtype=jnp.float32) * (-2.0 * math.log(10000.0) / HD)
     )
-    angles = positions.astype(jnp.float32)[:, None] * jnp.tile(frequency, features // half_size)
-    tables = (jnp.cos(angles), jnp.sin(angles))
+    angles = positions.astype(jnp.float32)[:, None] * frequency[None, :]
+    repeat = (1, features // half_size)
+    tables = (jnp.tile(jnp.cos(angles), repeat), jnp.tile(jnp.sin(angles), repeat))
     gain = norm_gain.astype(jnp.float32).reshape(1, model_width)
     core = lax.axis_index("core")
     swap_cores = [(0, 1), (1, 0)]
     mate_cache = lax.ppermute(kv_cache, "core", swap_cores)
-    new_keys, new_values = project(tokens, gain, weights, tables, (1, 2))
-    new_kv = jnp.stack([new_keys, new_values])
+    new_kv = project(tokens, gain, weights, tables, (1, 2))
     mate_new = lax.ppermute(new_kv, "core", swap_cores)
     relay_meta = jnp.stack(
         [group_len // BLK, group_start, core, jnp.int32(tok_count // BLK)]
     ).astype(jnp.int32)
     joined = relay(relay_meta, kv_cache, new_kv, mate_cache, mate_new, seq_count)
-    (queries,) = project(tokens, gain, weights, tables, (0,))
+    queries = project(tokens, gain, weights, tables, (0,))[0]
     joined, attn_kv = lax.optimization_barrier((joined, new_kv))
     received = lax.all_to_all(joined, "seq", 0, 0, tiled=True)
     decode_cache = received.transpose(1, 0, 2, 3).reshape(2, 1, seq_count, 1, BLK, 2 * features)

time: 147 us -> 141 us (0.959)
  other arithmetic: 18.4 us -> 13 us
  local copies, waits for them, and re-layouts: 10.6 us -> 13.9 us
  Pallas kernels: 63.9 us -> 60.9 us
    sin x1, other arithmetic: 3.88 us -> 0.42 us  [local(): jnp.sin(angles)]
    pallas_call x1, Pallas kernels: 11.9 us -> 8.86 us  [relay(): pl.pallas_call(relay_kernel, out_shape=jax.ShapeDtypeStruct((seq_count, 2...]
    another operation x1 -> x4, local copies, waits for them, and re-layouts: 0.01 us -> 2.54 us  [the longest x2 1.31 us: local(): jnp.tile(jnp.sin(angles), repeat)]
    unnamed x7 -> x9, local copies, waits for them, and re-layouts: 7.8 us -> 8.68 us
  transfers between devices with their start and end apart: 7 -> 7, of which waited for: 4 -> 4; matrix products, arithmetic and copies ran while one was open for 16% -> 15% of each run, Pallas kernels for 36% -> 37%
where the time goes in v9:
time: 141 us
  Pallas kernels  60.9 us (43%)
  waiting for transfers between devices  32 us (23%)
  starting transfers between devices  14.8 us (10%)
  local copies, waits for them, and re-layouts  13.9 us (10%)
  other arithmetic  13 us (9%)
  between operations  3.67 us (3%)
  matrix products  2.79 us (2%)
    pallas_call x1, Pallas kernels, attend(): pl.pallas_call(attention_kernel, out_shape=jax.ShapeDtypeStruct(queries.s...  34.9 us
    pallas_call x2, Pallas kernels, project(): pl.pallas_call(functools.partial(projection_kernel, parts=parts), out_sha...  17.1 us
    ppermute x3, waiting for transfers between devices, local(): summed = summed + lax.ppermute(chunk, 'x', pairs).astype(jnp.float32)  16.4 us
    all_to_all x1, waiting for transfers between devices, local(): received = lax.all_to_all(joined, 'seq', 0, 0, tiled=True)  11.8 us
    pallas_call x1, Pallas kernels, relay(): pl.pallas_call(relay_kernel, out_shape=jax.ShapeDtypeStruct((seq_count, 2...  8.86 us
    all_to_all x1, starting transfers between devices, local(): received = lax.all_to_all(joined, 'seq', 0, 0, tiled=True)  8.7 us
    unnamed x9, local copies, waits for them, and re-layouts  8.68 us
    ppermute x3, starting transfers between devices, local(): summed = summed + lax.ppermute(chunk, 'x', pairs).astype(jnp.float32)  5.66 us
  transfers between devices with their start and end apart: 7, of which 4 were waited for; matrix products, arithmetic and copies ran while one was open for 15% of the time, Pallas kernels for 37%

profile of v9, /device:TPU:0, one launch (start us, length us, event | category | flops | bytes accessed | tf_op | source)
XLA Modules:
  0.0 141.1 jit_solution(5872484863627425451)
XLA Ops:
  0.6 0.0 copy-start
  0.6 0.0 copy-start.3
  0.7 0.1 collective-permute-start
  0.8 0.8 pad_add_fusion
  1.6 0.1 constant_dynamic-slice_fusion
  1.7 0.6 fusion.14
  2.9 1.3 fusion.10
  4.2 0.4 multiply_sine_fusion
  4.6 0.1 tile.8
  4.7 1.1 copy.13.cos_ref
  5.9 0.1 tile.20
  6.0 1.2 copy.14.sin_ref
  7.2 0.0 copy-done.3
  7.2 0.6 reshape.124
  7.8 10.6 %shard_map.114.refs_1_.refs_5_.kn_ref.vn_ref = bf16[2,512,384]{2,1,0:T(8,128)(2,1)} custom-call(s32[2]{0:T(128)} %constant.110.clone.part_ref, bf16[512,3072]{1,0:T(8,128)(2,1)} %x_ref.3, f32[1,3072]{1,0:T(1,128)} %bitcast.50, bf16[3,3072,384]{2,1,0:T(8,128)(2,1)} %bitcast.43, f32[512,384]{1,0:T(8,128)} %copy.13.cos_ref, f32[512,384]{1,0:T(8,128)} %copy.14.sin_ref), custom_call_target="tpu_custom_call" | custom-call | tf_op jit(solution)/shard_map/pallas_call | solution.py:256
  18.4 0.3 collective-permute-start.1
  21.1 1.3 pad_add_fusion.2.meta_ref
  22.3 0.0 collective-permute-done.1.refs_3_.refs_7_
  22.3 0.0 copy-start.2
  22.4 0.0 collective-permute-done.refs_2_.refs_6_
  22.4 0.9 copy-done.2
  23.2 8.9 %shard_map.115 = bf16[16,2,128,768]{3,2,1,0:T(8,128)(2,1)} custom-call(s32[4]{0:T(128)} %pad_add_fusion.2.meta_ref, bf16[2,1,3584,384]{3,2,1,0:T(8,128)(2,1)} %vc_ref.1, bf16[2,512,384]{2,1,0:T(8,128)(2,1)} %shard_map.114.refs_1_.refs_5_.kn_ref.vn_ref, bf16[2,1,3584,384]{3,2,1,0:T(8,128)(2,1)} %collective-permute-done.refs_2_.refs_6_, ...), custom_call_target="tpu_custom_call" | custom-call | tf_op jit(solution)/shard_map/pallas_call | solution.py:193
  32.1 8.7 %all-to-all-start = ((bf16[16,2,128,768]{3,2,1,0:T(8,128)(2,1)}), bf16[16,2,128,768]{3,2,1,0:T(8,128)(2,1)}, u32[]{:S(2)}, u32[]{:S(2)}) async-start(bf16[16,2,128,768]{3,2,1,0:T(8,128)(2,1)} %shard_map.115), calls=%async_computation | async-start | bytes 12582912 | tf_op jit(solution)/shard_map/all_to_all | solution.py:316
  40.8 6.5 %shard_map.113 = bf16[1,512,384]{2,1,0:T(8,128)(2,1)} custom-call(s32[1]{0:T(128)} %constant.111.clone.part_ref, bf16[512,3072]{1,0:T(8,128)(2,1)} %x_ref.3, f32[1,3072]{1,0:T(1,128)} %bitcast.51, bf16[3,3072,384]{2,1,0:T(8,128)(2,1)} %bitcast.44, f32[512,384]{1,0:T(8,128)} %copy.13.cos_ref, f32[512,384]{1,0:T(8,128)} %copy.14.sin_ref), custom_call_target="tpu_custom_call" | custom-call | tf_op jit(solution)/shard_map/pallas_call | solution.py:256
  47.3 1.9 %pad_add_fusion.1.meta_ref = s32[2]{0:T(128)} fusion(s32[1]{0:T(128)} %bitcast.4, s32[1]{0:T(128)} %bitcast.3), kind=kLoop, calls=%fused_computation.33 | loop fusion | flops 2 | bytes 16 | tf_op jit(solution)/shard_map/stack | solution.py:319
  49.2 34.9 %shard_map.116 = bf16[512,384]{1,0:T(8,128)(2,1)} custom-call(s32[2]{0:T(128)} %pad_add_fusion.1.meta_ref, bf16[512,384]{1,0:T(8,128)(2,1)} %bitcast.49, bf16[2,1,3584,384]{3,2,1,0:T(8,128)(2,1)} %vc_ref.1, bf16[2,1,3584,384]{3,2,1,0:T(8,128)(2,1)} %vc_ref.1, bf16[2,512,384]{2,1,0:T(8,128)(2,1)} %shard_map.114.refs_1_.refs_5_.kn_ref.vn_ref, ...), custom_call_target="tpu_custom_call" | custom-call | tf_op jit(solution)/shard_map/pallas_call | solution.py:124
  84.1 0.0 copy-done
  84.1 2.8 %convolution_convert_fusion = bf16[512,3072]{1,0:T(8,128)(2,1)S(1)} fusion(bf16[512,384]{1,0:T(8,128)(2,1)} %shard_map.116, bf16[384,3072]{1,0:T(8,128)(2,1)S(1)} %copy-done), kind=kOutput, calls=%fused_computation | convolution fusion | flops 1209532416 | bytes 5898240 | tf_op jit(solution)/shard_map/dot_general | solution.py:322
  86.9 0.0 copy-start.1
  86.9 1.6 %copy-done.1 = bf16[512,3072]{1,0:T(8,128)(2,1)} copy-done((bf16[512,3072]{1,0:T(8,128)(2,1)}, bf16[512,3072]{1,0:T(8,128)(2,1)S(1)}, u32[]{:S(2)}) %copy-start.1) | copy-done | bytes 3145752
  88.5 1.3 dynamic-slice_bitcast_fusion
  89.8 0.0 collective-permute-start.2
  89.8 3.7 %collective-permute-done.2 = bf16[4,64,3072]{2,1,0:T(8,128)(2,1)} collective-permute-done((bf16[4,64,3072]{2,1,0:T(8,128)(2,1)}, bf16[4,64,3072]{2,1,0:T(8,128)(2,1)}, u32[]{:S(2)}, u32[]{:S(2)}) %collective-permute-start.2) | collective-permute-done | bytes 1572896 | tf_op jit(solution)/shard_map/ppermute | solution.py:328
  93.5 4.3 %fusion.13 = (bf16[4,64,3072]{2,1,0:T(8,128)(2,1)S(1)}, f32[4,64,3072]{2,1,0:T(8,128)}) fusion(bf16[4,64,3072]{2,1,0:T(8,128)(2,1)} %collective-permute-done.2, bf16[4,2,64,3072]{3,2,1,0:T(8,128)(2,1)} %bitcast.48, s32[]{:T(128)S(6)} %select_n.69), kind=kLoop, calls=%fused_computation.36 | loop fusion | flops 3145728 | bytes 7864324 | tf_op jit(solution)/shard_map/convert_element_type | solution.py:331
  97.8 0.8 dynamic-slice_bitcast_fusion.3
  98.6 1.5 %collective-permute-start.3 = (bf16[64,3072]{1,0:T(8,128)(2,1)}, bf16[64,3072]{1,0:T(8,128)(2,1)S(1)}, u32[]{:S(2)}, u32[]{:S(2)}) collective-permute-start(bf16[64,3072]{1,0:T(8,128)(2,1)} %get-tuple-element.12), channel_id=1, source_target_pairs={{0,2},{2,4},{4,6},{6,0},{1,3},{3,5},{5,7},{7,1},{8,10},{10,12},{12... | collective-permute-start | bytes 1179656 | tf_op jit(solution)/shard_map/ppermute | solution.py:337
  100.1 2.7 %collective-permute-start.4 = (bf16[64,3072]{1,0:T(8,128)(2,1)S(1)}, bf16[64,3072]{1,0:T(8,128)(2,1)}, u32[]{:S(2)}, u32[]{:S(2)}) collective-permute-start(bf16[64,3072]{1,0:T(8,128)(2,1)S(1)} %get-tuple-element.14), channel_id=1, source_target_pairs={{0,4},{2,6},{4,0},{6,2},{1,5},{3,7},{5,1},{7,3},{8,12},{10,14},{12... | collective-permute-start | bytes 1179656 | tf_op jit(solution)/shard_map/ppermute | solution.py:337
  102.9 1.4 %collective-permute-start.5 = (bf16[64,3072]{1,0:T(8,128)(2,1)S(1)}, bf16[64,3072]{1,0:T(8,128)(2,1)}, u32[]{:S(2)}, u32[]{:S(2)}) collective-permute-start(bf16[64,3072]{1,0:T(8,128)(2,1)S(1)} %get-tuple-element.13), channel_id=1, source_target_pairs={{0,6},{2,0},{4,2},{6,4},{1,7},{3,1},{5,3},{7,5},{8,14},{10,8},{12,... | collective-permute-start | bytes 1179656 | tf_op jit(solution)/shard_map/ppermute | solution.py:337
  104.3 6.9 %collective-permute-done.3 = bf16[64,3072]{1,0:T(8,128)(2,1)S(1)} collective-permute-done((bf16[64,3072]{1,0:T(8,128)(2,1)}, bf16[64,3072]{1,0:T(8,128)(2,1)S(1)}, u32[]{:S(2)}, u32[]{:S(2)}) %collective-permute-start.3) | collective-permute-done | bytes 393248 | tf_op jit(solution)/shard_map/ppermute | solution.py:337
  111.2 9.5 %collective-permute-done.4 = bf16[64,3072]{1,0:T(8,128)(2,1)} collective-permute-done((bf16[64,3072]{1,0:T(8,128)(2,1)S(1)}, bf16[64,3072]{1,0:T(8,128)(2,1)}, u32[]{:S(2)}, u32[]{:S(2)}) %collective-permute-start.4) | collective-permute-done | bytes 393248 | tf_op jit(solution)/shard_map/ppermute | solution.py:337
  120.7 0.0 collective-permute-done.5
  120.7 2.4 %fusion.3 = bf16[64,3072]{1,0:T(8,128)(2,1)} fusion(bf16[64,3072]{1,0:T(8,128)(2,1)} %collective-permute-done.5, bf16[64,3072]{1,0:T(8,128)(2,1)} %collective-permute-done.4, bf16[64,3072]{1,0:T(8,128)(2,1)S(1)} %collective-permute-done.3, f32[4,64,3072]{2,1,0:T(8,128)} %get-tuple-element.11, s32[]{:T(128)S(6)} %select_n.71, bf16[512,3072]{1,0:T(8,128)(2,1)} %x_ref.3, ...), kind=kLoop, calls=%fused_computation.7 | loop fusion | flops 1769472 | bytes 2752520 | tf_op jit(solution)/shard_map/convert_element_type | solution.py:339
  123.2 11.8 %all-to-all-done = bf16[16,2,128,768]{3,2,1,0:T(8,128)(2,1)} async-done(((bf16[16,2,128,768]{3,2,1,0:T(8,128)(2,1)}), bf16[16,2,128,768]{3,2,1,0:T(8,128)(2,1)}, u32[]{:S(2)}, u32[]{:S(2)}) %all-to-all-start) | async-done | bytes 6291488 | tf_op jit(solution)/shard_map/all_to_all | solution.py:316
  135.0 6.1 %copy.17 = bf16[2,1,16,1,128,768]{5,4,3,2,1,0:T(8,128)(2,1)} copy(bf16[2,1,16,1,128,768]{5,4,0,2,3,1:T(8,128)(2,1)} %bitcast.23) | data formatting | bytes 12582912
  (1 shorter events, 0.0 us)
Async XLA Ops:
  0.6 83.4 %copy-start = (bf16[384,3072]{1,0:T(8,128)(2,1)S(1)}, bf16[384,3072]{1,0:T(8,128)(2,1)}, u32[]{:S(2)}) copy-start(bf16[384,3072]{1,0:T(8,128)(2,1)} %param.13) | copy-start | bytes 7077892
  0.6 6.6 %copy-start.3 = (bf16[3072]{0:T(1024)(128)(2,1)S(1)}, bf16[3072]{0:T(1024)(128)(2,1)}, u32[]{:S(2)}) copy-start(bf16[3072]{0:T(1024)(128)(2,1)} %param.11) | copy-start | bytes 18436
  0.7 21.7 %collective-permute-start = (bf16[2,1,3584,384]{3,2,1,0:T(8,128)(2,1)}, bf16[2,1,3584,384]{3,2,1,0:T(8,128)(2,1)}, u32[]{:S(2)}, u32[]{:S(2)}) collective-permute-start(bf16[2,1,3584,384]{3,2,1,0:T(8,128)(2,1)} %vc_ref.1), channel_id=1, source_target_pairs={{0,1},{1,0},{2,3},{3,2},{4,5},{5,4},{6,7},{7,6},{8,9},{9,8},{10,11... | collective-permute-start | bytes 16515080 | tf_op jit(solution)/shard_map/ppermute | solution.py:307
  18.4 3.9 %collective-permute-start.1 = (bf16[2,512,384]{2,1,0:T(8,128)(2,1)}, bf16[2,512,384]{2,1,0:T(8,128)(2,1)S(1)}, u32[]{:S(2)}, u32[]{:S(2)}) collective-permute-start(bf16[2,512,384]{2,1,0:T(8,128)(2,1)} %shard_map.114.refs_1_.refs_5_.kn_ref.vn_ref), channel_id=1, source_target_pairs={{0,1},{1,0},{2,3},{3,2},{4,5},{5,4},{6,7},{7,6},{8,9},{9,8},{10,11... | collective-permute-start | bytes 2359304 | tf_op jit(solution)/shard_map/ppermute | solution.py:309
  22.3 0.9 copy-start.2
  32.1 102.9 %all-to-all-start = ((bf16[16,2,128,768]{3,2,1,0:T(8,128)(2,1)}), bf16[16,2,128,768]{3,2,1,0:T(8,128)(2,1)}, u32[]{:S(2)}, u32[]{:S(2)}) async-start(bf16[16,2,128,768]{3,2,1,0:T(8,128)(2,1)} %shard_map.115), calls=%async_computation | async-start | bytes 12582912 | tf_op jit(solution)/shard_map/all_to_all | solution.py:316
  86.9 1.6 %copy-start.1 = (bf16[512,3072]{1,0:T(8,128)(2,1)}, bf16[512,3072]{1,0:T(8,128)(2,1)S(1)}, u32[]{:S(2)}) copy-start(bf16[512,3072]{1,0:T(8,128)(2,1)S(1)} %convolution_convert_fusion) | copy-start | bytes 9437188
  89.8 3.8 %collective-permute-start.2 = (bf16[4,64,3072]{2,1,0:T(8,128)(2,1)}, bf16[4,64,3072]{2,1,0:T(8,128)(2,1)}, u32[]{:S(2)}, u32[]{:S(2)}) collective-permute-start(bf16[4,64,3072]{2,1,0:T(8,128)(2,1)} %dynamic-slice_bitcast_fusion), channel_id=1, source_target_pairs={{0,1},{1,0},{2,3},{3,2},{4,5},{5,4},{6,7},{7,6},{8,9},{9,8},{10,11... | collective-permute-start | bytes 4718600 | tf_op jit(solution)/shard_map/ppermute | solution.py:328
  98.6 12.6 %collective-permute-start.3 = (bf16[64,3072]{1,0:T(8,128)(2,1)}, bf16[64,3072]{1,0:T(8,128)(2,1)S(1)}, u32[]{:S(2)}, u32[]{:S(2)}) collective-permute-start(bf16[64,3072]{1,0:T(8,128)(2,1)} %get-tuple-element.12), channel_id=1, source_target_pairs={{0,2},{2,4},{4,6},{6,0},{1,3},{3,5},{5,7},{7,1},{8,10},{10,12},{12... | collective-permute-start | bytes 1179656 | tf_op jit(solution)/shard_map/ppermute | solution.py:337
  100.1 20.6 %collective-permute-start.4 = (bf16[64,3072]{1,0:T(8,128)(2,1)S(1)}, bf16[64,3072]{1,0:T(8,128)(2,1)}, u32[]{:S(2)}, u32[]{:S(2)}) collective-permute-start(bf16[64,3072]{1,0:T(8,128)(2,1)S(1)} %get-tuple-element.14), channel_id=1, source_target_pairs={{0,4},{2,6},{4,0},{6,2},{1,5},{3,7},{5,1},{7,3},{8,12},{10,14},{12... | collective-permute-start | bytes 1179656 | tf_op jit(solution)/shard_map/ppermute | solution.py:337
  102.9 17.9 %collective-permute-start.5 = (bf16[64,3072]{1,0:T(8,128)(2,1)S(1)}, bf16[64,3072]{1,0:T(8,128)(2,1)}, u32[]{:S(2)}, u32[]{:S(2)}) collective-permute-start(bf16[64,3072]{1,0:T(8,128)(2,1)S(1)} %get-tuple-element.13), channel_id=1, source_target_pairs={{0,6},{2,0},{4,2},{6,4},{1,7},{3,1},{5,3},{7,5},{8,14},{10,8},{12,... | collective-permute-start | bytes 1179656 | tf_op jit(solution)/shard_map/ppermute | solution.py:337

commit v10 on v9

--- a/solution.py
+++ b/solution.py
@@ -139,13 +139,12 @@
     )(meta, queries, kv_cache, kv_cache, new_kv, new_kv)
 
 
-def relay_kernel(meta_ref, *refs):
+def relay_kernel(meta_ref, *refs, new_blocks):
     out_ref = refs[-1]
     sources = refs[:-1]
-    len_blocks = meta_ref[0]
-    group_start = meta_ref[1]
-    core = meta_ref[2]
-    new_blocks = meta_ref[3]
+    len_blocks = meta_ref[0] // BLK
+    group_start = meta_ref[2]
+    core = meta_ref[3]
     per_step = out_ref.shape[0]
     rank_count = 2 * pl.num_programs(0) * per_step
     features = sources[1].shape[2]
@@ -171,18 +170,22 @@
     per_step = 2 if seq_count % 2 == 0 else 1
 
     def block_of(d, slot, m):
-        return (2 * (d * per_step + slot) + m[2] - m[1] + rank_count) % rank_count
+        return (2 * (d * per_step + slot) + m[3] - m[2] + rank_count) % rank_count
 
     def cache_spec(slot):
         return pl.BlockSpec(
             (2, 1, BLK, features),
-            lambda d, m: (0, 0, jnp.clip(block_of(d, slot, m), 0, m[0] - 1), 0),
+            lambda d, m: (0, 0, jnp.clip(block_of(d, slot, m), 0, m[0] // BLK - 1), 0),
         )
 
     def new_spec(slot):
         return pl.BlockSpec(
             (2, BLK, features),
-            lambda d, m: (0, jnp.clip(block_of(d, slot, m) - m[0], 0, new_blocks - 1), 0),
+            lambda d, m: (
+                0,
+                jnp.clip(block_of(d, slot, m) - m[0] // BLK, 0, new_blocks - 1),
+                0,
+            ),
         )
 
     in_specs = []
@@ -191,7 +194,7 @@
         in_specs += [cache_spec(slot), new_spec(slot), cache_spec(slot), new_spec(slot)]
         operands += [kv_cache, new_kv, mate_cache, mate_new]
     return pl.pallas_call(
-        relay_kernel,
+        functools.partial(relay_kernel, new_blocks=new_blocks),
         out_shape=jax.ShapeDtypeStruct((seq_count, 2, BLK, 2 * features), jnp.bfloat16),
         grid_spec=pltpu.PrefetchScalarGridSpec(
             num_scalar_prefetch=1,
@@ -216,7 +219,7 @@
     ).astype(jnp.bfloat16)
 
 
-def projection_kernel(part_ref, x_ref, gain_ref, w_ref, cos_ref, sin_ref, *refs, parts):
+def projection_kernel(part_ref, meta_ref, x_ref, gain_ref, w_ref, freq_ref, *refs, parts):
     out_refs = refs[:-1]
     normed_ref = refs[-1]
     step = pl.program_id(0)
@@ -231,13 +234,21 @@
     plain = jnp.dot(normed_ref[...], weights, preferred_element_type=jnp.float32)
 
     def rotated():
-        features = plain.shape[1]
+        rows, features = plain.shape
         half = HD // 2
+        group_len = meta_ref[0]
+        group_requests = meta_ref[1]
+        row = lax.broadcasted_iota(jnp.int32, (rows, 1), 0)
+        request = request_of(row, group_requests, rows)
+        count = (jnp.zeros((rows, 1), jnp.int32) + group_requests).astype(jnp.float32)
+        first = jnp.ceil((request * rows).astype(jnp.float32) / count).astype(jnp.int32)
+        positions = (group_len + row - first).astype(jnp.float32)
+        angles = positions * freq_ref[...]
         lane = lax.broadcasted_iota(jnp.int32, plain.shape, 1)
         ahead = pltpu.roll(plain, features - half, 1)
         behind = pltpu.roll(plain, half, 1)
         paired = jnp.where(lane % HD < half, -ahead, behind)
-        return (plain * cos_ref[...] + paired * sin_ref[...]).astype(jnp.bfloat16)
+        return (plain * jnp.cos(angles) + paired * jnp.sin(angles)).astype(jnp.bfloat16)
 
     for index, part in enumerate(parts):
 
@@ -247,29 +258,27 @@
             out_refs[0][index] = value
 
 
-def project(tokens, gain, weights, tables, parts):
+def project(meta, tokens, gain, weights, frequency, parts):
     _, width, features = weights.shape
     rows = tokens.shape[0]
-    full = pl.BlockSpec((rows, features), lambda s: (0, 0))
     table = jnp.asarray(parts, jnp.int32)
     out = jax.ShapeDtypeStruct((len(parts), rows, features), jnp.bfloat16)
     return pl.pallas_call(
         functools.partial(projection_kernel, parts=parts),
         out_shape=out,
         grid_spec=pltpu.PrefetchScalarGridSpec(
-            num_scalar_prefetch=1,
+            num_scalar_prefetch=2,
             grid=(len(parts),),
             in_specs=[
-                pl.BlockSpec((rows, width), lambda s, t: (0, 0)),
-                pl.BlockSpec((1, width), lambda s, t: (0, 0)),
-                pl.BlockSpec((1, width, features), lambda s, t: (t[s], 0, 0)),
-                pl.BlockSpec((rows, features), lambda s, t: (0, 0)),
-                pl.BlockSpec((rows, features), lambda s, t: (0, 0)),
+                pl.BlockSpec((rows, width), lambda s, t, m: (0, 0)),
+                pl.BlockSpec((1, width), lambda s, t, m: (0, 0)),
+                pl.BlockSpec((1, width, features), lambda s, t, m: (t[s], 0, 0)),
+                pl.BlockSpec((1, features), lambda s, t, m: (0, 0)),
             ],
-            out_specs=pl.BlockSpec((len(parts), rows, features), lambda s, t: (0, 0, 0)),
+            out_specs=pl.BlockSpec((len(parts), rows, features), lambda s, t, m: (0, 0, 0)),
             scratch_shapes=[pltpu.VMEM((rows, width), jnp.bfloat16)],
         ),
-    )(table, tokens, gain, weights, *tables)
+    )(table, meta, tokens, gain, weights, frequency)
 
 
 def local(tokens, norm_gain, w_qkv, w_out, kv_cache, cached_lengths, requests, block_start):
@@ -290,34 +299,25 @@
     inputs = tokens.astype(jnp.float32)
 
     weights = jnp.transpose(w_qkv, (1, 0, 2))
-    row_index = jnp.arange(tok_count, dtype=jnp.int32)
-    request = row_index * group_requests // tok_count
-    first_row = (request * tok_count + group_requests - 1) // group_requests
-    positions = group_len + row_index - first_row
     half_size = HD // 2
     frequency = jnp.exp(
         jnp.arange(half_size, dtype=jnp.float32) * (-2.0 * math.log(10000.0) / HD)
     )
-    angles = positions.astype(jnp.float32)[:, None] * frequency[None, :]
-    repeat = (1, features // half_size)
-    tables = (jnp.tile(jnp.cos(angles), repeat), jnp.tile(jnp.sin(angles), repeat))
+    frequency = jnp.tile(frequency, features // half_size).reshape(1, features)
     gain = norm_gain.astype(jnp.float32).reshape(1, model_width)
     core = lax.axis_index("core")
     swap_cores = [(0, 1), (1, 0)]
     mate_cache = lax.ppermute(kv_cache, "core", swap_cores)
-    new_kv = project(tokens, gain, weights, tables, (1, 2))
+    meta = jnp.concatenate([group_params, jnp.reshape(core, (1,))]).astype(jnp.int32)
+    new_kv = project(meta, tokens, gain, weights, frequency, (1, 2))
     mate_new = lax.ppermute(new_kv, "core", swap_cores)
-    relay_meta = jnp.stack(
-        [group_len // BLK, group_start, core, jnp.int32(tok_count // BLK)]
-    ).astype(jnp.int32)
-    joined = relay(relay_meta, kv_cache, new_kv, mate_cache, mate_new, seq_count)
-    queries = project(tokens, gain, weights, tables, (0,))[0]
+    joined = relay(meta, kv_cache, new_kv, mate_cache, mate_new, seq_count)
+    queries = project(meta, tokens, gain, weights, frequency, (0,))[0]
     joined, attn_kv = lax.optimization_barrier((joined, new_kv))
     received = lax.all_to_all(joined, "seq", 0, 0, tiled=True)
     decode_cache = received.transpose(1, 0, 2, 3).reshape(2, 1, seq_count, 1, BLK, 2 * features)
 
-    attn_meta = jnp.stack([group_len, group_requests]).astype(jnp.int32)
-    attended = attend(attn_meta, queries, kv_cache, attn_kv)
+    attended = attend(meta, queries, kv_cache, attn_kv)
     rows_dev = tok_count // tp_count
     partial = jnp.dot(attended, w_out, preferred_element_type=jnp.float32).astype(jnp.bfloat16)
     x_count = tp_count // 2

time: 141 us -> 139 us (0.986)
  Pallas kernels: 60.9 us -> 66.9 us
  other arithmetic: 13 us -> 9.46 us
  between operations: 3.67 us -> 0.69 us
  local copies, waits for them, and re-layouts: 13.9 us -> 11.6 us
    pallas_call x2, Pallas kernels: 17.1 us -> 22.5 us  [project(): pl.pallas_call(functools.partial(projection_kernel, parts=parts), out_sha...]
    another operation x2 -> x0, other arithmetic: 3.12 us -> none  [the longest x1 1.86 us: local(): attn_meta = jnp.stack([group_len, group_requests]).astype(jnp.int32)]
    ppermute x1, waiting for transfers between devices: 0.01 us -> 2.15 us  [local(): mate_new = lax.ppermute(new_kv, 'core', swap_cores)]
    another operation x4 -> x2, local copies, waits for them, and re-layouts: 2.54 us -> 0.68 us  [local(): frequency = jnp.tile(frequency, features // half_size).reshape(1, features)]
    all_to_all x1, waiting for transfers between devices: 11.8 us -> 10 us  [local(): received = lax.all_to_all(joined, 'seq', 0, 0, tiled=True)]
    unnamed x9 -> x7, local copies, waits for them, and re-layouts: 8.68 us -> 8.68 us
  transfers between devices with their start and end apart: 7 -> 7, of which waited for: 4 -> 5; matrix products, arithmetic and copies ran while one was open for 15% -> 11% of each run, Pallas kernels for 37% -> 42%
where the time goes in v10:
time: 139 us
  Pallas kernels  66.9 us (48%)
  waiting for transfers between devices  32.3 us (23%)
  starting transfers between devices  14.7 us (11%)
  local copies, waits for them, and re-layouts  11.6 us (8%)
  other arithmetic  9.46 us (7%)
  matrix products  2.79 us (2%)
    pallas_call x1, Pallas kernels, attend(): pl.pallas_call(attention_kernel, out_shape=jax.ShapeDtypeStruct(queries.s...  35.1 us
    pallas_call x2, Pallas kernels, project(): pl.pallas_call(functools.partial(projection_kernel, parts=parts), out_sha...  22.5 us
    ppermute x3, waiting for transfers between devices, local(): summed = summed + lax.ppermute(chunk, 'x', pairs).astype(jnp.float32)  16.4 us
    all_to_all x1, waiting for transfers between devices, local(): received = lax.all_to_all(joined, 'seq', 0, 0, tiled=True)  10 us
    pallas_call x1, Pallas kernels, relay(): pl.pallas_call(functools.partial(relay_kernel, new_blocks=new_blocks), ou...  9.23 us
    unnamed x7, local copies, waits for them, and re-layouts  8.68 us
    all_to_all x1, starting transfers between devices, local(): received = lax.all_to_all(joined, 'seq', 0, 0, tiled=True)  8.65 us
    ppermute x3, starting transfers between devices, local(): summed = summed + lax.ppermute(chunk, 'x', pairs).astype(jnp.float32)  5.65 us
  transfers between devices with their start and end apart: 7, of which 5 were waited for; matrix products, arithmetic and copies ran while one was open for 11% of the time, Pallas kernels for 42%

profile of v10, /device:TPU:0, one launch (start us, length us, event | category | flops | bytes accessed | tf_op | source)
XLA Modules:
  0.0 138.5 jit_solution(18193669980938794975)
XLA Ops:
  0.6 0.0 copy-start
  0.6 0.1 collective-permute-start
  0.7 1.4 %reshape.30 = f32[3072]{0:T(1024)} convert(bf16[3072]{0:T(1024)(128)(2,1)} %param.11) | non-fusion elementwise | flops 3072 | bytes 18432 | tf_op jit(solution)/shard_map/reshape | solution.py:307
  2.2 0.7 reshape_tile.5.freq_ref
  2.9 0.7 pad_add_fusion
  3.6 0.2 dynamic-slice_reduce_fusion
  3.8 0.6 pad_add_fusion.1.meta_ref
  4.3 13.1 %shard_map.114.refs_1_.refs_5_.kn_ref.vn_ref = bf16[2,512,384]{2,1,0:T(8,128)(2,1)} custom-call(s32[2]{0:T(128)} %constant.74.clone.part_ref, s32[4]{0:T(128)} %pad_add_fusion.1.meta_ref, bf16[512,3072]{1,0:T(8,128)(2,1)} %x_ref.3, f32[1,3072]{1,0:T(1,128)} %bitcast.40, bf16[3,3072,384]{2,1,0:T(8,128)(2,1)} %bitcast.35, f32[1,384]{1,0:T(1,128)} %reshape_tile.5.freq_ref), custom_call_target="tpu_custom_call" | custom-call | tf_op jit(solution)/shard_map/pallas_call | solution.py:266
  17.4 0.3 collective-permute-start.1
  17.8 2.2 %collective-permute-done.1.refs_3_.refs_7_ = bf16[2,512,384]{2,1,0:T(8,128)(2,1)S(1)} collective-permute-done((bf16[2,512,384]{2,1,0:T(8,128)(2,1)}, bf16[2,512,384]{2,1,0:T(8,128)(2,1)S(1)}, u32[]{:S(2)}, u32[]{:S(2)}) %collective-permute-start.1) | collective-permute-done | bytes 786464 | tf_op jit(solution)/shard_map/ppermute | solution.py:313
  19.9 0.0 copy-start.2
  19.9 0.0 collective-permute-done.refs_2_.refs_6_
  19.9 0.9 copy-done.2
  20.8 9.2 %shard_map.115 = bf16[16,2,128,768]{3,2,1,0:T(8,128)(2,1)} custom-call(s32[4]{0:T(128)} %pad_add_fusion.1.meta_ref, bf16[2,1,3584,384]{3,2,1,0:T(8,128)(2,1)} %vc_ref.1, bf16[2,512,384]{2,1,0:T(8,128)(2,1)} %shard_map.114.refs_1_.refs_5_.kn_ref.vn_ref, bf16[2,1,3584,384]{3,2,1,0:T(8,128)(2,1)} %collective-permute-done.refs_2_.refs_6_, ...), custom_call_target="tpu_custom_call" | custom-call | tf_op jit(solution)/shard_map/pallas_call | solution.py:196
  30.0 8.6 %all-to-all-start = ((bf16[16,2,128,768]{3,2,1,0:T(8,128)(2,1)}), bf16[16,2,128,768]{3,2,1,0:T(8,128)(2,1)}, u32[]{:S(2)}, u32[]{:S(2)}) async-start(bf16[16,2,128,768]{3,2,1,0:T(8,128)(2,1)} %shard_map.115), calls=%async_computation | async-start | bytes 12582912 | tf_op jit(solution)/shard_map/all_to_all | solution.py:317
  38.7 9.5 %shard_map.113 = bf16[1,512,384]{2,1,0:T(8,128)(2,1)} custom-call(s32[1]{0:T(128)} %constant.75.clone.part_ref, s32[4]{0:T(128)} %pad_add_fusion.1.meta_ref, bf16[512,3072]{1,0:T(8,128)(2,1)} %x_ref.3, f32[1,3072]{1,0:T(1,128)} %bitcast.41, bf16[3,3072,384]{2,1,0:T(8,128)(2,1)} %bitcast.36, f32[1,384]{1,0:T(1,128)} %reshape_tile.5.freq_ref), custom_call_target="tpu_custom_call" | custom-call | tf_op jit(solution)/shard_map/pallas_call | solution.py:266
  48.1 35.1 %shard_map.116 = bf16[512,384]{1,0:T(8,128)(2,1)} custom-call(s32[4]{0:T(128)} %pad_add_fusion.1.meta_ref, bf16[512,384]{1,0:T(8,128)(2,1)} %bitcast.39, bf16[2,1,3584,384]{3,2,1,0:T(8,128)(2,1)} %vc_ref.1, bf16[2,1,3584,384]{3,2,1,0:T(8,128)(2,1)} %vc_ref.1, bf16[2,512,384]{2,1,0:T(8,128)(2,1)} %shard_map.114.refs_1_.refs_5_.kn_ref.vn_ref, ...), custom_call_target="tpu_custom_call" | custom-call | tf_op jit(solution)/shard_map/pallas_call | solution.py:124
  83.3 0.0 copy-done
  83.3 2.8 %convolution_convert_fusion = bf16[512,3072]{1,0:T(8,128)(2,1)S(1)} fusion(bf16[512,384]{1,0:T(8,128)(2,1)} %shard_map.116, bf16[384,3072]{1,0:T(8,128)(2,1)S(1)} %copy-done), kind=kOutput, calls=%fused_computation | convolution fusion | flops 1209532416 | bytes 5898240 | tf_op jit(solution)/shard_map/dot_general | solution.py:322
  86.1 0.0 copy-start.1
  86.1 1.6 %copy-done.1 = bf16[512,3072]{1,0:T(8,128)(2,1)} copy-done((bf16[512,3072]{1,0:T(8,128)(2,1)}, bf16[512,3072]{1,0:T(8,128)(2,1)S(1)}, u32[]{:S(2)}) %copy-start.1) | copy-done | bytes 3145752
  87.7 1.3 dynamic-slice_bitcast_fusion
  89.0 0.0 collective-permute-start.2
  89.0 3.7 %collective-permute-done.2 = bf16[4,64,3072]{2,1,0:T(8,128)(2,1)} collective-permute-done((bf16[4,64,3072]{2,1,0:T(8,128)(2,1)}, bf16[4,64,3072]{2,1,0:T(8,128)(2,1)}, u32[]{:S(2)}, u32[]{:S(2)}) %collective-permute-start.2) | collective-permute-done | bytes 1572896 | tf_op jit(solution)/shard_map/ppermute | solution.py:328
  92.7 4.3 %fusion.4 = (bf16[4,64,3072]{2,1,0:T(8,128)(2,1)S(1)}, f32[4,64,3072]{2,1,0:T(8,128)}) fusion(bf16[4,64,3072]{2,1,0:T(8,128)(2,1)} %collective-permute-done.2, bf16[4,2,64,3072]{3,2,1,0:T(8,128)(2,1)} %bitcast.38, s32[]{:T(128)S(6)} %select_n.45), kind=kLoop, calls=%fused_computation.15 | loop fusion | flops 3145728 | bytes 7864324 | tf_op jit(solution)/shard_map/convert_element_type | solution.py:331
  97.0 0.8 dynamic-slice_bitcast_fusion.3
  97.8 1.5 %collective-permute-start.3 = (bf16[64,3072]{1,0:T(8,128)(2,1)}, bf16[64,3072]{1,0:T(8,128)(2,1)S(1)}, u32[]{:S(2)}, u32[]{:S(2)}) collective-permute-start(bf16[64,3072]{1,0:T(8,128)(2,1)} %get-tuple-element.12), channel_id=1, source_target_pairs={{0,2},{2,4},{4,6},{6,0},{1,3},{3,5},{5,7},{7,1},{8,10},{10,12},{12... | collective-permute-start | bytes 1179656 | tf_op jit(solution)/shard_map/ppermute | solution.py:337
  99.3 2.7 %collective-permute-start.4 = (bf16[64,3072]{1,0:T(8,128)(2,1)S(1)}, bf16[64,3072]{1,0:T(8,128)(2,1)}, u32[]{:S(2)}, u32[]{:S(2)}) collective-permute-start(bf16[64,3072]{1,0:T(8,128)(2,1)S(1)} %get-tuple-element.14), channel_id=1, source_target_pairs={{0,4},{2,6},{4,0},{6,2},{1,5},{3,7},{5,1},{7,3},{8,12},{10,14},{12... | collective-permute-start | bytes 1179656 | tf_op jit(solution)/shard_map/ppermute | solution.py:337
  102.1 1.4 %collective-permute-start.5 = (bf16[64,3072]{1,0:T(8,128)(2,1)S(1)}, bf16[64,3072]{1,0:T(8,128)(2,1)}, u32[]{:S(2)}, u32[]{:S(2)}) collective-permute-start(bf16[64,3072]{1,0:T(8,128)(2,1)S(1)} %get-tuple-element.13), channel_id=1, source_target_pairs={{0,6},{2,0},{4,2},{6,4},{1,7},{3,1},{5,3},{7,5},{8,14},{10,8},{12,... | collective-permute-start | bytes 1179656 | tf_op jit(solution)/shard_map/ppermute | solution.py:337
  103.5 6.9 %collective-permute-done.3 = bf16[64,3072]{1,0:T(8,128)(2,1)S(1)} collective-permute-done((bf16[64,3072]{1,0:T(8,128)(2,1)}, bf16[64,3072]{1,0:T(8,128)(2,1)S(1)}, u32[]{:S(2)}, u32[]{:S(2)}) %collective-permute-start.3) | collective-permute-done | bytes 393248 | tf_op jit(solution)/shard_map/ppermute | solution.py:337
  110.4 9.5 %collective-permute-done.4 = bf16[64,3072]{1,0:T(8,128)(2,1)} collective-permute-done((bf16[64,3072]{1,0:T(8,128)(2,1)S(1)}, bf16[64,3072]{1,0:T(8,128)(2,1)}, u32[]{:S(2)}, u32[]{:S(2)}) %collective-permute-start.4) | collective-permute-done | bytes 393248 | tf_op jit(solution)/shard_map/ppermute | solution.py:337
  119.9 0.0 collective-permute-done.5
  119.9 2.4 %fusion.3 = bf16[64,3072]{1,0:T(8,128)(2,1)} fusion(bf16[64,3072]{1,0:T(8,128)(2,1)} %collective-permute-done.5, bf16[64,3072]{1,0:T(8,128)(2,1)} %collective-permute-done.4, bf16[64,3072]{1,0:T(8,128)(2,1)S(1)} %collective-permute-done.3, f32[4,64,3072]{2,1,0:T(8,128)} %get-tuple-element.11, s32[]{:T(128)S(6)} %select_n.47, bf16[512,3072]{1,0:T(8,128)(2,1)} %x_ref.3, ...), kind=kLoop, calls=%fused_computation.7 | loop fusion | flops 1769472 | bytes 2752520 | tf_op jit(solution)/shard_map/convert_element_type | solution.py:339
  122.4 10.0 %all-to-all-done = bf16[16,2,128,768]{3,2,1,0:T(8,128)(2,1)} async-done(((bf16[16,2,128,768]{3,2,1,0:T(8,128)(2,1)}), bf16[16,2,128,768]{3,2,1,0:T(8,128)(2,1)}, u32[]{:S(2)}, u32[]{:S(2)}) %all-to-all-start) | async-done | bytes 6291488 | tf_op jit(solution)/shard_map/all_to_all | solution.py:317
  132.4 6.1 %copy.13 = bf16[2,1,16,1,128,768]{5,4,3,2,1,0:T(8,128)(2,1)} copy(bf16[2,1,16,1,128,768]{5,4,0,2,3,1:T(8,128)(2,1)} %bitcast.15) | data formatting | bytes 12582912
  (2 shorter events, 0.0 us)
Async XLA Ops:
  0.6 82.6 %copy-start = (bf16[384,3072]{1,0:T(8,128)(2,1)S(1)}, bf16[384,3072]{1,0:T(8,128)(2,1)}, u32[]{:S(2)}) copy-start(bf16[384,3072]{1,0:T(8,128)(2,1)} %param.13) | copy-start | bytes 7077892
  0.6 19.3 %collective-permute-start = (bf16[2,1,3584,384]{3,2,1,0:T(8,128)(2,1)}, bf16[2,1,3584,384]{3,2,1,0:T(8,128)(2,1)}, u32[]{:S(2)}, u32[]{:S(2)}) collective-permute-start(bf16[2,1,3584,384]{3,2,1,0:T(8,128)(2,1)} %vc_ref.1), channel_id=1, source_target_pairs={{0,1},{1,0},{2,3},{3,2},{4,5},{5,4},{6,7},{7,6},{8,9},{9,8},{10,11... | collective-permute-start | bytes 16515080 | tf_op jit(solution)/shard_map/ppermute | solution.py:310
  17.4 2.5 %collective-permute-start.1 = (bf16[2,512,384]{2,1,0:T(8,128)(2,1)}, bf16[2,512,384]{2,1,0:T(8,128)(2,1)S(1)}, u32[]{:S(2)}, u32[]{:S(2)}) collective-permute-start(bf16[2,512,384]{2,1,0:T(8,128)(2,1)} %shard_map.114.refs_1_.refs_5_.kn_ref.vn_ref), channel_id=1, source_target_pairs={{0,1},{1,0},{2,3},{3,2},{4,5},{5,4},{6,7},{7,6},{8,9},{9,8},{10,11... | collective-permute-start | bytes 2359304 | tf_op jit(solution)/shard_map/ppermute | solution.py:313
  19.9 0.9 copy-start.2
  30.0 102.3 %all-to-all-start = ((bf16[16,2,128,768]{3,2,1,0:T(8,128)(2,1)}), bf16[16,2,128,768]{3,2,1,0:T(8,128)(2,1)}, u32[]{:S(2)}, u32[]{:S(2)}) async-start(bf16[16,2,128,768]{3,2,1,0:T(8,128)(2,1)} %shard_map.115), calls=%async_computation | async-start | bytes 12582912 | tf_op jit(solution)/shard_map/all_to_all | solution.py:317
  86.1 1.7 %copy-start.1 = (bf16[512,3072]{1,0:T(8,128)(2,1)}, bf16[512,3072]{1,0:T(8,128)(2,1)S(1)}, u32[]{:S(2)}) copy-start(bf16[512,3072]{1,0:T(8,128)(2,1)S(1)} %convolution_convert_fusion) | copy-start | bytes 9437188
  89.0 3.8 %collective-permute-start.2 = (bf16[4,64,3072]{2,1,0:T(8,128)(2,1)}, bf16[4,64,3072]{2,1,0:T(8,128)(2,1)}, u32[]{:S(2)}, u32[]{:S(2)}) collective-permute-start(bf16[4,64,3072]{2,1,0:T(8,128)(2,1)} %dynamic-slice_bitcast_fusion), channel_id=1, source_target_pairs={{0,1},{1,0},{2,3},{3,2},{4,5},{5,4},{6,7},{7,6},{8,9},{9,8},{10,11... | collective-permute-start | bytes 4718600 | tf_op jit(solution)/shard_map/ppermute | solution.py:328
  97.8 12.6 %collective-permute-start.3 = (bf16[64,3072]{1,0:T(8,128)(2,1)}, bf16[64,3072]{1,0:T(8,128)(2,1)S(1)}, u32[]{:S(2)}, u32[]{:S(2)}) collective-permute-start(bf16[64,3072]{1,0:T(8,128)(2,1)} %get-tuple-element.12), channel_id=1, source_target_pairs={{0,2},{2,4},{4,6},{6,0},{1,3},{3,5},{5,7},{7,1},{8,10},{10,12},{12... | collective-permute-start | bytes 1179656 | tf_op jit(solution)/shard_map/ppermute | solution.py:337
  99.3 20.6 %collective-permute-start.4 = (bf16[64,3072]{1,0:T(8,128)(2,1)S(1)}, bf16[64,3072]{1,0:T(8,128)(2,1)}, u32[]{:S(2)}, u32[]{:S(2)}) collective-permute-start(bf16[64,3072]{1,0:T(8,128)(2,1)S(1)} %get-tuple-element.14), channel_id=1, source_target_pairs={{0,4},{2,6},{4,0},{6,2},{1,5},{3,7},{5,1},{7,3},{8,12},{10,14},{12... | collective-permute-start | bytes 1179656 | tf_op jit(solution)/shard_map/ppermute | solution.py:337
  102.1 17.9 %collective-permute-start.5 = (bf16[64,3072]{1,0:T(8,128)(2,1)S(1)}, bf16[64,3072]{1,0:T(8,128)(2,1)}, u32[]{:S(2)}, u32[]{:S(2)}) collective-permute-start(bf16[64,3072]{1,0:T(8,128)(2,1)S(1)} %get-tuple-element.13), channel_id=1, source_target_pairs={{0,6},{2,0},{4,2},{6,4},{1,7},{3,1},{5,3},{7,5},{8,14},{10,8},{12,... | collective-permute-start | bytes 1179656 | tf_op jit(solution)/shard_map/ppermute | solution.py:337

commit v11 on v10

--- a/solution.py
+++ b/solution.py
@@ -167,7 +167,7 @@
     features = kv_cache.shape[3]
     new_blocks = new_kv.shape[1] // BLK
     rank_count = 2 * seq_count
-    per_step = 2 if seq_count % 2 == 0 else 1
+    per_step = 4 if seq_count % 4 == 0 else 1
 
     def block_of(d, slot, m):
         return (2 * (d * per_step + slot) + m[3] - m[2] + rank_count) % rank_count
@@ -228,7 +228,8 @@
     def _():
         inputs = x_ref[...].astype(jnp.float32)
         inverse_rms = lax.rsqrt(jnp.mean(inputs * inputs, axis=-1, keepdims=True) + 1e-05)
-        normed_ref[...] = (inputs * inverse_rms * gain_ref[...]).astype(jnp.bfloat16)
+        gain = gain_ref[...].astype(jnp.float32)
+        normed_ref[...] = (inputs * inverse_rms * gain).astype(jnp.bfloat16)
 
     weights = w_ref[0]
     plain = jnp.dot(normed_ref[...], weights, preferred_element_type=jnp.float32)
@@ -304,7 +305,7 @@
         jnp.arange(half_size, dtype=jnp.float32) * (-2.0 * math.log(10000.0) / HD)
     )
     frequency = jnp.tile(frequency, features // half_size).reshape(1, features)
-    gain = norm_gain.astype(jnp.float32).reshape(1, model_width)
+    gain = norm_gain.reshape(1, model_width)
     core = lax.axis_index("core")
     swap_cores = [(0, 1), (1, 0)]
     mate_cache = lax.ppermute(kv_cache, "core", swap_cores)

time: 139 us -> 138 us (level)
  local copies, waits for them, and re-layouts: 11.6 us -> 13.1 us
  other arithmetic: 9.46 us -> 8.03 us
    reshape x0 -> x1, local copies, waits for them, and re-layouts: none -> 1.44 us  [local(): gain = norm_gain.reshape(1, model_width)]
    reshape x1 -> x0, other arithmetic: 1.43 us -> none  [local(): gain = norm_gain.astype(jnp.float32).reshape(1, model_width)]
where the time goes in v11:
time: 138 us
  Pallas kernels  66.2 us (48%)
  waiting for transfers between devices  33.4 us (24%)
  starting transfers between devices  13.9 us (10%)
  local copies, waits for them, and re-layouts  13.1 us (9%)
  other arithmetic  8.03 us (6%)
  matrix products  2.79 us (2%)
    pallas_call x1, Pallas kernels, attend(): pl.pallas_call(attention_kernel, out_shape=jax.ShapeDtypeStruct(queries.s...  35.1 us
    pallas_call x2, Pallas kernels, project(): pl.pallas_call(functools.partial(projection_kernel, parts=parts), out_sha...  22.5 us
    ppermute x3, waiting for transfers between devices, local(): summed = summed + lax.ppermute(chunk, 'x', pairs).astype(jnp.float32)  16.4 us
    all_to_all x1, waiting for transfers between devices, local(): received = lax.all_to_all(joined, 'seq', 0, 0, tiled=True)  11.2 us
    unnamed x7, local copies, waits for them, and re-layouts  8.68 us
    pallas_call x1, Pallas kernels, relay(): pl.pallas_call(functools.partial(relay_kernel, new_blocks=new_blocks), ou...  8.59 us
    all_to_all x1, starting transfers between devices, local(): received = lax.all_to_all(joined, 'seq', 0, 0, tiled=True)  7.75 us
    ppermute x3, starting transfers between devices, local(): summed = summed + lax.ppermute(chunk, 'x', pairs).astype(jnp.float32)  5.65 us
  transfers between devices with their start and end apart: 7, of which 5 were waited for; matrix products, arithmetic and copies ran while one was open for 11% of the time, Pallas kernels for 42%

profile of v11, /device:TPU:0, one launch (start us, length us, event | category | flops | bytes accessed | tf_op | source)
XLA Modules:
  0.0 138.1 jit_solution(12320881181810048511)
XLA Ops:
  0.6 0.0 copy-start
  0.6 0.1 collective-permute-start
  0.7 1.4 %reshape.24.gain_ref = bf16[1,3072]{1,0:T(2,128)(2,1)} reshape(bf16[3072]{0:T(1024)(128)(2,1)} %param.11) | data formatting | bytes 12288 | tf_op jit(solution)/shard_map/reshape | solution.py:308
  2.2 0.7 reshape_tile.5.freq_ref
  2.9 0.7 pad_add_fusion
  3.6 0.2 dynamic-slice_reduce_fusion
  3.8 0.6 pad_add_fusion.1.meta_ref
  4.4 13.1 %shard_map.114.refs_1_.refs_5_.refs_9_.refs_13_.kn_ref.vn_ref = bf16[2,512,384]{2,1,0:T(8,128)(2,1)} custom-call(s32[2]{0:T(128)} %constant.74.clone.part_ref, s32[4]{0:T(128)} %pad_add_fusion.1.meta_ref, bf16[512,3072]{1,0:T(8,128)(2,1)} %x_ref.3, bf16[1,3072]{1,0:T(2,128)(2,1)} %reshape.24.gain_ref, bf16[3,3072,384]{2,1,0:T(8,128)(2,1)} %bitcast.34, ...), custom_call_target="tpu_custom_call" | custom-call | tf_op jit(solution)/shard_map/pallas_call | solution.py:267
  17.4 0.3 collective-permute-start.1
  17.8 2.2 %collective-permute-done.1.refs_3_.refs_7_.refs_11_.refs_15_ = bf16[2,512,384]{2,1,0:T(8,128)(2,1)S(1)} collective-permute-done((bf16[2,512,384]{2,1,0:T(8,128)(2,1)}, bf16[2,512,384]{2,1,0:T(8,128)(2,1)S(1)}, u32[]{:S(2)}, u32[]{:S(2)}) %collective-permute-start.1) | collective-permute-done | bytes 786464 | tf_op jit(solution)/shard_map/ppermute | solution.py:314
  19.9 0.0 copy-start.1
  19.9 0.0 collective-permute-done.refs_2_.refs_6_.refs_10_.refs_14_
  19.9 0.9 copy-done.1
  20.8 8.6 %shard_map.115 = bf16[16,2,128,768]{3,2,1,0:T(8,128)(2,1)} custom-call(s32[4]{0:T(128)} %pad_add_fusion.1.meta_ref, bf16[2,1,3584,384]{3,2,1,0:T(8,128)(2,1)} %vc_ref.1, bf16[2,512,384]{2,1,0:T(8,128)(2,1)} %shard_map.114.refs_1_.refs_5_.refs_9_.refs_13_.kn_ref.vn_ref, bf16[2,1,3584,384]{3,2,1,0:T(8,128)(2,1)} %collective-permute-done.refs_2_.refs_6_.refs_10_.refs_14_, ...), custom_call_target="tpu_custom_call" | custom-call | tf_op jit(solution)/shard_map/pallas_call | solution.py:196
  29.4 7.7 %all-to-all-start = ((bf16[16,2,128,768]{3,2,1,0:T(8,128)(2,1)}), bf16[16,2,128,768]{3,2,1,0:T(8,128)(2,1)}, u32[]{:S(2)}, u32[]{:S(2)}) async-start(bf16[16,2,128,768]{3,2,1,0:T(8,128)(2,1)} %shard_map.115), calls=%async_computation | async-start | bytes 12582912 | tf_op jit(solution)/shard_map/all_to_all | solution.py:318
  37.1 9.4 %shard_map.113 = bf16[1,512,384]{2,1,0:T(8,128)(2,1)} custom-call(s32[1]{0:T(128)} %constant.75.clone.part_ref, s32[4]{0:T(128)} %pad_add_fusion.1.meta_ref, bf16[512,3072]{1,0:T(8,128)(2,1)} %x_ref.3, bf16[1,3072]{1,0:T(2,128)(2,1)} %reshape.24.gain_ref, bf16[3,3072,384]{2,1,0:T(8,128)(2,1)} %bitcast.35, f32[1,384]{1,0:T(1,128)} %reshape_tile.5.freq_ref), custom_call_target="tpu_custom_call" | custom-call | tf_op jit(solution)/shard_map/pallas_call | solution.py:267
  46.6 35.1 %shard_map.116 = bf16[512,384]{1,0:T(8,128)(2,1)} custom-call(s32[4]{0:T(128)} %pad_add_fusion.1.meta_ref, bf16[512,384]{1,0:T(8,128)(2,1)} %bitcast.38, bf16[2,1,3584,384]{3,2,1,0:T(8,128)(2,1)} %vc_ref.1, bf16[2,1,3584,384]{3,2,1,0:T(8,128)(2,1)} %vc_ref.1, bf16[2,512,384]{2,1,0:T(8,128)(2,1)} %shard_map.114.refs_1_.refs_5_.refs_9_.refs_13_.kn_ref.vn_ref, ...), custom_call_target="tpu_custom_call" | custom-call | tf_op jit(solution)/shard_map/pallas_call | solution.py:124
  81.7 0.0 copy-done
  81.7 2.8 %convolution_convert_fusion = bf16[512,3072]{1,0:T(8,128)(2,1)S(1)} fusion(bf16[512,384]{1,0:T(8,128)(2,1)} %shard_map.116, bf16[384,3072]{1,0:T(8,128)(2,1)S(1)} %copy-done), kind=kOutput, calls=%fused_computation | convolution fusion | flops 1209532416 | bytes 5898240 | tf_op jit(solution)/shard_map/dot_general | solution.py:323
  84.5 0.0 copy-start.2
  84.5 1.6 %copy-done.2 = bf16[512,3072]{1,0:T(8,128)(2,1)} copy-done((bf16[512,3072]{1,0:T(8,128)(2,1)}, bf16[512,3072]{1,0:T(8,128)(2,1)S(1)}, u32[]{:S(2)}) %copy-start.2) | copy-done | bytes 3145752
  86.2 1.3 dynamic-slice_bitcast_fusion
  87.4 0.1 collective-permute-start.2
  87.5 3.7 %collective-permute-done.2 = bf16[4,64,3072]{2,1,0:T(8,128)(2,1)} collective-permute-done((bf16[4,64,3072]{2,1,0:T(8,128)(2,1)}, bf16[4,64,3072]{2,1,0:T(8,128)(2,1)}, u32[]{:S(2)}, u32[]{:S(2)}) %collective-permute-start.2) | collective-permute-done | bytes 1572896 | tf_op jit(solution)/shard_map/ppermute | solution.py:329
  91.2 4.3 %fusion.4 = (bf16[4,64,3072]{2,1,0:T(8,128)(2,1)S(1)}, f32[4,64,3072]{2,1,0:T(8,128)}) fusion(bf16[4,64,3072]{2,1,0:T(8,128)(2,1)} %collective-permute-done.2, bf16[4,2,64,3072]{3,2,1,0:T(8,128)(2,1)} %bitcast.37, s32[]{:T(128)S(6)} %select_n.45), kind=kLoop, calls=%fused_computation.15 | loop fusion | flops 3145728 | bytes 7864324 | tf_op jit(solution)/shard_map/convert_element_type | solution.py:332
  95.5 0.8 dynamic-slice_bitcast_fusion.3
  96.3 1.5 %collective-permute-start.3 = (bf16[64,3072]{1,0:T(8,128)(2,1)}, bf16[64,3072]{1,0:T(8,128)(2,1)S(1)}, u32[]{:S(2)}, u32[]{:S(2)}) collective-permute-start(bf16[64,3072]{1,0:T(8,128)(2,1)} %get-tuple-element.12), channel_id=1, source_target_pairs={{0,2},{2,4},{4,6},{6,0},{1,3},{3,5},{5,7},{7,1},{8,10},{10,12},{12... | collective-permute-start | bytes 1179656 | tf_op jit(solution)/shard_map/ppermute | solution.py:338
  97.8 2.7 %collective-permute-start.4 = (bf16[64,3072]{1,0:T(8,128)(2,1)S(1)}, bf16[64,3072]{1,0:T(8,128)(2,1)}, u32[]{:S(2)}, u32[]{:S(2)}) collective-permute-start(bf16[64,3072]{1,0:T(8,128)(2,1)S(1)} %get-tuple-element.14), channel_id=1, source_target_pairs={{0,4},{2,6},{4,0},{6,2},{1,5},{3,7},{5,1},{7,3},{8,12},{10,14},{12... | collective-permute-start | bytes 1179656 | tf_op jit(solution)/shard_map/ppermute | solution.py:338
  100.5 1.4 %collective-permute-start.5 = (bf16[64,3072]{1,0:T(8,128)(2,1)S(1)}, bf16[64,3072]{1,0:T(8,128)(2,1)}, u32[]{:S(2)}, u32[]{:S(2)}) collective-permute-start(bf16[64,3072]{1,0:T(8,128)(2,1)S(1)} %get-tuple-element.13), channel_id=1, source_target_pairs={{0,6},{2,0},{4,2},{6,4},{1,7},{3,1},{5,3},{7,5},{8,14},{10,8},{12,... | collective-permute-start | bytes 1179656 | tf_op jit(solution)/shard_map/ppermute | solution.py:338
  101.9 6.9 %collective-permute-done.3 = bf16[64,3072]{1,0:T(8,128)(2,1)S(1)} collective-permute-done((bf16[64,3072]{1,0:T(8,128)(2,1)}, bf16[64,3072]{1,0:T(8,128)(2,1)S(1)}, u32[]{:S(2)}, u32[]{:S(2)}) %collective-permute-start.3) | collective-permute-done | bytes 393248 | tf_op jit(solution)/shard_map/ppermute | solution.py:338
  108.9 9.5 %collective-permute-done.4 = bf16[64,3072]{1,0:T(8,128)(2,1)} collective-permute-done((bf16[64,3072]{1,0:T(8,128)(2,1)S(1)}, bf16[64,3072]{1,0:T(8,128)(2,1)}, u32[]{:S(2)}, u32[]{:S(2)}) %collective-permute-start.4) | collective-permute-done | bytes 393248 | tf_op jit(solution)/shard_map/ppermute | solution.py:338
  118.4 0.0 collective-permute-done.5
  118.4 2.4 %fusion.3 = bf16[64,3072]{1,0:T(8,128)(2,1)} fusion(bf16[64,3072]{1,0:T(8,128)(2,1)} %collective-permute-done.5, bf16[64,3072]{1,0:T(8,128)(2,1)} %collective-permute-done.4, bf16[64,3072]{1,0:T(8,128)(2,1)S(1)} %collective-permute-done.3, f32[4,64,3072]{2,1,0:T(8,128)} %get-tuple-element.11, s32[]{:T(128)S(6)} %select_n.47, bf16[512,3072]{1,0:T(8,128)(2,1)} %x_ref.3, ...), kind=kLoop, calls=%fused_computation.7 | loop fusion | flops 1769472 | bytes 2752520 | tf_op jit(solution)/shard_map/convert_element_type | solution.py:340
  120.8 11.2 %all-to-all-done = bf16[16,2,128,768]{3,2,1,0:T(8,128)(2,1)} async-done(((bf16[16,2,128,768]{3,2,1,0:T(8,128)(2,1)}), bf16[16,2,128,768]{3,2,1,0:T(8,128)(2,1)}, u32[]{:S(2)}, u32[]{:S(2)}) %all-to-all-start) | async-done | bytes 6291488 | tf_op jit(solution)/shard_map/all_to_all | solution.py:318
  132.0 6.1 %copy.13 = bf16[2,1,16,1,128,768]{5,4,3,2,1,0:T(8,128)(2,1)} copy(bf16[2,1,16,1,128,768]{5,4,0,2,3,1:T(8,128)(2,1)} %bitcast.14) | data formatting | bytes 12582912
  (2 shorter events, 0.0 us)
Async XLA Ops:
  0.6 81.1 %copy-start = (bf16[384,3072]{1,0:T(8,128)(2,1)S(1)}, bf16[384,3072]{1,0:T(8,128)(2,1)}, u32[]{:S(2)}) copy-start(bf16[384,3072]{1,0:T(8,128)(2,1)} %param.13) | copy-start | bytes 7077892
  0.6 19.3 %collective-permute-start = (bf16[2,1,3584,384]{3,2,1,0:T(8,128)(2,1)}, bf16[2,1,3584,384]{3,2,1,0:T(8,128)(2,1)}, u32[]{:S(2)}, u32[]{:S(2)}) collective-permute-start(bf16[2,1,3584,384]{3,2,1,0:T(8,128)(2,1)} %vc_ref.1), channel_id=1, source_target_pairs={{0,1},{1,0},{2,3},{3,2},{4,5},{5,4},{6,7},{7,6},{8,9},{9,8},{10,11... | collective-permute-start | bytes 16515080 | tf_op jit(solution)/shard_map/ppermute | solution.py:311
  17.4 2.5 %collective-permute-start.1 = (bf16[2,512,384]{2,1,0:T(8,128)(2,1)}, bf16[2,512,384]{2,1,0:T(8,128)(2,1)S(1)}, u32[]{:S(2)}, u32[]{:S(2)}) collective-permute-start(bf16[2,512,384]{2,1,0:T(8,128)(2,1)} %shard_map.114.refs_1_.refs_5_.refs_9_.refs_13_.kn_ref.vn_ref), channel_id=1, source_target_pairs={{0,1},{1,0},{2,3},{3,2},{4,5},{5,4},{6,7},{7,6},{8,9},{9,8},{10,11... | collective-permute-start | bytes 2359304 | tf_op jit(solution)/shard_map/ppermute | solution.py:314
  19.9 0.9 copy-start.1
  29.4 102.6 %all-to-all-start = ((bf16[16,2,128,768]{3,2,1,0:T(8,128)(2,1)}), bf16[16,2,128,768]{3,2,1,0:T(8,128)(2,1)}, u32[]{:S(2)}, u32[]{:S(2)}) async-start(bf16[16,2,128,768]{3,2,1,0:T(8,128)(2,1)} %shard_map.115), calls=%async_computation | async-start | bytes 12582912 | tf_op jit(solution)/shard_map/all_to_all | solution.py:318
  84.5 1.7 %copy-start.2 = (bf16[512,3072]{1,0:T(8,128)(2,1)}, bf16[512,3072]{1,0:T(8,128)(2,1)S(1)}, u32[]{:S(2)}) copy-start(bf16[512,3072]{1,0:T(8,128)(2,1)S(1)} %convolution_convert_fusion) | copy-start | bytes 9437188
  87.4 3.8 %collective-permute-start.2 = (bf16[4,64,3072]{2,1,0:T(8,128)(2,1)}, bf16[4,64,3072]{2,1,0:T(8,128)(2,1)}, u32[]{:S(2)}, u32[]{:S(2)}) collective-permute-start(bf16[4,64,3072]{2,1,0:T(8,128)(2,1)} %dynamic-slice_bitcast_fusion), channel_id=1, source_target_pairs={{0,1},{1,0},{2,3},{3,2},{4,5},{5,4},{6,7},{7,6},{8,9},{9,8},{10,11... | collective-permute-start | bytes 4718600 | tf_op jit(solution)/shard_map/ppermute | solution.py:329
  96.3 12.6 %collective-permute-start.3 = (bf16[64,3072]{1,0:T(8,128)(2,1)}, bf16[64,3072]{1,0:T(8,128)(2,1)S(1)}, u32[]{:S(2)}, u32[]{:S(2)}) collective-permute-start(bf16[64,3072]{1,0:T(8,128)(2,1)} %get-tuple-element.12), channel_id=1, source_target_pairs={{0,2},{2,4},{4,6},{6,0},{1,3},{3,5},{5,7},{7,1},{8,10},{10,12},{12... | collective-permute-start | bytes 1179656 | tf_op jit(solution)/shard_map/ppermute | solution.py:338
  97.8 20.6 %collective-permute-start.4 = (bf16[64,3072]{1,0:T(8,128)(2,1)S(1)}, bf16[64,3072]{1,0:T(8,128)(2,1)}, u32[]{:S(2)}, u32[]{:S(2)}) collective-permute-start(bf16[64,3072]{1,0:T(8,128)(2,1)S(1)} %get-tuple-element.14), channel_id=1, source_target_pairs={{0,4},{2,6},{4,0},{6,2},{1,5},{3,7},{5,1},{7,3},{8,12},{10,14},{12... | collective-permute-start | bytes 1179656 | tf_op jit(solution)/shard_map/ppermute | solution.py:338
  100.5 17.9 %collective-permute-start.5 = (bf16[64,3072]{1,0:T(8,128)(2,1)S(1)}, bf16[64,3072]{1,0:T(8,128)(2,1)}, u32[]{:S(2)}, u32[]{:S(2)}) collective-permute-start(bf16[64,3072]{1,0:T(8,128)(2,1)S(1)} %get-tuple-element.13), channel_id=1, source_target_pairs={{0,6},{2,0},{4,2},{6,4},{1,7},{3,1},{5,3},{7,5},{8,14},{10,8},{12,... | collective-permute-start | bytes 1179656 | tf_op jit(solution)/shard_map/ppermute | solution.py:338

commit v12 on v11

--- a/solution.py
+++ b/solution.py
@@ -207,6 +207,24 @@
     )(meta, *operands)
 
 
+def regroup_kernel(in_ref, out_ref):
+    out_ref[0, 0, :, 0] = in_ref[:, 0]
+
+
+def regroup(received):
+    sources, kinds, rows, width = received.shape
+    per_step = 4 if sources % 4 == 0 else 1
+    return pl.pallas_call(
+        regroup_kernel,
+        out_shape=jax.ShapeDtypeStruct((kinds, 1, sources, 1, rows, width), received.dtype),
+        grid=(kinds, sources // per_step),
+        in_specs=[pl.BlockSpec((per_step, 1, rows, width), lambda k, g: (g, k, 0, 0))],
+        out_specs=pl.BlockSpec(
+            (1, 1, per_step, 1, rows, width), lambda k, g: (k, 0, g, 0, 0, 0)
+        ),
+    )(received)
+
+
 def half_swap(features):
     half = HD // 2
     rows = lax.broadcasted_iota(jnp.int32, (features, features), 0)
@@ -316,7 +334,7 @@
     queries = project(meta, tokens, gain, weights, frequency, (0,))[0]
     joined, attn_kv = lax.optimization_barrier((joined, new_kv))
     received = lax.all_to_all(joined, "seq", 0, 0, tiled=True)
-    decode_cache = received.transpose(1, 0, 2, 3).reshape(2, 1, seq_count, 1, BLK, 2 * features)
+    decode_cache = regroup(received)
 
     attended = attend(meta, queries, kv_cache, attn_kv)
     rows_dev = tok_count // tp_count

time: 138 us -> 140 us (1.014)
  Pallas kernels: 66.2 us -> 73.6 us
  local copies, waits for them, and re-layouts: 13.1 us -> 6.93 us
    pallas_call x0 -> x1, Pallas kernels: none -> 7.83 us  [regroup(): pl.pallas_call(regroup_kernel, out_shape=jax.ShapeDtypeStruct((kinds, 1,...]
    unnamed x7 -> x6, local copies, waits for them, and re-layouts: 8.68 us -> 2.54 us
  transfers between devices with their start and end apart: 7 -> 7, of which waited for: 5 -> 5; matrix products, arithmetic and copies ran while one was open for 11% -> 11% of each run, Pallas kernels for 42% -> 41%
where the time goes in v12:
time: 140 us
  Pallas kernels  73.6 us (53%)
  waiting for transfers between devices  33.8 us (24%)
  starting transfers between devices  14.2 us (10%)
  other arithmetic  8.03 us (6%)
  local copies, waits for them, and re-layouts  6.93 us (5%)
  matrix products  2.79 us (2%)
    pallas_call x1, Pallas kernels, attend(): pl.pallas_call(attention_kernel, out_shape=jax.ShapeDtypeStruct(queries.s...  35.1 us
    pallas_call x2, Pallas kernels, project(): pl.pallas_call(functools.partial(projection_kernel, parts=parts), out_sha...  22.5 us
    ppermute x3, waiting for transfers between devices, local(): summed = summed + lax.ppermute(chunk, 'x', pairs).astype(jnp.float32)  16.4 us
    all_to_all x1, waiting for transfers between devices, local(): received = lax.all_to_all(joined, 'seq', 0, 0, tiled=True)  11.6 us
    pallas_call x1, Pallas kernels, relay(): pl.pallas_call(functools.partial(relay_kernel, new_blocks=new_blocks), ou...  8.15 us
    all_to_all x1, starting transfers between devices, local(): received = lax.all_to_all(joined, 'seq', 0, 0, tiled=True)  7.99 us
    pallas_call x1, Pallas kernels, regroup(): pl.pallas_call(regroup_kernel, out_shape=jax.ShapeDtypeStruct((kinds, 1,...  7.83 us
    ppermute x3, starting transfers between devices, local(): summed = summed + lax.ppermute(chunk, 'x', pairs).astype(jnp.float32)  5.66 us
  transfers between devices with their start and end apart: 7, of which 5 were waited for; matrix products, arithmetic and copies ran while one was open for 11% of the time, Pallas kernels for 41%

profile of v12, /device:TPU:0, one launch (start us, length us, event | category | flops | bytes accessed | tf_op | source)
XLA Modules:
  0.0 140.1 jit_solution(12403719477999582095)
XLA Ops:
  0.6 0.0 copy-start
  0.6 0.1 collective-permute-start
  0.7 1.4 %reshape.21.gain_ref = bf16[1,3072]{1,0:T(2,128)(2,1)} reshape(bf16[3072]{0:T(1024)(128)(2,1)} %param.11) | data formatting | bytes 12288 | tf_op jit(solution)/shard_map/reshape | solution.py:326
  2.2 0.7 reshape_tile.5.freq_ref
  2.9 0.7 pad_add_fusion
  3.6 0.2 dynamic-slice_reduce_fusion
  3.8 0.6 pad_add_fusion.1.meta_ref
  4.4 13.1 %shard_map.114.refs_1_.refs_5_.refs_9_.refs_13_.kn_ref.vn_ref = bf16[2,512,384]{2,1,0:T(8,128)(2,1)} custom-call(s32[2]{0:T(128)} %constant.74.clone.part_ref, s32[4]{0:T(128)} %pad_add_fusion.1.meta_ref, bf16[512,3072]{1,0:T(8,128)(2,1)} %x_ref.3, bf16[1,3072]{1,0:T(2,128)(2,1)} %reshape.21.gain_ref, bf16[3,3072,384]{2,1,0:T(8,128)(2,1)} %bitcast.31, ...), custom_call_target="tpu_custom_call" | custom-call | tf_op jit(solution)/shard_map/pallas_call | solution.py:285
  17.4 0.3 collective-permute-start.1
  17.8 2.2 %collective-permute-done.1.refs_3_.refs_7_.refs_11_.refs_15_ = bf16[2,512,384]{2,1,0:T(8,128)(2,1)S(1)} collective-permute-done((bf16[2,512,384]{2,1,0:T(8,128)(2,1)}, bf16[2,512,384]{2,1,0:T(8,128)(2,1)S(1)}, u32[]{:S(2)}, u32[]{:S(2)}) %collective-permute-start.1) | collective-permute-done | bytes 786464 | tf_op jit(solution)/shard_map/ppermute | solution.py:332
  19.9 0.0 copy-start.1
  19.9 0.0 collective-permute-done.refs_2_.refs_6_.refs_10_.refs_14_
  19.9 0.9 copy-done.1
  20.8 8.1 %shard_map.115 = bf16[16,2,128,768]{3,2,1,0:T(8,128)(2,1)} custom-call(s32[4]{0:T(128)} %pad_add_fusion.1.meta_ref, bf16[2,1,3584,384]{3,2,1,0:T(8,128)(2,1)} %vc_ref.1, bf16[2,512,384]{2,1,0:T(8,128)(2,1)} %shard_map.114.refs_1_.refs_5_.refs_9_.refs_13_.kn_ref.vn_ref, bf16[2,1,3584,384]{3,2,1,0:T(8,128)(2,1)} %collective-permute-done.refs_2_.refs_6_.refs_10_.refs_14_, ...), custom_call_target="tpu_custom_call" | custom-call | tf_op jit(solution)/shard_map/pallas_call | solution.py:196
  28.9 8.0 %all-to-all-start = ((bf16[16,2,128,768]{3,2,1,0:T(8,128)(2,1)}), bf16[16,2,128,768]{3,2,1,0:T(8,128)(2,1)}, u32[]{:S(2)}, u32[]{:S(2)}) async-start(bf16[16,2,128,768]{3,2,1,0:T(8,128)(2,1)} %shard_map.115), calls=%async_computation | async-start | bytes 12582912 | tf_op jit(solution)/shard_map/all_to_all | solution.py:336
  36.9 9.4 %shard_map.113 = bf16[1,512,384]{2,1,0:T(8,128)(2,1)} custom-call(s32[1]{0:T(128)} %constant.75.clone.part_ref, s32[4]{0:T(128)} %pad_add_fusion.1.meta_ref, bf16[512,3072]{1,0:T(8,128)(2,1)} %x_ref.3, bf16[1,3072]{1,0:T(2,128)(2,1)} %reshape.21.gain_ref, bf16[3,3072,384]{2,1,0:T(8,128)(2,1)} %bitcast.32, f32[1,384]{1,0:T(1,128)} %reshape_tile.5.freq_ref), custom_call_target="tpu_custom_call" | custom-call | tf_op jit(solution)/shard_map/pallas_call | solution.py:285
  46.4 35.1 %shard_map.116 = bf16[512,384]{1,0:T(8,128)(2,1)} custom-call(s32[4]{0:T(128)} %pad_add_fusion.1.meta_ref, bf16[512,384]{1,0:T(8,128)(2,1)} %bitcast.35, bf16[2,1,3584,384]{3,2,1,0:T(8,128)(2,1)} %vc_ref.1, bf16[2,1,3584,384]{3,2,1,0:T(8,128)(2,1)} %vc_ref.1, bf16[2,512,384]{2,1,0:T(8,128)(2,1)} %shard_map.114.refs_1_.refs_5_.refs_9_.refs_13_.kn_ref.vn_ref, ...), custom_call_target="tpu_custom_call" | custom-call | tf_op jit(solution)/shard_map/pallas_call | solution.py:124
  81.5 0.0 copy-done
  81.5 2.8 %convolution_convert_fusion = bf16[512,3072]{1,0:T(8,128)(2,1)S(1)} fusion(bf16[512,384]{1,0:T(8,128)(2,1)} %shard_map.116, bf16[384,3072]{1,0:T(8,128)(2,1)S(1)} %copy-done), kind=kOutput, calls=%fused_computation | convolution fusion | flops 1209532416 | bytes 5898240 | tf_op jit(solution)/shard_map/dot_general | solution.py:341
  84.3 0.0 copy-start.2
  84.3 1.6 %copy-done.2 = bf16[512,3072]{1,0:T(8,128)(2,1)} copy-done((bf16[512,3072]{1,0:T(8,128)(2,1)}, bf16[512,3072]{1,0:T(8,128)(2,1)S(1)}, u32[]{:S(2)}) %copy-start.2) | copy-done | bytes 3145752
  86.0 1.3 dynamic-slice_bitcast_fusion
  87.2 0.1 collective-permute-start.2
  87.4 3.6 %collective-permute-done.2 = bf16[4,64,3072]{2,1,0:T(8,128)(2,1)} collective-permute-done((bf16[4,64,3072]{2,1,0:T(8,128)(2,1)}, bf16[4,64,3072]{2,1,0:T(8,128)(2,1)}, u32[]{:S(2)}, u32[]{:S(2)}) %collective-permute-start.2) | collective-permute-done | bytes 1572896 | tf_op jit(solution)/shard_map/ppermute | solution.py:347
  91.0 4.3 %fusion.4 = (bf16[4,64,3072]{2,1,0:T(8,128)(2,1)S(1)}, f32[4,64,3072]{2,1,0:T(8,128)}) fusion(bf16[4,64,3072]{2,1,0:T(8,128)(2,1)} %collective-permute-done.2, bf16[4,2,64,3072]{3,2,1,0:T(8,128)(2,1)} %bitcast.34, s32[]{:T(128)S(6)} %select_n.45), kind=kLoop, calls=%fused_computation.15 | loop fusion | flops 3145728 | bytes 7864324 | tf_op jit(solution)/shard_map/convert_element_type | solution.py:350
  95.3 0.8 dynamic-slice_bitcast_fusion.3
  96.1 1.5 %collective-permute-start.3 = (bf16[64,3072]{1,0:T(8,128)(2,1)}, bf16[64,3072]{1,0:T(8,128)(2,1)S(1)}, u32[]{:S(2)}, u32[]{:S(2)}) collective-permute-start(bf16[64,3072]{1,0:T(8,128)(2,1)} %get-tuple-element.8), channel_id=1, source_target_pairs={{0,2},{2,4},{4,6},{6,0},{1,3},{3,5},{5,7},{7,1},{8,10},{10,12},{12... | collective-permute-start | bytes 1179656 | tf_op jit(solution)/shard_map/ppermute | solution.py:356
  97.6 2.7 %collective-permute-start.4 = (bf16[64,3072]{1,0:T(8,128)(2,1)S(1)}, bf16[64,3072]{1,0:T(8,128)(2,1)}, u32[]{:S(2)}, u32[]{:S(2)}) collective-permute-start(bf16[64,3072]{1,0:T(8,128)(2,1)S(1)} %get-tuple-element.10), channel_id=1, source_target_pairs={{0,4},{2,6},{4,0},{6,2},{1,5},{3,7},{5,1},{7,3},{8,12},{10,14},{12... | collective-permute-start | bytes 1179656 | tf_op jit(solution)/shard_map/ppermute | solution.py:356
  100.3 1.4 %collective-permute-start.5 = (bf16[64,3072]{1,0:T(8,128)(2,1)S(1)}, bf16[64,3072]{1,0:T(8,128)(2,1)}, u32[]{:S(2)}, u32[]{:S(2)}) collective-permute-start(bf16[64,3072]{1,0:T(8,128)(2,1)S(1)} %get-tuple-element.9), channel_id=1, source_target_pairs={{0,6},{2,0},{4,2},{6,4},{1,7},{3,1},{5,3},{7,5},{8,14},{10,8},{12,... | collective-permute-start | bytes 1179656 | tf_op jit(solution)/shard_map/ppermute | solution.py:356
  101.8 6.9 %collective-permute-done.3 = bf16[64,3072]{1,0:T(8,128)(2,1)S(1)} collective-permute-done((bf16[64,3072]{1,0:T(8,128)(2,1)}, bf16[64,3072]{1,0:T(8,128)(2,1)S(1)}, u32[]{:S(2)}, u32[]{:S(2)}) %collective-permute-start.3) | collective-permute-done | bytes 393248 | tf_op jit(solution)/shard_map/ppermute | solution.py:356
  108.7 9.5 %collective-permute-done.4 = bf16[64,3072]{1,0:T(8,128)(2,1)} collective-permute-done((bf16[64,3072]{1,0:T(8,128)(2,1)S(1)}, bf16[64,3072]{1,0:T(8,128)(2,1)}, u32[]{:S(2)}, u32[]{:S(2)}) %collective-permute-start.4) | collective-permute-done | bytes 393248 | tf_op jit(solution)/shard_map/ppermute | solution.py:356
  118.2 0.0 collective-permute-done.5
  118.2 2.4 %fusion.3 = bf16[64,3072]{1,0:T(8,128)(2,1)} fusion(bf16[64,3072]{1,0:T(8,128)(2,1)} %collective-permute-done.5, bf16[64,3072]{1,0:T(8,128)(2,1)} %collective-permute-done.4, bf16[64,3072]{1,0:T(8,128)(2,1)S(1)} %collective-permute-done.3, f32[4,64,3072]{2,1,0:T(8,128)} %get-tuple-element.7, s32[]{:T(128)S(6)} %select_n.47, bf16[512,3072]{1,0:T(8,128)(2,1)} %x_ref.3, ...), kind=kLoop, calls=%fused_computation.7 | loop fusion | flops 1769472 | bytes 2752520 | tf_op jit(solution)/shard_map/convert_element_type | solution.py:358
  120.6 11.6 %all-to-all-done.in_ref = bf16[16,2,128,768]{3,2,1,0:T(8,128)(2,1)} async-done(((bf16[16,2,128,768]{3,2,1,0:T(8,128)(2,1)}), bf16[16,2,128,768]{3,2,1,0:T(8,128)(2,1)}, u32[]{:S(2)}, u32[]{:S(2)}) %all-to-all-start) | async-done | bytes 6291488 | tf_op jit(solution)/shard_map/all_to_all | solution.py:336
  132.2 7.8 %shard_map.117 = bf16[2,1,16,1,128,768]{5,4,3,2,1,0:T(8,128)(2,1)} custom-call(bf16[16,2,128,768]{3,2,1,0:T(8,128)(2,1)} %all-to-all-done.in_ref), custom_call_target="tpu_custom_call" | custom-call | tf_op jit(solution)/shard_map/pallas_call | solution.py:217
  (2 shorter events, 0.0 us)
Async XLA Ops:
  0.6 80.9 %copy-start = (bf16[384,3072]{1,0:T(8,128)(2,1)S(1)}, bf16[384,3072]{1,0:T(8,128)(2,1)}, u32[]{:S(2)}) copy-start(bf16[384,3072]{1,0:T(8,128)(2,1)} %param.13) | copy-start | bytes 7077892
  0.6 19.3 %collective-permute-start = (bf16[2,1,3584,384]{3,2,1,0:T(8,128)(2,1)}, bf16[2,1,3584,384]{3,2,1,0:T(8,128)(2,1)}, u32[]{:S(2)}, u32[]{:S(2)}) collective-permute-start(bf16[2,1,3584,384]{3,2,1,0:T(8,128)(2,1)} %vc_ref.1), channel_id=1, source_target_pairs={{0,1},{1,0},{2,3},{3,2},{4,5},{5,4},{6,7},{7,6},{8,9},{9,8},{10,11... | collective-permute-start | bytes 16515080 | tf_op jit(solution)/shard_map/ppermute | solution.py:329
  17.4 2.5 %collective-permute-start.1 = (bf16[2,512,384]{2,1,0:T(8,128)(2,1)}, bf16[2,512,384]{2,1,0:T(8,128)(2,1)S(1)}, u32[]{:S(2)}, u32[]{:S(2)}) collective-permute-start(bf16[2,512,384]{2,1,0:T(8,128)(2,1)} %shard_map.114.refs_1_.refs_5_.refs_9_.refs_13_.kn_ref.vn_ref), channel_id=1, source_target_pairs={{0,1},{1,0},{2,3},{3,2},{4,5},{5,4},{6,7},{7,6},{8,9},{9,8},{10,11... | collective-permute-start | bytes 2359304 | tf_op jit(solution)/shard_map/ppermute | solution.py:332
  19.9 0.9 copy-start.1
  28.9 103.3 %all-to-all-start = ((bf16[16,2,128,768]{3,2,1,0:T(8,128)(2,1)}), bf16[16,2,128,768]{3,2,1,0:T(8,128)(2,1)}, u32[]{:S(2)}, u32[]{:S(2)}) async-start(bf16[16,2,128,768]{3,2,1,0:T(8,128)(2,1)} %shard_map.115), calls=%async_computation | async-start | bytes 12582912 | tf_op jit(solution)/shard_map/all_to_all | solution.py:336
  84.3 1.7 %copy-start.2 = (bf16[512,3072]{1,0:T(8,128)(2,1)}, bf16[512,3072]{1,0:T(8,128)(2,1)S(1)}, u32[]{:S(2)}) copy-start(bf16[512,3072]{1,0:T(8,128)(2,1)S(1)} %convolution_convert_fusion) | copy-start | bytes 9437188
  87.2 3.8 %collective-permute-start.2 = (bf16[4,64,3072]{2,1,0:T(8,128)(2,1)}, bf16[4,64,3072]{2,1,0:T(8,128)(2,1)}, u32[]{:S(2)}, u32[]{:S(2)}) collective-permute-start(bf16[4,64,3072]{2,1,0:T(8,128)(2,1)} %dynamic-slice_bitcast_fusion), channel_id=1, source_target_pairs={{0,1},{1,0},{2,3},{3,2},{4,5},{5,4},{6,7},{7,6},{8,9},{9,8},{10,11... | collective-permute-start | bytes 4718600 | tf_op jit(solution)/shard_map/ppermute | solution.py:347
  96.1 12.6 %collective-permute-start.3 = (bf16[64,3072]{1,0:T(8,128)(2,1)}, bf16[64,3072]{1,0:T(8,128)(2,1)S(1)}, u32[]{:S(2)}, u32[]{:S(2)}) collective-permute-start(bf16[64,3072]{1,0:T(8,128)(2,1)} %get-tuple-element.8), channel_id=1, source_target_pairs={{0,2},{2,4},{4,6},{6,0},{1,3},{3,5},{5,7},{7,1},{8,10},{10,12},{12... | collective-permute-start | bytes 1179656 | tf_op jit(solution)/shard_map/ppermute | solution.py:356
  97.6 20.6 %collective-permute-start.4 = (bf16[64,3072]{1,0:T(8,128)(2,1)S(1)}, bf16[64,3072]{1,0:T(8,128)(2,1)}, u32[]{:S(2)}, u32[]{:S(2)}) collective-permute-start(bf16[64,3072]{1,0:T(8,128)(2,1)S(1)} %get-tuple-element.10), channel_id=1, source_target_pairs={{0,4},{2,6},{4,0},{6,2},{1,5},{3,7},{5,1},{7,3},{8,12},{10,14},{12... | collective-permute-start | bytes 1179656 | tf_op jit(solution)/shard_map/ppermute | solution.py:356
  100.3 17.9 %collective-permute-start.5 = (bf16[64,3072]{1,0:T(8,128)(2,1)S(1)}, bf16[64,3072]{1,0:T(8,128)(2,1)}, u32[]{:S(2)}, u32[]{:S(2)}) collective-permute-start(bf16[64,3072]{1,0:T(8,128)(2,1)S(1)} %get-tuple-element.9), channel_id=1, source_target_pairs={{0,6},{2,0},{4,2},{6,4},{1,7},{3,1},{5,3},{7,5},{8,14},{10,8},{12,... | collective-permute-start | bytes 1179656 | tf_op jit(solution)/shard_map/ppermute | solution.py:356

commit v13 on v11

--- a/solution.py
+++ b/solution.py
@@ -219,67 +219,61 @@
     ).astype(jnp.bfloat16)
 
 
-def projection_kernel(part_ref, meta_ref, x_ref, gain_ref, w_ref, freq_ref, *refs, parts):
-    out_refs = refs[:-1]
-    normed_ref = refs[-1]
-    step = pl.program_id(0)
-
-    @pl.when(step == 0)
-    def _():
-        inputs = x_ref[...].astype(jnp.float32)
-        inverse_rms = lax.rsqrt(jnp.mean(inputs * inputs, axis=-1, keepdims=True) + 1e-05)
-        gain = gain_ref[...].astype(jnp.float32)
-        normed_ref[...] = (inputs * inverse_rms * gain).astype(jnp.bfloat16)
-
-    weights = w_ref[0]
-    plain = jnp.dot(normed_ref[...], weights, preferred_element_type=jnp.float32)
-
-    def rotated():
-        rows, features = plain.shape
+def projection_kernel(meta_ref, x_ref, gain_ref, freq_ref, *refs, parts):
+    w_refs = refs[: len(parts)]
+    out_ref = refs[len(parts)]
+    rows = x_ref.shape[0]
+    tok_count = rows * pl.num_programs(0)
+    inputs = x_ref[...].astype(jnp.float32)
+    inverse_rms = lax.rsqrt(jnp.mean(inputs * inputs, axis=-1, keepdims=True) + 1e-05)
+    gain = gain_ref[...].astype(jnp.float32)
+    normed = (inputs * inverse_rms * gain).astype(jnp.bfloat16)
+    for index, part in enumerate(parts):
+        plain = jnp.dot(normed, w_refs[index][0], preferred_element_type=jnp.float32)
+        if part == 2:
+            out_ref[index] = plain.astype(out_ref.dtype)
+            continue
+        features = plain.shape[1]
         half = HD // 2
         group_len = meta_ref[0]
         group_requests = meta_ref[1]
-        row = lax.broadcasted_iota(jnp.int32, (rows, 1), 0)
-        request = request_of(row, group_requests, rows)
+        row = pl.program_id(0) * rows + lax.broadcasted_iota(jnp.int32, (rows, 1), 0)
+        request = request_of(row, group_requests, tok_count)
         count = (jnp.zeros((rows, 1), jnp.int32) + group_requests).astype(jnp.float32)
-        first = jnp.ceil((request * rows).astype(jnp.float32) / count).astype(jnp.int32)
+        first = jnp.ceil((request * tok_count).astype(jnp.float32) / count).astype(jnp.int32)
         positions = (group_len + row - first).astype(jnp.float32)
         angles = positions * freq_ref[...]
         lane = lax.broadcasted_iota(jnp.int32, plain.shape, 1)
         ahead = pltpu.roll(plain, features - half, 1)
         behind = pltpu.roll(plain, half, 1)
         paired = jnp.where(lane % HD < half, -ahead, behind)
-        return (plain * jnp.cos(angles) + paired * jnp.sin(angles)).astype(jnp.bfloat16)
-
-    for index, part in enumerate(parts):
-
-        @pl.when(step == index)
-        def _():
-            value = rotated() if part < 2 else plain.astype(jnp.bfloat16)
-            out_refs[0][index] = value
+        rotated = plain * jnp.cos(angles) + paired * jnp.sin(angles)
+        out_ref[index] = rotated.astype(out_ref.dtype)
 
 
 def project(meta, tokens, gain, weights, frequency, parts):
     _, width, features = weights.shape
-    rows = tokens.shape[0]
-    table = jnp.asarray(parts, jnp.int32)
-    out = jax.ShapeDtypeStruct((len(parts), rows, features), jnp.bfloat16)
+    tok_count = tokens.shape[0]
+    rows = 128 if tok_count % 128 == 0 else tok_count
+
+    def weight_spec(part):
+        return pl.BlockSpec((1, width, features), lambda r, m: (part, 0, 0))
+
     return pl.pallas_call(
         functools.partial(projection_kernel, parts=parts),
-        out_shape=out,
+        out_shape=jax.ShapeDtypeStruct((len(parts), tok_count, features), jnp.bfloat16),
         grid_spec=pltpu.PrefetchScalarGridSpec(
-            num_scalar_prefetch=2,
-            grid=(len(parts),),
+            num_scalar_prefetch=1,
+            grid=(tok_count // rows,),
             in_specs=[
-                pl.BlockSpec((rows, width), lambda s, t, m: (0, 0)),
-                pl.BlockSpec((1, width), lambda s, t, m: (0, 0)),
-                pl.BlockSpec((1, width, features), lambda s, t, m: (t[s], 0, 0)),
-                pl.BlockSpec((1, features), lambda s, t, m: (0, 0)),
-            ],
-            out_specs=pl.BlockSpec((len(parts), rows, features), lambda s, t, m: (0, 0, 0)),
-            scratch_shapes=[pltpu.VMEM((rows, width), jnp.bfloat16)],
+                pl.BlockSpec((rows, width), lambda r, m: (r, 0)),
+                pl.BlockSpec((1, width), lambda r, m: (0, 0)),
+                pl.BlockSpec((1, features), lambda r, m: (0, 0)),
+            ]
+            + [weight_spec(part) for part in parts],
+            out_specs=pl.BlockSpec((len(parts), rows, features), lambda r, m: (0, r, 0)),
         ),
-    )(table, meta, tokens, gain, weights, frequency)
+    )(meta, tokens, gain, frequency, *(weights for _ in parts))
 
 
 def local(tokens, norm_gain, w_qkv, w_out, kv_cache, cached_lengths, requests, block_start):

time: 138 us -> 137 us (level)
  Pallas kernels: 66.2 us -> 63.9 us
    pallas_call x2, Pallas kernels: 22.5 us -> 20.8 us  [project(): pl.pallas_call(functools.partial(projection_kernel, parts=parts), out_sha...]
  transfers between devices with their start and end apart: 7 -> 7, of which waited for: 5 -> 5; matrix products, arithmetic and copies ran while one was open for 11% -> 11% of each run, Pallas kernels for 42% -> 41%
where the time goes in v13:
time: 137 us
  Pallas kernels  63.9 us (47%)
  waiting for transfers between devices  34.3 us (25%)
  starting transfers between devices  14.6 us (11%)
  local copies, waits for them, and re-layouts  13.1 us (10%)
  other arithmetic  8.03 us (6%)
  matrix products  2.79 us (2%)
    pallas_call x1, Pallas kernels, attend(): pl.pallas_call(attention_kernel, out_shape=jax.ShapeDtypeStruct(queries.s...  34.9 us
    pallas_call x2, Pallas kernels, project(): pl.pallas_call(functools.partial(projection_kernel, parts=parts), out_sha...  20.8 us
    ppermute x3, waiting for transfers between devices, local(): summed = summed + lax.ppermute(chunk, 'x', pairs).astype(jnp.float32)  16.5 us
    all_to_all x1, waiting for transfers between devices, local(): received = lax.all_to_all(joined, 'seq', 0, 0, tiled=True)  12.1 us
    unnamed x7, local copies, waits for them, and re-layouts  8.68 us
    all_to_all x1, starting transfers between devices, local(): received = lax.all_to_all(joined, 'seq', 0, 0, tiled=True)  8.28 us
    pallas_call x1, Pallas kernels, relay(): pl.pallas_call(functools.partial(relay_kernel, new_blocks=new_blocks), ou...  8.2 us
    ppermute x3, starting transfers between devices, local(): summed = summed + lax.ppermute(chunk, 'x', pairs).astype(jnp.float32)  5.67 us
  transfers between devices with their start and end apart: 7, of which 5 were waited for; matrix products, arithmetic and copies ran while one was open for 11% of the time, Pallas kernels for 41%

profile of v13, /device:TPU:0, one launch (start us, length us, event | category | flops | bytes accessed | tf_op | source)
XLA Modules:
  0.0 137.4 jit_solution(10067671699385918488)
XLA Ops:
  0.6 0.0 copy-start
  0.6 0.1 collective-permute-start
  0.7 1.4 %reshape.24.gain_ref = bf16[1,3072]{1,0:T(2,128)(2,1)} reshape(bf16[3072]{0:T(1024)(128)(2,1)} %param.9) | data formatting | bytes 12288 | tf_op jit(solution)/shard_map/reshape | solution.py:302
  2.2 0.7 reshape_tile.5.freq_ref
  2.9 0.7 pad_add_fusion
  3.6 0.2 dynamic-slice_reduce_fusion
  3.8 0.6 pad_add_fusion.1.meta_ref
  4.4 11.4 %shard_map.96.refs_1_.refs_5_.refs_9_.refs_13_.kn_ref.vn_ref = bf16[2,512,384]{2,1,0:T(8,128)(2,1)} custom-call(s32[4]{0:T(128)} %pad_add_fusion.1.meta_ref, bf16[512,3072]{1,0:T(8,128)(2,1)} %x_ref.3, bf16[1,3072]{1,0:T(2,128)(2,1)} %reshape.24.gain_ref, f32[1,384]{1,0:T(1,128)} %reshape_tile.5.freq_ref, bf16[3,3072,384]{2,1,0:T(8,128)(2,1)} %bitcast.34, ...), custom_call_target="tpu_custom_call" | custom-call | tf_op jit(solution)/shard_map/pallas_call | solution.py:262
  15.8 0.3 collective-permute-start.1
  16.1 2.2 %collective-permute-done.1.refs_3_.refs_7_.refs_11_.refs_15_ = bf16[2,512,384]{2,1,0:T(8,128)(2,1)S(1)} collective-permute-done((bf16[2,512,384]{2,1,0:T(8,128)(2,1)}, bf16[2,512,384]{2,1,0:T(8,128)(2,1)S(1)}, u32[]{:S(2)}, u32[]{:S(2)}) %collective-permute-start.1) | collective-permute-done | bytes 786464 | tf_op jit(solution)/shard_map/ppermute | solution.py:308
  18.3 0.0 copy-start.1
  18.3 0.0 collective-permute-done.refs_2_.refs_6_.refs_10_.refs_14_
  18.3 0.9 copy-done.1
  19.2 8.2 %shard_map.97 = bf16[16,2,128,768]{3,2,1,0:T(8,128)(2,1)} custom-call(s32[4]{0:T(128)} %pad_add_fusion.1.meta_ref, bf16[2,1,3584,384]{3,2,1,0:T(8,128)(2,1)} %vc_ref.1, bf16[2,512,384]{2,1,0:T(8,128)(2,1)} %shard_map.96.refs_1_.refs_5_.refs_9_.refs_13_.kn_ref.vn_ref, bf16[2,1,3584,384]{3,2,1,0:T(8,128)(2,1)} %collective-permute-done.refs_2_.refs_6_.refs_10_.refs_14_, ...), custom_call_target="tpu_custom_call" | custom-call | tf_op jit(solution)/shard_map/pallas_call | solution.py:196
  27.4 8.3 %all-to-all-start = ((bf16[16,2,128,768]{3,2,1,0:T(8,128)(2,1)}), bf16[16,2,128,768]{3,2,1,0:T(8,128)(2,1)}, u32[]{:S(2)}, u32[]{:S(2)}) async-start(bf16[16,2,128,768]{3,2,1,0:T(8,128)(2,1)} %shard_map.97), calls=%async_computation | async-start | bytes 12582912 | tf_op jit(solution)/shard_map/all_to_all | solution.py:312
  35.6 9.4 %shard_map.95 = bf16[1,512,384]{2,1,0:T(8,128)(2,1)} custom-call(s32[4]{0:T(128)} %pad_add_fusion.1.meta_ref, bf16[512,3072]{1,0:T(8,128)(2,1)} %x_ref.3, bf16[1,3072]{1,0:T(2,128)(2,1)} %reshape.24.gain_ref, f32[1,384]{1,0:T(1,128)} %reshape_tile.5.freq_ref, bf16[3,3072,384]{2,1,0:T(8,128)(2,1)} %bitcast.36), custom_call_target="tpu_custom_call" | custom-call | tf_op jit(solution)/shard_map/pallas_call | solution.py:262
  45.0 34.9 %shard_map.98 = bf16[512,384]{1,0:T(8,128)(2,1)} custom-call(s32[4]{0:T(128)} %pad_add_fusion.1.meta_ref, bf16[512,384]{1,0:T(8,128)(2,1)} %bitcast.39, bf16[2,1,3584,384]{3,2,1,0:T(8,128)(2,1)} %vc_ref.1, bf16[2,1,3584,384]{3,2,1,0:T(8,128)(2,1)} %vc_ref.1, bf16[2,512,384]{2,1,0:T(8,128)(2,1)} %shard_map.96.refs_1_.refs_5_.refs_9_.refs_13_.kn_ref.vn_ref, ...), custom_call_target="tpu_custom_call" | custom-call | tf_op jit(solution)/shard_map/pallas_call | solution.py:124
  79.9 0.0 copy-done
  79.9 2.8 %convolution_convert_fusion = bf16[512,3072]{1,0:T(8,128)(2,1)S(1)} fusion(bf16[512,384]{1,0:T(8,128)(2,1)} %shard_map.98, bf16[384,3072]{1,0:T(8,128)(2,1)S(1)} %copy-done), kind=kOutput, calls=%fused_computation | convolution fusion | flops 1209532416 | bytes 5898240 | tf_op jit(solution)/shard_map/dot_general | solution.py:317
  82.7 0.0 copy-start.2
  82.8 1.6 %copy-done.2 = bf16[512,3072]{1,0:T(8,128)(2,1)} copy-done((bf16[512,3072]{1,0:T(8,128)(2,1)}, bf16[512,3072]{1,0:T(8,128)(2,1)S(1)}, u32[]{:S(2)}) %copy-start.2) | copy-done | bytes 3145752
  84.4 1.3 dynamic-slice_bitcast_fusion
  85.7 0.2 collective-permute-start.2
  85.9 3.5 %collective-permute-done.2 = bf16[4,64,3072]{2,1,0:T(8,128)(2,1)} collective-permute-done((bf16[4,64,3072]{2,1,0:T(8,128)(2,1)}, bf16[4,64,3072]{2,1,0:T(8,128)(2,1)}, u32[]{:S(2)}, u32[]{:S(2)}) %collective-permute-start.2) | collective-permute-done | bytes 1572896 | tf_op jit(solution)/shard_map/ppermute | solution.py:323
  89.4 4.3 %fusion.4 = (bf16[4,64,3072]{2,1,0:T(8,128)(2,1)S(1)}, f32[4,64,3072]{2,1,0:T(8,128)}) fusion(bf16[4,64,3072]{2,1,0:T(8,128)(2,1)} %collective-permute-done.2, bf16[4,2,64,3072]{3,2,1,0:T(8,128)(2,1)} %bitcast.38, s32[]{:T(128)S(6)} %select_n.45), kind=kLoop, calls=%fused_computation.15 | loop fusion | flops 3145728 | bytes 7864324 | tf_op jit(solution)/shard_map/convert_element_type | solution.py:326
  93.7 0.8 dynamic-slice_bitcast_fusion.3
  94.5 1.5 %collective-permute-start.3 = (bf16[64,3072]{1,0:T(8,128)(2,1)}, bf16[64,3072]{1,0:T(8,128)(2,1)S(1)}, u32[]{:S(2)}, u32[]{:S(2)}) collective-permute-start(bf16[64,3072]{1,0:T(8,128)(2,1)} %get-tuple-element.12), channel_id=1, source_target_pairs={{0,2},{2,4},{4,6},{6,0},{1,3},{3,5},{5,7},{7,1},{8,10},{10,12},{12... | collective-permute-start | bytes 1179656 | tf_op jit(solution)/shard_map/ppermute | solution.py:332
  96.0 2.7 %collective-permute-start.4 = (bf16[64,3072]{1,0:T(8,128)(2,1)S(1)}, bf16[64,3072]{1,0:T(8,128)(2,1)}, u32[]{:S(2)}, u32[]{:S(2)}) collective-permute-start(bf16[64,3072]{1,0:T(8,128)(2,1)S(1)} %get-tuple-element.14), channel_id=1, source_target_pairs={{0,4},{2,6},{4,0},{6,2},{1,5},{3,7},{5,1},{7,3},{8,12},{10,14},{12... | collective-permute-start | bytes 1179656 | tf_op jit(solution)/shard_map/ppermute | solution.py:332
  98.8 1.4 %collective-permute-start.5 = (bf16[64,3072]{1,0:T(8,128)(2,1)S(1)}, bf16[64,3072]{1,0:T(8,128)(2,1)}, u32[]{:S(2)}, u32[]{:S(2)}) collective-permute-start(bf16[64,3072]{1,0:T(8,128)(2,1)S(1)} %get-tuple-element.13), channel_id=1, source_target_pairs={{0,6},{2,0},{4,2},{6,4},{1,7},{3,1},{5,3},{7,5},{8,14},{10,8},{12,... | collective-permute-start | bytes 1179656 | tf_op jit(solution)/shard_map/ppermute | solution.py:332
  100.2 7.0 %collective-permute-done.3 = bf16[64,3072]{1,0:T(8,128)(2,1)S(1)} collective-permute-done((bf16[64,3072]{1,0:T(8,128)(2,1)}, bf16[64,3072]{1,0:T(8,128)(2,1)S(1)}, u32[]{:S(2)}, u32[]{:S(2)}) %collective-permute-start.3) | collective-permute-done | bytes 393248 | tf_op jit(solution)/shard_map/ppermute | solution.py:332
  107.2 9.5 %collective-permute-done.4 = bf16[64,3072]{1,0:T(8,128)(2,1)} collective-permute-done((bf16[64,3072]{1,0:T(8,128)(2,1)S(1)}, bf16[64,3072]{1,0:T(8,128)(2,1)}, u32[]{:S(2)}, u32[]{:S(2)}) %collective-permute-start.4) | collective-permute-done | bytes 393248 | tf_op jit(solution)/shard_map/ppermute | solution.py:332
  116.7 0.0 collective-permute-done.5
  116.7 2.4 %fusion.3 = bf16[64,3072]{1,0:T(8,128)(2,1)} fusion(bf16[64,3072]{1,0:T(8,128)(2,1)} %collective-permute-done.5, bf16[64,3072]{1,0:T(8,128)(2,1)} %collective-permute-done.4, bf16[64,3072]{1,0:T(8,128)(2,1)S(1)} %collective-permute-done.3, f32[4,64,3072]{2,1,0:T(8,128)} %get-tuple-element.11, s32[]{:T(128)S(6)} %select_n.47, bf16[512,3072]{1,0:T(8,128)(2,1)} %x_ref.3, ...), kind=kLoop, calls=%fused_computation.7 | loop fusion | flops 1769472 | bytes 2752520 | tf_op jit(solution)/shard_map/convert_element_type | solution.py:334
  119.1 12.1 %all-to-all-done = bf16[16,2,128,768]{3,2,1,0:T(8,128)(2,1)} async-done(((bf16[16,2,128,768]{3,2,1,0:T(8,128)(2,1)}), bf16[16,2,128,768]{3,2,1,0:T(8,128)(2,1)}, u32[]{:S(2)}, u32[]{:S(2)}) %all-to-all-start) | async-done | bytes 6291488 | tf_op jit(solution)/shard_map/all_to_all | solution.py:312
  131.2 6.1 %copy.11 = bf16[2,1,16,1,128,768]{5,4,3,2,1,0:T(8,128)(2,1)} copy(bf16[2,1,16,1,128,768]{5,4,0,2,3,1:T(8,128)(2,1)} %bitcast.14) | data formatting | bytes 12582912
  (2 shorter events, 0.0 us)
Async XLA Ops:
  0.6 79.3 %copy-start = (bf16[384,3072]{1,0:T(8,128)(2,1)S(1)}, bf16[384,3072]{1,0:T(8,128)(2,1)}, u32[]{:S(2)}) copy-start(bf16[384,3072]{1,0:T(8,128)(2,1)} %param.11) | copy-start | bytes 7077892
  0.6 17.6 %collective-permute-start = (bf16[2,1,3584,384]{3,2,1,0:T(8,128)(2,1)}, bf16[2,1,3584,384]{3,2,1,0:T(8,128)(2,1)}, u32[]{:S(2)}, u32[]{:S(2)}) collective-permute-start(bf16[2,1,3584,384]{3,2,1,0:T(8,128)(2,1)} %vc_ref.1), channel_id=1, source_target_pairs={{0,1},{1,0},{2,3},{3,2},{4,5},{5,4},{6,7},{7,6},{8,9},{9,8},{10,11... | collective-permute-start | bytes 16515080 | tf_op jit(solution)/shard_map/ppermute | solution.py:305
  15.8 2.5 %collective-permute-start.1 = (bf16[2,512,384]{2,1,0:T(8,128)(2,1)}, bf16[2,512,384]{2,1,0:T(8,128)(2,1)S(1)}, u32[]{:S(2)}, u32[]{:S(2)}) collective-permute-start(bf16[2,512,384]{2,1,0:T(8,128)(2,1)} %shard_map.96.refs_1_.refs_5_.refs_9_.refs_13_.kn_ref.vn_ref), channel_id=1, source_target_pairs={{0,1},{1,0},{2,3},{3,2},{4,5},{5,4},{6,7},{7,6},{8,9},{9,8},{10,11... | collective-permute-start | bytes 2359304 | tf_op jit(solution)/shard_map/ppermute | solution.py:308
  18.3 0.9 copy-start.1
  27.4 103.9 %all-to-all-start = ((bf16[16,2,128,768]{3,2,1,0:T(8,128)(2,1)}), bf16[16,2,128,768]{3,2,1,0:T(8,128)(2,1)}, u32[]{:S(2)}, u32[]{:S(2)}) async-start(bf16[16,2,128,768]{3,2,1,0:T(8,128)(2,1)} %shard_map.97), calls=%async_computation | async-start | bytes 12582912 | tf_op jit(solution)/shard_map/all_to_all | solution.py:312
  82.7 1.7 %copy-start.2 = (bf16[512,3072]{1,0:T(8,128)(2,1)}, bf16[512,3072]{1,0:T(8,128)(2,1)S(1)}, u32[]{:S(2)}) copy-start(bf16[512,3072]{1,0:T(8,128)(2,1)S(1)} %convolution_convert_fusion) | copy-start | bytes 9437188
  85.7 3.8 %collective-permute-start.2 = (bf16[4,64,3072]{2,1,0:T(8,128)(2,1)}, bf16[4,64,3072]{2,1,0:T(8,128)(2,1)}, u32[]{:S(2)}, u32[]{:S(2)}) collective-permute-start(bf16[4,64,3072]{2,1,0:T(8,128)(2,1)} %dynamic-slice_bitcast_fusion), channel_id=1, source_target_pairs={{0,1},{1,0},{2,3},{3,2},{4,5},{5,4},{6,7},{7,6},{8,9},{9,8},{10,11... | collective-permute-start | bytes 4718600 | tf_op jit(solution)/shard_map/ppermute | solution.py:323
  94.5 12.7 %collective-permute-start.3 = (bf16[64,3072]{1,0:T(8,128)(2,1)}, bf16[64,3072]{1,0:T(8,128)(2,1)S(1)}, u32[]{:S(2)}, u32[]{:S(2)}) collective-permute-start(bf16[64,3072]{1,0:T(8,128)(2,1)} %get-tuple-element.12), channel_id=1, source_target_pairs={{0,2},{2,4},{4,6},{6,0},{1,3},{3,5},{5,7},{7,1},{8,10},{10,12},{12... | collective-permute-start | bytes 1179656 | tf_op jit(solution)/shard_map/ppermute | solution.py:332
  96.0 20.7 %collective-permute-start.4 = (bf16[64,3072]{1,0:T(8,128)(2,1)S(1)}, bf16[64,3072]{1,0:T(8,128)(2,1)}, u32[]{:S(2)}, u32[]{:S(2)}) collective-permute-start(bf16[64,3072]{1,0:T(8,128)(2,1)S(1)} %get-tuple-element.14), channel_id=1, source_target_pairs={{0,4},{2,6},{4,0},{6,2},{1,5},{3,7},{5,1},{7,3},{8,12},{10,14},{12... | collective-permute-start | bytes 1179656 | tf_op jit(solution)/shard_map/ppermute | solution.py:332
  98.8 17.9 %collective-permute-start.5 = (bf16[64,3072]{1,0:T(8,128)(2,1)S(1)}, bf16[64,3072]{1,0:T(8,128)(2,1)}, u32[]{:S(2)}, u32[]{:S(2)}) collective-permute-start(bf16[64,3072]{1,0:T(8,128)(2,1)S(1)} %get-tuple-element.13), channel_id=1, source_target_pairs={{0,6},{2,0},{4,2},{6,4},{1,7},{3,1},{5,3},{7,5},{8,14},{10,8},{12,... | collective-permute-start | bytes 1179656 | tf_op jit(solution)/shard_map/ppermute | solution.py:332

commit v14 on v13

--- a/solution.py
+++ b/solution.py
@@ -226,7 +226,7 @@
     tok_count = rows * pl.num_programs(0)
     inputs = x_ref[...].astype(jnp.float32)
     inverse_rms = lax.rsqrt(jnp.mean(inputs * inputs, axis=-1, keepdims=True) + 1e-05)
-    gain = gain_ref[...].astype(jnp.float32)
+    gain = gain_ref[...].astype(jnp.float32).reshape(1, inputs.shape[1])
     normed = (inputs * inverse_rms * gain).astype(jnp.bfloat16)
     for index, part in enumerate(parts):
         plain = jnp.dot(normed, w_refs[index][0], preferred_element_type=jnp.float32)
@@ -267,7 +267,7 @@
             grid=(tok_count // rows,),
             in_specs=[
                 pl.BlockSpec((rows, width), lambda r, m: (r, 0)),
-                pl.BlockSpec((1, width), lambda r, m: (0, 0)),
+                pl.BlockSpec((width,), lambda r, m: (0,)),
                 pl.BlockSpec((1, features), lambda r, m: (0, 0)),
             ]
             + [weight_spec(part) for part in parts],
@@ -299,7 +299,7 @@
         jnp.arange(half_size, dtype=jnp.float32) * (-2.0 * math.log(10000.0) / HD)
     )
     frequency = jnp.tile(frequency, features // half_size).reshape(1, features)
-    gain = norm_gain.reshape(1, model_width)
+    gain = norm_gain
     core = lax.axis_index("core")
     swap_cores = [(0, 1), (1, 0)]
     mate_cache = lax.ppermute(kv_cache, "core", swap_cores)

time: 137 us -> 136 us (level)
  local copies, waits for them, and re-layouts: 13.1 us -> 11.6 us
    reshape x1 -> x0, local copies, waits for them, and re-layouts: 1.44 us -> none  [local(): gain = norm_gain.reshape(1, model_width)]
  transfers between devices with their start and end apart: 7 -> 7, of which waited for: 5 -> 5; matrix products, arithmetic and copies ran while one was open for 11% -> 10% of each run, Pallas kernels for 41% -> 41%
where the time goes in v14:
time: 136 us; the launch traced here: 135 us
  Pallas kernels  63.6 us (47%)
  waiting for transfers between devices  33.9 us (25%)
  starting transfers between devices  14.8 us (11%)
  local copies, waits for them, and re-layouts  11.6 us (9%)
  other arithmetic  8.03 us (6%)
  matrix products  2.79 us (2%)
    pallas_call x1, Pallas kernels, attend(): pl.pallas_call(attention_kernel, out_shape=jax.ShapeDtypeStruct(queries.s...  34.9 us
    pallas_call x2, Pallas kernels, project(): pl.pallas_call(functools.partial(projection_kernel, parts=parts), out_sha...  20.9 us
    ppermute x3, waiting for transfers between devices, local(): summed = summed + lax.ppermute(chunk, 'x', pairs).astype(jnp.float32)  16.4 us
    all_to_all x1, waiting for transfers between devices, local(): received = lax.all_to_all(joined, 'seq', 0, 0, tiled=True)  11.7 us
    unnamed x7, local copies, waits for them, and re-layouts  8.68 us
    all_to_all x1, starting transfers between devices, local(): received = lax.all_to_all(joined, 'seq', 0, 0, tiled=True)  8.46 us
    pallas_call x1, Pallas kernels, relay(): pl.pallas_call(functools.partial(relay_kernel, new_blocks=new_blocks), ou...  7.78 us
    ppermute x3, starting transfers between devices, local(): summed = summed + lax.ppermute(chunk, 'x', pairs).astype(jnp.float32)  5.65 us
  transfers between devices with their start and end apart: 7, of which 5 were waited for; matrix products, arithmetic and copies ran while one was open for 10% of the time, Pallas kernels for 41%

profile of v14, /device:TPU:0, one launch (start us, length us, event | category | flops | bytes accessed | tf_op | source)
XLA Modules:
  0.0 135.4 jit_solution(17975530306775604341)
XLA Ops:
  0.6 0.0 copy-start
  0.6 0.1 collective-permute-start
  0.8 0.7 reshape_tile.5.freq_ref
  1.4 0.7 pad_add_fusion
  2.1 0.2 dynamic-slice_reduce_fusion
  2.3 0.6 pad_add_fusion.1.meta_ref
  2.9 11.5 %shard_map.96.refs_1_.refs_5_.refs_9_.refs_13_.kn_ref.vn_ref = bf16[2,512,384]{2,1,0:T(8,128)(2,1)} custom-call(s32[4]{0:T(128)} %pad_add_fusion.1.meta_ref, bf16[512,3072]{1,0:T(8,128)(2,1)} %x_ref.3, bf16[3072]{0:T(1024)(128)(2,1)} %gain_ref.3, f32[1,384]{1,0:T(1,128)} %reshape_tile.5.freq_ref, bf16[3,3072,384]{2,1,0:T(8,128)(2,1)} %bitcast.34, ...), custom_call_target="tpu_custom_call" | custom-call | tf_op jit(solution)/shard_map/pallas_call | solution.py:262
  14.4 0.5 collective-permute-start.1
  14.9 2.1 %collective-permute-done.1.refs_3_.refs_7_.refs_11_.refs_15_ = bf16[2,512,384]{2,1,0:T(8,128)(2,1)S(1)} collective-permute-done((bf16[2,512,384]{2,1,0:T(8,128)(2,1)}, bf16[2,512,384]{2,1,0:T(8,128)(2,1)S(1)}, u32[]{:S(2)}, u32[]{:S(2)}) %collective-permute-start.1) | collective-permute-done | bytes 786464 | tf_op jit(solution)/shard_map/ppermute | solution.py:308
  17.0 0.0 copy-start.1
  17.0 0.0 collective-permute-done.refs_2_.refs_6_.refs_10_.refs_14_
  17.0 0.9 copy-done.1
  17.9 7.8 %shard_map.97 = bf16[16,2,128,768]{3,2,1,0:T(8,128)(2,1)} custom-call(s32[4]{0:T(128)} %pad_add_fusion.1.meta_ref, bf16[2,1,3584,384]{3,2,1,0:T(8,128)(2,1)} %vc_ref.1, bf16[2,512,384]{2,1,0:T(8,128)(2,1)} %shard_map.96.refs_1_.refs_5_.refs_9_.refs_13_.kn_ref.vn_ref, bf16[2,1,3584,384]{3,2,1,0:T(8,128)(2,1)} %collective-permute-done.refs_2_.refs_6_.refs_10_.refs_14_, ...), custom_call_target="tpu_custom_call" | custom-call | tf_op jit(solution)/shard_map/pallas_call | solution.py:196
  25.7 8.5 %all-to-all-start = ((bf16[16,2,128,768]{3,2,1,0:T(8,128)(2,1)}), bf16[16,2,128,768]{3,2,1,0:T(8,128)(2,1)}, u32[]{:S(2)}, u32[]{:S(2)}) async-start(bf16[16,2,128,768]{3,2,1,0:T(8,128)(2,1)} %shard_map.97), calls=%async_computation | async-start | bytes 12582912 | tf_op jit(solution)/shard_map/all_to_all | solution.py:312
  34.1 9.4 %shard_map.95 = bf16[1,512,384]{2,1,0:T(8,128)(2,1)} custom-call(s32[4]{0:T(128)} %pad_add_fusion.1.meta_ref, bf16[512,3072]{1,0:T(8,128)(2,1)} %x_ref.3, bf16[3072]{0:T(1024)(128)(2,1)} %gain_ref.3, f32[1,384]{1,0:T(1,128)} %reshape_tile.5.freq_ref, bf16[3,3072,384]{2,1,0:T(8,128)(2,1)} %bitcast.36), custom_call_target="tpu_custom_call" | custom-call | tf_op jit(solution)/shard_map/pallas_call | solution.py:262
  43.6 34.9 %shard_map.98 = bf16[512,384]{1,0:T(8,128)(2,1)} custom-call(s32[4]{0:T(128)} %pad_add_fusion.1.meta_ref, bf16[512,384]{1,0:T(8,128)(2,1)} %bitcast.39, bf16[2,1,3584,384]{3,2,1,0:T(8,128)(2,1)} %vc_ref.1, bf16[2,1,3584,384]{3,2,1,0:T(8,128)(2,1)} %vc_ref.1, bf16[2,512,384]{2,1,0:T(8,128)(2,1)} %shard_map.96.refs_1_.refs_5_.refs_9_.refs_13_.kn_ref.vn_ref, ...), custom_call_target="tpu_custom_call" | custom-call | tf_op jit(solution)/shard_map/pallas_call | solution.py:124
  78.5 0.0 copy-done
  78.5 2.8 %convolution_convert_fusion = bf16[512,3072]{1,0:T(8,128)(2,1)S(1)} fusion(bf16[512,384]{1,0:T(8,128)(2,1)} %shard_map.98, bf16[384,3072]{1,0:T(8,128)(2,1)S(1)} %copy-done), kind=kOutput, calls=%fused_computation | convolution fusion | flops 1209532416 | bytes 5898240 | tf_op jit(solution)/shard_map/dot_general | solution.py:317
  81.3 0.0 copy-start.2
  81.3 1.6 %copy-done.2 = bf16[512,3072]{1,0:T(8,128)(2,1)} copy-done((bf16[512,3072]{1,0:T(8,128)(2,1)}, bf16[512,3072]{1,0:T(8,128)(2,1)S(1)}, u32[]{:S(2)}) %copy-start.2) | copy-done | bytes 3145752
  82.9 1.3 dynamic-slice_bitcast_fusion
  84.2 0.1 collective-permute-start.2
  84.3 3.6 %collective-permute-done.2 = bf16[4,64,3072]{2,1,0:T(8,128)(2,1)} collective-permute-done((bf16[4,64,3072]{2,1,0:T(8,128)(2,1)}, bf16[4,64,3072]{2,1,0:T(8,128)(2,1)}, u32[]{:S(2)}, u32[]{:S(2)}) %collective-permute-start.2) | collective-permute-done | bytes 1572896 | tf_op jit(solution)/shard_map/ppermute | solution.py:323
  88.0 4.3 %fusion.4 = (bf16[4,64,3072]{2,1,0:T(8,128)(2,1)S(1)}, f32[4,64,3072]{2,1,0:T(8,128)}) fusion(bf16[4,64,3072]{2,1,0:T(8,128)(2,1)} %collective-permute-done.2, bf16[4,2,64,3072]{3,2,1,0:T(8,128)(2,1)} %bitcast.38, s32[]{:T(128)S(6)} %select_n.45), kind=kLoop, calls=%fused_computation.15 | loop fusion | flops 3145728 | bytes 7864324 | tf_op jit(solution)/shard_map/convert_element_type | solution.py:326
  92.2 0.8 dynamic-slice_bitcast_fusion.3
  93.1 1.5 %collective-permute-start.3 = (bf16[64,3072]{1,0:T(8,128)(2,1)}, bf16[64,3072]{1,0:T(8,128)(2,1)S(1)}, u32[]{:S(2)}, u32[]{:S(2)}) collective-permute-start(bf16[64,3072]{1,0:T(8,128)(2,1)} %get-tuple-element.12), channel_id=1, source_target_pairs={{0,2},{2,4},{4,6},{6,0},{1,3},{3,5},{5,7},{7,1},{8,10},{10,12},{12... | collective-permute-start | bytes 1179656 | tf_op jit(solution)/shard_map/ppermute | solution.py:332
  94.6 2.7 %collective-permute-start.4 = (bf16[64,3072]{1,0:T(8,128)(2,1)S(1)}, bf16[64,3072]{1,0:T(8,128)(2,1)}, u32[]{:S(2)}, u32[]{:S(2)}) collective-permute-start(bf16[64,3072]{1,0:T(8,128)(2,1)S(1)} %get-tuple-element.14), channel_id=1, source_target_pairs={{0,4},{2,6},{4,0},{6,2},{1,5},{3,7},{5,1},{7,3},{8,12},{10,14},{12... | collective-permute-start | bytes 1179656 | tf_op jit(solution)/shard_map/ppermute | solution.py:332
  97.3 1.4 %collective-permute-start.5 = (bf16[64,3072]{1,0:T(8,128)(2,1)S(1)}, bf16[64,3072]{1,0:T(8,128)(2,1)}, u32[]{:S(2)}, u32[]{:S(2)}) collective-permute-start(bf16[64,3072]{1,0:T(8,128)(2,1)S(1)} %get-tuple-element.13), channel_id=1, source_target_pairs={{0,6},{2,0},{4,2},{6,4},{1,7},{3,1},{5,3},{7,5},{8,14},{10,8},{12,... | collective-permute-start | bytes 1179656 | tf_op jit(solution)/shard_map/ppermute | solution.py:332
  98.7 6.9 %collective-permute-done.3 = bf16[64,3072]{1,0:T(8,128)(2,1)S(1)} collective-permute-done((bf16[64,3072]{1,0:T(8,128)(2,1)}, bf16[64,3072]{1,0:T(8,128)(2,1)S(1)}, u32[]{:S(2)}, u32[]{:S(2)}) %collective-permute-start.3) | collective-permute-done | bytes 393248 | tf_op jit(solution)/shard_map/ppermute | solution.py:332
  105.6 9.5 %collective-permute-done.4 = bf16[64,3072]{1,0:T(8,128)(2,1)} collective-permute-done((bf16[64,3072]{1,0:T(8,128)(2,1)S(1)}, bf16[64,3072]{1,0:T(8,128)(2,1)}, u32[]{:S(2)}, u32[]{:S(2)}) %collective-permute-start.4) | collective-permute-done | bytes 393248 | tf_op jit(solution)/shard_map/ppermute | solution.py:332
  115.2 0.0 collective-permute-done.5
  115.2 2.4 %fusion.3 = bf16[64,3072]{1,0:T(8,128)(2,1)} fusion(bf16[64,3072]{1,0:T(8,128)(2,1)} %collective-permute-done.5, bf16[64,3072]{1,0:T(8,128)(2,1)} %collective-permute-done.4, bf16[64,3072]{1,0:T(8,128)(2,1)S(1)} %collective-permute-done.3, f32[4,64,3072]{2,1,0:T(8,128)} %get-tuple-element.11, s32[]{:T(128)S(6)} %select_n.47, bf16[512,3072]{1,0:T(8,128)(2,1)} %x_ref.3, ...), kind=kLoop, calls=%fused_computation.7 | loop fusion | flops 1769472 | bytes 2752520 | tf_op jit(solution)/shard_map/convert_element_type | solution.py:334
  117.6 11.7 %all-to-all-done = bf16[16,2,128,768]{3,2,1,0:T(8,128)(2,1)} async-done(((bf16[16,2,128,768]{3,2,1,0:T(8,128)(2,1)}), bf16[16,2,128,768]{3,2,1,0:T(8,128)(2,1)}, u32[]{:S(2)}, u32[]{:S(2)}) %all-to-all-start) | async-done | bytes 6291488 | tf_op jit(solution)/shard_map/all_to_all | solution.py:312
  129.3 6.1 %copy.11 = bf16[2,1,16,1,128,768]{5,4,3,2,1,0:T(8,128)(2,1)} copy(bf16[2,1,16,1,128,768]{5,4,0,2,3,1:T(8,128)(2,1)} %bitcast.14) | data formatting | bytes 12582912
  (2 shorter events, 0.0 us)
Async XLA Ops:
  0.6 77.8 %copy-start = (bf16[384,3072]{1,0:T(8,128)(2,1)S(1)}, bf16[384,3072]{1,0:T(8,128)(2,1)}, u32[]{:S(2)}) copy-start(bf16[384,3072]{1,0:T(8,128)(2,1)} %param.11) | copy-start | bytes 7077892
  0.6 16.4 %collective-permute-start = (bf16[2,1,3584,384]{3,2,1,0:T(8,128)(2,1)}, bf16[2,1,3584,384]{3,2,1,0:T(8,128)(2,1)}, u32[]{:S(2)}, u32[]{:S(2)}) collective-permute-start(bf16[2,1,3584,384]{3,2,1,0:T(8,128)(2,1)} %vc_ref.1), channel_id=1, source_target_pairs={{0,1},{1,0},{2,3},{3,2},{4,5},{5,4},{6,7},{7,6},{8,9},{9,8},{10,11... | collective-permute-start | bytes 16515080 | tf_op jit(solution)/shard_map/ppermute | solution.py:305
  14.4 2.6 %collective-permute-start.1 = (bf16[2,512,384]{2,1,0:T(8,128)(2,1)}, bf16[2,512,384]{2,1,0:T(8,128)(2,1)S(1)}, u32[]{:S(2)}, u32[]{:S(2)}) collective-permute-start(bf16[2,512,384]{2,1,0:T(8,128)(2,1)} %shard_map.96.refs_1_.refs_5_.refs_9_.refs_13_.kn_ref.vn_ref), channel_id=1, source_target_pairs={{0,1},{1,0},{2,3},{3,2},{4,5},{5,4},{6,7},{7,6},{8,9},{9,8},{10,11... | collective-permute-start | bytes 2359304 | tf_op jit(solution)/shard_map/ppermute | solution.py:308
  17.0 0.9 copy-start.1
  25.7 103.6 %all-to-all-start = ((bf16[16,2,128,768]{3,2,1,0:T(8,128)(2,1)}), bf16[16,2,128,768]{3,2,1,0:T(8,128)(2,1)}, u32[]{:S(2)}, u32[]{:S(2)}) async-start(bf16[16,2,128,768]{3,2,1,0:T(8,128)(2,1)} %shard_map.97), calls=%async_computation | async-start | bytes 12582912 | tf_op jit(solution)/shard_map/all_to_all | solution.py:312
  81.3 1.7 %copy-start.2 = (bf16[512,3072]{1,0:T(8,128)(2,1)}, bf16[512,3072]{1,0:T(8,128)(2,1)S(1)}, u32[]{:S(2)}) copy-start(bf16[512,3072]{1,0:T(8,128)(2,1)S(1)} %convolution_convert_fusion) | copy-start | bytes 9437188
  84.2 3.8 %collective-permute-start.2 = (bf16[4,64,3072]{2,1,0:T(8,128)(2,1)}, bf16[4,64,3072]{2,1,0:T(8,128)(2,1)}, u32[]{:S(2)}, u32[]{:S(2)}) collective-permute-start(bf16[4,64,3072]{2,1,0:T(8,128)(2,1)} %dynamic-slice_bitcast_fusion), channel_id=1, source_target_pairs={{0,1},{1,0},{2,3},{3,2},{4,5},{5,4},{6,7},{7,6},{8,9},{9,8},{10,11... | collective-permute-start | bytes 4718600 | tf_op jit(solution)/shard_map/ppermute | solution.py:323
  93.1 12.6 %collective-permute-start.3 = (bf16[64,3072]{1,0:T(8,128)(2,1)}, bf16[64,3072]{1,0:T(8,128)(2,1)S(1)}, u32[]{:S(2)}, u32[]{:S(2)}) collective-permute-start(bf16[64,3072]{1,0:T(8,128)(2,1)} %get-tuple-element.12), channel_id=1, source_target_pairs={{0,2},{2,4},{4,6},{6,0},{1,3},{3,5},{5,7},{7,1},{8,10},{10,12},{12... | collective-permute-start | bytes 1179656 | tf_op jit(solution)/shard_map/ppermute | solution.py:332
  94.6 20.6 %collective-permute-start.4 = (bf16[64,3072]{1,0:T(8,128)(2,1)S(1)}, bf16[64,3072]{1,0:T(8,128)(2,1)}, u32[]{:S(2)}, u32[]{:S(2)}) collective-permute-start(bf16[64,3072]{1,0:T(8,128)(2,1)S(1)} %get-tuple-element.14), channel_id=1, source_target_pairs={{0,4},{2,6},{4,0},{6,2},{1,5},{3,7},{5,1},{7,3},{8,12},{10,14},{12... | collective-permute-start | bytes 1179656 | tf_op jit(solution)/shard_map/ppermute | solution.py:332
  97.3 17.9 %collective-permute-start.5 = (bf16[64,3072]{1,0:T(8,128)(2,1)S(1)}, bf16[64,3072]{1,0:T(8,128)(2,1)}, u32[]{:S(2)}, u32[]{:S(2)}) collective-permute-start(bf16[64,3072]{1,0:T(8,128)(2,1)S(1)} %get-tuple-element.13), channel_id=1, source_target_pairs={{0,6},{2,0},{4,2},{6,4},{1,7},{3,1},{5,3},{7,5},{8,14},{10,8},{12,... | collective-permute-start | bytes 1179656 | tf_op jit(solution)/shard_map/ppermute | solution.py:332

commit v15 on v14

--- a/solution.py
+++ b/solution.py
@@ -242,7 +242,7 @@
         count = (jnp.zeros((rows, 1), jnp.int32) + group_requests).astype(jnp.float32)
         first = jnp.ceil((request * tok_count).astype(jnp.float32) / count).astype(jnp.int32)
         positions = (group_len + row - first).astype(jnp.float32)
-        angles = positions * freq_ref[...]
+        angles = positions * freq_ref[...].reshape(1, features)
         lane = lax.broadcasted_iota(jnp.int32, plain.shape, 1)
         ahead = pltpu.roll(plain, features - half, 1)
         behind = pltpu.roll(plain, half, 1)
@@ -268,7 +268,7 @@
             in_specs=[
                 pl.BlockSpec((rows, width), lambda r, m: (r, 0)),
                 pl.BlockSpec((width,), lambda r, m: (0,)),
-                pl.BlockSpec((1, features), lambda r, m: (0, 0)),
+                pl.BlockSpec((features,), lambda r, m: (0,)),
             ]
             + [weight_spec(part) for part in parts],
             out_specs=pl.BlockSpec((len(parts), rows, features), lambda r, m: (0, r, 0)),
@@ -298,7 +298,7 @@
     frequency = jnp.exp(
         jnp.arange(half_size, dtype=jnp.float32) * (-2.0 * math.log(10000.0) / HD)
     )
-    frequency = jnp.tile(frequency, features // half_size).reshape(1, features)
+    frequency = jnp.tile(frequency, features // half_size)
     gain = norm_gain
     core = lax.axis_index("core")
     swap_cores = [(0, 1), (1, 0)]

time: 136 us -> 136 us (level)
  no operation moved by 1% of the time
where the time goes in v15:
time: 136 us; the launch traced here: 135 us
  Pallas kernels  64 us (47%)
  waiting for transfers between devices  33.4 us (25%)
  starting transfers between devices  14.6 us (11%)
  local copies, waits for them, and re-layouts  11.6 us (9%)
  other arithmetic  8.03 us (6%)
  matrix products  2.79 us (2%)
    pallas_call x1, Pallas kernels, attend(): pl.pallas_call(attention_kernel, out_shape=jax.ShapeDtypeStruct(queries.s...  34.9 us
    pallas_call x2, Pallas kernels, project(): pl.pallas_call(functools.partial(projection_kernel, parts=parts), out_sha...  20.9 us
    ppermute x3, waiting for transfers between devices, local(): summed = summed + lax.ppermute(chunk, 'x', pairs).astype(jnp.float32)  16.4 us
    all_to_all x1, waiting for transfers between devices, local(): received = lax.all_to_all(joined, 'seq', 0, 0, tiled=True)  11.1 us
    unnamed x7, local copies, waits for them, and re-layouts  8.68 us
    all_to_all x1, starting transfers between devices, local(): received = lax.all_to_all(joined, 'seq', 0, 0, tiled=True)  8.38 us
    pallas_call x1, Pallas kernels, relay(): pl.pallas_call(functools.partial(relay_kernel, new_blocks=new_blocks), ou...  8.23 us
    ppermute x3, starting transfers between devices, local(): summed = summed + lax.ppermute(chunk, 'x', pairs).astype(jnp.float32)  5.65 us
  transfers between devices with their start and end apart: 7, of which 5 were waited for; matrix products, arithmetic and copies ran while one was open for 10% of the time, Pallas kernels for 41%

profile of v15, /device:TPU:0, one launch (start us, length us, event | category | flops | bytes accessed | tf_op | source)
XLA Modules:
  0.0 135.3 jit_solution(11193357405770500527)
XLA Ops:
  0.6 0.0 copy-start
  0.6 0.1 collective-permute-start
  0.8 0.7 tile.14.freq_ref
  1.4 0.7 pad_add_fusion
  2.1 0.2 dynamic-slice_reduce_fusion
  2.3 0.6 pad_add_fusion.1.meta_ref
  2.9 11.5 %shard_map.96.refs_1_.refs_5_.refs_9_.refs_13_.kn_ref.vn_ref = bf16[2,512,384]{2,1,0:T(8,128)(2,1)} custom-call(s32[4]{0:T(128)} %pad_add_fusion.1.meta_ref, bf16[512,3072]{1,0:T(8,128)(2,1)} %x_ref.3, bf16[3072]{0:T(1024)(128)(2,1)} %gain_ref.3, f32[384]{0:T(512)} %tile.14.freq_ref, bf16[3,3072,384]{2,1,0:T(8,128)(2,1)} %bitcast.34, ...), custom_call_target="tpu_custom_call" | custom-call | tf_op jit(solution)/shard_map/pallas_call | solution.py:262
  14.4 0.5 collective-permute-start.1
  14.9 2.1 %collective-permute-done.1.refs_3_.refs_7_.refs_11_.refs_15_ = bf16[2,512,384]{2,1,0:T(8,128)(2,1)S(1)} collective-permute-done((bf16[2,512,384]{2,1,0:T(8,128)(2,1)}, bf16[2,512,384]{2,1,0:T(8,128)(2,1)S(1)}, u32[]{:S(2)}, u32[]{:S(2)}) %collective-permute-start.1) | collective-permute-done | bytes 786464 | tf_op jit(solution)/shard_map/ppermute | solution.py:308
  17.0 0.0 copy-start.1
  17.0 0.0 collective-permute-done.refs_2_.refs_6_.refs_10_.refs_14_
  17.0 0.9 copy-done.1
  17.9 8.2 %shard_map.97 = bf16[16,2,128,768]{3,2,1,0:T(8,128)(2,1)} custom-call(s32[4]{0:T(128)} %pad_add_fusion.1.meta_ref, bf16[2,1,3584,384]{3,2,1,0:T(8,128)(2,1)} %vc_ref.1, bf16[2,512,384]{2,1,0:T(8,128)(2,1)} %shard_map.96.refs_1_.refs_5_.refs_9_.refs_13_.kn_ref.vn_ref, bf16[2,1,3584,384]{3,2,1,0:T(8,128)(2,1)} %collective-permute-done.refs_2_.refs_6_.refs_10_.refs_14_, ...), custom_call_target="tpu_custom_call" | custom-call | tf_op jit(solution)/shard_map/pallas_call | solution.py:196
  26.1 8.4 %all-to-all-start = ((bf16[16,2,128,768]{3,2,1,0:T(8,128)(2,1)}), bf16[16,2,128,768]{3,2,1,0:T(8,128)(2,1)}, u32[]{:S(2)}, u32[]{:S(2)}) async-start(bf16[16,2,128,768]{3,2,1,0:T(8,128)(2,1)} %shard_map.97), calls=%async_computation | async-start | bytes 12582912 | tf_op jit(solution)/shard_map/all_to_all | solution.py:312
  34.5 9.4 %shard_map.95 = bf16[1,512,384]{2,1,0:T(8,128)(2,1)} custom-call(s32[4]{0:T(128)} %pad_add_fusion.1.meta_ref, bf16[512,3072]{1,0:T(8,128)(2,1)} %x_ref.3, bf16[3072]{0:T(1024)(128)(2,1)} %gain_ref.3, f32[384]{0:T(512)} %tile.14.freq_ref, bf16[3,3072,384]{2,1,0:T(8,128)(2,1)} %bitcast.36), custom_call_target="tpu_custom_call" | custom-call | tf_op jit(solution)/shard_map/pallas_call | solution.py:262
  43.9 34.9 %shard_map.98 = bf16[512,384]{1,0:T(8,128)(2,1)} custom-call(s32[4]{0:T(128)} %pad_add_fusion.1.meta_ref, bf16[512,384]{1,0:T(8,128)(2,1)} %bitcast.39, bf16[2,1,3584,384]{3,2,1,0:T(8,128)(2,1)} %vc_ref.1, bf16[2,1,3584,384]{3,2,1,0:T(8,128)(2,1)} %vc_ref.1, bf16[2,512,384]{2,1,0:T(8,128)(2,1)} %shard_map.96.refs_1_.refs_5_.refs_9_.refs_13_.kn_ref.vn_ref, ...), custom_call_target="tpu_custom_call" | custom-call | tf_op jit(solution)/shard_map/pallas_call | solution.py:124
  78.8 0.0 copy-done
  78.8 2.8 %convolution_convert_fusion = bf16[512,3072]{1,0:T(8,128)(2,1)S(1)} fusion(bf16[512,384]{1,0:T(8,128)(2,1)} %shard_map.98, bf16[384,3072]{1,0:T(8,128)(2,1)S(1)} %copy-done), kind=kOutput, calls=%fused_computation | convolution fusion | flops 1209532416 | bytes 5898240 | tf_op jit(solution)/shard_map/dot_general | solution.py:317
  81.6 0.0 copy-start.2
  81.7 1.6 %copy-done.2 = bf16[512,3072]{1,0:T(8,128)(2,1)} copy-done((bf16[512,3072]{1,0:T(8,128)(2,1)}, bf16[512,3072]{1,0:T(8,128)(2,1)S(1)}, u32[]{:S(2)}) %copy-start.2) | copy-done | bytes 3145752
  83.3 1.3 dynamic-slice_bitcast_fusion
  84.6 0.0 collective-permute-start.2
  84.6 3.7 %collective-permute-done.2 = bf16[4,64,3072]{2,1,0:T(8,128)(2,1)} collective-permute-done((bf16[4,64,3072]{2,1,0:T(8,128)(2,1)}, bf16[4,64,3072]{2,1,0:T(8,128)(2,1)}, u32[]{:S(2)}, u32[]{:S(2)}) %collective-permute-start.2) | collective-permute-done | bytes 1572896 | tf_op jit(solution)/shard_map/ppermute | solution.py:323
  88.3 4.3 %fusion.4 = (bf16[4,64,3072]{2,1,0:T(8,128)(2,1)S(1)}, f32[4,64,3072]{2,1,0:T(8,128)}) fusion(bf16[4,64,3072]{2,1,0:T(8,128)(2,1)} %collective-permute-done.2, bf16[4,2,64,3072]{3,2,1,0:T(8,128)(2,1)} %bitcast.38, s32[]{:T(128)S(6)} %select_n.45), kind=kLoop, calls=%fused_computation.15 | loop fusion | flops 3145728 | bytes 7864324 | tf_op jit(solution)/shard_map/convert_element_type | solution.py:326
  92.6 0.8 dynamic-slice_bitcast_fusion.3
  93.4 1.5 %collective-permute-start.3 = (bf16[64,3072]{1,0:T(8,128)(2,1)}, bf16[64,3072]{1,0:T(8,128)(2,1)S(1)}, u32[]{:S(2)}, u32[]{:S(2)}) collective-permute-start(bf16[64,3072]{1,0:T(8,128)(2,1)} %get-tuple-element.12), channel_id=1, source_target_pairs={{0,2},{2,4},{4,6},{6,0},{1,3},{3,5},{5,7},{7,1},{8,10},{10,12},{12... | collective-permute-start | bytes 1179656 | tf_op jit(solution)/shard_map/ppermute | solution.py:332
  94.9 2.7 %collective-permute-start.4 = (bf16[64,3072]{1,0:T(8,128)(2,1)S(1)}, bf16[64,3072]{1,0:T(8,128)(2,1)}, u32[]{:S(2)}, u32[]{:S(2)}) collective-permute-start(bf16[64,3072]{1,0:T(8,128)(2,1)S(1)} %get-tuple-element.14), channel_id=1, source_target_pairs={{0,4},{2,6},{4,0},{6,2},{1,5},{3,7},{5,1},{7,3},{8,12},{10,14},{12... | collective-permute-start | bytes 1179656 | tf_op jit(solution)/shard_map/ppermute | solution.py:332
  97.6 1.4 %collective-permute-start.5 = (bf16[64,3072]{1,0:T(8,128)(2,1)S(1)}, bf16[64,3072]{1,0:T(8,128)(2,1)}, u32[]{:S(2)}, u32[]{:S(2)}) collective-permute-start(bf16[64,3072]{1,0:T(8,128)(2,1)S(1)} %get-tuple-element.13), channel_id=1, source_target_pairs={{0,6},{2,0},{4,2},{6,4},{1,7},{3,1},{5,3},{7,5},{8,14},{10,8},{12,... | collective-permute-start | bytes 1179656 | tf_op jit(solution)/shard_map/ppermute | solution.py:332
  99.1 6.9 %collective-permute-done.3 = bf16[64,3072]{1,0:T(8,128)(2,1)S(1)} collective-permute-done((bf16[64,3072]{1,0:T(8,128)(2,1)}, bf16[64,3072]{1,0:T(8,128)(2,1)S(1)}, u32[]{:S(2)}, u32[]{:S(2)}) %collective-permute-start.3) | collective-permute-done | bytes 393248 | tf_op jit(solution)/shard_map/ppermute | solution.py:332
  106.0 9.5 %collective-permute-done.4 = bf16[64,3072]{1,0:T(8,128)(2,1)} collective-permute-done((bf16[64,3072]{1,0:T(8,128)(2,1)S(1)}, bf16[64,3072]{1,0:T(8,128)(2,1)}, u32[]{:S(2)}, u32[]{:S(2)}) %collective-permute-start.4) | collective-permute-done | bytes 393248 | tf_op jit(solution)/shard_map/ppermute | solution.py:332
  115.5 0.0 collective-permute-done.5
  115.5 2.4 %fusion.3 = bf16[64,3072]{1,0:T(8,128)(2,1)} fusion(bf16[64,3072]{1,0:T(8,128)(2,1)} %collective-permute-done.5, bf16[64,3072]{1,0:T(8,128)(2,1)} %collective-permute-done.4, bf16[64,3072]{1,0:T(8,128)(2,1)S(1)} %collective-permute-done.3, f32[4,64,3072]{2,1,0:T(8,128)} %get-tuple-element.11, s32[]{:T(128)S(6)} %select_n.47, bf16[512,3072]{1,0:T(8,128)(2,1)} %x_ref.3, ...), kind=kLoop, calls=%fused_computation.7 | loop fusion | flops 1769472 | bytes 2752520 | tf_op jit(solution)/shard_map/convert_element_type | solution.py:334
  118.0 11.1 %all-to-all-done = bf16[16,2,128,768]{3,2,1,0:T(8,128)(2,1)} async-done(((bf16[16,2,128,768]{3,2,1,0:T(8,128)(2,1)}), bf16[16,2,128,768]{3,2,1,0:T(8,128)(2,1)}, u32[]{:S(2)}, u32[]{:S(2)}) %all-to-all-start) | async-done | bytes 6291488 | tf_op jit(solution)/shard_map/all_to_all | solution.py:312
  129.1 6.1 %copy.11 = bf16[2,1,16,1,128,768]{5,4,3,2,1,0:T(8,128)(2,1)} copy(bf16[2,1,16,1,128,768]{5,4,0,2,3,1:T(8,128)(2,1)} %bitcast.14) | data formatting | bytes 12582912
  (2 shorter events, 0.0 us)
Async XLA Ops:
  0.6 78.2 %copy-start = (bf16[384,3072]{1,0:T(8,128)(2,1)S(1)}, bf16[384,3072]{1,0:T(8,128)(2,1)}, u32[]{:S(2)}) copy-start(bf16[384,3072]{1,0:T(8,128)(2,1)} %param.11) | copy-start | bytes 7077892
  0.6 16.4 %collective-permute-start = (bf16[2,1,3584,384]{3,2,1,0:T(8,128)(2,1)}, bf16[2,1,3584,384]{3,2,1,0:T(8,128)(2,1)}, u32[]{:S(2)}, u32[]{:S(2)}) collective-permute-start(bf16[2,1,3584,384]{3,2,1,0:T(8,128)(2,1)} %vc_ref.1), channel_id=1, source_target_pairs={{0,1},{1,0},{2,3},{3,2},{4,5},{5,4},{6,7},{7,6},{8,9},{9,8},{10,11... | collective-permute-start | bytes 16515080 | tf_op jit(solution)/shard_map/ppermute | solution.py:305
  14.4 2.6 %collective-permute-start.1 = (bf16[2,512,384]{2,1,0:T(8,128)(2,1)}, bf16[2,512,384]{2,1,0:T(8,128)(2,1)S(1)}, u32[]{:S(2)}, u32[]{:S(2)}) collective-permute-start(bf16[2,512,384]{2,1,0:T(8,128)(2,1)} %shard_map.96.refs_1_.refs_5_.refs_9_.refs_13_.kn_ref.vn_ref), channel_id=1, source_target_pairs={{0,1},{1,0},{2,3},{3,2},{4,5},{5,4},{6,7},{7,6},{8,9},{9,8},{10,11... | collective-permute-start | bytes 2359304 | tf_op jit(solution)/shard_map/ppermute | solution.py:308
  17.0 0.9 copy-start.1
  26.1 103.0 %all-to-all-start = ((bf16[16,2,128,768]{3,2,1,0:T(8,128)(2,1)}), bf16[16,2,128,768]{3,2,1,0:T(8,128)(2,1)}, u32[]{:S(2)}, u32[]{:S(2)}) async-start(bf16[16,2,128,768]{3,2,1,0:T(8,128)(2,1)} %shard_map.97), calls=%async_computation | async-start | bytes 12582912 | tf_op jit(solution)/shard_map/all_to_all | solution.py:312
  81.6 1.7 %copy-start.2 = (bf16[512,3072]{1,0:T(8,128)(2,1)}, bf16[512,3072]{1,0:T(8,128)(2,1)S(1)}, u32[]{:S(2)}) copy-start(bf16[512,3072]{1,0:T(8,128)(2,1)S(1)} %convolution_convert_fusion) | copy-start | bytes 9437188
  84.6 3.8 %collective-permute-start.2 = (bf16[4,64,3072]{2,1,0:T(8,128)(2,1)}, bf16[4,64,3072]{2,1,0:T(8,128)(2,1)}, u32[]{:S(2)}, u32[]{:S(2)}) collective-permute-start(bf16[4,64,3072]{2,1,0:T(8,128)(2,1)} %dynamic-slice_bitcast_fusion), channel_id=1, source_target_pairs={{0,1},{1,0},{2,3},{3,2},{4,5},{5,4},{6,7},{7,6},{8,9},{9,8},{10,11... | collective-permute-start | bytes 4718600 | tf_op jit(solution)/shard_map/ppermute | solution.py:323
  93.4 12.6 %collective-permute-start.3 = (bf16[64,3072]{1,0:T(8,128)(2,1)}, bf16[64,3072]{1,0:T(8,128)(2,1)S(1)}, u32[]{:S(2)}, u32[]{:S(2)}) collective-permute-start(bf16[64,3072]{1,0:T(8,128)(2,1)} %get-tuple-element.12), channel_id=1, source_target_pairs={{0,2},{2,4},{4,6},{6,0},{1,3},{3,5},{5,7},{7,1},{8,10},{10,12},{12... | collective-permute-start | bytes 1179656 | tf_op jit(solution)/shard_map/ppermute | solution.py:332
  94.9 20.6 %collective-permute-start.4 = (bf16[64,3072]{1,0:T(8,128)(2,1)S(1)}, bf16[64,3072]{1,0:T(8,128)(2,1)}, u32[]{:S(2)}, u32[]{:S(2)}) collective-permute-start(bf16[64,3072]{1,0:T(8,128)(2,1)S(1)} %get-tuple-element.14), channel_id=1, source_target_pairs={{0,4},{2,6},{4,0},{6,2},{1,5},{3,7},{5,1},{7,3},{8,12},{10,14},{12... | collective-permute-start | bytes 1179656 | tf_op jit(solution)/shard_map/ppermute | solution.py:332
  97.6 17.9 %collective-permute-start.5 = (bf16[64,3072]{1,0:T(8,128)(2,1)S(1)}, bf16[64,3072]{1,0:T(8,128)(2,1)}, u32[]{:S(2)}, u32[]{:S(2)}) collective-permute-start(bf16[64,3072]{1,0:T(8,128)(2,1)S(1)} %get-tuple-element.13), channel_id=1, source_target_pairs={{0,6},{2,0},{4,2},{6,4},{1,7},{3,1},{5,3},{7,5},{8,14},{10,8},{12,... | collective-permute-start | bytes 1179656 | tf_op jit(solution)/shard_map/ppermute | solution.py:332

commit v16 on v14

--- a/solution.py
+++ b/solution.py
@@ -285,8 +285,12 @@
     features = w_qkv.shape[2]
     head_count = features // HD
     cache_len = kv_cache.shape[2]
-    group_params = lax.dynamic_index_in_dim(
-        jnp.stack([cached_lengths, requests, block_start], axis=1), group_idx, keepdims=False
+    core = lax.axis_index("core")
+    group_table = jnp.stack(
+        [cached_lengths, requests, block_start, jnp.zeros_like(cached_lengths) + core], axis=1
+    )
+    group_params = lax.dynamic_index_in_dim(group_table, group_idx, keepdims=False).astype(
+        jnp.int32
     )
     group_len = group_params[0]
     group_requests = group_params[1]
@@ -300,10 +304,9 @@
     )
     frequency = jnp.tile(frequency, features // half_size).reshape(1, features)
     gain = norm_gain
-    core = lax.axis_index("core")
     swap_cores = [(0, 1), (1, 0)]
     mate_cache = lax.ppermute(kv_cache, "core", swap_cores)
-    meta = jnp.concatenate([group_params, jnp.reshape(core, (1,))]).astype(jnp.int32)
+    meta = group_params
     new_kv = project(meta, tokens, gain, weights, frequency, (1, 2))
     mate_new = lax.ppermute(new_kv, "core", swap_cores)
     joined = relay(meta, kv_cache, new_kv, mate_cache, mate_new, seq_count)

time: 136 us -> 136 us (level)
  no operation moved by 1% of the time
where the time goes in v16:
time: 136 us; the launch traced here: 135 us
  Pallas kernels  63.7 us (47%)
  waiting for transfers between devices  33.3 us (24%)
  starting transfers between devices  14.9 us (11%)
  local copies, waits for them, and re-layouts  12.2 us (9%)
  other arithmetic  7.49 us (6%)
  matrix products  2.79 us (2%)
    pallas_call x1, Pallas kernels, attend(): pl.pallas_call(attention_kernel, out_shape=jax.ShapeDtypeStruct(queries.s...  34.9 us
    pallas_call x2, Pallas kernels, project(): pl.pallas_call(functools.partial(projection_kernel, parts=parts), out_sha...  20.9 us
    ppermute x3, waiting for transfers between devices, local(): summed = summed + lax.ppermute(chunk, 'x', pairs).astype(jnp.float32)  16.4 us
    all_to_all x1, waiting for transfers between devices, local(): received = lax.all_to_all(joined, 'seq', 0, 0, tiled=True)  11 us
    unnamed x7, local copies, waits for them, and re-layouts  8.68 us
    all_to_all x1, starting transfers between devices, local(): received = lax.all_to_all(joined, 'seq', 0, 0, tiled=True)  8.68 us
    pallas_call x1, Pallas kernels, relay(): pl.pallas_call(functools.partial(relay_kernel, new_blocks=new_blocks), ou...  7.89 us
    ppermute x3, starting transfers between devices, local(): summed = summed + lax.ppermute(chunk, 'x', pairs).astype(jnp.float32)  5.65 us
  transfers between devices with their start and end apart: 7, of which 5 were waited for; matrix products, arithmetic and copies ran while one was open for 10% of the time, Pallas kernels for 41%

profile of v16, /device:TPU:0, one launch (start us, length us, event | category | flops | bytes accessed | tf_op | source)
XLA Modules:
  0.0 135.2 jit_solution(3565319346416529968)
XLA Ops:
  0.6 0.0 copy-start
  0.6 0.1 collective-permute-start
  0.7 0.1 pad.3.clone
  0.8 0.7 reshape_tile.5.freq_ref
  1.5 0.8 add_add_fusion
  2.3 0.7 dynamic-slice_reduce_fusion.meta_ref
  3.0 11.5 %shard_map.96.refs_1_.refs_5_.refs_9_.refs_13_.kn_ref.vn_ref = bf16[2,512,384]{2,1,0:T(8,128)(2,1)} custom-call(s32[4]{0:T(128)} %dynamic-slice_reduce_fusion.meta_ref, bf16[512,3072]{1,0:T(8,128)(2,1)} %x_ref.3, bf16[3072]{0:T(1024)(128)(2,1)} %gain_ref.3, f32[1,384]{1,0:T(1,128)} %reshape_tile.5.freq_ref, bf16[3,3072,384]{2,1,0:T(8,128)(2,1)} %bitcast.34, ...), custom_call_target="tpu_custom_call" | custom-call | tf_op jit(solution)/shard_map/pallas_call | solution.py:262
  14.4 0.5 collective-permute-start.1
  14.9 2.1 %collective-permute-done.1.refs_3_.refs_7_.refs_11_.refs_15_ = bf16[2,512,384]{2,1,0:T(8,128)(2,1)S(1)} collective-permute-done((bf16[2,512,384]{2,1,0:T(8,128)(2,1)}, bf16[2,512,384]{2,1,0:T(8,128)(2,1)S(1)}, u32[]{:S(2)}, u32[]{:S(2)}) %collective-permute-start.1) | collective-permute-done | bytes 786464 | tf_op jit(solution)/shard_map/ppermute | solution.py:311
  17.1 0.0 copy-start.1
  17.1 0.0 collective-permute-done.refs_2_.refs_6_.refs_10_.refs_14_
  17.1 0.9 copy-done.1
  17.9 7.9 %shard_map.97 = bf16[16,2,128,768]{3,2,1,0:T(8,128)(2,1)} custom-call(s32[4]{0:T(128)} %dynamic-slice_reduce_fusion.meta_ref, bf16[2,1,3584,384]{3,2,1,0:T(8,128)(2,1)} %vc_ref.1, bf16[2,512,384]{2,1,0:T(8,128)(2,1)} %shard_map.96.refs_1_.refs_5_.refs_9_.refs_13_.kn_ref.vn_ref, ...), custom_call_target="tpu_custom_call" | custom-call | tf_op jit(solution)/shard_map/pallas_call | solution.py:196
  25.8 8.7 %all-to-all-start = ((bf16[16,2,128,768]{3,2,1,0:T(8,128)(2,1)}), bf16[16,2,128,768]{3,2,1,0:T(8,128)(2,1)}, u32[]{:S(2)}, u32[]{:S(2)}) async-start(bf16[16,2,128,768]{3,2,1,0:T(8,128)(2,1)} %shard_map.97), calls=%async_computation | async-start | bytes 12582912 | tf_op jit(solution)/shard_map/all_to_all | solution.py:315
  34.5 9.4 %shard_map.95 = bf16[1,512,384]{2,1,0:T(8,128)(2,1)} custom-call(s32[4]{0:T(128)} %dynamic-slice_reduce_fusion.meta_ref, bf16[512,3072]{1,0:T(8,128)(2,1)} %x_ref.3, bf16[3072]{0:T(1024)(128)(2,1)} %gain_ref.3, f32[1,384]{1,0:T(1,128)} %reshape_tile.5.freq_ref, bf16[3,3072,384]{2,1,0:T(8,128)(2,1)} %bitcast.36), custom_call_target="tpu_custom_call" | custom-call | tf_op jit(solution)/shard_map/pallas_call | solution.py:262
  44.0 34.9 %shard_map.98 = bf16[512,384]{1,0:T(8,128)(2,1)} custom-call(s32[4]{0:T(128)} %dynamic-slice_reduce_fusion.meta_ref, bf16[512,384]{1,0:T(8,128)(2,1)} %bitcast.39, bf16[2,1,3584,384]{3,2,1,0:T(8,128)(2,1)} %vc_ref.1, bf16[2,1,3584,384]{3,2,1,0:T(8,128)(2,1)} %vc_ref.1, bf16[2,512,384]{2,1,0:T(8,128)(2,1)} %shard_map.96.refs_1_.refs_5_.refs_9_.refs_13_.kn_ref.vn_ref, ...), custom_call_target="tpu_custom_call" | custom-call | tf_op jit(solution)/shard_map/pallas_call | solution.py:124
  78.9 0.0 copy-done
  78.9 2.8 %convolution_convert_fusion = bf16[512,3072]{1,0:T(8,128)(2,1)S(1)} fusion(bf16[512,384]{1,0:T(8,128)(2,1)} %shard_map.98, bf16[384,3072]{1,0:T(8,128)(2,1)S(1)} %copy-done), kind=kOutput, calls=%fused_computation | convolution fusion | flops 1209532416 | bytes 5898240 | tf_op jit(solution)/shard_map/dot_general | solution.py:320
  81.7 0.0 copy-start.2
  81.7 1.6 %copy-done.2 = bf16[512,3072]{1,0:T(8,128)(2,1)} copy-done((bf16[512,3072]{1,0:T(8,128)(2,1)}, bf16[512,3072]{1,0:T(8,128)(2,1)S(1)}, u32[]{:S(2)}) %copy-start.2) | copy-done | bytes 3145752
  83.3 1.3 dynamic-slice_bitcast_fusion
  84.6 0.0 collective-permute-start.2
  84.6 3.7 %collective-permute-done.2 = bf16[4,64,3072]{2,1,0:T(8,128)(2,1)} collective-permute-done((bf16[4,64,3072]{2,1,0:T(8,128)(2,1)}, bf16[4,64,3072]{2,1,0:T(8,128)(2,1)}, u32[]{:S(2)}, u32[]{:S(2)}) %collective-permute-start.2) | collective-permute-done | bytes 1572896 | tf_op jit(solution)/shard_map/ppermute | solution.py:326
  88.3 4.3 %fusion.4 = (bf16[4,64,3072]{2,1,0:T(8,128)(2,1)S(1)}, f32[4,64,3072]{2,1,0:T(8,128)}) fusion(bf16[4,64,3072]{2,1,0:T(8,128)(2,1)} %collective-permute-done.2, bf16[4,2,64,3072]{3,2,1,0:T(8,128)(2,1)} %bitcast.38, s32[]{:T(128)S(6)} %select_n.45), kind=kLoop, calls=%fused_computation.14 | loop fusion | flops 3145728 | bytes 7864324 | tf_op jit(solution)/shard_map/convert_element_type | solution.py:329
  92.6 0.8 dynamic-slice_bitcast_fusion.3
  93.5 1.5 %collective-permute-start.3 = (bf16[64,3072]{1,0:T(8,128)(2,1)}, bf16[64,3072]{1,0:T(8,128)(2,1)S(1)}, u32[]{:S(2)}, u32[]{:S(2)}) collective-permute-start(bf16[64,3072]{1,0:T(8,128)(2,1)} %get-tuple-element.12), channel_id=1, source_target_pairs={{0,2},{2,4},{4,6},{6,0},{1,3},{3,5},{5,7},{7,1},{8,10},{10,12},{12... | collective-permute-start | bytes 1179656 | tf_op jit(solution)/shard_map/ppermute | solution.py:335
  94.9 2.7 %collective-permute-start.4 = (bf16[64,3072]{1,0:T(8,128)(2,1)S(1)}, bf16[64,3072]{1,0:T(8,128)(2,1)}, u32[]{:S(2)}, u32[]{:S(2)}) collective-permute-start(bf16[64,3072]{1,0:T(8,128)(2,1)S(1)} %get-tuple-element.14), channel_id=1, source_target_pairs={{0,4},{2,6},{4,0},{6,2},{1,5},{3,7},{5,1},{7,3},{8,12},{10,14},{12... | collective-permute-start | bytes 1179656 | tf_op jit(solution)/shard_map/ppermute | solution.py:335
  97.7 1.4 %collective-permute-start.5 = (bf16[64,3072]{1,0:T(8,128)(2,1)S(1)}, bf16[64,3072]{1,0:T(8,128)(2,1)}, u32[]{:S(2)}, u32[]{:S(2)}) collective-permute-start(bf16[64,3072]{1,0:T(8,128)(2,1)S(1)} %get-tuple-element.13), channel_id=1, source_target_pairs={{0,6},{2,0},{4,2},{6,4},{1,7},{3,1},{5,3},{7,5},{8,14},{10,8},{12,... | collective-permute-start | bytes 1179656 | tf_op jit(solution)/shard_map/ppermute | solution.py:335
  99.1 6.9 %collective-permute-done.3 = bf16[64,3072]{1,0:T(8,128)(2,1)S(1)} collective-permute-done((bf16[64,3072]{1,0:T(8,128)(2,1)}, bf16[64,3072]{1,0:T(8,128)(2,1)S(1)}, u32[]{:S(2)}, u32[]{:S(2)}) %collective-permute-start.3) | collective-permute-done | bytes 393248 | tf_op jit(solution)/shard_map/ppermute | solution.py:335
  106.0 9.5 %collective-permute-done.4 = bf16[64,3072]{1,0:T(8,128)(2,1)} collective-permute-done((bf16[64,3072]{1,0:T(8,128)(2,1)S(1)}, bf16[64,3072]{1,0:T(8,128)(2,1)}, u32[]{:S(2)}, u32[]{:S(2)}) %collective-permute-start.4) | collective-permute-done | bytes 393248 | tf_op jit(solution)/shard_map/ppermute | solution.py:335
  115.5 0.0 collective-permute-done.5
  115.5 2.4 %fusion.3 = bf16[64,3072]{1,0:T(8,128)(2,1)} fusion(bf16[64,3072]{1,0:T(8,128)(2,1)} %collective-permute-done.5, bf16[64,3072]{1,0:T(8,128)(2,1)} %collective-permute-done.4, bf16[64,3072]{1,0:T(8,128)(2,1)S(1)} %collective-permute-done.3, f32[4,64,3072]{2,1,0:T(8,128)} %get-tuple-element.11, s32[]{:T(128)S(6)} %select_n.47, bf16[512,3072]{1,0:T(8,128)(2,1)} %x_ref.3, ...), kind=kLoop, calls=%fused_computation.7 | loop fusion | flops 1769472 | bytes 2752520 | tf_op jit(solution)/shard_map/convert_element_type | solution.py:337
  118.0 11.0 %all-to-all-done = bf16[16,2,128,768]{3,2,1,0:T(8,128)(2,1)} async-done(((bf16[16,2,128,768]{3,2,1,0:T(8,128)(2,1)}), bf16[16,2,128,768]{3,2,1,0:T(8,128)(2,1)}, u32[]{:S(2)}, u32[]{:S(2)}) %all-to-all-start) | async-done | bytes 6291488 | tf_op jit(solution)/shard_map/all_to_all | solution.py:315
  129.0 6.1 %copy.11 = bf16[2,1,16,1,128,768]{5,4,3,2,1,0:T(8,128)(2,1)} copy(bf16[2,1,16,1,128,768]{5,4,0,2,3,1:T(8,128)(2,1)} %bitcast.13) | data formatting | bytes 12582912
  (2 shorter events, 0.0 us)
Async XLA Ops:
  0.6 78.2 %copy-start = (bf16[384,3072]{1,0:T(8,128)(2,1)S(1)}, bf16[384,3072]{1,0:T(8,128)(2,1)}, u32[]{:S(2)}) copy-start(bf16[384,3072]{1,0:T(8,128)(2,1)} %param.11) | copy-start | bytes 7077892
  0.6 16.4 %collective-permute-start = (bf16[2,1,3584,384]{3,2,1,0:T(8,128)(2,1)}, bf16[2,1,3584,384]{3,2,1,0:T(8,128)(2,1)}, u32[]{:S(2)}, u32[]{:S(2)}) collective-permute-start(bf16[2,1,3584,384]{3,2,1,0:T(8,128)(2,1)} %vc_ref.1), channel_id=1, source_target_pairs={{0,1},{1,0},{2,3},{3,2},{4,5},{5,4},{6,7},{7,6},{8,9},{9,8},{10,11... | collective-permute-start | bytes 16515080 | tf_op jit(solution)/shard_map/ppermute | solution.py:308
  14.4 2.6 %collective-permute-start.1 = (bf16[2,512,384]{2,1,0:T(8,128)(2,1)}, bf16[2,512,384]{2,1,0:T(8,128)(2,1)S(1)}, u32[]{:S(2)}, u32[]{:S(2)}) collective-permute-start(bf16[2,512,384]{2,1,0:T(8,128)(2,1)} %shard_map.96.refs_1_.refs_5_.refs_9_.refs_13_.kn_ref.vn_ref), channel_id=1, source_target_pairs={{0,1},{1,0},{2,3},{3,2},{4,5},{5,4},{6,7},{7,6},{8,9},{9,8},{10,11... | collective-permute-start | bytes 2359304 | tf_op jit(solution)/shard_map/ppermute | solution.py:311
  17.1 0.9 copy-start.1
  25.8 103.2 %all-to-all-start = ((bf16[16,2,128,768]{3,2,1,0:T(8,128)(2,1)}), bf16[16,2,128,768]{3,2,1,0:T(8,128)(2,1)}, u32[]{:S(2)}, u32[]{:S(2)}) async-start(bf16[16,2,128,768]{3,2,1,0:T(8,128)(2,1)} %shard_map.97), calls=%async_computation | async-start | bytes 12582912 | tf_op jit(solution)/shard_map/all_to_all | solution.py:315
  81.7 1.7 %copy-start.2 = (bf16[512,3072]{1,0:T(8,128)(2,1)}, bf16[512,3072]{1,0:T(8,128)(2,1)S(1)}, u32[]{:S(2)}) copy-start(bf16[512,3072]{1,0:T(8,128)(2,1)S(1)} %convolution_convert_fusion) | copy-start | bytes 9437188
  84.6 3.8 %collective-permute-start.2 = (bf16[4,64,3072]{2,1,0:T(8,128)(2,1)}, bf16[4,64,3072]{2,1,0:T(8,128)(2,1)}, u32[]{:S(2)}, u32[]{:S(2)}) collective-permute-start(bf16[4,64,3072]{2,1,0:T(8,128)(2,1)} %dynamic-slice_bitcast_fusion), channel_id=1, source_target_pairs={{0,1},{1,0},{2,3},{3,2},{4,5},{5,4},{6,7},{7,6},{8,9},{9,8},{10,11... | collective-permute-start | bytes 4718600 | tf_op jit(solution)/shard_map/ppermute | solution.py:326
  93.5 12.6 %collective-permute-start.3 = (bf16[64,3072]{1,0:T(8,128)(2,1)}, bf16[64,3072]{1,0:T(8,128)(2,1)S(1)}, u32[]{:S(2)}, u32[]{:S(2)}) collective-permute-start(bf16[64,3072]{1,0:T(8,128)(2,1)} %get-tuple-element.12), channel_id=1, source_target_pairs={{0,2},{2,4},{4,6},{6,0},{1,3},{3,5},{5,7},{7,1},{8,10},{10,12},{12... | collective-permute-start | bytes 1179656 | tf_op jit(solution)/shard_map/ppermute | solution.py:335
  94.9 20.6 %collective-permute-start.4 = (bf16[64,3072]{1,0:T(8,128)(2,1)S(1)}, bf16[64,3072]{1,0:T(8,128)(2,1)}, u32[]{:S(2)}, u32[]{:S(2)}) collective-permute-start(bf16[64,3072]{1,0:T(8,128)(2,1)S(1)} %get-tuple-element.14), channel_id=1, source_target_pairs={{0,4},{2,6},{4,0},{6,2},{1,5},{3,7},{5,1},{7,3},{8,12},{10,14},{12... | collective-permute-start | bytes 1179656 | tf_op jit(solution)/shard_map/ppermute | solution.py:335
  97.7 17.9 %collective-permute-start.5 = (bf16[64,3072]{1,0:T(8,128)(2,1)S(1)}, bf16[64,3072]{1,0:T(8,128)(2,1)}, u32[]{:S(2)}, u32[]{:S(2)}) collective-permute-start(bf16[64,3072]{1,0:T(8,128)(2,1)S(1)} %get-tuple-element.13), channel_id=1, source_target_pairs={{0,6},{2,0},{4,2},{6,4},{1,7},{3,1},{5,3},{7,5},{8,14},{10,8},{12,... | collective-permute-start | bytes 1179656 | tf_op jit(solution)/shard_map/ppermute | solution.py:335

commit v17 on v14

--- a/solution.py
+++ b/solution.py
@@ -254,7 +254,7 @@
 def project(meta, tokens, gain, weights, frequency, parts):
     _, width, features = weights.shape
     tok_count = tokens.shape[0]
-    rows = 128 if tok_count % 128 == 0 else tok_count
+    rows = 256 if tok_count % 256 == 0 else tok_count
 
     def weight_spec(part):
         return pl.BlockSpec((1, width, features), lambda r, m: (part, 0, 0))

time: 136 us -> 136 us (level)
  no operation moved by 1% of the time
where the time goes in v17:
time: 136 us; the launch traced here: 134 us
  Pallas kernels  64 us (47%)
  waiting for transfers between devices  32.7 us (24%)
  starting transfers between devices  14.7 us (11%)
  local copies, waits for them, and re-layouts  11.6 us (9%)
  other arithmetic  8.03 us (6%)
  matrix products  2.79 us (2%)
    pallas_call x1, Pallas kernels, attend(): pl.pallas_call(attention_kernel, out_shape=jax.ShapeDtypeStruct(queries.s...  34.9 us
    pallas_call x2, Pallas kernels, project(): pl.pallas_call(functools.partial(projection_kernel, parts=parts), out_sha...  20.6 us
    ppermute x3, waiting for transfers between devices, local(): summed = summed + lax.ppermute(chunk, 'x', pairs).astype(jnp.float32)  16.4 us
    all_to_all x1, waiting for transfers between devices, local(): received = lax.all_to_all(joined, 'seq', 0, 0, tiled=True)  10.4 us
    unnamed x7, local copies, waits for them, and re-layouts  8.68 us
    all_to_all x1, starting transfers between devices, local(): received = lax.all_to_all(joined, 'seq', 0, 0, tiled=True)  8.44 us
    pallas_call x1, Pallas kernels, relay(): pl.pallas_call(functools.partial(relay_kernel, new_blocks=new_blocks), ou...  8.42 us
    ppermute x3, starting transfers between devices, local(): summed = summed + lax.ppermute(chunk, 'x', pairs).astype(jnp.float32)  5.66 us
  transfers between devices with their start and end apart: 7, of which 5 were waited for; matrix products, arithmetic and copies ran while one was open for 10% of the time, Pallas kernels for 41%

profile of v17, /device:TPU:0, one launch (start us, length us, event | category | flops | bytes accessed | tf_op | source)
XLA Modules:
  0.0 134.5 jit_solution(6593749548459112991)
XLA Ops:
  0.6 0.0 copy-start
  0.6 0.1 collective-permute-start
  0.8 0.7 reshape_tile.5.freq_ref
  1.4 0.7 pad_add_fusion
  2.1 0.2 dynamic-slice_reduce_fusion
  2.3 0.6 pad_add_fusion.1.meta_ref
  2.9 11.5 %shard_map.96.refs_1_.refs_5_.refs_9_.refs_13_.kn_ref.vn_ref = bf16[2,512,384]{2,1,0:T(8,128)(2,1)} custom-call(s32[4]{0:T(128)} %pad_add_fusion.1.meta_ref, bf16[512,3072]{1,0:T(8,128)(2,1)} %x_ref.3, bf16[3072]{0:T(1024)(128)(2,1)} %gain_ref.3, f32[1,384]{1,0:T(1,128)} %reshape_tile.5.freq_ref, bf16[3,3072,384]{2,1,0:T(8,128)(2,1)} %bitcast.34, ...), custom_call_target="tpu_custom_call" | custom-call | tf_op jit(solution)/shard_map/pallas_call | solution.py:262
  14.4 0.5 collective-permute-start.1
  14.9 2.1 %collective-permute-done.1.refs_3_.refs_7_.refs_11_.refs_15_ = bf16[2,512,384]{2,1,0:T(8,128)(2,1)S(1)} collective-permute-done((bf16[2,512,384]{2,1,0:T(8,128)(2,1)}, bf16[2,512,384]{2,1,0:T(8,128)(2,1)S(1)}, u32[]{:S(2)}, u32[]{:S(2)}) %collective-permute-start.1) | collective-permute-done | bytes 786464 | tf_op jit(solution)/shard_map/ppermute | solution.py:308
  17.0 0.0 copy-start.1
  17.0 0.0 collective-permute-done.refs_2_.refs_6_.refs_10_.refs_14_
  17.0 0.9 copy-done.1
  17.9 8.4 %shard_map.97 = bf16[16,2,128,768]{3,2,1,0:T(8,128)(2,1)} custom-call(s32[4]{0:T(128)} %pad_add_fusion.1.meta_ref, bf16[2,1,3584,384]{3,2,1,0:T(8,128)(2,1)} %vc_ref.1, bf16[2,512,384]{2,1,0:T(8,128)(2,1)} %shard_map.96.refs_1_.refs_5_.refs_9_.refs_13_.kn_ref.vn_ref, bf16[2,1,3584,384]{3,2,1,0:T(8,128)(2,1)} %collective-permute-done.refs_2_.refs_6_.refs_10_.refs_14_, ...), custom_call_target="tpu_custom_call" | custom-call | tf_op jit(solution)/shard_map/pallas_call | solution.py:196
  26.3 8.4 %all-to-all-start = ((bf16[16,2,128,768]{3,2,1,0:T(8,128)(2,1)}), bf16[16,2,128,768]{3,2,1,0:T(8,128)(2,1)}, u32[]{:S(2)}, u32[]{:S(2)}) async-start(bf16[16,2,128,768]{3,2,1,0:T(8,128)(2,1)} %shard_map.97), calls=%async_computation | async-start | bytes 12582912 | tf_op jit(solution)/shard_map/all_to_all | solution.py:312
  34.8 9.2 %shard_map.95 = bf16[1,512,384]{2,1,0:T(8,128)(2,1)} custom-call(s32[4]{0:T(128)} %pad_add_fusion.1.meta_ref, bf16[512,3072]{1,0:T(8,128)(2,1)} %x_ref.3, bf16[3072]{0:T(1024)(128)(2,1)} %gain_ref.3, f32[1,384]{1,0:T(1,128)} %reshape_tile.5.freq_ref, bf16[3,3072,384]{2,1,0:T(8,128)(2,1)} %bitcast.36), custom_call_target="tpu_custom_call" | custom-call | tf_op jit(solution)/shard_map/pallas_call | solution.py:262
  43.9 34.9 %shard_map.98 = bf16[512,384]{1,0:T(8,128)(2,1)} custom-call(s32[4]{0:T(128)} %pad_add_fusion.1.meta_ref, bf16[512,384]{1,0:T(8,128)(2,1)} %bitcast.39, bf16[2,1,3584,384]{3,2,1,0:T(8,128)(2,1)} %vc_ref.1, bf16[2,1,3584,384]{3,2,1,0:T(8,128)(2,1)} %vc_ref.1, bf16[2,512,384]{2,1,0:T(8,128)(2,1)} %shard_map.96.refs_1_.refs_5_.refs_9_.refs_13_.kn_ref.vn_ref, ...), custom_call_target="tpu_custom_call" | custom-call | tf_op jit(solution)/shard_map/pallas_call | solution.py:124
  78.8 0.0 copy-done
  78.8 2.8 %convolution_convert_fusion = bf16[512,3072]{1,0:T(8,128)(2,1)S(1)} fusion(bf16[512,384]{1,0:T(8,128)(2,1)} %shard_map.98, bf16[384,3072]{1,0:T(8,128)(2,1)S(1)} %copy-done), kind=kOutput, calls=%fused_computation | convolution fusion | flops 1209532416 | bytes 5898240 | tf_op jit(solution)/shard_map/dot_general | solution.py:317
  81.6 0.0 copy-start.2
  81.7 1.6 %copy-done.2 = bf16[512,3072]{1,0:T(8,128)(2,1)} copy-done((bf16[512,3072]{1,0:T(8,128)(2,1)}, bf16[512,3072]{1,0:T(8,128)(2,1)S(1)}, u32[]{:S(2)}) %copy-start.2) | copy-done | bytes 3145752
  83.3 1.3 dynamic-slice_bitcast_fusion
  84.6 0.0 collective-permute-start.2
  84.6 3.7 %collective-permute-done.2 = bf16[4,64,3072]{2,1,0:T(8,128)(2,1)} collective-permute-done((bf16[4,64,3072]{2,1,0:T(8,128)(2,1)}, bf16[4,64,3072]{2,1,0:T(8,128)(2,1)}, u32[]{:S(2)}, u32[]{:S(2)}) %collective-permute-start.2) | collective-permute-done | bytes 1572896 | tf_op jit(solution)/shard_map/ppermute | solution.py:323
  88.3 4.3 %fusion.4 = (bf16[4,64,3072]{2,1,0:T(8,128)(2,1)S(1)}, f32[4,64,3072]{2,1,0:T(8,128)}) fusion(bf16[4,64,3072]{2,1,0:T(8,128)(2,1)} %collective-permute-done.2, bf16[4,2,64,3072]{3,2,1,0:T(8,128)(2,1)} %bitcast.38, s32[]{:T(128)S(6)} %select_n.45), kind=kLoop, calls=%fused_computation.15 | loop fusion | flops 3145728 | bytes 7864324 | tf_op jit(solution)/shard_map/convert_element_type | solution.py:326
  92.6 0.8 dynamic-slice_bitcast_fusion.3
  93.4 1.5 %collective-permute-start.3 = (bf16[64,3072]{1,0:T(8,128)(2,1)}, bf16[64,3072]{1,0:T(8,128)(2,1)S(1)}, u32[]{:S(2)}, u32[]{:S(2)}) collective-permute-start(bf16[64,3072]{1,0:T(8,128)(2,1)} %get-tuple-element.12), channel_id=1, source_target_pairs={{0,2},{2,4},{4,6},{6,0},{1,3},{3,5},{5,7},{7,1},{8,10},{10,12},{12... | collective-permute-start | bytes 1179656 | tf_op jit(solution)/shard_map/ppermute | solution.py:332
  94.9 2.7 %collective-permute-start.4 = (bf16[64,3072]{1,0:T(8,128)(2,1)S(1)}, bf16[64,3072]{1,0:T(8,128)(2,1)}, u32[]{:S(2)}, u32[]{:S(2)}) collective-permute-start(bf16[64,3072]{1,0:T(8,128)(2,1)S(1)} %get-tuple-element.14), channel_id=1, source_target_pairs={{0,4},{2,6},{4,0},{6,2},{1,5},{3,7},{5,1},{7,3},{8,12},{10,14},{12... | collective-permute-start | bytes 1179656 | tf_op jit(solution)/shard_map/ppermute | solution.py:332
  97.6 1.4 %collective-permute-start.5 = (bf16[64,3072]{1,0:T(8,128)(2,1)S(1)}, bf16[64,3072]{1,0:T(8,128)(2,1)}, u32[]{:S(2)}, u32[]{:S(2)}) collective-permute-start(bf16[64,3072]{1,0:T(8,128)(2,1)S(1)} %get-tuple-element.13), channel_id=1, source_target_pairs={{0,6},{2,0},{4,2},{6,4},{1,7},{3,1},{5,3},{7,5},{8,14},{10,8},{12,... | collective-permute-start | bytes 1179656 | tf_op jit(solution)/shard_map/ppermute | solution.py:332
  99.1 6.9 %collective-permute-done.3 = bf16[64,3072]{1,0:T(8,128)(2,1)S(1)} collective-permute-done((bf16[64,3072]{1,0:T(8,128)(2,1)}, bf16[64,3072]{1,0:T(8,128)(2,1)S(1)}, u32[]{:S(2)}, u32[]{:S(2)}) %collective-permute-start.3) | collective-permute-done | bytes 393248 | tf_op jit(solution)/shard_map/ppermute | solution.py:332
  106.0 9.5 %collective-permute-done.4 = bf16[64,3072]{1,0:T(8,128)(2,1)} collective-permute-done((bf16[64,3072]{1,0:T(8,128)(2,1)S(1)}, bf16[64,3072]{1,0:T(8,128)(2,1)}, u32[]{:S(2)}, u32[]{:S(2)}) %collective-permute-start.4) | collective-permute-done | bytes 393248 | tf_op jit(solution)/shard_map/ppermute | solution.py:332
  115.5 0.0 collective-permute-done.5
  115.5 2.4 %fusion.3 = bf16[64,3072]{1,0:T(8,128)(2,1)} fusion(bf16[64,3072]{1,0:T(8,128)(2,1)} %collective-permute-done.5, bf16[64,3072]{1,0:T(8,128)(2,1)} %collective-permute-done.4, bf16[64,3072]{1,0:T(8,128)(2,1)S(1)} %collective-permute-done.3, f32[4,64,3072]{2,1,0:T(8,128)} %get-tuple-element.11, s32[]{:T(128)S(6)} %select_n.47, bf16[512,3072]{1,0:T(8,128)(2,1)} %x_ref.3, ...), kind=kLoop, calls=%fused_computation.7 | loop fusion | flops 1769472 | bytes 2752520 | tf_op jit(solution)/shard_map/convert_element_type | solution.py:334
  118.0 10.4 %all-to-all-done = bf16[16,2,128,768]{3,2,1,0:T(8,128)(2,1)} async-done(((bf16[16,2,128,768]{3,2,1,0:T(8,128)(2,1)}), bf16[16,2,128,768]{3,2,1,0:T(8,128)(2,1)}, u32[]{:S(2)}, u32[]{:S(2)}) %all-to-all-start) | async-done | bytes 6291488 | tf_op jit(solution)/shard_map/all_to_all | solution.py:312
  128.3 6.1 %copy.11 = bf16[2,1,16,1,128,768]{5,4,3,2,1,0:T(8,128)(2,1)} copy(bf16[2,1,16,1,128,768]{5,4,0,2,3,1:T(8,128)(2,1)} %bitcast.14) | data formatting | bytes 12582912
  (2 shorter events, 0.0 us)
Async XLA Ops:
  0.6 78.2 %copy-start = (bf16[384,3072]{1,0:T(8,128)(2,1)S(1)}, bf16[384,3072]{1,0:T(8,128)(2,1)}, u32[]{:S(2)}) copy-start(bf16[384,3072]{1,0:T(8,128)(2,1)} %param.11) | copy-start | bytes 7077892
  0.6 16.4 %collective-permute-start = (bf16[2,1,3584,384]{3,2,1,0:T(8,128)(2,1)}, bf16[2,1,3584,384]{3,2,1,0:T(8,128)(2,1)}, u32[]{:S(2)}, u32[]{:S(2)}) collective-permute-start(bf16[2,1,3584,384]{3,2,1,0:T(8,128)(2,1)} %vc_ref.1), channel_id=1, source_target_pairs={{0,1},{1,0},{2,3},{3,2},{4,5},{5,4},{6,7},{7,6},{8,9},{9,8},{10,11... | collective-permute-start | bytes 16515080 | tf_op jit(solution)/shard_map/ppermute | solution.py:305
  14.4 2.6 %collective-permute-start.1 = (bf16[2,512,384]{2,1,0:T(8,128)(2,1)}, bf16[2,512,384]{2,1,0:T(8,128)(2,1)S(1)}, u32[]{:S(2)}, u32[]{:S(2)}) collective-permute-start(bf16[2,512,384]{2,1,0:T(8,128)(2,1)} %shard_map.96.refs_1_.refs_5_.refs_9_.refs_13_.kn_ref.vn_ref), channel_id=1, source_target_pairs={{0,1},{1,0},{2,3},{3,2},{4,5},{5,4},{6,7},{7,6},{8,9},{9,8},{10,11... | collective-permute-start | bytes 2359304 | tf_op jit(solution)/shard_map/ppermute | solution.py:308
  17.0 0.9 copy-start.1
  26.3 102.0 %all-to-all-start = ((bf16[16,2,128,768]{3,2,1,0:T(8,128)(2,1)}), bf16[16,2,128,768]{3,2,1,0:T(8,128)(2,1)}, u32[]{:S(2)}, u32[]{:S(2)}) async-start(bf16[16,2,128,768]{3,2,1,0:T(8,128)(2,1)} %shard_map.97), calls=%async_computation | async-start | bytes 12582912 | tf_op jit(solution)/shard_map/all_to_all | solution.py:312
  81.6 1.7 %copy-start.2 = (bf16[512,3072]{1,0:T(8,128)(2,1)}, bf16[512,3072]{1,0:T(8,128)(2,1)S(1)}, u32[]{:S(2)}) copy-start(bf16[512,3072]{1,0:T(8,128)(2,1)S(1)} %convolution_convert_fusion) | copy-start | bytes 9437188
  84.6 3.8 %collective-permute-start.2 = (bf16[4,64,3072]{2,1,0:T(8,128)(2,1)}, bf16[4,64,3072]{2,1,0:T(8,128)(2,1)}, u32[]{:S(2)}, u32[]{:S(2)}) collective-permute-start(bf16[4,64,3072]{2,1,0:T(8,128)(2,1)} %dynamic-slice_bitcast_fusion), channel_id=1, source_target_pairs={{0,1},{1,0},{2,3},{3,2},{4,5},{5,4},{6,7},{7,6},{8,9},{9,8},{10,11... | collective-permute-start | bytes 4718600 | tf_op jit(solution)/shard_map/ppermute | solution.py:323
  93.4 12.6 %collective-permute-start.3 = (bf16[64,3072]{1,0:T(8,128)(2,1)}, bf16[64,3072]{1,0:T(8,128)(2,1)S(1)}, u32[]{:S(2)}, u32[]{:S(2)}) collective-permute-start(bf16[64,3072]{1,0:T(8,128)(2,1)} %get-tuple-element.12), channel_id=1, source_target_pairs={{0,2},{2,4},{4,6},{6,0},{1,3},{3,5},{5,7},{7,1},{8,10},{10,12},{12... | collective-permute-start | bytes 1179656 | tf_op jit(solution)/shard_map/ppermute | solution.py:332
  94.9 20.6 %collective-permute-start.4 = (bf16[64,3072]{1,0:T(8,128)(2,1)S(1)}, bf16[64,3072]{1,0:T(8,128)(2,1)}, u32[]{:S(2)}, u32[]{:S(2)}) collective-permute-start(bf16[64,3072]{1,0:T(8,128)(2,1)S(1)} %get-tuple-element.14), channel_id=1, source_target_pairs={{0,4},{2,6},{4,0},{6,2},{1,5},{3,7},{5,1},{7,3},{8,12},{10,14},{12... | collective-permute-start | bytes 1179656 | tf_op jit(solution)/shard_map/ppermute | solution.py:332
  97.6 17.9 %collective-permute-start.5 = (bf16[64,3072]{1,0:T(8,128)(2,1)S(1)}, bf16[64,3072]{1,0:T(8,128)(2,1)}, u32[]{:S(2)}, u32[]{:S(2)}) collective-permute-start(bf16[64,3072]{1,0:T(8,128)(2,1)S(1)} %get-tuple-element.13), channel_id=1, source_target_pairs={{0,6},{2,0},{4,2},{6,4},{1,7},{3,1},{5,3},{7,5},{8,14},{10,8},{12,... | collective-permute-start | bytes 1179656 | tf_op jit(solution)/shard_map/ppermute | solution.py:332

commit v18 on v14

--- a/solution.py
+++ b/solution.py
@@ -167,7 +167,7 @@
     features = kv_cache.shape[3]
     new_blocks = new_kv.shape[1] // BLK
     rank_count = 2 * seq_count
-    per_step = 4 if seq_count % 4 == 0 else 1
+    per_step = 8 if seq_count % 8 == 0 else 1
 
     def block_of(d, slot, m):
         return (2 * (d * per_step + slot) + m[3] - m[2] + rank_count) % rank_count

time: 136 us -> 137 us (level); the launches traced: 135 us -> 138 us
  waiting for transfers between devices: 33.9 us -> 35.3 us
    all_to_all x1, waiting for transfers between devices: 11.7 us -> 13.1 us  [local(): received = lax.all_to_all(joined, 'seq', 0, 0, tiled=True)]
  transfers between devices with their start and end apart: 7 -> 7, of which waited for: 5 -> 5; matrix products, arithmetic and copies ran while one was open for 10% -> 10% of each run, Pallas kernels for 41% -> 40%
where the time goes in v18:
time: 137 us; the launch traced here: 138 us
  Pallas kernels  64.8 us (47%)
  waiting for transfers between devices  35.3 us (26%)
  starting transfers between devices  14.6 us (11%)
  local copies, waits for them, and re-layouts  11.6 us (8%)
  other arithmetic  8.03 us (6%)
  matrix products  2.79 us (2%)
    pallas_call x1, Pallas kernels, attend(): pl.pallas_call(attention_kernel, out_shape=jax.ShapeDtypeStruct(queries.s...  34.9 us
    pallas_call x2, Pallas kernels, project(): pl.pallas_call(functools.partial(projection_kernel, parts=parts), out_sha...  20.9 us
    ppermute x3, waiting for transfers between devices, local(): summed = summed + lax.ppermute(chunk, 'x', pairs).astype(jnp.float32)  16.7 us
    all_to_all x1, waiting for transfers between devices, local(): received = lax.all_to_all(joined, 'seq', 0, 0, tiled=True)  13.1 us
    pallas_call x1, Pallas kernels, relay(): pl.pallas_call(functools.partial(relay_kernel, new_blocks=new_blocks), ou...  9.01 us
    unnamed x7, local copies, waits for them, and re-layouts  8.68 us
    all_to_all x1, starting transfers between devices, local(): received = lax.all_to_all(joined, 'seq', 0, 0, tiled=True)  7.92 us
    ppermute x3, starting transfers between devices, local(): summed = summed + lax.ppermute(chunk, 'x', pairs).astype(jnp.float32)  5.66 us
  transfers between devices with their start and end apart: 7, of which 5 were waited for; matrix products, arithmetic and copies ran while one was open for 10% of the time, Pallas kernels for 40%

profile of v18, /device:TPU:0, one launch (start us, length us, event | category | flops | bytes accessed | tf_op | source)
XLA Modules:
  0.0 137.9 jit_solution(8026144700995294827)
XLA Ops:
  0.6 0.0 copy-start
  0.6 0.1 collective-permute-start
  0.8 0.7 reshape_tile.5.freq_ref
  1.4 0.7 pad_add_fusion
  2.1 0.2 dynamic-slice_reduce_fusion
  2.3 0.6 pad_add_fusion.1.meta_ref
  2.9 11.5 %shard_map.96.refs_1_.refs_5_.refs_9_.refs_13_.refs_17_.refs_21_.refs_25_.refs_29_.kn_ref.vn_ref = bf16[2,512,384]{2,1,0:T(8,128)(2,1)} custom-call(s32[4]{0:T(128)} %pad_add_fusion.1.meta_ref, bf16[512,3072]{1,0:T(8,128)(2,1)} %x_ref.3, bf16[3072]{0:T(1024)(128)(2,1)} %gain_ref.3, f32[1,384]{1,0:T(1,128)} %reshape_tile.5.freq_ref, ...), custom_call_target="tpu_custom_call" | custom-call | tf_op jit(solution)/shard_map/pallas_call | solution.py:262
  14.4 0.5 collective-permute-start.1
  14.9 2.1 %collective-permute-done.1.refs_3_.refs_7_.refs_11_.refs_15_.refs_19_.refs_23_.refs_27_.refs_31_ = bf16[2,512,384]{2,1,0:T(8,128)(2,1)S(1)} collective-permute-done((bf16[2,512,384]{2,1,0:T(8,128)(2,1)}, bf16[2,512,384]{2,1,0:T(8,128)(2,1)S(1)}, u32[]{:S(2)}, u32[]{:S(2)}) %collective-permute-start.1) | collective-permute-done | bytes 786464 | tf_op jit(solution)/shard_map/ppermute | solution.py:308
  17.0 0.0 copy-start.1
  17.0 0.0 collective-permute-done.refs_2_.refs_6_.refs_10_.refs_14_.refs_18_.refs_22_.refs_26_.refs_30_
  17.0 0.9 copy-done.1
  17.9 9.0 %shard_map.97 = bf16[16,2,128,768]{3,2,1,0:T(8,128)(2,1)} custom-call(s32[4]{0:T(128)} %pad_add_fusion.1.meta_ref, bf16[2,1,3584,384]{3,2,1,0:T(8,128)(2,1)} %vc_ref.1, bf16[2,512,384]{2,1,0:T(8,128)(2,1)} %shard_map.96.refs_1_.refs_5_.refs_9_.refs_13_.refs_17_.refs_21_.refs_25_.refs_29_.kn_ref.vn_ref, ...), custom_call_target="tpu_custom_call" | custom-call | tf_op jit(solution)/shard_map/pallas_call | solution.py:196
  26.9 7.9 %all-to-all-start = ((bf16[16,2,128,768]{3,2,1,0:T(8,128)(2,1)}), bf16[16,2,128,768]{3,2,1,0:T(8,128)(2,1)}, u32[]{:S(2)}, u32[]{:S(2)}) async-start(bf16[16,2,128,768]{3,2,1,0:T(8,128)(2,1)} %shard_map.97), calls=%async_computation | async-start | bytes 12582912 | tf_op jit(solution)/shard_map/all_to_all | solution.py:312
  34.8 9.4 %shard_map.95 = bf16[1,512,384]{2,1,0:T(8,128)(2,1)} custom-call(s32[4]{0:T(128)} %pad_add_fusion.1.meta_ref, bf16[512,3072]{1,0:T(8,128)(2,1)} %x_ref.3, bf16[3072]{0:T(1024)(128)(2,1)} %gain_ref.3, f32[1,384]{1,0:T(1,128)} %reshape_tile.5.freq_ref, bf16[3,3072,384]{2,1,0:T(8,128)(2,1)} %bitcast.36), custom_call_target="tpu_custom_call" | custom-call | tf_op jit(solution)/shard_map/pallas_call | solution.py:262
  44.3 34.9 %shard_map.98 = bf16[512,384]{1,0:T(8,128)(2,1)} custom-call(s32[4]{0:T(128)} %pad_add_fusion.1.meta_ref, bf16[512,384]{1,0:T(8,128)(2,1)} %bitcast.39, bf16[2,1,3584,384]{3,2,1,0:T(8,128)(2,1)} %vc_ref.1, bf16[2,1,3584,384]{3,2,1,0:T(8,128)(2,1)} %vc_ref.1, ...), custom_call_target="tpu_custom_call" | custom-call | tf_op jit(solution)/shard_map/pallas_call | solution.py:124
  79.2 0.0 copy-done
  79.2 2.8 %convolution_convert_fusion = bf16[512,3072]{1,0:T(8,128)(2,1)S(1)} fusion(bf16[512,384]{1,0:T(8,128)(2,1)} %shard_map.98, bf16[384,3072]{1,0:T(8,128)(2,1)S(1)} %copy-done), kind=kOutput, calls=%fused_computation | convolution fusion | flops 1209532416 | bytes 5898240 | tf_op jit(solution)/shard_map/dot_general | solution.py:317
  82.0 0.0 copy-start.2
  82.0 1.6 %copy-done.2 = bf16[512,3072]{1,0:T(8,128)(2,1)} copy-done((bf16[512,3072]{1,0:T(8,128)(2,1)}, bf16[512,3072]{1,0:T(8,128)(2,1)S(1)}, u32[]{:S(2)}) %copy-start.2) | copy-done | bytes 3145752
  83.6 1.3 dynamic-slice_bitcast_fusion
  84.9 0.5 collective-permute-start.2
  85.4 3.4 %collective-permute-done.2 = bf16[4,64,3072]{2,1,0:T(8,128)(2,1)} collective-permute-done((bf16[4,64,3072]{2,1,0:T(8,128)(2,1)}, bf16[4,64,3072]{2,1,0:T(8,128)(2,1)}, u32[]{:S(2)}, u32[]{:S(2)}) %collective-permute-start.2) | collective-permute-done | bytes 1572896 | tf_op jit(solution)/shard_map/ppermute | solution.py:323
  88.8 4.3 %fusion.4 = (bf16[4,64,3072]{2,1,0:T(8,128)(2,1)S(1)}, f32[4,64,3072]{2,1,0:T(8,128)}) fusion(bf16[4,64,3072]{2,1,0:T(8,128)(2,1)} %collective-permute-done.2, bf16[4,2,64,3072]{3,2,1,0:T(8,128)(2,1)} %bitcast.38, s32[]{:T(128)S(6)} %select_n.45), kind=kLoop, calls=%fused_computation.15 | loop fusion | flops 3145728 | bytes 7864324 | tf_op jit(solution)/shard_map/convert_element_type | solution.py:326
  93.0 0.8 dynamic-slice_bitcast_fusion.3
  93.9 1.5 %collective-permute-start.3 = (bf16[64,3072]{1,0:T(8,128)(2,1)}, bf16[64,3072]{1,0:T(8,128)(2,1)S(1)}, u32[]{:S(2)}, u32[]{:S(2)}) collective-permute-start(bf16[64,3072]{1,0:T(8,128)(2,1)} %get-tuple-element.12), channel_id=1, source_target_pairs={{0,2},{2,4},{4,6},{6,0},{1,3},{3,5},{5,7},{7,1},{8,10},{10,12},{12... | collective-permute-start | bytes 1179656 | tf_op jit(solution)/shard_map/ppermute | solution.py:332
  95.4 2.7 %collective-permute-start.4 = (bf16[64,3072]{1,0:T(8,128)(2,1)S(1)}, bf16[64,3072]{1,0:T(8,128)(2,1)}, u32[]{:S(2)}, u32[]{:S(2)}) collective-permute-start(bf16[64,3072]{1,0:T(8,128)(2,1)S(1)} %get-tuple-element.14), channel_id=1, source_target_pairs={{0,4},{2,6},{4,0},{6,2},{1,5},{3,7},{5,1},{7,3},{8,12},{10,14},{12... | collective-permute-start | bytes 1179656 | tf_op jit(solution)/shard_map/ppermute | solution.py:332
  98.1 1.4 %collective-permute-start.5 = (bf16[64,3072]{1,0:T(8,128)(2,1)S(1)}, bf16[64,3072]{1,0:T(8,128)(2,1)}, u32[]{:S(2)}, u32[]{:S(2)}) collective-permute-start(bf16[64,3072]{1,0:T(8,128)(2,1)S(1)} %get-tuple-element.13), channel_id=1, source_target_pairs={{0,6},{2,0},{4,2},{6,4},{1,7},{3,1},{5,3},{7,5},{8,14},{10,8},{12,... | collective-permute-start | bytes 1179656 | tf_op jit(solution)/shard_map/ppermute | solution.py:332
  99.5 7.2 %collective-permute-done.3 = bf16[64,3072]{1,0:T(8,128)(2,1)S(1)} collective-permute-done((bf16[64,3072]{1,0:T(8,128)(2,1)}, bf16[64,3072]{1,0:T(8,128)(2,1)S(1)}, u32[]{:S(2)}, u32[]{:S(2)}) %collective-permute-start.3) | collective-permute-done | bytes 393248 | tf_op jit(solution)/shard_map/ppermute | solution.py:332
  106.7 9.5 %collective-permute-done.4 = bf16[64,3072]{1,0:T(8,128)(2,1)} collective-permute-done((bf16[64,3072]{1,0:T(8,128)(2,1)S(1)}, bf16[64,3072]{1,0:T(8,128)(2,1)}, u32[]{:S(2)}, u32[]{:S(2)}) %collective-permute-start.4) | collective-permute-done | bytes 393248 | tf_op jit(solution)/shard_map/ppermute | solution.py:332
  116.2 0.0 collective-permute-done.5
  116.2 2.4 %fusion.3 = bf16[64,3072]{1,0:T(8,128)(2,1)} fusion(bf16[64,3072]{1,0:T(8,128)(2,1)} %collective-permute-done.5, bf16[64,3072]{1,0:T(8,128)(2,1)} %collective-permute-done.4, bf16[64,3072]{1,0:T(8,128)(2,1)S(1)} %collective-permute-done.3, f32[4,64,3072]{2,1,0:T(8,128)} %get-tuple-element.11, s32[]{:T(128)S(6)} %select_n.47, bf16[512,3072]{1,0:T(8,128)(2,1)} %x_ref.3, ...), kind=kLoop, calls=%fused_computation.7 | loop fusion | flops 1769472 | bytes 2752520 | tf_op jit(solution)/shard_map/convert_element_type | solution.py:334
  118.7 13.1 %all-to-all-done = bf16[16,2,128,768]{3,2,1,0:T(8,128)(2,1)} async-done(((bf16[16,2,128,768]{3,2,1,0:T(8,128)(2,1)}), bf16[16,2,128,768]{3,2,1,0:T(8,128)(2,1)}, u32[]{:S(2)}, u32[]{:S(2)}) %all-to-all-start) | async-done | bytes 6291488 | tf_op jit(solution)/shard_map/all_to_all | solution.py:312
  131.8 6.1 %copy.11 = bf16[2,1,16,1,128,768]{5,4,3,2,1,0:T(8,128)(2,1)} copy(bf16[2,1,16,1,128,768]{5,4,0,2,3,1:T(8,128)(2,1)} %bitcast.14) | data formatting | bytes 12582912
  (2 shorter events, 0.0 us)
Async XLA Ops:
  0.6 78.5 %copy-start = (bf16[384,3072]{1,0:T(8,128)(2,1)S(1)}, bf16[384,3072]{1,0:T(8,128)(2,1)}, u32[]{:S(2)}) copy-start(bf16[384,3072]{1,0:T(8,128)(2,1)} %param.11) | copy-start | bytes 7077892
  0.6 16.4 %collective-permute-start = (bf16[2,1,3584,384]{3,2,1,0:T(8,128)(2,1)}, bf16[2,1,3584,384]{3,2,1,0:T(8,128)(2,1)}, u32[]{:S(2)}, u32[]{:S(2)}) collective-permute-start(bf16[2,1,3584,384]{3,2,1,0:T(8,128)(2,1)} %vc_ref.1), channel_id=1, source_target_pairs={{0,1},{1,0},{2,3},{3,2},{4,5},{5,4},{6,7},{7,6},{8,9},{9,8},{10,11... | collective-permute-start | bytes 16515080 | tf_op jit(solution)/shard_map/ppermute | solution.py:305
  14.4 2.6 %collective-permute-start.1 = (bf16[2,512,384]{2,1,0:T(8,128)(2,1)}, bf16[2,512,384]{2,1,0:T(8,128)(2,1)S(1)}, u32[]{:S(2)}, u32[]{:S(2)}) collective-permute-start(bf16[2,512,384]{2,1,0:T(8,128)(2,1)} %shard_map.96.refs_1_.refs_5_.refs_9_.refs_13_.refs_17_.refs_21_.refs_25_.refs_29_.kn_ref.vn_ref), channel_id=1, source_target_pairs={{0,1},{1,0},{2,3},{3,2},{4,5},{5,4},{6,7},{7,6},{8,9},{9,8},{10,11... | collective-permute-start | bytes 2359304 | tf_op jit(solution)/shard_map/ppermute | solution.py:308
  17.0 0.9 copy-start.1
  26.9 104.9 %all-to-all-start = ((bf16[16,2,128,768]{3,2,1,0:T(8,128)(2,1)}), bf16[16,2,128,768]{3,2,1,0:T(8,128)(2,1)}, u32[]{:S(2)}, u32[]{:S(2)}) async-start(bf16[16,2,128,768]{3,2,1,0:T(8,128)(2,1)} %shard_map.97), calls=%async_computation | async-start | bytes 12582912 | tf_op jit(solution)/shard_map/all_to_all | solution.py:312
  82.0 1.7 %copy-start.2 = (bf16[512,3072]{1,0:T(8,128)(2,1)}, bf16[512,3072]{1,0:T(8,128)(2,1)S(1)}, u32[]{:S(2)}) copy-start(bf16[512,3072]{1,0:T(8,128)(2,1)S(1)} %convolution_convert_fusion) | copy-start | bytes 9437188
  84.9 3.9 %collective-permute-start.2 = (bf16[4,64,3072]{2,1,0:T(8,128)(2,1)}, bf16[4,64,3072]{2,1,0:T(8,128)(2,1)}, u32[]{:S(2)}, u32[]{:S(2)}) collective-permute-start(bf16[4,64,3072]{2,1,0:T(8,128)(2,1)} %dynamic-slice_bitcast_fusion), channel_id=1, source_target_pairs={{0,1},{1,0},{2,3},{3,2},{4,5},{5,4},{6,7},{7,6},{8,9},{9,8},{10,11... | collective-permute-start | bytes 4718600 | tf_op jit(solution)/shard_map/ppermute | solution.py:323
  93.9 12.8 %collective-permute-start.3 = (bf16[64,3072]{1,0:T(8,128)(2,1)}, bf16[64,3072]{1,0:T(8,128)(2,1)S(1)}, u32[]{:S(2)}, u32[]{:S(2)}) collective-permute-start(bf16[64,3072]{1,0:T(8,128)(2,1)} %get-tuple-element.12), channel_id=1, source_target_pairs={{0,2},{2,4},{4,6},{6,0},{1,3},{3,5},{5,7},{7,1},{8,10},{10,12},{12... | collective-permute-start | bytes 1179656 | tf_op jit(solution)/shard_map/ppermute | solution.py:332
  95.4 20.8 %collective-permute-start.4 = (bf16[64,3072]{1,0:T(8,128)(2,1)S(1)}, bf16[64,3072]{1,0:T(8,128)(2,1)}, u32[]{:S(2)}, u32[]{:S(2)}) collective-permute-start(bf16[64,3072]{1,0:T(8,128)(2,1)S(1)} %get-tuple-element.14), channel_id=1, source_target_pairs={{0,4},{2,6},{4,0},{6,2},{1,5},{3,7},{5,1},{7,3},{8,12},{10,14},{12... | collective-permute-start | bytes 1179656 | tf_op jit(solution)/shard_map/ppermute | solution.py:332
  98.1 18.1 %collective-permute-start.5 = (bf16[64,3072]{1,0:T(8,128)(2,1)S(1)}, bf16[64,3072]{1,0:T(8,128)(2,1)}, u32[]{:S(2)}, u32[]{:S(2)}) collective-permute-start(bf16[64,3072]{1,0:T(8,128)(2,1)S(1)} %get-tuple-element.13), channel_id=1, source_target_pairs={{0,6},{2,0},{4,2},{6,4},{1,7},{3,1},{5,3},{7,5},{8,14},{10,8},{12,... | collective-permute-start | bytes 1179656 | tf_op jit(solution)/shard_map/ppermute | solution.py:332
